TPU v7x, 32 devices: a whole 2x2x4 slice. The times are simulated.
32 devices in a mesh: dp: 4 (over y, core), seq: 8 (over z, x).
Axes of the slice: x: 2, y: 2, z: 4, core: 2. Of those that a mesh axis runs over, the one named last changes fastest.
Arguments:
- layer_input: bfloat16 [4, 4096, 1024], P('dp', 'seq'), may hold values from -28 to 28
- w_query: bfloat16 [1024, 1024], replicated, may hold values from -0.1875 to 0.1875
- w_key: bfloat16 [1024, 1024], replicated, may hold values from -0.1875 to 0.1875
- w_value: bfloat16 [1024, 1024], replicated, may hold values from -0.1875 to 0.1875
- w_out: bfloat16 [1024, 1024], replicated, may hold values from -0.1875 to 0.1875
- offsets: int32 [3], replicated, may hold values from 0 to 3
- grad_out: bfloat16 [4, 4096, 1024], P('dp', 'seq'), may hold values from -6 to 6
Outputs:
- layer_output: bfloat16 [4, 4096, 1024], P('dp', 'seq')
- grad_x: bfloat16 [4, 4096, 1024], P('dp', 'seq')
- grad_query: float32 [1024, 1024], P('seq')
- grad_key: float32 [1024, 1024], P('seq')
- grad_value: float32 [1024, 1024], P('seq')
- grad_outw: float32 [1024, 1024], P('seq')
All inputs are finite; a program needn't handle non-finite values.
Results may differ from a plain program's by a relative error of at most 0.018.
The roundings to bfloat16 on the way count: a program that leaves them out, or rounds other values in their place, can miss the bound.
Values may be sent and summed in bfloat16 or wider, within the bound.
No kernel may reach another device: no remote copies, remote signals or barrier semaphores. Data moves between devices by JAX's collectives and lax.ppermute only.
A program may use at most 192 MiB of HBM per device.

v0:
```python
import jax
import jax.numpy as jnp
from jax import lax
from jax.sharding import PartitionSpec as P

HEADS = 16
BLOCK = 128


def partner(array, axis, apart):
    return lax.ppermute(array, axis, [(i, i ^ 1 << apart) for i in range(lax.axis_size(axis))])


def swap_blocks(keys_local, values_local, offsets, levels):
    remote = []
    for level in range(levels):
        start = offsets[level] * BLOCK
        pair = jnp.stack(
            [
                lax.dynamic_slice_in_dim(keys_local, start, BLOCK, 0),
                lax.dynamic_slice_in_dim(values_local, start, BLOCK, 0),
            ]
        )
        remote.append(partner(pair, "seq", level))
    return remote


def gradient_terms(sources):
    parts = []
    for left, right in sources:
        parts.append(jnp.dot(left.T, right, preferred_element_type=jnp.float32))
    return jnp.concatenate(parts, axis=1)


def body(layer_input, w_query, w_key, w_value, w_out, offsets, grad_out):
    rows = layer_input[0]
    cot = grad_out[0]
    tok = rows.shape[0]
    width = rows.shape[1]
    head = width // HEADS
    scale = head ** (-0.5)
    levels = lax.axis_size("seq").bit_length() - 1
    query = jnp.dot(rows, w_query, preferred_element_type=jnp.float32).astype(jnp.bfloat16)
    keys_local = jnp.dot(rows, w_key, preferred_element_type=jnp.float32).astype(jnp.bfloat16)
    values_local = jnp.dot(rows, w_value, preferred_element_type=jnp.float32).astype(jnp.bfloat16)
    remote = swap_blocks(keys_local, values_local, offsets, levels)
    all_keys = jnp.concatenate([keys_local] + [piece[0] for piece in remote], 0)
    all_values = jnp.concatenate([values_local] + [piece[1] for piece in remote], 0)
    total_keys = all_keys.shape[0]
    group = min(tok, 512)
    count = tok // group

    def split3(a):
        return a.reshape(a.shape[0], HEADS, head)

    def forward(query_group):
        scores = (
            jnp.einsum(
                "qhe,khe->hqk",
                split3(query_group),
                split3(all_keys),
                preferred_element_type=jnp.float32,
            )
            * scale
        )
        top = jnp.max(scores, axis=-1, keepdims=True)
        lse = top + jnp.log(jnp.sum(jnp.exp(scores - top), axis=-1, keepdims=True))
        prob_b = jnp.exp(scores - lse).astype(jnp.bfloat16)
        attended = jnp.einsum(
            "hqk,khe->qhe", prob_b, split3(all_values), preferred_element_type=jnp.float32
        )
        return (attended.reshape(group, width).astype(jnp.bfloat16), lse)

    query_groups = query.reshape(count, group, width)
    att_groups, lses = lax.map(forward, query_groups)
    attended = att_groups.reshape(tok, width)
    result = jnp.dot(attended, w_out, preferred_element_type=jnp.float32).astype(jnp.bfloat16)
    d_att = jnp.dot(cot, w_out.T, preferred_element_type=jnp.float32).astype(jnp.bfloat16)

    def backward(carry, item):
        query_group, dgroup, lse = item
        scores = (
            jnp.einsum(
                "qhe,khe->hqk",
                split3(query_group),
                split3(all_keys),
                preferred_element_type=jnp.float32,
            )
            * scale
        )
        prob = jnp.exp(scores - lse)
        prob_b = prob.astype(jnp.bfloat16)
        dprob = jnp.einsum(
            "qhe,khe->hqk", split3(dgroup), split3(all_values), preferred_element_type=jnp.float32
        )
        delta = jnp.sum(prob * dprob, axis=-1, keepdims=True)
        dscore = (prob * (dprob - delta) * scale).astype(jnp.bfloat16)
        dquery = jnp.einsum(
            "hqk,khe->qhe", dscore, split3(all_keys), preferred_element_type=jnp.float32
        )
        dkeys = jnp.einsum(
            "hqk,qhe->khe", dscore, split3(query_group), preferred_element_type=jnp.float32
        )
        dvalues = jnp.einsum(
            "hqk,qhe->khe", prob_b, split3(dgroup), preferred_element_type=jnp.float32
        )
        new_carry = (
            carry[0] + dkeys.reshape(total_keys, width),
            carry[1] + dvalues.reshape(total_keys, width),
        )
        return (new_carry, dquery.reshape(group, width).astype(jnp.bfloat16))

    empty = jnp.zeros((total_keys, width), jnp.float32)
    (dk_acc, dv_acc), dq_groups = lax.scan(
        backward, (empty, empty), (query_groups, d_att.reshape(count, group, width), lses)
    )
    dquery = dq_groups.reshape(tok, width)
    dkey_sum = dk_acc[:tok]
    dvalue_sum = dv_acc[:tok]
    for level in range(levels):
        low = tok + level * BLOCK
        piece = jnp.stack([dk_acc[low : low + BLOCK], dv_acc[low : low + BLOCK]])
        returned = partner(piece.astype(jnp.bfloat16), "seq", level).astype(piece.dtype)
        start = offsets[level] * BLOCK
        dkey_sum = lax.dynamic_update_slice_in_dim(
            dkey_sum, lax.dynamic_slice_in_dim(dkey_sum, start, BLOCK, 0) + returned[0], start, 0
        )
        dvalue_sum = lax.dynamic_update_slice_in_dim(
            dvalue_sum,
            lax.dynamic_slice_in_dim(dvalue_sum, start, BLOCK, 0) + returned[1],
            start,
            0,
        )
    dkey = dkey_sum.astype(jnp.bfloat16)
    dvalue = dvalue_sum.astype(jnp.bfloat16)
    total = jnp.dot(dquery, w_query.T, preferred_element_type=jnp.float32)
    total = total + jnp.dot(dkey, w_key.T, preferred_element_type=jnp.float32)
    total = total + jnp.dot(dvalue, w_value.T, preferred_element_type=jnp.float32)
    grad_input = total.astype(jnp.bfloat16)
    sources = ((rows, dquery), (rows, dkey), (rows, dvalue), (attended, cot))
    part = lax.psum_scatter(
        gradient_terms(sources).astype(jnp.bfloat16), "seq", scatter_dimension=0, tiled=True
    )
    summed = lax.psum(part, "dp").astype(jnp.float32)
    return (
        result[None],
        grad_input[None],
        summed[:, :width],
        summed[:, width : 2 * width],
        summed[:, 2 * width : 3 * width],
        summed[:, 3 * width :],
    )


def solution(mesh):
    return jax.shard_map(
        body,
        mesh=mesh,
        in_specs=(P("dp", "seq", None), P(), P(), P(), P(), P(), P("dp", "seq", None)),
        out_specs=(
            P("dp", "seq", None),
            P("dp", "seq", None),
            P("seq", None),
            P("seq", None),
            P("seq", None),
            P("seq", None),
        ),
        check_vma=False,
    )
```

profile of v0, /device:TPU:1, one launch (start us, length us, event | category | flops | bytes accessed | tf_op | source)
XLA Modules:
  0.0 489.2 jit_solution(11821833035171614596)
XLA Ops:
  10.6 3.3 convolution_convert_fusion.4
  21.4 2.3 collective-permute-start.2
  28.0 2.3 convolution_convert_fusion.1
  30.3 2.5 copy.37
  37.9 4.9 %collective-permute-done.1 = bf16[2,128,1024]{2,1,0:T(8,128)(2,1)} collective-permute-done((bf16[2,128,1024]{2,1,0:T(8,128)(2,1)}, bf16[2,128,1024]{2,1,0:T(8,128)(2,1)}, u32[]{:S(2)}, u32[]{:S(2)}) %collective-permute-start.1) | collective-permute-done | bytes 524320 | tf_op jit(solution)/shard_map/ppermute | solution.py:11
  58.5 15.5 %multiply_reduce_fusion.1 = (f32[16,512]{1,0:T(8,128)S(1)}, f32[16,512,896]{2,1,0:T(8,128)}) fusion(bf16[512,16,64]{0,2,1:T(8,128)(2,1)} %bitcast.130, bf16[128,16,64]{0,2,1:T(8,128)(2,1)} %bitcast.144, bf16[128,16,64]{0,2,1:T(8,128)(2,1)} %bitcast.142, bf16[128,16,64]{0,2,1:T(8,128)(2,1)} %bitcast.146, bf16[512,16,64]{0,2,1:T(8,128)(2,1)} %bitcast.132), kind=kOutput, calls=%fused_computation.6 | convolution fusion | flops 961536000 | bytes 32276480 | tf_op jit(solution)/shard_map/while/body/eval_jaxpr/qhe,khe->hqk/dot_general | solution.py:58
  74.0 13.1 %exponential_reduce_fusion = f32[16,512]{1,0:T(8,128)S(1)} fusion(f32[16,512,896]{2,1,0:T(8,128)} %get-tuple-element.101, f32[16,512]{1,0:T(8,128)S(1)} %get-tuple-element.100), kind=kLoop, calls=%fused_computation.5 | loop fusion | flops 22011904 | bytes 29425664 | tf_op jit(solution)/shard_map/while/body/eval_jaxpr/reduce_sum | solution.py:67
  87.2 11.7 %fusion.60 = f32[16,512,896]{2,1,0:T(8,128)} fusion(bf16[512,16,64]{0,2,1:T(8,128)(2,1)S(1)} %bitcast.125, bf16[128,16,64]{0,2,1:T(8,128)(2,1)S(1)} %bitcast.139, bf16[128,16,64]{0,2,1:T(8,128)(2,1)S(1)} %bitcast.136, bf16[128,16,64]{0,2,1:T(8,128)(2,1)S(1)} %bitcast.141, bf16[512,16,64]{0,2,1:T(8,128)(2,1)S(1)} %bitcast.128), kind=kOutput, calls=%fused_computation.72 | convolution fusion | flops 946864128 | bytes 32243712 | tf_op jit(solution)/shard_map/while/body/eval_jaxpr/qhe,khe->hqk/dot_general | solution.py:93
  98.8 60.7 %fusion.29 = bf16[16,64,512]{2,1,0:T(8,128)(2,1)} fusion(f32[16,512,896]{2,1,0:T(8,128)} %fusion.60, f32[16,512,896]{2,1,0:T(8,128)} %get-tuple-element.101, f32[16,512]{1,0:T(8,128)S(1)} %log_add_fusion, bf16[128,16,64]{0,2,1:T(8,128)(2,1)} %bitcast.145, bf16[128,16,64]{0,2,1:T(8,128)(2,1)} %bitcast.143, bf16[128,16,64]{0,2,1:T(8,128)(2,1)} %bitcast.147, ...), kind=kOutput, calls=%fused_computation.31 | convolution fusion | flops 1013457792 | bytes 61636608 | tf_op jit(solution)/shard_map/while/body/eval_jaxpr/hqk,khe->qhe/dot_general | solution.py:98
  159.5 54.9 %fusion.81 = (bf16[896,16,64]{0,2,1:T(8,128)(2,1)}, f32[896,16,64]{0,2,1:T(8,128)}) fusion(bf16[512,16,64]{0,2,1:T(8,128)(2,1)} %bitcast.131, f32[16,512,896]{2,1,0:T(8,128)} %fusion.60, f32[16,512,896]{2,1,0:T(8,128)} %get-tuple-element.101, f32[16,512]{1,0:T(8,128)S(1)} %log_add_fusion), kind=kOutput, calls=%fused_computation.98 | convolution fusion | flops 1006510976 | bytes 65306624 | tf_op jit(solution)/shard_map/while/body/eval_jaxpr/hqk,qhe->khe/dot_general | solution.py:101
  214.4 13.6 %fusion.26 = bf16[16,64,512]{2,1,0:T(8,128)(2,1)} fusion(f32[16,512,896]{2,1,0:T(8,128)} %get-tuple-element.101, f32[16,512]{1,0:T(8,128)S(1)} %log_add_fusion, bf16[128,16,64]{0,2,1:T(8,128)(2,1)} %bitcast.138, bf16[128,16,64]{0,2,1:T(8,128)(2,1)S(1)} %bitcast.137, bf16[128,16,64]{0,2,1:T(8,128)(2,1)} %bitcast.140, bf16[512,16,64]{0,2,1:T(8,128)(2,1)} %bitcast.127), kind=kOutput, calls=%fused_computation.25 | convolution fusion | flops 969408512 | bytes 32276480 | tf_op jit(solution)/shard_map/while/body/eval_jaxpr/hqk,khe->qhe/dot_general | solution.py:69
  228.0 11.8 %fusion.80 = (bf16[896,16,64]{0,2,1:T(8,128)(2,1)S(1)}, f32[896,16,64]{0,2,1:T(8,128)S(1)}) fusion(bf16[512,16,64]{0,2,1:T(8,128)(2,1)S(1)} %bitcast.126, f32[16,512,896]{2,1,0:T(8,128)} %get-tuple-element.101, f32[16,512]{1,0:T(8,128)S(1)} %log_add_fusion), kind=kOutput, calls=%fused_computation.97 | convolution fusion | flops 962461696 | bytes 35946496 | tf_op jit(solution)/shard_map/while/body/eval_jaxpr/hqk,qhe->khe/dot_general | solution.py:104
  242.7 2.5 collective-permute-start.5
  249.7 4.0 collective-permute-done.3
  253.7 12.5 %collective-permute-done.4 = bf16[2,128,1024]{1,2,0:T(8,128)(2,1)S(1)} collective-permute-done((bf16[2,128,1024]{1,2,0:T(8,128)(2,1)S(1)}, bf16[2,128,1024]{1,2,0:T(8,128)(2,1)S(1)}, u32[]{:S(2)}, u32[]{:S(2)}) %collective-permute-start.4) | collective-permute-done | bytes 524320 | tf_op jit(solution)/shard_map/ppermute | solution.py:11
  270.6 4.0 pad_maximum_fusion
  274.6 11.5 %copy.51 = bf16[1024,4096]{1,0:T(8,128)(2,1)} copy(bf16[1024,4096]{0,1:T(8,128)(2,1)} %pad_maximum_fusion) | data formatting | bytes 16777216
  288.5 2.7 fusion.84
  291.2 2.7 fusion.57
  293.9 142.4 %reduce-scatter.4.cloned.1.call-done = bf16[128,4096]{1,0:T(8,128)(2,1)} async-done(((bf16[1024,4096]{1,0:T(8,128)(2,1)}), bf16[128,4096]{1,0:T(8,128)(2,1)}) %reduce-scatter.4.cloned.1.call-update) | async-done | bytes 1048592
  436.2 2.3 copy.52
  438.5 5.8 %fusion.33 = bf16[1,512,1024]{2,1,0:T(8,128)(2,1)} fusion(bf16[1024,1024]{1,0:T(8,128)(2,1)} %param.10, f32[512,1024]{1,0:T(8,128)} %fusion.84, f32[512,1024]{1,0:T(8,128)} %fusion.57, f32[512,1024]{0,1:T(8,128)} %copy-done.1), kind=kOutput, calls=%fused_computation.33 | convolution fusion | flops 1075838976 | bytes 9437184 | tf_op jit(solution)/shard_map/dot_general | solution.py:138
  444.3 29.3 %all-reduce.2.cloned.1.call-done = bf16[128,4096]{0,1:T(8,128)(2,1)} async-done(((bf16[128,4096]{0,1:T(8,128)(2,1)}), bf16[128,4096]{0,1:T(8,128)(2,1)}) %all-reduce.2.cloned.1.call-update) | async-done | bytes 1048592 | tf_op jit(solution)/shard_map/psum | solution.py:144
  473.6 2.3 fusion.75
  (93 shorter events, 54.1 us)
Async XLA Ops:
  7.2 20.9 %copy-start = (bf16[1024,1024]{1,0:T(8,128)(2,1)S(1)}, bf16[1024,1024]{1,0:T(8,128)(2,1)}, u32[]{:S(2)}) copy-start(bf16[1024,1024]{1,0:T(8,128)(2,1)} %param.11) | copy-start | bytes 6291460
  7.2 429.1 %reduce-scatter.4.cloned.1.call-start = ((), (), s32[]{:S(2)}) async-start(), calls=%async_computation.2 | async-start | bytes 9437184
  10.6 3.3 copy-start.8
  10.6 3.3 copy-start.15
  16.2 9.6 %copy-start.10 = (bf16[1024,1024]{1,0:T(8,128)(2,1)S(1)}, bf16[1024,1024]{1,0:T(8,128)(2,1)}, u32[]{:S(2)}) copy-start(bf16[1024,1024]{1,0:T(8,128)(2,1)} %param.8) | copy-start | bytes 6291460
  16.2 9.6 %copy-start.16 = (bf16[1,512,1024]{2,1,0:T(8,128)(2,1)S(1)}, bf16[1,512,1024]{2,1,0:T(8,128)(2,1)}, u32[]{:S(2)}) copy-start(bf16[1,512,1024]{2,1,0:T(8,128)(2,1)} %param.7) | copy-start | bytes 3145732
  18.5 24.4 %collective-permute-start.1 = (bf16[2,128,1024]{2,1,0:T(8,128)(2,1)}, bf16[2,128,1024]{2,1,0:T(8,128)(2,1)}, u32[]{:S(2)}, u32[]{:S(2)}) collective-permute-start(bf16[2,128,1024]{2,1,0:T(8,128)(2,1)} %pad_maximum_fusion.4), channel_id=1, source_target_pairs={{0,2},{1,3},{2,0},{3,1},{4,6},{5,7},{6,4},{7,5},{8,10},{9,11},{10,... | collective-permute-start | bytes 1572872 | tf_op jit(solution)/shard_map/ppermute | solution.py:11
  21.4 26.2 %collective-permute-start.2 = (bf16[2,128,1024]{2,1,0:T(8,128)(2,1)}, bf16[2,128,1024]{2,1,0:T(8,128)(2,1)}, u32[]{:S(2)}, u32[]{:S(2)}) collective-permute-start(bf16[2,128,1024]{2,1,0:T(8,128)(2,1)} %pad_maximum_fusion.5), channel_id=1, source_target_pairs={{0,4},{1,5},{2,6},{3,7},{4,0},{5,1},{6,2},{7,3},{8,12},{9,13},{10,... | collective-permute-start | bytes 1572872 | tf_op jit(solution)/shard_map/ppermute | solution.py:11
  24.6 3.5 copy-start.13
  24.6 28.5 %collective-permute-start = (bf16[2,128,1024]{2,1,0:T(8,128)(2,1)}, bf16[2,128,1024]{2,1,0:T(8,128)(2,1)}, u32[]{:S(2)}, u32[]{:S(2)}) collective-permute-start(bf16[2,128,1024]{2,1,0:T(8,128)(2,1)} %pad_maximum_fusion.3), channel_id=1, source_target_pairs={{0,1},{1,0},{2,3},{3,2},{4,5},{5,4},{6,7},{7,6},{8,9},{9,8},{10,11... | collective-permute-start | bytes 1572872 | tf_op jit(solution)/shard_map/ppermute | solution.py:11
  74.0 13.2 %copy-start.2 = (bf16[512,1024]{0,1:T(8,128)(2,1)S(1)}, bf16[512,1024]{0,1:T(8,128)(2,1)}, u32[]{:S(2)}) copy-start(bf16[512,1024]{0,1:T(8,128)(2,1)} %copy.37) | copy-start | bytes 3145732
  74.0 13.2 %copy-start.6 = (bf16[1,128,1024]{1,2,0:T(8,128)(2,1)S(1)}, bf16[1,128,1024]{1,2,0:T(8,128)(2,1)}, u32[]{:S(2)}) copy-start(bf16[1,128,1024]{1,2,0:T(8,128)(2,1)} %copy.40) | copy-start | bytes 786436
  74.0 13.2 %copy-start.7 = (bf16[1,128,1024]{1,2,0:T(8,128)(2,1)S(1)}, bf16[1,128,1024]{1,2,0:T(8,128)(2,1)}, u32[]{:S(2)}) copy-start(bf16[1,128,1024]{1,2,0:T(8,128)(2,1)} %copy.38) | copy-start | bytes 786436
  239.8 5.5 %copy-start.9 = (f32[896,16,64]{0,2,1:T(8,128)S(1)}, f32[896,16,64]{0,2,1:T(8,128)}, u32[]{:S(2)}) copy-start(f32[896,16,64]{0,2,1:T(8,128)} %get-tuple-element.105) | copy-start | bytes 11010052
  241.4 12.3 %collective-permute-start.3 = (bf16[2,128,1024]{1,2,0:T(8,128)(2,1)S(1)}, bf16[2,128,1024]{1,2,0:T(8,128)(2,1)S(1)}, u32[]{:S(2)}, u32[]{:S(2)}) collective-permute-start(bf16[2,128,1024]{1,2,0:T(8,128)(2,1)S(1)} %pad_maximum_fusion.6), channel_id=1, source_target_pairs={{0,1},{1,0},{2,3},{3,2},{4,5},{5,4},{6,7},{7,6},{8,9},{9,8},{10,11... | collective-permute-start | bytes 1572872 | tf_op jit(solution)/shard_map/ppermute | solution.py:11
  242.6 23.6 %collective-permute-start.4 = (bf16[2,128,1024]{1,2,0:T(8,128)(2,1)S(1)}, bf16[2,128,1024]{1,2,0:T(8,128)(2,1)S(1)}, u32[]{:S(2)}, u32[]{:S(2)}) collective-permute-start(bf16[2,128,1024]{1,2,0:T(8,128)(2,1)S(1)} %pad_maximum_fusion.7), channel_id=1, source_target_pairs={{0,2},{1,3},{2,0},{3,1},{4,6},{5,7},{6,4},{7,5},{8,10},{9,11},{10,... | collective-permute-start | bytes 1572872 | tf_op jit(solution)/shard_map/ppermute | solution.py:11
  242.7 24.2 %collective-permute-start.5 = (bf16[2,128,1024]{1,2,0:T(8,128)(2,1)S(1)}, bf16[2,128,1024]{1,2,0:T(8,128)(2,1)S(1)}, u32[]{:S(2)}, u32[]{:S(2)}) collective-permute-start(bf16[2,128,1024]{1,2,0:T(8,128)(2,1)S(1)} %pad_maximum_fusion.8), channel_id=1, source_target_pairs={{0,4},{1,5},{2,6},{3,7},{4,0},{5,1},{6,2},{7,3},{8,12},{9,13},{10,... | collective-permute-start | bytes 1572872 | tf_op jit(solution)/shard_map/ppermute | solution.py:11
  245.2 1.6 copy-start.14
  267.4 1.9 copy-start.3
  286.2 187.4 %all-reduce.2.cloned.1.call-start = ((), (), s32[]{:S(2)}) async-start(), calls=%async_computation.1 | async-start | bytes 2097152 | tf_op jit(solution)/shard_map/psum | solution.py:144
  286.2 2.3 copy-start.11
  286.2 2.3 copy-start.19
  288.5 2.7 copy-start.4
  288.5 2.7 copy-start.12
  (4 other events, 5.4 us)
Sparse Core Ops, SparseCore 0:
  286.3 149.9 reduce-scatter.3
  438.7 34.7 all-reduce.1
where the time goes:
time: 495 us; the launch traced here: 489 us
  matrix products  197 us (40%)
  waiting for transfers between devices  193 us (39%)
  local copies, waits for them, and re-layouts  52.2 us (11%)
  other arithmetic  21.1 us (4%)
  between operations  16.8 us (3%)
  starting transfers between devices  9.44 us (2%)
    unnamed x3, waiting for transfers between devices  142 us
    dot_general x1, matrix products, backward(): jnp.einsum('hqk,khe->qhe', dscore, split3(all_keys), preferred_element_ty...  60.7 us
    dot_general x1, matrix products, backward(): jnp.einsum('hqk,qhe->khe', dscore, split3(query_group), preferred_element...  54.9 us
    psum x1, waiting for transfers between devices, body(): summed = lax.psum(part, 'dp').astype(jnp.float32)  29.3 us
    unnamed x46, local copies, waits for them, and re-layouts  21.9 us
    ppermute x6, waiting for transfers between devices, partner(): lax.ppermute(array, axis, [(i, i ^ 1 << apart) for i in range(lax.axis_si...  21.4 us
    dot_general x1, matrix products, forward(): jnp.einsum('qhe,khe->hqk', split3(query_group), split3(all_keys), preferr...  15.5 us
    dot_general x1, matrix products, forward(): jnp.einsum('hqk,khe->qhe', prob_b, split3(all_values), preferred_element_...  13.6 us
  transfers between devices with their start and end apart: 8, of which 5 were waited for; matrix products, arithmetic and copies ran while one was open for 8% of the time, Pallas kernels for 0%

commit v1 on v0

v1 whole, which is shorter than its diff:
```python
import functools

import jax
import jax.numpy as jnp
from jax import lax
from jax.experimental import pallas as pl
from jax.experimental.pallas import tpu as pltpu
from jax.sharding import PartitionSpec as P

HEADS = 16
BLOCK = 128
LANES = 128


def partner(array, axis, apart):
    return lax.ppermute(array, axis, [(i, i ^ 1 << apart) for i in range(lax.axis_size(axis))])


def swap_blocks(keys_local, values_local, offsets, levels):
    remote = []
    for level in range(levels):
        start = offsets[level] * BLOCK
        pair = jnp.stack(
            [
                lax.dynamic_slice_in_dim(keys_local, start, BLOCK, 0),
                lax.dynamic_slice_in_dim(values_local, start, BLOCK, 0),
            ]
        )
        remote.append(partner(pair, "seq", level))
    return remote


def attention_kernel(q_ref, k_ref, v_ref, do_ref, att_ref, dq_ref, dk_ref, dv_ref, *, head, scale):
    q = q_ref[...]
    k = k_ref[...]
    v = v_ref[...]
    do = do_ref[...]
    width = q.shape[1]
    lane = lax.broadcasted_iota(jnp.int32, (1, width), 1)
    outs = None
    for j in range(width // head):
        inside = (lane >= j * head) & (lane < (j + 1) * head)
        qm = jnp.where(inside, q * jnp.asarray(scale, q.dtype), jnp.zeros_like(q))
        dom = jnp.where(inside, do, jnp.zeros_like(do))
        s = lax.dot_general(qm, k, (((1,), (1,)), ((), ())), preferred_element_type=jnp.float32)
        top = jnp.max(s, axis=-1, keepdims=True)
        e = jnp.exp(s - top)
        p = e * (1.0 / jnp.sum(e, axis=-1, keepdims=True))
        pb = p.astype(jnp.bfloat16)
        a = jnp.dot(pb, v, preferred_element_type=jnp.float32)
        dp = lax.dot_general(dom, v, (((1,), (1,)), ((), ())), preferred_element_type=jnp.float32)
        delta = jnp.sum(p * dp, axis=-1, keepdims=True)
        ds = (p * (dp - delta) * scale).astype(jnp.bfloat16)
        dq = jnp.dot(ds, k, preferred_element_type=jnp.float32)
        dk = lax.dot_general(ds, q, (((0,), (0,)), ((), ())), preferred_element_type=jnp.float32)
        dv = lax.dot_general(pb, do, (((0,), (0,)), ((), ())), preferred_element_type=jnp.float32)
        if outs is None:
            outs = [a, dq, dk, dv]
        else:
            outs = [jnp.where(inside, new, old) for new, old in zip([a, dq, dk, dv], outs)]
    att_ref[...] = outs[0].astype(att_ref.dtype)
    dq_ref[...] = outs[1].astype(dq_ref.dtype)
    dk_ref[...] = outs[2]
    dv_ref[...] = outs[3]


def attention(query, keys, values, d_att, head):
    tok, width = query.shape
    total = keys.shape[0]
    steps = width // LANES
    qspec = pl.BlockSpec((tok, LANES), lambda i: (0, i))
    kspec = pl.BlockSpec((total, LANES), lambda i: (0, i))
    return pl.pallas_call(
        functools.partial(attention_kernel, head=head, scale=head ** -0.5),
        grid=(steps,),
        in_specs=[qspec, kspec, kspec, qspec],
        out_specs=[qspec, qspec, kspec, kspec],
        out_shape=[
            jax.ShapeDtypeStruct((tok, width), jnp.bfloat16),
            jax.ShapeDtypeStruct((tok, width), jnp.bfloat16),
            jax.ShapeDtypeStruct((total, width), jnp.float32),
            jax.ShapeDtypeStruct((total, width), jnp.float32),
        ],
        compiler_params=pltpu.CompilerParams(vmem_limit_bytes=60 * 1024 * 1024),
        cost_estimate=pl.CostEstimate(
            flops=12 * tok * total * width * (LANES // head),
            transcendentals=tok * total * (width // head),
            bytes_accessed=4 * tok * width + 12 * total * width,
        ),
    )(query, keys, values, d_att)


def gradient_terms(sources):
    parts = []
    for left, right in sources:
        parts.append(jnp.dot(left.T, right, preferred_element_type=jnp.float32))
    return jnp.concatenate(parts, axis=1)


def reduce_gradients(terms):
    n_dp = lax.axis_size("dp")
    half = terms.shape[1] // 2
    core = lax.axis_index("dp") % 2
    mine = lax.dynamic_slice_in_dim(terms, core * half, half, 1)
    other = lax.dynamic_slice_in_dim(terms, (1 - core) * half, half, 1)
    got = lax.ppermute(other.astype(jnp.bfloat16), "dp", [(i, i ^ 1) for i in range(n_dp)])
    summed = (mine + got.astype(jnp.float32)).astype(jnp.bfloat16)
    part = lax.psum_scatter(summed, "seq", scatter_dimension=0, tiled=True)
    if n_dp > 2:
        across = lax.ppermute(part, "dp", [(i, i ^ 2) for i in range(n_dp)])
        part = (part.astype(jnp.float32) + across.astype(jnp.float32)).astype(jnp.bfloat16)
    back = lax.ppermute(part, "dp", [(i, i ^ 1) for i in range(n_dp)])
    first = jnp.where(core == 0, part, back)
    second = jnp.where(core == 0, back, part)
    return jnp.concatenate([first, second], axis=1).astype(jnp.float32)


def body(layer_input, w_query, w_key, w_value, w_out, offsets, grad_out):
    rows = layer_input[0]
    cot = grad_out[0]
    tok = rows.shape[0]
    width = rows.shape[1]
    head = width // HEADS
    levels = lax.axis_size("seq").bit_length() - 1
    query = jnp.dot(rows, w_query, preferred_element_type=jnp.float32).astype(jnp.bfloat16)
    keys_local = jnp.dot(rows, w_key, preferred_element_type=jnp.float32).astype(jnp.bfloat16)
    values_local = jnp.dot(rows, w_value, preferred_element_type=jnp.float32).astype(jnp.bfloat16)
    remote = swap_blocks(keys_local, values_local, offsets, levels)
    all_keys = jnp.concatenate([keys_local] + [piece[0] for piece in remote], 0)
    all_values = jnp.concatenate([values_local] + [piece[1] for piece in remote], 0)
    d_att = jnp.dot(cot, w_out.T, preferred_element_type=jnp.float32).astype(jnp.bfloat16)
    attended, dquery, dk_acc, dv_acc = attention(query, all_keys, all_values, d_att, head)
    result = jnp.dot(attended, w_out, preferred_element_type=jnp.float32).astype(jnp.bfloat16)
    dkey_sum = dk_acc[:tok]
    dvalue_sum = dv_acc[:tok]
    for level in range(levels):
        low = tok + level * BLOCK
        piece = jnp.stack([dk_acc[low : low + BLOCK], dv_acc[low : low + BLOCK]])
        returned = partner(piece.astype(jnp.bfloat16), "seq", level).astype(piece.dtype)
        start = offsets[level] * BLOCK
        dkey_sum = lax.dynamic_update_slice_in_dim(
            dkey_sum, lax.dynamic_slice_in_dim(dkey_sum, start, BLOCK, 0) + returned[0], start, 0
        )
        dvalue_sum = lax.dynamic_update_slice_in_dim(
            dvalue_sum,
            lax.dynamic_slice_in_dim(dvalue_sum, start, BLOCK, 0) + returned[1],
            start,
            0,
        )
    dkey = dkey_sum.astype(jnp.bfloat16)
    dvalue = dvalue_sum.astype(jnp.bfloat16)
    total = jnp.dot(dquery, w_query.T, preferred_element_type=jnp.float32)
    total = total + jnp.dot(dkey, w_key.T, preferred_element_type=jnp.float32)
    total = total + jnp.dot(dvalue, w_value.T, preferred_element_type=jnp.float32)
    grad_input = total.astype(jnp.bfloat16)
    sources = ((rows, dquery), (rows, dkey), (rows, dvalue), (attended, cot))
    summed = reduce_gradients(gradient_terms(sources))
    return (
        result[None],
        grad_input[None],
        summed[:, :width],
        summed[:, width : 2 * width],
        summed[:, 2 * width : 3 * width],
        summed[:, 3 * width :],
    )


def solution(mesh):
    return jax.shard_map(
        body,
        mesh=mesh,
        in_specs=(P("dp", "seq", None), P(), P(), P(), P(), P(), P("dp", "seq", None)),
        out_specs=(
            P("dp", "seq", None),
            P("dp", "seq", None),
            P("seq", None),
            P("seq", None),
            P("seq", None),
            P("seq", None),
        ),
        check_vma=False,
    )
```

time: 495 us -> 286 us (0.58); the launches traced: 489 us -> 285 us
  matrix products: 197 us -> 31.4 us
  waiting for transfers between devices: 193 us -> 122 us
  Pallas kernels: 0 us -> 38 us
  local copies, waits for them, and re-layouts: 52.2 us -> 33.8 us
  starting transfers between devices: 9.44 us -> 19.8 us
    dot_general x6 -> x0, matrix products: 168 us -> none  [the longest x1 60.7 us: backward(): jnp.einsum('hqk,khe->qhe', dscore, split3(all_keys), preferred_element_ty...]
    unnamed x3 -> x2, waiting for transfers between devices: 142 us -> 83.5 us
    pallas_call x0 -> x1, Pallas kernels: none -> 38 us  [attention(): pl.pallas_call(functools.partial(attention_kernel, head=head, scale=head...]
    psum x1 -> x0, waiting for transfers between devices: 29.3 us -> none  [body(): summed = lax.psum(part, 'dp').astype(jnp.float32)]
    slice x11 -> x0, local copies, waits for them, and re-layouts: 17.2 us -> none  [the longest x6 10.3 us: body(): piece[1]]
    ppermute x0 -> x3, waiting for transfers between devices: none -> 14.2 us  [the longest x1 7.13 us: reduce_gradients(): lax.ppermute(other.astype(jnp.bfloat16), 'dp', [(i, i ^ 1) for i in range...]
    reduce_sum x1 -> x0, other arithmetic: 13.1 us -> none  [forward(): lse = top + jnp.log(jnp.sum(jnp.exp(scores - top), axis=-1, keepdims=True))]
    convert_element_type x0 -> x3, other arithmetic: none -> 8.58 us  [the longest x1 8.31 us: reduce_gradients(): summed = (mine + got.astype(jnp.float32)).astype(jnp.bfloat16)]
  transfers between devices with their start and end apart: 8 -> 10, of which waited for: 5 -> 6; matrix products, arithmetic and copies ran while one was open for 8% -> 9% of each run, Pallas kernels for 0% -> 0%
where the time goes in v1:
time: 286 us; the launch traced here: 285 us
  waiting for transfers between devices  122 us (43%)
  Pallas kernels  38 us (13%)
  local copies, waits for them, and re-layouts  33.8 us (12%)
  matrix products  31.4 us (11%)
  other arithmetic  24.1 us (8%)
  starting transfers between devices  19.8 us (7%)
  between operations  16.3 us (6%)
    unnamed x2, waiting for transfers between devices  83.5 us
    pallas_call x1, Pallas kernels, attention(): pl.pallas_call(functools.partial(attention_kernel, head=head, scale=head...  38 us
    ppermute x6, waiting for transfers between devices, partner(): lax.ppermute(array, axis, [(i, i ^ 1 << apart) for i in range(lax.axis_si...  24.3 us
    unnamed x46, local copies, waits for them, and re-layouts  23.4 us
    ppermute x6, starting transfers between devices, partner(): lax.ppermute(array, axis, [(i, i ^ 1 << apart) for i in range(lax.axis_si...  11.3 us
    dot_general x4, matrix products, gradient_terms(): parts.append(jnp.dot(left.T, right, preferred_element_type=jnp.float32))  11.3 us
    convert_element_type x1, other arithmetic, reduce_gradients(): summed = (mine + got.astype(jnp.float32)).astype(jnp.bfloat16)  8.31 us
    ppermute x1, waiting for transfers between devices, reduce_gradients(): lax.ppermute(other.astype(jnp.bfloat16), 'dp', [(i, i ^ 1) for i in range...  7.13 us
  transfers between devices with their start and end apart: 10, of which 6 were waited for; matrix products, arithmetic and copies ran while one was open for 9% of the time, Pallas kernels for 0%

profile of v1, /device:TPU:1, one launch (start us, length us, event | category | flops | bytes accessed | tf_op | source)
XLA Modules:
  0.0 285.4 jit_solution(1458606661025771890)
XLA Ops:
  10.6 4.3 %convolution_convert_fusion.2 = bf16[512,1024]{1,0:T(8,128)(2,1)} fusion(bf16[1024,1024]{1,0:T(8,128)(2,1)} %param.10, bf16[1,512,1024]{2,1,0:T(8,128)(2,1)} %param.7), kind=kOutput, calls=%fused_computation.11 | convolution fusion | flops 1074266112 | bytes 4194304 | tf_op jit(solution)/shard_map/dot_general | solution.py:127
  14.9 2.3 convolution_convert_fusion.3
  19.5 3.1 %collective-permute-start.2 = (bf16[2,128,1024]{2,1,0:T(8,128)(2,1)}, bf16[2,128,1024]{2,1,0:T(8,128)(2,1)}, u32[]{:S(2)}, u32[]{:S(2)}) collective-permute-start(bf16[2,128,1024]{2,1,0:T(8,128)(2,1)} %pad_maximum_fusion.5), channel_id=1, source_target_pairs={{0,4},{1,5},{2,6},{3,7},{4,0},{5,1},{6,2},{7,3},{8,12},{9,13},{10,... | collective-permute-start | bytes 1572872 | tf_op jit(solution)/shard_map/ppermute | solution.py:16
  26.8 2.2 convolution_convert_fusion.4.q_ref
  29.1 2.3 convolution_convert_fusion.1.do_ref
  31.4 14.5 %collective-permute-done.2 = bf16[2,128,1024]{2,1,0:T(8,128)(2,1)} collective-permute-done((bf16[2,128,1024]{2,1,0:T(8,128)(2,1)}, bf16[2,128,1024]{2,1,0:T(8,128)(2,1)}, u32[]{:S(2)}, u32[]{:S(2)}) %collective-permute-start.2) | collective-permute-done | bytes 524320 | tf_op jit(solution)/shard_map/ppermute | solution.py:16
  52.1 38.0 %shard_map.118 = (bf16[512,1024]{1,0:T(8,128)(2,1)}, bf16[512,1024]{1,0:T(8,128)(2,1)}, f32[896,1024]{1,0:T(8,128)}, f32[896,1024]{1,0:T(8,128)}) custom-call(bf16[512,1024]{1,0:T(8,128)(2,1)} %convolution_convert_fusion.4.q_ref, bf16[896,1024]{1,0:T(8,128)(2,1)} %pad_maximum_fusion.1.k_ref, bf16[896,1024]{1,0:T(8,128)(2,1)} %pad_maximum_fusion.2.v_ref, ...), custom_call_target="tpu_custom_call" | custom-call | flops 11274289152 | bytes 13107200 | tf_op jit(solution)/shard_map/pallas_call | solution.py:73
  90.1 2.5 convert.23
  96.3 3.2 %collective-permute-start.5 = (bf16[2,128,1024]{2,1,0:T(8,128)(2,1)S(1)}, bf16[2,128,1024]{2,1,0:T(8,128)(2,1)S(1)}, u32[]{:S(2)}, u32[]{:S(2)}) collective-permute-start(bf16[2,128,1024]{2,1,0:T(8,128)(2,1)S(1)} %pad_maximum_fusion.8), channel_id=1, source_target_pairs={{0,4},{1,5},{2,6},{3,7},{4,0},{5,1},{6,2},{7,3},{8,12},{9,13},{10,... | collective-permute-start | bytes 1572872 | tf_op jit(solution)/shard_map/ppermute | solution.py:16
  99.5 3.3 %fusion.2 = f32[1024,1024]{0,1:T(8,128)} fusion(bf16[512,1024]{1,0:T(8,128)(2,1)S(1)} %copy-done.13, bf16[1,512,1024]{2,1,0:T(8,128)(2,1)S(1)} %copy-done.16), kind=kOutput, calls=%fused_computation.17 | convolution fusion | flops 1073741824 | bytes 6291456 | tf_op jit(solution)/shard_map/dot_general | solution.py:96
  104.3 3.3 %convolution_bitcast_fusion.2 = f32[1024,1024]{0,1:T(8,128)} fusion(bf16[512,1024]{1,0:T(8,128)(2,1)S(1)} %copy-done.12, bf16[1,512,1024]{2,1,0:T(8,128)(2,1)S(1)} %copy-done.6), kind=kOutput, calls=%fused_computation.5 | convolution fusion | flops 1073741824 | bytes 6291456 | tf_op jit(solution)/shard_map/dot_general | solution.py:96
  107.7 9.5 %collective-permute-done.4 = bf16[2,128,1024]{2,1,0:T(8,128)(2,1)S(1)} collective-permute-done((bf16[2,128,1024]{2,1,0:T(8,128)(2,1)S(1)}, bf16[2,128,1024]{2,1,0:T(8,128)(2,1)S(1)}, u32[]{:S(2)}, u32[]{:S(2)}) %collective-permute-start.4) | collective-permute-done | bytes 524320 | tf_op jit(solution)/shard_map/ppermute | solution.py:16
  120.4 3.4 %convolution_bitcast_fusion.1 = f32[1024,1024]{0,1:T(8,128)} fusion(bf16[1,512,1024]{2,1,0:T(8,128)(2,1)S(1)} %copy-done.6, f32[512,1024]{1,0:T(8,128)S(1)} %get-tuple-element.39), kind=kOutput, calls=%fused_computation.4 | convolution fusion | flops 1074266112 | bytes 7340032 | tf_op jit(solution)/shard_map/dot_general | solution.py:96
  123.8 6.2 %pad_maximum_fusion = f32[1024,4096]{0,1:T(8,128)S(1)} fusion(f32[1024,1024]{0,1:T(8,128)} %fusion.2, f32[1024,1024]{0,1:T(8,128)S(1)} %convolution_bitcast_fusion, f32[1024,1024]{0,1:T(8,128)} %convolution_bitcast_fusion.1, f32[1024,1024]{0,1:T(8,128)} %convolution_bitcast_fusion.2), kind=kLoop, calls=%fused_computation | loop fusion | flops 12582912 | bytes 33554432 | tf_op jit(solution)/shard_map/concatenate | solution.py:97
  130.0 5.7 %copy-done.1 = f32[1024,4096]{0,1:T(8,128)} copy-done((f32[1024,4096]{0,1:T(8,128)}, f32[1024,4096]{0,1:T(8,128)S(1)}, u32[]{:S(2)}) %copy-start.1) | copy-done | bytes 16777240
  135.8 2.7 dynamic-slice_convert_fusion
  138.5 5.6 %collective-permute-start.6 = (bf16[1024,2048]{0,1:T(8,128)(2,1)}, bf16[1024,2048]{0,1:T(8,128)(2,1)}, u32[]{:S(2)}, u32[]{:S(2)}) collective-permute-start(bf16[1024,2048]{0,1:T(8,128)(2,1)} %dynamic-slice_convert_fusion), channel_id=1, source_target_pairs={{0,8},{8,0},{16,24},{24,16},{1,9},{9,1},{17,25},{25,17},{2,10},{10... | collective-permute-start | bytes 12582920 | tf_op jit(solution)/shard_map/ppermute | solution.py:106
  144.0 7.1 %collective-permute-done.6 = bf16[1024,2048]{0,1:T(8,128)(2,1)} collective-permute-done((bf16[1024,2048]{0,1:T(8,128)(2,1)}, bf16[1024,2048]{0,1:T(8,128)(2,1)}, u32[]{:S(2)}, u32[]{:S(2)}) %collective-permute-start.6) | collective-permute-done | bytes 4194336 | tf_op jit(solution)/shard_map/ppermute | solution.py:106
  151.2 8.3 %add_convert_fusion = bf16[1024,2048]{0,1:T(8,128)(2,1)} fusion(bf16[1024,2048]{0,1:T(8,128)(2,1)} %collective-permute-done.6, f32[1024,4096]{0,1:T(8,128)} %copy-done.1, s32[]{:T(128)S(6)} %select_n.54), kind=kLoop, calls=%fused_computation.1 | loop fusion | flops 6291456 | bytes 16777220 | tf_op jit(solution)/shard_map/convert_element_type | solution.py:107
  159.5 6.6 %copy.21 = bf16[1024,2048]{1,0:T(8,128)(2,1)} copy(bf16[1024,2048]{0,1:T(8,128)(2,1)} %add_convert_fusion) | data formatting | bytes 8388608
  169.5 83.5 %reduce-scatter.4.cloned.1.call-done = bf16[128,2048]{1,0:T(8,128)(2,1)} async-done(((bf16[1024,2048]{1,0:T(8,128)(2,1)}), bf16[128,2048]{1,0:T(8,128)(2,1)}) %reduce-scatter.4.cloned.1.call-update) | async-done | bytes 524304
  255.5 3.2 %fusion.30 = f32[512,1024]{1,0:T(8,128)S(1)} fusion(bf16[512,1024]{1,0:T(8,128)(2,1)} %get-tuple-element.11, bf16[1024,1024]{1,0:T(8,128)(2,1)} %param.8), kind=kOutput, calls=%fused_computation.78 | convolution fusion | flops 1073741824 | bytes 5242880 | tf_op jit(solution)/shard_map/dot_general | solution.py:152
  260.1 7.1 %collective-permute-done.7 = bf16[128,2048]{0,1:T(8,128)(2,1)S(1)} collective-permute-done((bf16[128,2048]{0,1:T(8,128)(2,1)S(1)}, bf16[128,2048]{0,1:T(8,128)(2,1)S(1)}, u32[]{:S(2)}, u32[]{:S(2)}) %collective-permute-start.7) | collective-permute-done | bytes 524320 | tf_op jit(solution)/shard_map/ppermute | solution.py:110
  268.9 2.3 fusion.1
  (88 shorter events, 38.9 us)
Async XLA Ops:
  7.2 21.9 %copy-start = (bf16[1024,1024]{1,0:T(8,128)(2,1)S(1)}, bf16[1024,1024]{1,0:T(8,128)(2,1)}, u32[]{:S(2)}) copy-start(bf16[1024,1024]{1,0:T(8,128)(2,1)} %param.11) | copy-start | bytes 6291460
  7.2 245.8 %reduce-scatter.4.cloned.1.call-start = ((), (), s32[]{:S(2)}) async-start(), calls=%async_computation.1 | async-start | bytes 4718592
  10.6 4.3 %copy-start.6 = (bf16[1,512,1024]{2,1,0:T(8,128)(2,1)S(1)}, bf16[1,512,1024]{2,1,0:T(8,128)(2,1)}, u32[]{:S(2)}) copy-start(bf16[1,512,1024]{2,1,0:T(8,128)(2,1)} %param.7) | copy-start | bytes 3145732
  10.6 4.3 %copy-start.18 = (bf16[1024,1024]{1,0:T(8,128)(2,1)S(1)}, bf16[1024,1024]{1,0:T(8,128)(2,1)}, u32[]{:S(2)}) copy-start(bf16[1024,1024]{1,0:T(8,128)(2,1)} %param.9) | copy-start | bytes 6291460
  18.7 8.2 %copy-start.17 = (bf16[1024,1024]{1,0:T(8,128)(2,1)S(1)}, bf16[1024,1024]{1,0:T(8,128)(2,1)}, u32[]{:S(2)}) copy-start(bf16[1024,1024]{1,0:T(8,128)(2,1)} %param.8) | copy-start | bytes 6291460
  19.5 26.4 %collective-permute-start.2 = (bf16[2,128,1024]{2,1,0:T(8,128)(2,1)}, bf16[2,128,1024]{2,1,0:T(8,128)(2,1)}, u32[]{:S(2)}, u32[]{:S(2)}) collective-permute-start(bf16[2,128,1024]{2,1,0:T(8,128)(2,1)} %pad_maximum_fusion.5), channel_id=1, source_target_pairs={{0,4},{1,5},{2,6},{3,7},{4,0},{5,1},{6,2},{7,3},{8,12},{9,13},{10,... | collective-permute-start | bytes 1572872 | tf_op jit(solution)/shard_map/ppermute | solution.py:16
  23.5 23.5 %collective-permute-start.1 = (bf16[2,128,1024]{2,1,0:T(8,128)(2,1)}, bf16[2,128,1024]{2,1,0:T(8,128)(2,1)}, u32[]{:S(2)}, u32[]{:S(2)}) collective-permute-start(bf16[2,128,1024]{2,1,0:T(8,128)(2,1)} %pad_maximum_fusion.4), channel_id=1, source_target_pairs={{0,2},{1,3},{2,0},{3,1},{4,6},{5,7},{6,4},{7,5},{8,10},{9,11},{10,... | collective-permute-start | bytes 1572872 | tf_op jit(solution)/shard_map/ppermute | solution.py:16
  25.6 3.5 %copy-start.15 = (bf16[1,512,1024]{2,1,0:T(8,128)(2,1)S(1)}, bf16[1,512,1024]{2,1,0:T(8,128)(2,1)}, u32[]{:S(2)}) copy-start(bf16[1,512,1024]{2,1,0:T(8,128)(2,1)} %param.13) | copy-start | bytes 3145732
  25.6 22.4 %collective-permute-start = (bf16[2,128,1024]{2,1,0:T(8,128)(2,1)}, bf16[2,128,1024]{2,1,0:T(8,128)(2,1)}, u32[]{:S(2)}, u32[]{:S(2)}) collective-permute-start(bf16[2,128,1024]{2,1,0:T(8,128)(2,1)} %pad_maximum_fusion.3), channel_id=1, source_target_pairs={{0,1},{1,0},{2,3},{3,2},{4,5},{5,4},{6,7},{7,6},{8,9},{9,8},{10,11... | collective-permute-start | bytes 1572872 | tf_op jit(solution)/shard_map/ppermute | solution.py:16
  31.4 17.7 %copy-start.10 = (bf16[512,1024]{1,0:T(8,128)(2,1)S(1)}, bf16[512,1024]{1,0:T(8,128)(2,1)}, u32[]{:S(2)}) copy-start(bf16[512,1024]{1,0:T(8,128)(2,1)} %convolution_convert_fusion.3) | copy-start | bytes 3145732
  93.5 5.9 %copy-start.13 = (bf16[512,1024]{1,0:T(8,128)(2,1)S(1)}, bf16[512,1024]{1,0:T(8,128)(2,1)}, u32[]{:S(2)}) copy-start(bf16[512,1024]{1,0:T(8,128)(2,1)} %get-tuple-element.10) | copy-start | bytes 3145732
  93.6 5.9 %copy-start.16 = (bf16[1,512,1024]{2,1,0:T(8,128)(2,1)S(1)}, bf16[1,512,1024]{2,1,0:T(8,128)(2,1)}, u32[]{:S(2)}) copy-start(bf16[1,512,1024]{2,1,0:T(8,128)(2,1)} %param.13) | copy-start | bytes 3145732
  93.7 13.9 %collective-permute-start.3 = (bf16[2,128,1024]{2,1,0:T(8,128)(2,1)S(1)}, bf16[2,128,1024]{2,1,0:T(8,128)(2,1)S(1)}, u32[]{:S(2)}, u32[]{:S(2)}) collective-permute-start(bf16[2,128,1024]{2,1,0:T(8,128)(2,1)S(1)} %pad_maximum_fusion.6), channel_id=1, source_target_pairs={{0,1},{1,0},{2,3},{3,2},{4,5},{5,4},{6,7},{7,6},{8,9},{9,8},{10,11... | collective-permute-start | bytes 1572872 | tf_op jit(solution)/shard_map/ppermute | solution.py:16
  94.8 22.5 %collective-permute-start.4 = (bf16[2,128,1024]{2,1,0:T(8,128)(2,1)S(1)}, bf16[2,128,1024]{2,1,0:T(8,128)(2,1)S(1)}, u32[]{:S(2)}, u32[]{:S(2)}) collective-permute-start(bf16[2,128,1024]{2,1,0:T(8,128)(2,1)S(1)} %pad_maximum_fusion.7), channel_id=1, source_target_pairs={{0,2},{1,3},{2,0},{3,1},{4,6},{5,7},{6,4},{7,5},{8,10},{9,11},{10,... | collective-permute-start | bytes 1572872 | tf_op jit(solution)/shard_map/ppermute | solution.py:16
  96.3 21.7 %collective-permute-start.5 = (bf16[2,128,1024]{2,1,0:T(8,128)(2,1)S(1)}, bf16[2,128,1024]{2,1,0:T(8,128)(2,1)S(1)}, u32[]{:S(2)}, u32[]{:S(2)}) collective-permute-start(bf16[2,128,1024]{2,1,0:T(8,128)(2,1)S(1)} %pad_maximum_fusion.8), channel_id=1, source_target_pairs={{0,4},{1,5},{2,6},{3,7},{4,0},{5,1},{6,2},{7,3},{8,12},{9,13},{10,... | collective-permute-start | bytes 1572872 | tf_op jit(solution)/shard_map/ppermute | solution.py:16
  99.5 3.3 %copy-start.8 = (f32[896,1024]{1,0:T(8,128)S(1)}, f32[896,1024]{1,0:T(8,128)}, u32[]{:S(2)}) copy-start(f32[896,1024]{1,0:T(8,128)} %get-tuple-element.13) | copy-start | bytes 11010052
  130.0 5.8 %copy-start.1 = (f32[1024,4096]{0,1:T(8,128)}, f32[1024,4096]{0,1:T(8,128)S(1)}, u32[]{:S(2)}) copy-start(f32[1024,4096]{0,1:T(8,128)S(1)} %pad_maximum_fusion) | copy-start | bytes 50331652
  138.5 12.7 %collective-permute-start.6 = (bf16[1024,2048]{0,1:T(8,128)(2,1)}, bf16[1024,2048]{0,1:T(8,128)(2,1)}, u32[]{:S(2)}, u32[]{:S(2)}) collective-permute-start(bf16[1024,2048]{0,1:T(8,128)(2,1)} %dynamic-slice_convert_fusion), channel_id=1, source_target_pairs={{0,8},{8,0},{16,24},{24,16},{1,9},{9,1},{17,25},{25,17},{2,10},{10... | collective-permute-start | bytes 12582920 | tf_op jit(solution)/shard_map/ppermute | solution.py:106
  254.3 4.5 %copy-start.5 = (f32[512,1024]{1,0:T(8,128)S(1)}, f32[512,1024]{1,0:T(8,128)}, u32[]{:S(2)}) copy-start(f32[512,1024]{1,0:T(8,128)} %copy-done.4) | copy-start | bytes 6291460
  254.3 4.5 %copy-start.19 = (bf16[1024,1024]{1,0:T(8,128)(2,1)S(1)}, bf16[1024,1024]{1,0:T(8,128)(2,1)}, u32[]{:S(2)}) copy-start(bf16[1024,1024]{1,0:T(8,128)(2,1)} %param.9) | copy-start | bytes 6291460
  254.3 12.9 %collective-permute-start.7 = (bf16[128,2048]{0,1:T(8,128)(2,1)S(1)}, bf16[128,2048]{0,1:T(8,128)(2,1)S(1)}, u32[]{:S(2)}, u32[]{:S(2)}) collective-permute-start(bf16[128,2048]{0,1:T(8,128)(2,1)S(1)} %copy.22), channel_id=1, source_target_pairs={{0,16},{8,24},{16,0},{24,8},{1,17},{9,25},{17,1},{25,9},{2,18},{10... | collective-permute-start | bytes 1572872 | tf_op jit(solution)/shard_map/ppermute | solution.py:110
  258.8 10.1 %copy-start.3 = (f32[512,1024]{1,0:T(8,128)S(1)}, f32[512,1024]{1,0:T(8,128)}, u32[]{:S(2)}) copy-start(f32[512,1024]{1,0:T(8,128)} %copy-done.2) | copy-start | bytes 6291460
  258.8 10.1 %copy-start.11 = (bf16[1024,1024]{1,0:T(8,128)(2,1)S(1)}, bf16[1024,1024]{1,0:T(8,128)(2,1)}, u32[]{:S(2)}) copy-start(bf16[1024,1024]{1,0:T(8,128)(2,1)} %param.10) | copy-start | bytes 6291460
  267.3 3.8 %collective-permute-start.8 = (bf16[128,2048]{0,1:T(8,128)(2,1)S(1)}, bf16[128,2048]{0,1:T(8,128)(2,1)S(1)}, u32[]{:S(2)}, u32[]{:S(2)}) collective-permute-start(bf16[128,2048]{0,1:T(8,128)(2,1)S(1)} %add_convert_fusion.2), channel_id=1, source_target_pairs={{0,8},{8,0},{16,24},{24,16},{1,9},{9,1},{17,25},{25,17},{2,10},{10... | collective-permute-start | bytes 1572872 | tf_op jit(solution)/shard_map/ppermute | solution.py:112
  (6 other events, 10.5 us)
Sparse Core Ops, SparseCore 0:
  166.2 86.7 reduce-scatter.3

commit v2 on v1

--- a/solution.py
+++ b/solution.py
@@ -93,26 +93,72 @@
 def gradient_terms(sources):
     parts = []
     for left, right in sources:
-        parts.append(jnp.dot(left.T, right, preferred_element_type=jnp.float32))
+        parts.append(jnp.dot(left.T, right, preferred_element_type=jnp.float32).astype(jnp.bfloat16))
     return jnp.concatenate(parts, axis=1)
+
+
+def exchange(array, axis, mask):
+    return lax.ppermute(array, axis, [(i, i ^ mask) for i in range(lax.axis_size(axis))])
+
+
+def add_bf16(a, b):
+    return (a.astype(jnp.float32) + b.astype(jnp.float32)).astype(jnp.bfloat16)
+
+
+def halve(data, steps):
+    for kind, axis, mask, bit, at in steps:
+        keep = lax.dynamic_index_in_dim(data, bit, at, keepdims=False)
+        send = lax.dynamic_index_in_dim(data, 1 - bit, at, keepdims=False)
+        data = add_bf16(keep, exchange(send, axis, mask))
+    return data
 
 
 def reduce_gradients(terms):
     n_dp = lax.axis_size("dp")
-    half = terms.shape[1] // 2
-    core = lax.axis_index("dp") % 2
+    n_seq = lax.axis_size("seq")
+    seq_bits = n_seq.bit_length() - 1
+    dp_bits = n_dp.bit_length() - 1
+    rows, width = terms.shape
+    half = width // 2
+    blk = rows // n_seq
+    dp_i = lax.axis_index("dp")
+    seq_i = lax.axis_index("seq")
+    core = dp_i % 2
     mine = lax.dynamic_slice_in_dim(terms, core * half, half, 1)
     other = lax.dynamic_slice_in_dim(terms, (1 - core) * half, half, 1)
-    got = lax.ppermute(other.astype(jnp.bfloat16), "dp", [(i, i ^ 1) for i in range(n_dp)])
-    summed = (mine + got.astype(jnp.float32)).astype(jnp.bfloat16)
-    part = lax.psum_scatter(summed, "seq", scatter_dimension=0, tiled=True)
-    if n_dp > 2:
-        across = lax.ppermute(part, "dp", [(i, i ^ 2) for i in range(n_dp)])
-        part = (part.astype(jnp.float32) + across.astype(jnp.float32)).astype(jnp.bfloat16)
-    back = lax.ppermute(part, "dp", [(i, i ^ 1) for i in range(n_dp)])
-    first = jnp.where(core == 0, part, back)
-    second = jnp.where(core == 0, back, part)
-    return jnp.concatenate([first, second], axis=1).astype(jnp.float32)
+    summed = add_bf16(mine, exchange(other, "dp", 1))
+    dims = [("seq", 0)] + [("dp", b) for b in range(1, dp_bits)] + [("seq", b) for b in range(1, seq_bits)]
+    first = dims[:3]
+    n_parts = len(first)
+    cuts = [(half // LANES) * p // n_parts * LANES for p in range(n_parts + 1)]
+    pieces = []
+    for p in range(n_parts):
+        order = first[p:] + first[:p] + dims[3:]
+        data = summed[:, cuts[p] : cuts[p + 1]]
+        data = data.reshape([2] * seq_bits + [2] * (dp_bits - 1) + [blk >> (dp_bits - 1), cuts[p + 1] - cuts[p]])
+        steps = []
+        removed = []
+        for axis, b in order:
+            if axis == "seq":
+                at = seq_bits - 1 - b
+                bit = (seq_i >> b) % 2
+            else:
+                at = seq_bits + (dp_bits - 1 - b)
+                bit = (dp_i >> b) % 2
+            shift = sum(1 for r in removed if r < at)
+            removed.append(at)
+            steps.append((axis, axis, 1 << b, bit, at - shift))
+        data = halve(data, steps)
+        for b in range(1, dp_bits):
+            got = exchange(data, "dp", 1 << b)
+            low = (dp_i >> b) % 2 == 0
+            data = jnp.where(low, jnp.concatenate([data, got], 0), jnp.concatenate([got, data], 0))
+        pieces.append(data)
+    part = jnp.concatenate(pieces, axis=1)
+    back = exchange(part, "dp", 1)
+    low = core == 0
+    result = jnp.where(low, jnp.concatenate([part, back], 1), jnp.concatenate([back, part], 1))
+    return result.astype(jnp.float32)
 
 
 def body(layer_input, w_query, w_key, w_value, w_out, offsets, grad_out):

time: 286 us -> 221 us (0.77)
  waiting for transfers between devices: 122 us -> 63.5 us
  starting transfers between devices: 19.8 us -> 36.3 us
  between operations: 16.3 us -> 3.14 us
  other arithmetic: 24.1 us -> 17.7 us
  matrix products: 31.4 us -> 26 us
    unnamed x2 -> x0, waiting for transfers between devices: 83.5 us -> none
    ppermute x3 -> x17, waiting for transfers between devices: 14.2 us -> 33.9 us  [exchange(): lax.ppermute(array, axis, [(i, i ^ mask) for i in range(lax.axis_size(axi...]
    unnamed x46 -> x50, local copies, waits for them, and re-layouts: 23.4 us -> 6.13 us
    ppermute x3 -> x17, starting transfers between devices: 8.42 us -> 25 us  [exchange(): lax.ppermute(array, axis, [(i, i ^ mask) for i in range(lax.axis_size(axi...]
    slice x0 -> x5, local copies, waits for them, and re-layouts: none -> 10.7 us  [reduce_gradients(): data = summed[:, cuts[p]:cuts[p + 1]]]
    dynamic_slice x0 -> x3, local copies, waits for them, and re-layouts: none -> 6.08 us  [the longest x1 2.69 us: reduce_gradients(): other = lax.dynamic_slice_in_dim(terms, (1 - core) * half, half, 1)]
    dot_general x4, matrix products: 11.3 us -> 5.26 us  [gradient_terms(): jnp.dot(left.T, right, preferred_element_type=jnp.float32)]
    ppermute x6, waiting for transfers between devices: 24.3 us -> 29.5 us  [partner(): lax.ppermute(array, axis, [(i, i ^ 1 << apart) for i in range(lax.axis_si...]
  transfers between devices with their start and end apart: 10 -> 23, of which waited for: 6 -> 13; matrix products, arithmetic and copies ran while one was open for 9% -> 16% of each run, Pallas kernels for 0% -> 0%
where the time goes in v2:
time: 221 us; the launch traced here: 220 us
  waiting for transfers between devices  63.5 us (29%)
  Pallas kernels  38.1 us (17%)
  starting transfers between devices  36.3 us (16%)
  local copies, waits for them, and re-layouts  35.8 us (16%)
  matrix products  26 us (12%)
  other arithmetic  17.7 us (8%)
  between operations  3.14 us (1%)
    pallas_call x1, Pallas kernels, attention(): pl.pallas_call(functools.partial(attention_kernel, head=head, scale=head...  38.1 us
    ppermute x17, waiting for transfers between devices, exchange(): lax.ppermute(array, axis, [(i, i ^ mask) for i in range(lax.axis_size(axi...  33.9 us
    ppermute x6, waiting for transfers between devices, partner(): lax.ppermute(array, axis, [(i, i ^ 1 << apart) for i in range(lax.axis_si...  29.5 us
    ppermute x17, starting transfers between devices, exchange(): lax.ppermute(array, axis, [(i, i ^ mask) for i in range(lax.axis_size(axi...  25 us
    ppermute x6, starting transfers between devices, partner(): lax.ppermute(array, axis, [(i, i ^ 1 << apart) for i in range(lax.axis_si...  11.3 us
    slice x5, local copies, waits for them, and re-layouts, reduce_gradients(): data = summed[:, cuts[p]:cuts[p + 1]]  10.7 us
    convert_element_type x13, other arithmetic, add_bf16(): return (a.astype(jnp.float32) + b.astype(jnp.float32)).astype(jnp.bfloat16)  8.89 us
    unnamed x50, local copies, waits for them, and re-layouts  6.13 us
  transfers between devices with their start and end apart: 23, of which 13 were waited for; matrix products, arithmetic and copies ran while one was open for 16% of the time, Pallas kernels for 0%

profile of v2, /device:TPU:1, one launch (start us, length us, event | category | flops | bytes accessed | tf_op | source)
XLA Modules:
  0.0 220.5 jit_solution(11412943356211204854)
XLA Ops:
  4.0 3.3 %convolution_convert_fusion.3 = bf16[512,1024]{1,0:T(8,128)(2,1)S(1)} fusion(bf16[1024,1024]{1,0:T(8,128)(2,1)} %param.10, bf16[1,512,1024]{2,1,0:T(8,128)(2,1)} %param.7), kind=kOutput, calls=%fused_computation.13 | convolution fusion | flops 1074266112 | bytes 4194304 | tf_op jit(solution)/shard_map/dot_general | solution.py:173
  11.7 3.1 %collective-permute-start.2 = (bf16[2,128,1024]{2,1,0:T(8,128)(2,1)}, bf16[2,128,1024]{2,1,0:T(8,128)(2,1)}, u32[]{:S(2)}, u32[]{:S(2)}) collective-permute-start(bf16[2,128,1024]{2,1,0:T(8,128)(2,1)} %pad_maximum_fusion.5), channel_id=1, source_target_pairs={{0,4},{1,5},{2,6},{3,7},{4,0},{5,1},{6,2},{7,3},{8,12},{9,13},{10,... | collective-permute-start | bytes 1572872 | tf_op jit(solution)/shard_map/ppermute | solution.py:16
  23.6 14.5 %collective-permute-done.2 = bf16[2,128,1024]{2,1,0:T(8,128)(2,1)} collective-permute-done((bf16[2,128,1024]{2,1,0:T(8,128)(2,1)}, bf16[2,128,1024]{2,1,0:T(8,128)(2,1)}, u32[]{:S(2)}, u32[]{:S(2)}) %collective-permute-start.2) | collective-permute-done | bytes 524320 | tf_op jit(solution)/shard_map/ppermute | solution.py:16
  44.2 38.1 %shard_map.118 = (bf16[512,1024]{1,0:T(8,128)(2,1)}, bf16[512,1024]{1,0:T(8,128)(2,1)}, f32[896,1024]{1,0:T(8,128)}, f32[896,1024]{1,0:T(8,128)}) custom-call(bf16[512,1024]{1,0:T(8,128)(2,1)} %convolution_convert_fusion.5.q_ref, bf16[896,1024]{1,0:T(8,128)(2,1)} %pad_maximum_fusion.1.k_ref, bf16[896,1024]{1,0:T(8,128)(2,1)} %pad_maximum_fusion.2.v_ref, ...), custom_call_target="tpu_custom_call" | custom-call | flops 11274289152 | bytes 13107200 | tf_op jit(solution)/shard_map/pallas_call | solution.py:73
  90.2 3.2 %collective-permute-start.5 = (bf16[2,128,1024]{2,1,0:T(8,128)(2,1)S(1)}, bf16[2,128,1024]{2,1,0:T(8,128)(2,1)S(1)}, u32[]{:S(2)}, u32[]{:S(2)}) collective-permute-start(bf16[2,128,1024]{2,1,0:T(8,128)(2,1)S(1)} %pad_maximum_fusion.8), channel_id=1, source_target_pairs={{0,4},{1,5},{2,6},{3,7},{4,0},{5,1},{6,2},{7,3},{8,12},{9,13},{10,... | collective-permute-start | bytes 1572872 | tf_op jit(solution)/shard_map/ppermute | solution.py:16
  96.2 3.6 %collective-permute-done.3 = bf16[2,128,1024]{2,1,0:T(8,128)(2,1)S(1)} collective-permute-done((bf16[2,128,1024]{2,1,0:T(8,128)(2,1)S(1)}, bf16[2,128,1024]{2,1,0:T(8,128)(2,1)S(1)}, u32[]{:S(2)}, u32[]{:S(2)}) %collective-permute-start.3) | collective-permute-done | bytes 524320 | tf_op jit(solution)/shard_map/ppermute | solution.py:16
  99.9 11.3 %collective-permute-done.4 = bf16[2,128,1024]{2,1,0:T(8,128)(2,1)S(1)} collective-permute-done((bf16[2,128,1024]{2,1,0:T(8,128)(2,1)S(1)}, bf16[2,128,1024]{2,1,0:T(8,128)(2,1)S(1)}, u32[]{:S(2)}, u32[]{:S(2)}) %collective-permute-start.4) | collective-permute-done | bytes 524320 | tf_op jit(solution)/shard_map/ppermute | solution.py:16
  117.0 2.7 %constant_dynamic-slice_fusion.2 = bf16[1024,2048]{0,1:T(8,128)(2,1)} fusion(bf16[1024,4096]{0,1:T(8,128)(2,1)S(1)} %pad_maximum_fusion, s32[]{:T(128)S(6)} %select_n.161), kind=kLoop, calls=%fused_computation.116 | loop fusion | bytes 8388612 | tf_op jit(solution)/shard_map/dynamic_slice | solution.py:128
  121.5 5.6 %collective-permute-start.6 = (bf16[1024,2048]{0,1:T(8,128)(2,1)}, bf16[1024,2048]{0,1:T(8,128)(2,1)}, u32[]{:S(2)}, u32[]{:S(2)}) collective-permute-start(bf16[1024,2048]{0,1:T(8,128)(2,1)} %constant_dynamic-slice_fusion.2), channel_id=1, source_target_pairs={{0,8},{8,0},{16,24},{24,16},{1,9},{9,1},{17,25},{25,17},{2,10},{10... | collective-permute-start | bytes 12582920 | tf_op jit(solution)/shard_map/ppermute | solution.py:101
  129.3 4.9 %collective-permute-done.6 = bf16[1024,2048]{0,1:T(8,128)(2,1)} collective-permute-done((bf16[1024,2048]{0,1:T(8,128)(2,1)}, bf16[1024,2048]{0,1:T(8,128)(2,1)}, u32[]{:S(2)}, u32[]{:S(2)}) %collective-permute-start.6) | collective-permute-done | bytes 4194336 | tf_op jit(solution)/shard_map/ppermute | solution.py:101
  134.2 5.6 %add_convert_fusion = bf16[1024,2048]{0,1:T(8,128)(2,1)S(1)} fusion(bf16[1024,2048]{0,1:T(8,128)(2,1)} %collective-permute-done.6, bf16[1024,4096]{0,1:T(8,128)(2,1)} %copy-done.1, s32[]{:T(128)S(6)} %select_n.160), kind=kLoop, calls=%fused_computation.1 | loop fusion | flops 8388608 | bytes 12582916 | tf_op jit(solution)/shard_map/convert_element_type | solution.py:105
  142.2 2.4 %copy.20 = bf16[1024,640]{1,0:T(8,128)(2,1)} copy(bf16[1024,640]{0,1:T(8,128)(2,1)} %get-tuple-element.15) | data formatting | bytes 2621440 | tf_op jit(solution)/shard_map/slice | solution.py:137
  144.6 2.5 %constant_dynamic-slice_fusion.1 = (bf16[2,2,2,1,64,640]{5,4,3,2,1,0:T(8,128)(2,1)}, bf16[2,2,2,1,64,640]{5,4,3,2,1,0:T(8,128)(2,1)S(1)}) fusion(bf16[2,2,2,2,64,640]{5,4,3,2,1,0:T(8,128)(2,1)} %bitcast.185, s32[]{:T(128)S(6)} %select_n.165, s32[]{:T(128)S(6)} %select_n.166), kind=kLoop, calls=%fused_computation.115 | loop fusion | bytes 2621448 | tf_op jit(solution)/shard_map/jit(dynamic_index_in_dim)/dynamic_slice | solution.py:110
  149.2 2.6 %fusion.43 = f32[512,1024]{1,0:T(8,128)} fusion(bf16[512,1024]{1,0:T(8,128)(2,1)S(1)} %copy-done.24, bf16[1024,1024]{1,0:T(8,128)(2,1)S(1)} %copy-done.15), kind=kOutput, calls=%fused_computation.120 | convolution fusion | flops 1073741824 | bytes 5242880 | tf_op jit(solution)/shard_map/dot_general | solution.py:198
  151.9 2.8 %slice.149 = bf16[1024,768]{0,1:T(8,128)(2,1)} slice(bf16[1024,2048]{0,1:T(8,128)(2,1)} %copy-done.2), slice={[0:1024], [1280:2048]} | slice | bytes 3145728 | tf_op jit(solution)/shard_map/slice | solution.py:137
  154.7 2.6 %copy.23 = bf16[1024,768]{1,0:T(8,128)(2,1)} copy(bf16[1024,768]{0,1:T(8,128)(2,1)} %slice.149) | data formatting | bytes 3145728 | tf_op jit(solution)/shard_map/slice | solution.py:137
  162.2 3.5 %fusion.32 = f32[512,1024]{1,0:T(8,128)S(1)} fusion(bf16[1024,1024]{1,0:T(8,128)(2,1)} %param.9, f32[512,1024]{1,0:T(8,128)} %copy-done.7), kind=kOutput, calls=%fused_computation.70 | convolution fusion | flops 1074266112 | bytes 6291456 | tf_op jit(solution)/shard_map/dot_general | solution.py:199
  168.7 8.7 %collective-permute-done.7 = bf16[2,2,2,64,640]{4,3,2,1,0:T(8,128)(2,1)S(1)} collective-permute-done((bf16[2,2,2,64,640]{4,3,2,1,0:T(8,128)(2,1)S(1)}, bf16[2,2,2,64,640]{4,3,2,1,0:T(8,128)(2,1)S(1)}, u32[]{:S(2)}, u32[]{:S(2)}) %collective-permute-start.7) | collective-permute-done | bytes 655392 | tf_op jit(solution)/shard_map/ppermute | solution.py:101
  179.7 5.2 %collective-permute-done.13 = bf16[2,2,64,640]{3,2,0,1:T(8,128)(2,1)S(1)} collective-permute-done((bf16[2,2,64,640]{3,2,0,1:T(8,128)(2,1)S(1)}, bf16[2,2,64,640]{3,2,0,1:T(8,128)(2,1)S(1)}, u32[]{:S(2)}, u32[]{:S(2)}) %collective-permute-start.13) | collective-permute-done | bytes 327712 | tf_op jit(solution)/shard_map/ppermute | solution.py:101
  186.8 4.7 %collective-permute-done.14 = bf16[2,64,640]{2,1,0:T(8,128)(2,1)S(1)} collective-permute-done((bf16[2,64,640]{2,1,0:T(8,128)(2,1)S(1)}, bf16[2,64,640]{2,1,0:T(8,128)(2,1)S(1)}, u32[]{:S(2)}, u32[]{:S(2)}) %collective-permute-start.14) | collective-permute-done | bytes 163872 | tf_op jit(solution)/shard_map/ppermute | solution.py:101
  191.5 2.4 %collective-permute-start.15 = (bf16[64,640]{1,0:T(8,128)(2,1)S(1)}, bf16[64,640]{1,0:T(8,128)(2,1)S(1)}, u32[]{:S(2)}, u32[]{:S(2)}) collective-permute-start(bf16[64,640]{1,0:T(8,128)(2,1)S(1)} %dynamic-slice_bitcast_fusion.15), channel_id=1, source_target_pairs={{0,4},{1,5},{2,6},{3,7},{4,0},{5,1},{6,2},{7,3},{8,12},{9,13},{10,... | collective-permute-start | bytes 245768 | tf_op jit(solution)/shard_map/ppermute | solution.py:101
  201.7 4.6 %collective-permute-done.20 = bf16[64,768]{1,0:T(8,128)(2,1)S(1)} collective-permute-done((bf16[64,768]{1,0:T(8,128)(2,1)S(1)}, bf16[64,768]{1,0:T(8,128)(2,1)S(1)}, u32[]{:S(2)}, u32[]{:S(2)}) %collective-permute-start.20) | collective-permute-done | bytes 98336 | tf_op jit(solution)/shard_map/ppermute | solution.py:101
  206.9 3.2 %collective-permute-done.21 = bf16[64,768]{1,0:T(8,128)(2,1)S(1)} collective-permute-done((bf16[64,768]{1,0:T(8,128)(2,1)S(1)}, bf16[64,768]{1,0:T(8,128)(2,1)S(1)}, u32[]{:S(2)}, u32[]{:S(2)}) %collective-permute-start.21) | collective-permute-done | bytes 98336 | tf_op jit(solution)/shard_map/ppermute | solution.py:101
  210.3 6.3 %collective-permute-start.22 = (bf16[128,2048]{1,0:T(8,128)(2,1)S(1)}, bf16[128,2048]{1,0:T(8,128)(2,1)S(1)}, u32[]{:S(2)}, u32[]{:S(2)}) collective-permute-start(bf16[128,2048]{1,0:T(8,128)(2,1)S(1)} %pad_maximum_fusion.9), channel_id=1, source_target_pairs={{0,8},{8,0},{16,24},{24,16},{1,9},{9,1},{17,25},{25,17},{2,10},{10... | collective-permute-start | bytes 1572872 | tf_op jit(solution)/shard_map/ppermute | solution.py:101
  (149 shorter events, 70.0 us)
Async XLA Ops:
  11.7 26.4 %collective-permute-start.2 = (bf16[2,128,1024]{2,1,0:T(8,128)(2,1)}, bf16[2,128,1024]{2,1,0:T(8,128)(2,1)}, u32[]{:S(2)}, u32[]{:S(2)}) collective-permute-start(bf16[2,128,1024]{2,1,0:T(8,128)(2,1)} %pad_maximum_fusion.5), channel_id=1, source_target_pairs={{0,4},{1,5},{2,6},{3,7},{4,0},{5,1},{6,2},{7,3},{8,12},{9,13},{10,... | collective-permute-start | bytes 1572872 | tf_op jit(solution)/shard_map/ppermute | solution.py:16
  15.7 23.5 %collective-permute-start.1 = (bf16[2,128,1024]{2,1,0:T(8,128)(2,1)}, bf16[2,128,1024]{2,1,0:T(8,128)(2,1)}, u32[]{:S(2)}, u32[]{:S(2)}) collective-permute-start(bf16[2,128,1024]{2,1,0:T(8,128)(2,1)} %pad_maximum_fusion.4), channel_id=1, source_target_pairs={{0,2},{1,3},{2,0},{3,1},{4,6},{5,7},{6,4},{7,5},{8,10},{9,11},{10,... | collective-permute-start | bytes 1572872 | tf_op jit(solution)/shard_map/ppermute | solution.py:16
  17.8 22.4 %collective-permute-start = (bf16[2,128,1024]{2,1,0:T(8,128)(2,1)}, bf16[2,128,1024]{2,1,0:T(8,128)(2,1)}, u32[]{:S(2)}, u32[]{:S(2)}) collective-permute-start(bf16[2,128,1024]{2,1,0:T(8,128)(2,1)} %pad_maximum_fusion.3), channel_id=1, source_target_pairs={{0,1},{1,0},{2,3},{3,2},{4,5},{5,4},{6,7},{7,6},{8,9},{9,8},{10,11... | collective-permute-start | bytes 1572872 | tf_op jit(solution)/shard_map/ppermute | solution.py:16
  87.6 12.2 %collective-permute-start.3 = (bf16[2,128,1024]{2,1,0:T(8,128)(2,1)S(1)}, bf16[2,128,1024]{2,1,0:T(8,128)(2,1)S(1)}, u32[]{:S(2)}, u32[]{:S(2)}) collective-permute-start(bf16[2,128,1024]{2,1,0:T(8,128)(2,1)S(1)} %pad_maximum_fusion.6), channel_id=1, source_target_pairs={{0,1},{1,0},{2,3},{3,2},{4,5},{5,4},{6,7},{7,6},{8,9},{9,8},{10,11... | collective-permute-start | bytes 1572872 | tf_op jit(solution)/shard_map/ppermute | solution.py:16
  88.7 22.5 %collective-permute-start.4 = (bf16[2,128,1024]{2,1,0:T(8,128)(2,1)S(1)}, bf16[2,128,1024]{2,1,0:T(8,128)(2,1)S(1)}, u32[]{:S(2)}, u32[]{:S(2)}) collective-permute-start(bf16[2,128,1024]{2,1,0:T(8,128)(2,1)S(1)} %pad_maximum_fusion.7), channel_id=1, source_target_pairs={{0,2},{1,3},{2,0},{3,1},{4,6},{5,7},{6,4},{7,5},{8,10},{9,11},{10,... | collective-permute-start | bytes 1572872 | tf_op jit(solution)/shard_map/ppermute | solution.py:16
  90.2 21.7 %collective-permute-start.5 = (bf16[2,128,1024]{2,1,0:T(8,128)(2,1)S(1)}, bf16[2,128,1024]{2,1,0:T(8,128)(2,1)S(1)}, u32[]{:S(2)}, u32[]{:S(2)}) collective-permute-start(bf16[2,128,1024]{2,1,0:T(8,128)(2,1)S(1)} %pad_maximum_fusion.8), channel_id=1, source_target_pairs={{0,4},{1,5},{2,6},{3,7},{4,0},{5,1},{6,2},{7,3},{8,12},{9,13},{10,... | collective-permute-start | bytes 1572872 | tf_op jit(solution)/shard_map/ppermute | solution.py:16
  121.5 12.7 %collective-permute-start.6 = (bf16[1024,2048]{0,1:T(8,128)(2,1)}, bf16[1024,2048]{0,1:T(8,128)(2,1)}, u32[]{:S(2)}, u32[]{:S(2)}) collective-permute-start(bf16[1024,2048]{0,1:T(8,128)(2,1)} %constant_dynamic-slice_fusion.2), channel_id=1, source_target_pairs={{0,8},{8,0},{16,24},{24,16},{1,9},{9,1},{17,25},{25,17},{2,10},{10... | collective-permute-start | bytes 12582920 | tf_op jit(solution)/shard_map/ppermute | solution.py:101
  148.0 17.8 %collective-permute-start.12 = (bf16[2,2,2,64,640]{4,3,0,2,1:T(8,128)(2,1)}, bf16[2,2,2,64,640]{4,3,0,2,1:T(8,128)(2,1)}, u32[]{:S(2)}, u32[]{:S(2)}) collective-permute-start(bf16[2,2,2,64,640]{4,3,0,2,1:T(8,128)(2,1)} %bitcast.180), channel_id=1, source_target_pairs={{0,16},{8,24},{16,0},{24,8},{1,17},{9,25},{17,1},{25,9},{2,18},{10... | collective-permute-start | bytes 1966088 | tf_op jit(solution)/shard_map/ppermute | solution.py:101
  159.3 18.8 %collective-permute-start.17 = (bf16[2,2,2,64,768]{4,3,2,1,0:T(8,128)(2,1)}, bf16[2,2,2,64,768]{4,3,2,1,0:T(8,128)(2,1)}, u32[]{:S(2)}, u32[]{:S(2)}) collective-permute-start(bf16[2,2,2,64,768]{4,3,2,1,0:T(8,128)(2,1)} %dynamic-slice_bitcast_fusion), channel_id=1, source_target_pairs={{0,2},{1,3},{2,0},{3,1},{4,6},{5,7},{6,4},{7,5},{8,10},{9,11},{10,... | collective-permute-start | bytes 2359304 | tf_op jit(solution)/shard_map/ppermute | solution.py:101
  161.9 15.6 %collective-permute-start.7 = (bf16[2,2,2,64,640]{4,3,2,1,0:T(8,128)(2,1)S(1)}, bf16[2,2,2,64,640]{4,3,2,1,0:T(8,128)(2,1)S(1)}, u32[]{:S(2)}, u32[]{:S(2)}) collective-permute-start(bf16[2,2,2,64,640]{4,3,2,1,0:T(8,128)(2,1)S(1)} %dynamic-slice_bitcast_fusion.1), channel_id=1, source_target_pairs={{0,1},{1,0},{2,3},{3,2},{4,5},{5,4},{6,7},{7,6},{8,9},{9,8},{10,11... | collective-permute-start | bytes 1966088 | tf_op jit(solution)/shard_map/ppermute | solution.py:101
  167.2 17.8 %collective-permute-start.13 = (bf16[2,2,64,640]{3,2,0,1:T(8,128)(2,1)S(1)}, bf16[2,2,64,640]{3,2,0,1:T(8,128)(2,1)S(1)}, u32[]{:S(2)}, u32[]{:S(2)}) collective-permute-start(bf16[2,2,64,640]{3,2,0,1:T(8,128)(2,1)S(1)} %dynamic-slice_bitcast_fusion.3), channel_id=1, source_target_pairs={{0,2},{1,3},{2,0},{3,1},{4,6},{5,7},{6,4},{7,5},{8,10},{9,11},{10,... | collective-permute-start | bytes 983048 | tf_op jit(solution)/shard_map/ppermute | solution.py:101
  177.7 7.7 %collective-permute-start.8 = (bf16[2,2,64,640]{3,2,1,0:T(8,128)(2,1)S(1)}, bf16[2,2,64,640]{3,2,1,0:T(8,128)(2,1)S(1)}, u32[]{:S(2)}, u32[]{:S(2)}) collective-permute-start(bf16[2,2,64,640]{3,2,1,0:T(8,128)(2,1)S(1)} %dynamic-slice_bitcast_fusion.4), channel_id=1, source_target_pairs={{0,16},{8,24},{16,0},{24,8},{1,17},{9,25},{17,1},{25,9},{2,18},{10... | collective-permute-start | bytes 983048 | tf_op jit(solution)/shard_map/ppermute | solution.py:101
  179.4 14.7 %collective-permute-start.18 = (bf16[2,2,64,768]{3,2,1,0:T(8,128)(2,1)S(1)}, bf16[2,2,64,768]{3,2,1,0:T(8,128)(2,1)S(1)}, u32[]{:S(2)}, u32[]{:S(2)}) collective-permute-start(bf16[2,2,64,768]{3,2,1,0:T(8,128)(2,1)S(1)} %dynamic-slice_bitcast_fusion.2), channel_id=1, source_target_pairs={{0,1},{1,0},{2,3},{3,2},{4,5},{5,4},{6,7},{7,6},{8,9},{9,8},{10,11... | collective-permute-start | bytes 1179656 | tf_op jit(solution)/shard_map/ppermute | solution.py:101
  185.1 6.3 %collective-permute-start.14 = (bf16[2,64,640]{2,1,0:T(8,128)(2,1)S(1)}, bf16[2,64,640]{2,1,0:T(8,128)(2,1)S(1)}, u32[]{:S(2)}, u32[]{:S(2)}) collective-permute-start(bf16[2,64,640]{2,1,0:T(8,128)(2,1)S(1)} %dynamic-slice_bitcast_fusion.12), channel_id=1, source_target_pairs={{0,1},{1,0},{2,3},{3,2},{4,5},{5,4},{6,7},{7,6},{8,9},{9,8},{10,11... | collective-permute-start | bytes 491528 | tf_op jit(solution)/shard_map/ppermute | solution.py:101
  185.6 8.4 %collective-permute-start.9 = (bf16[2,64,640]{2,1,0:T(8,128)(2,1)S(1)}, bf16[2,64,640]{2,1,0:T(8,128)(2,1)S(1)}, u32[]{:S(2)}, u32[]{:S(2)}) collective-permute-start(bf16[2,64,640]{2,1,0:T(8,128)(2,1)S(1)} %dynamic-slice_bitcast_fusion.13), channel_id=1, source_target_pairs={{0,2},{1,3},{2,0},{3,1},{4,6},{5,7},{6,4},{7,5},{8,10},{9,11},{10,... | collective-permute-start | bytes 491528 | tf_op jit(solution)/shard_map/ppermute | solution.py:101
  191.5 25.1 %copy-start.13 = (f32[512,1024]{1,0:T(8,128)S(1)}, f32[512,1024]{1,0:T(8,128)}, u32[]{:S(2)}) copy-start(f32[512,1024]{1,0:T(8,128)} %fusion.43) | copy-start | bytes 6291460
  191.5 4.3 %collective-permute-start.15 = (bf16[64,640]{1,0:T(8,128)(2,1)S(1)}, bf16[64,640]{1,0:T(8,128)(2,1)S(1)}, u32[]{:S(2)}, u32[]{:S(2)}) collective-permute-start(bf16[64,640]{1,0:T(8,128)(2,1)S(1)} %dynamic-slice_bitcast_fusion.15), channel_id=1, source_target_pairs={{0,4},{1,5},{2,6},{3,7},{4,0},{5,1},{6,2},{7,3},{8,12},{9,13},{10,... | collective-permute-start | bytes 245768 | tf_op jit(solution)/shard_map/ppermute | solution.py:101
  194.0 5.6 %collective-permute-start.10 = (bf16[64,640]{1,0:T(8,128)(2,1)S(1)}, bf16[64,640]{1,0:T(8,128)(2,1)S(1)}, u32[]{:S(2)}, u32[]{:S(2)}) collective-permute-start(bf16[64,640]{1,0:T(8,128)(2,1)S(1)} %dynamic-slice_bitcast_fusion.16), channel_id=1, source_target_pairs={{0,4},{1,5},{2,6},{3,7},{4,0},{5,1},{6,2},{7,3},{8,12},{9,13},{10,... | collective-permute-start | bytes 245768 | tf_op jit(solution)/shard_map/ppermute | solution.py:101
  194.3 6.9 %collective-permute-start.19 = (bf16[2,64,768]{2,1,0:T(8,128)(2,1)S(1)}, bf16[2,64,768]{2,1,0:T(8,128)(2,1)S(1)}, u32[]{:S(2)}, u32[]{:S(2)}) collective-permute-start(bf16[2,64,768]{2,1,0:T(8,128)(2,1)S(1)} %dynamic-slice_bitcast_fusion.11), channel_id=1, source_target_pairs={{0,16},{8,24},{16,0},{24,8},{1,17},{9,25},{17,1},{25,9},{2,18},{10... | collective-permute-start | bytes 589832 | tf_op jit(solution)/shard_map/ppermute | solution.py:101
  195.8 5.8 %collective-permute-start.16 = (bf16[64,640]{1,0:T(8,128)(2,1)S(1)}, bf16[64,640]{1,0:T(8,128)(2,1)S(1)}, u32[]{:S(2)}, u32[]{:S(2)}) collective-permute-start(bf16[64,640]{1,0:T(8,128)(2,1)S(1)} %fusion.38), channel_id=1, source_target_pairs={{0,16},{8,24},{16,0},{24,8},{1,17},{9,25},{17,1},{25,9},{2,18},{10... | collective-permute-start | bytes 245768 | tf_op jit(solution)/shard_map/ppermute | solution.py:101
  199.6 7.3 %collective-permute-start.11 = (bf16[64,640]{1,0:T(8,128)(2,1)S(1)}, bf16[64,640]{1,0:T(8,128)(2,1)S(1)}, u32[]{:S(2)}, u32[]{:S(2)}) collective-permute-start(bf16[64,640]{1,0:T(8,128)(2,1)S(1)} %fusion.39), channel_id=1, source_target_pairs={{0,16},{8,24},{16,0},{24,8},{1,17},{9,25},{17,1},{25,9},{2,18},{10... | collective-permute-start | bytes 245768 | tf_op jit(solution)/shard_map/ppermute | solution.py:101
  201.3 5.0 %collective-permute-start.20 = (bf16[64,768]{1,0:T(8,128)(2,1)S(1)}, bf16[64,768]{1,0:T(8,128)(2,1)S(1)}, u32[]{:S(2)}, u32[]{:S(2)}) collective-permute-start(bf16[64,768]{1,0:T(8,128)(2,1)S(1)} %dynamic-slice_bitcast_fusion.14), channel_id=1, source_target_pairs={{0,4},{1,5},{2,6},{3,7},{4,0},{5,1},{6,2},{7,3},{8,12},{9,13},{10,... | collective-permute-start | bytes 294920 | tf_op jit(solution)/shard_map/ppermute | solution.py:101
  206.3 3.8 %collective-permute-start.21 = (bf16[64,768]{1,0:T(8,128)(2,1)S(1)}, bf16[64,768]{1,0:T(8,128)(2,1)S(1)}, u32[]{:S(2)}, u32[]{:S(2)}) collective-permute-start(bf16[64,768]{1,0:T(8,128)(2,1)S(1)} %fusion.37), channel_id=1, source_target_pairs={{0,16},{8,24},{16,0},{24,8},{1,17},{9,25},{17,1},{25,9},{2,18},{10... | collective-permute-start | bytes 294920 | tf_op jit(solution)/shard_map/ppermute | solution.py:101
  210.3 8.5 %collective-permute-start.22 = (bf16[128,2048]{1,0:T(8,128)(2,1)S(1)}, bf16[128,2048]{1,0:T(8,128)(2,1)S(1)}, u32[]{:S(2)}, u32[]{:S(2)}) collective-permute-start(bf16[128,2048]{1,0:T(8,128)(2,1)S(1)} %pad_maximum_fusion.9), channel_id=1, source_target_pairs={{0,8},{8,0},{16,24},{24,16},{1,9},{9,1},{17,25},{25,17},{2,10},{10... | collective-permute-start | bytes 1572872 | tf_op jit(solution)/shard_map/ppermute | solution.py:101
  (24 other events, 175.2 us)

commit v3 on v2

--- a/solution.py
+++ b/solution.py
@@ -90,13 +90,6 @@
     )(query, keys, values, d_att)
 
 
-def gradient_terms(sources):
-    parts = []
-    for left, right in sources:
-        parts.append(jnp.dot(left.T, right, preferred_element_type=jnp.float32).astype(jnp.bfloat16))
-    return jnp.concatenate(parts, axis=1)
-
-
 def exchange(array, axis, mask):
     return lax.ppermute(array, axis, [(i, i ^ mask) for i in range(lax.axis_size(axis))])
 
@@ -105,38 +98,53 @@
     return (a.astype(jnp.float32) + b.astype(jnp.float32)).astype(jnp.bfloat16)
 
 
-def halve(data, steps):
-    for kind, axis, mask, bit, at in steps:
-        keep = lax.dynamic_index_in_dim(data, bit, at, keepdims=False)
-        send = lax.dynamic_index_in_dim(data, 1 - bit, at, keepdims=False)
-        data = add_bf16(keep, exchange(send, axis, mask))
-    return data
-
-
-def reduce_gradients(terms):
+def term(left, right, lo, hi):
+    return jnp.dot(left.T, right[:, lo:hi], preferred_element_type=jnp.float32).astype(jnp.bfloat16)
+
+
+def reduce_gradients(sources):
     n_dp = lax.axis_size("dp")
     n_seq = lax.axis_size("seq")
     seq_bits = n_seq.bit_length() - 1
     dp_bits = n_dp.bit_length() - 1
-    rows, width = terms.shape
-    half = width // 2
+    width = sources[0][1].shape[1]
+    rows = sources[0][0].shape[1]
     blk = rows // n_seq
     dp_i = lax.axis_index("dp")
     seq_i = lax.axis_index("seq")
-    core = dp_i % 2
-    mine = lax.dynamic_slice_in_dim(terms, core * half, half, 1)
-    other = lax.dynamic_slice_in_dim(terms, (1 - core) * half, half, 1)
-    summed = add_bf16(mine, exchange(other, "dp", 1))
+    low = dp_i % 2 == 0
+
+    def pick(a, b):
+        return jnp.where(low, a, b)
+
+    keep = [
+        (sources[0][0], pick(sources[0][1], sources[2][1])),
+        (pick(sources[1][0], sources[3][0]), pick(sources[1][1], sources[3][1])),
+    ]
+    send = [
+        (sources[2][0], pick(sources[2][1], sources[0][1])),
+        (pick(sources[3][0], sources[1][0]), pick(sources[3][1], sources[1][1])),
+    ]
     dims = [("seq", 0)] + [("dp", b) for b in range(1, dp_bits)] + [("seq", b) for b in range(1, seq_bits)]
     first = dims[:3]
     n_parts = len(first)
-    cuts = [(half // LANES) * p // n_parts * LANES for p in range(n_parts + 1)]
+    units = 2 * width // LANES
+    cuts = [units * p // n_parts * LANES for p in range(n_parts + 1)]
+    shape = [2] * seq_bits + [2] * (dp_bits - 1) + [blk >> (dp_bits - 1)]
     pieces = []
     for p in range(n_parts):
         order = first[p:] + first[:p] + dims[3:]
-        data = summed[:, cuts[p] : cuts[p + 1]]
-        data = data.reshape([2] * seq_bits + [2] * (dp_bits - 1) + [blk >> (dp_bits - 1), cuts[p + 1] - cuts[p]])
-        steps = []
+        datas = []
+        spans = []
+        for g in range(2):
+            lo = max(cuts[p], g * width) - g * width
+            hi = min(cuts[p + 1], (g + 1) * width) - g * width
+            if hi > lo:
+                spans.append((g, lo, hi))
+        sends = [term(*send[g], lo, hi) for g, lo, hi in spans]
+        keeps = [term(*keep[g], lo, hi) for g, lo, hi in spans]
+        got = exchange(sends, "dp", 1)
+        datas = [add_bf16(k, r).reshape(shape + [k.shape[1]]) for k, r in zip(keeps, got)]
         removed = []
         for axis, b in order:
             if axis == "seq":
@@ -145,20 +153,29 @@
             else:
                 at = seq_bits + (dp_bits - 1 - b)
                 bit = (dp_i >> b) % 2
-            shift = sum(1 for r in removed if r < at)
+            at_now = at - sum(1 for r in removed if r < at)
             removed.append(at)
-            steps.append((axis, axis, 1 << b, bit, at - shift))
-        data = halve(data, steps)
+            kept = [lax.dynamic_index_in_dim(d, bit, at_now, keepdims=False) for d in datas]
+            out = [lax.dynamic_index_in_dim(d, 1 - bit, at_now, keepdims=False) for d in datas]
+            datas = [add_bf16(k, r) for k, r in zip(kept, exchange(out, axis, 1 << b))]
         for b in range(1, dp_bits):
-            got = exchange(data, "dp", 1 << b)
-            low = (dp_i >> b) % 2 == 0
-            data = jnp.where(low, jnp.concatenate([data, got], 0), jnp.concatenate([got, data], 0))
-        pieces.append(data)
+            got = exchange(datas, "dp", 1 << b)
+            first_half = (dp_i >> b) % 2 == 0
+            datas = [
+                jnp.where(first_half, jnp.concatenate([d, r], 0), jnp.concatenate([r, d], 0))
+                for d, r in zip(datas, got)
+            ]
+        pieces.extend(datas)
     part = jnp.concatenate(pieces, axis=1)
     back = exchange(part, "dp", 1)
-    low = core == 0
-    result = jnp.where(low, jnp.concatenate([part, back], 1), jnp.concatenate([back, part], 1))
-    return result.astype(jnp.float32)
+    mine = [part[:, :width], part[:, width:]]
+    other = [back[:, :width], back[:, width:]]
+    return (
+        pick(mine[0], other[0]).astype(jnp.float32),
+        pick(mine[1], other[1]).astype(jnp.float32),
+        pick(other[0], mine[0]).astype(jnp.float32),
+        pick(other[1], mine[1]).astype(jnp.float32),
+    )
 
 
 def body(layer_input, w_query, w_key, w_value, w_out, offsets, grad_out):
@@ -200,15 +217,8 @@
     total = total + jnp.dot(dvalue, w_value.T, preferred_element_type=jnp.float32)
     grad_input = total.astype(jnp.bfloat16)
     sources = ((rows, dquery), (rows, dkey), (rows, dvalue), (attended, cot))
-    summed = reduce_gradients(gradient_terms(sources))
-    return (
-        result[None],
-        grad_input[None],
-        summed[:, :width],
-        summed[:, width : 2 * width],
-        summed[:, 2 * width : 3 * width],
-        summed[:, 3 * width :],
-    )
+    grads = reduce_gradients(sources)
+    return (result[None], grad_input[None]) + grads
 
 
 def solution(mesh):

time: 221 us -> 213 us (0.964)
  local copies, waits for them, and re-layouts: 35.8 us -> 13.5 us
  starting transfers between devices: 36.3 us -> 52.7 us
  matrix products: 26 us -> 31.6 us
  other arithmetic: 17.7 us -> 13.3 us
  waiting for transfers between devices: 63.5 us -> 60.2 us
    ppermute x17 -> x25, starting transfers between devices: 25 us -> 41.4 us  [exchange(): lax.ppermute(array, axis, [(i, i ^ mask) for i in range(lax.axis_size(axi...]
    slice x6 -> x0, local copies, waits for them, and re-layouts: 12.1 us -> none  [the longest x5 10.7 us: reduce_gradients(): data = summed[:, cuts[p]:cuts[p + 1]]]
    convert_element_type x13 -> x16, other arithmetic: 8.89 us -> 1.95 us  [add_bf16(): return (a.astype(jnp.float32) + b.astype(jnp.float32)).astype(jnp.bfloat16)]
    ppermute x6, waiting for transfers between devices: 29.5 us -> 23.1 us  [partner(): lax.ppermute(array, axis, [(i, i ^ 1 << apart) for i in range(lax.axis_si...]
    dot_general x4 -> x8, matrix products: 5.26 us -> 11.6 us  [term(): jnp.dot(left.T, right[:, lo:hi], preferred_element_type=jnp.float32)]
    dynamic_slice x3 -> x6, local copies, waits for them, and re-layouts: 6.08 us -> 0.35 us  [the longest x3 0.24 us: reduce_gradients(): lax.dynamic_index_in_dim(d, bit, at_now, keepdims=False)]
    ppermute x17 -> x25, waiting for transfers between devices: 33.9 us -> 37.2 us  [exchange(): lax.ppermute(array, axis, [(i, i ^ mask) for i in range(lax.axis_size(axi...]
    squeeze x11 -> x13, local copies, waits for them, and re-layouts: 3.44 us -> 0.31 us  [reduce_gradients(): lax.dynamic_index_in_dim(d, 1 - bit, at_now, keepdims=False)]
  transfers between devices with their start and end apart: 23 -> 31, of which waited for: 13 -> 16; matrix products, arithmetic and copies ran while one was open for 16% -> 16% of each run, Pallas kernels for 0% -> 0%
where the time goes in v3:
time: 213 us
  waiting for transfers between devices  60.2 us (28%)
  starting transfers between devices  52.7 us (25%)
  Pallas kernels  38 us (18%)
  matrix products  31.6 us (15%)
  local copies, waits for them, and re-layouts  13.5 us (6%)
  other arithmetic  13.3 us (6%)
  between operations  3.27 us (2%)
    ppermute x25, starting transfers between devices, exchange(): lax.ppermute(array, axis, [(i, i ^ mask) for i in range(lax.axis_size(axi...  41.4 us
    pallas_call x1, Pallas kernels, attention(): pl.pallas_call(functools.partial(attention_kernel, head=head, scale=head...  38 us
    ppermute x25, waiting for transfers between devices, exchange(): lax.ppermute(array, axis, [(i, i ^ mask) for i in range(lax.axis_size(axi...  37.2 us
    ppermute x6, waiting for transfers between devices, partner(): lax.ppermute(array, axis, [(i, i ^ 1 << apart) for i in range(lax.axis_si...  23.1 us
    dot_general x8, matrix products, term(): jnp.dot(left.T, right[:, lo:hi], preferred_element_type=jnp.float32)  11.6 us
    ppermute x6, starting transfers between devices, partner(): lax.ppermute(array, axis, [(i, i ^ 1 << apart) for i in range(lax.axis_si...  11.3 us
    unnamed x56, local copies, waits for them, and re-layouts  5.13 us
    dot_general x1, matrix products, body(): jnp.dot(rows, w_value, preferred_element_type=jnp.float32)  4.28 us
  transfers between devices with their start and end apart: 31, of which 16 were waited for; matrix products, arithmetic and copies ran while one was open for 16% of the time, Pallas kernels for 0%

profile of v3, /device:TPU:1, one launch (start us, length us, event | category | flops | bytes accessed | tf_op | source)
XLA Modules:
  0.0 212.7 jit_solution(9171003736368968156)
XLA Ops:
  4.1 4.3 %convolution_convert_fusion.6 = bf16[512,1024]{1,0:T(8,128)(2,1)} fusion(bf16[1024,1024]{1,0:T(8,128)(2,1)} %param.10, bf16[1,512,1024]{2,1,0:T(8,128)(2,1)} %param.7), kind=kOutput, calls=%fused_computation.16 | convolution fusion | flops 1074266112 | bytes 4194304 | tf_op jit(solution)/shard_map/dot_general | solution.py:190
  16.8 2.3 %collective-permute-start.2 = (bf16[2,128,1024]{2,1,0:T(8,128)(2,1)}, bf16[2,128,1024]{2,1,0:T(8,128)(2,1)}, u32[]{:S(2)}, u32[]{:S(2)}) collective-permute-start(bf16[2,128,1024]{2,1,0:T(8,128)(2,1)} %pad_maximum_fusion.4), channel_id=1, source_target_pairs={{0,4},{1,5},{2,6},{3,7},{4,0},{5,1},{6,2},{7,3},{8,12},{9,13},{10,... | collective-permute-start | bytes 1572872 | tf_op jit(solution)/shard_map/ppermute | solution.py:16
  21.4 2.3 %convolution_convert_fusion.5.do_ref = bf16[512,1024]{1,0:T(8,128)(2,1)} fusion(bf16[1024,1024]{1,0:T(8,128)(2,1)S(1)} %copy-done.17, bf16[1,512,1024]{2,1,0:T(8,128)(2,1)S(1)} %copy-done.10), kind=kOutput, calls=%fused_computation.15 | convolution fusion | flops 1074266112 | bytes 4194304 | tf_op jit(solution)/shard_map/dot_general | solution.py:194
  26.8 10.9 %collective-permute-done.1 = bf16[2,128,1024]{2,1,0:T(8,128)(2,1)} collective-permute-done((bf16[2,128,1024]{2,1,0:T(8,128)(2,1)}, bf16[2,128,1024]{2,1,0:T(8,128)(2,1)}, u32[]{:S(2)}, u32[]{:S(2)}) %collective-permute-start.1) | collective-permute-done | bytes 524320 | tf_op jit(solution)/shard_map/ppermute | solution.py:16
  42.7 38.0 %shard_map.118 = (bf16[512,1024]{1,0:T(8,128)(2,1)}, bf16[512,1024]{1,0:T(8,128)(2,1)}, f32[896,1024]{1,0:T(8,128)}, f32[896,1024]{1,0:T(8,128)}) custom-call(bf16[512,1024]{1,0:T(8,128)(2,1)} %convolution_convert_fusion.8.q_ref, bf16[896,1024]{1,0:T(8,128)(2,1)} %pad_maximum_fusion.k_ref, bf16[896,1024]{1,0:T(8,128)(2,1)} %pad_maximum_fusion.1.v_ref, ...), custom_call_target="tpu_custom_call" | custom-call | flops 11274289152 | bytes 13107200 | tf_op jit(solution)/shard_map/pallas_call | solution.py:73
  80.7 2.5 %convert.40 = bf16[896,1024]{1,0:T(8,128)(2,1)S(1)} convert(f32[896,1024]{1,0:T(8,128)} %get-tuple-element.12) | non-fusion elementwise | flops 917504 | bytes 5505024 | tf_op jit(solution)/shard_map/convert.35
  86.5 3.2 %collective-permute-start.4 = (bf16[2,128,1024]{2,1,0:T(8,128)(2,1)S(1)}, bf16[2,128,1024]{2,1,0:T(8,128)(2,1)S(1)}, u32[]{:S(2)}, u32[]{:S(2)}) collective-permute-start(bf16[2,128,1024]{2,1,0:T(8,128)(2,1)S(1)} %pad_maximum_fusion.6), channel_id=1, source_target_pairs={{0,2},{1,3},{2,0},{3,1},{4,6},{5,7},{6,4},{7,5},{8,10},{9,11},{10,... | collective-permute-start | bytes 1572872 | tf_op jit(solution)/shard_map/ppermute | solution.py:16
  90.1 2.7 %fusion.55 = f32[512,1024]{1,0:T(8,128)} fusion(bf16[512,1024]{1,0:T(8,128)(2,1)S(1)} %copy-done.16, bf16[1024,1024]{1,0:T(8,128)(2,1)S(1)} %copy-done), kind=kOutput, calls=%fused_computation.163 | convolution fusion | flops 1073741824 | bytes 5242880 | tf_op jit(solution)/shard_map/dot_general | solution.py:215
  97.0 9.5 %collective-permute-done.4 = bf16[2,128,1024]{2,1,0:T(8,128)(2,1)S(1)} collective-permute-done((bf16[2,128,1024]{2,1,0:T(8,128)(2,1)S(1)}, bf16[2,128,1024]{2,1,0:T(8,128)(2,1)S(1)}, u32[]{:S(2)}, u32[]{:S(2)}) %collective-permute-start.4) | collective-permute-done | bytes 524320 | tf_op jit(solution)/shard_map/ppermute | solution.py:16
  112.0 4.1 %collective-permute-start.18 = (bf16[1024,256]{1,0:T(8,128)(2,1)S(1)}, bf16[1024,256]{1,0:T(8,128)(2,1)S(1)}, u32[]{:S(2)}, u32[]{:S(2)}) collective-permute-start(bf16[1024,256]{1,0:T(8,128)(2,1)S(1)} %convolution_convert_fusion.11), channel_id=1, source_target_pairs={{0,8},{8,0},{16,24},{24,16},{1,9},{9,1},{17,25},{25,17},{2,10},{10... | collective-permute-start | bytes 1572872 | tf_op jit(solution)/shard_map/ppermute | solution.py:94
  121.4 2.7 %fusion.52 = f32[512,1024]{1,0:T(8,128)} fusion(bf16[1024,1024]{1,0:T(8,128)(2,1)S(1)} %copy-done.20, f32[512,1024]{1,0:T(8,128)S(1)} %get-tuple-element.27), kind=kOutput, calls=%fused_computation.160 | convolution fusion | flops 1074266112 | bytes 6291456 | tf_op jit(solution)/shard_map/dot_general | solution.py:216
  124.1 3.9 %collective-permute-done.19 = bf16[2,2,2,64,256]{4,3,0,2,1:T(8,128)(2,1)S(1)} collective-permute-done((bf16[2,2,2,64,256]{4,3,0,2,1:T(8,128)(2,1)S(1)}, bf16[2,2,2,64,256]{4,3,0,2,1:T(8,128)(2,1)S(1)}, u32[]{:S(2)}, u32[]{:S(2)}) %collective-permute-start.19) | collective-permute-done | bytes 262176 | tf_op jit(solution)/shard_map/ppermute | solution.py:94
  130.1 2.2 %collective-permute-done.20 = bf16[2,2,64,256]{3,2,0,1:T(8,128)(2,1)S(1)} collective-permute-done((bf16[2,2,64,256]{3,2,0,1:T(8,128)(2,1)S(1)}, bf16[2,2,64,256]{3,2,0,1:T(8,128)(2,1)S(1)}, u32[]{:S(2)}, u32[]{:S(2)}) %collective-permute-start.20) | collective-permute-done | bytes 131104 | tf_op jit(solution)/shard_map/ppermute | solution.py:94
  135.6 2.8 %collective-permute-start.22 = (bf16[64,256]{1,0:T(8,128)(2,1)S(1)}, bf16[64,256]{1,0:T(8,128)(2,1)S(1)}, u32[]{:S(2)}, u32[]{:S(2)}) collective-permute-start(bf16[64,256]{1,0:T(8,128)(2,1)S(1)} %dynamic-slice_bitcast_fusion.18), channel_id=1, source_target_pairs={{0,4},{1,5},{2,6},{3,7},{4,0},{5,1},{6,2},{7,3},{8,12},{9,13},{10,... | collective-permute-start | bytes 98312 | tf_op jit(solution)/shard_map/ppermute | solution.py:94
  140.7 3.0 %collective-permute-start.24 = (bf16[1024,768]{1,0:T(8,128)(2,1)}, bf16[1024,768]{1,0:T(8,128)(2,1)}, u32[]{:S(2)}, u32[]{:S(2)}) collective-permute-start(bf16[1024,768]{1,0:T(8,128)(2,1)} %convolution_convert_fusion), channel_id=1, source_target_pairs={{0,8},{8,0},{16,24},{24,16},{1,9},{9,1},{17,25},{25,17},{2,10},{10... | collective-permute-start | bytes 4718600 | tf_op jit(solution)/shard_map/ppermute | solution.py:94
  156.2 2.8 %add_convert_fusion = bf16[1024,768]{1,0:T(8,128)(2,1)S(1)} fusion(bf16[1024,768]{1,0:T(8,128)(2,1)} %collective-permute-done.24, bf16[512,1024]{1,0:T(8,128)(2,1)S(1)} %copy-done.13, bf16[512,1024]{1,0:T(8,128)(2,1)} %get-tuple-element.10, bf16[1,512,1024]{2,1,0:T(8,128)(2,1)S(1)} %copy-done.25, pred[]{:T(512)S(6)} %eq.25), kind=kOutput, calls=%fused_computation | convolution fusion | flops 809762816 | bytes 6029313 | tf_op jit(solution)/shard_map/dot_general | solution.py:102
  160.8 14.8 %collective-permute-done.16 = bf16[64,384]{1,0:T(8,128)(2,1)S(1)} collective-permute-done((bf16[64,384]{1,0:T(8,128)(2,1)S(1)}, bf16[64,384]{1,0:T(8,128)(2,1)S(1)}, u32[]{:S(2)}, u32[]{:S(2)}) %collective-permute-start.16) | collective-permute-done | bytes 49184 | tf_op jit(solution)/shard_map/ppermute | solution.py:94
  179.0 3.2 %collective-permute-done.8 = bf16[2,2,64,640]{3,2,1,0:T(8,128)(2,1)S(1)} collective-permute-done((bf16[2,2,64,640]{3,2,1,0:T(8,128)(2,1)S(1)}, bf16[2,2,64,640]{3,2,1,0:T(8,128)(2,1)S(1)}, u32[]{:S(2)}, u32[]{:S(2)}) %collective-permute-start.8) | collective-permute-done | bytes 327712 | tf_op jit(solution)/shard_map/ppermute | solution.py:94
  182.4 2.3 %collective-permute-done.26 = bf16[2,2,64,768]{3,2,0,1:T(8,128)(2,1)S(1)} collective-permute-done((bf16[2,2,64,768]{3,2,0,1:T(8,128)(2,1)S(1)}, bf16[2,2,64,768]{3,2,0,1:T(8,128)(2,1)S(1)}, u32[]{:S(2)}, u32[]{:S(2)}) %collective-permute-start.26) | collective-permute-done | bytes 393248 | tf_op jit(solution)/shard_map/ppermute | solution.py:94
  186.9 2.9 %collective-permute-start.10 = (bf16[64,640]{1,0:T(8,128)(2,1)S(1)}, bf16[64,640]{1,0:T(8,128)(2,1)S(1)}, u32[]{:S(2)}, u32[]{:S(2)}) collective-permute-start(bf16[64,640]{1,0:T(8,128)(2,1)S(1)} %dynamic-slice_bitcast_fusion.15), channel_id=1, source_target_pairs={{0,4},{1,5},{2,6},{3,7},{4,0},{5,1},{6,2},{7,3},{8,12},{9,13},{10,... | collective-permute-start | bytes 245768 | tf_op jit(solution)/shard_map/ppermute | solution.py:94
  189.8 2.8 %collective-permute-start.28 = (bf16[64,768]{1,0:T(8,128)(2,1)S(1)}, bf16[64,768]{1,0:T(8,128)(2,1)S(1)}, u32[]{:S(2)}, u32[]{:S(2)}) collective-permute-start(bf16[64,768]{1,0:T(8,128)(2,1)S(1)} %dynamic-slice_bitcast_fusion.13), channel_id=1, source_target_pairs={{0,4},{1,5},{2,6},{3,7},{4,0},{5,1},{6,2},{7,3},{8,12},{9,13},{10,... | collective-permute-start | bytes 294920 | tf_op jit(solution)/shard_map/ppermute | solution.py:94
  196.7 2.3 %collective-permute-done.29 = bf16[64,768]{1,0:T(8,128)(2,1)S(1)} collective-permute-done((bf16[64,768]{1,0:T(8,128)(2,1)S(1)}, bf16[64,768]{1,0:T(8,128)(2,1)S(1)}, u32[]{:S(2)}, u32[]{:S(2)}) %collective-permute-start.29) | collective-permute-done | bytes 98336 | tf_op jit(solution)/shard_map/ppermute | solution.py:94
  199.0 9.8 %collective-permute-start.30 = (bf16[128,2048]{1,0:T(8,128)(2,1)S(1)}, bf16[128,2048]{1,0:T(8,128)(2,1)S(1)}, u32[]{:S(2)}, u32[]{:S(2)}) collective-permute-start(bf16[128,2048]{1,0:T(8,128)(2,1)S(1)} %pad_maximum_fusion.8), channel_id=1, source_target_pairs={{0,8},{8,0},{16,24},{24,16},{1,9},{9,1},{17,25},{25,17},{2,10},{10... | collective-permute-start | bytes 1572872 | tf_op jit(solution)/shard_map/ppermute | solution.py:94
  208.9 2.3 %fusion.5 = bf16[1,512,1024]{2,1,0:T(8,128)(2,1)} fusion(bf16[1024,1024]{1,0:T(8,128)(2,1)S(1)} %copy-done.7, f32[512,1024]{1,0:T(8,128)S(1)} %copy-done.8, f32[512,1024]{1,0:T(8,128)S(1)} %copy-done.9, f32[512,1024]{1,0:T(8,128)S(1)} %copy-done.3), kind=kOutput, calls=%fused_computation.23 | convolution fusion | flops 1075838976 | bytes 9437184 | tf_op jit(solution)/shard_map/dot_general | solution.py:217
  (181 shorter events, 71.7 us)
Async XLA Ops:
  11.8 14.0 %collective-permute-start = (bf16[2,128,1024]{2,1,0:T(8,128)(2,1)}, bf16[2,128,1024]{2,1,0:T(8,128)(2,1)}, u32[]{:S(2)}, u32[]{:S(2)}) collective-permute-start(bf16[2,128,1024]{2,1,0:T(8,128)(2,1)} %pad_maximum_fusion.2), channel_id=1, source_target_pairs={{0,1},{1,0},{2,3},{3,2},{4,5},{5,4},{6,7},{7,6},{8,9},{9,8},{10,11... | collective-permute-start | bytes 1572872 | tf_op jit(solution)/shard_map/ppermute | solution.py:16
  14.7 23.1 %collective-permute-start.1 = (bf16[2,128,1024]{2,1,0:T(8,128)(2,1)}, bf16[2,128,1024]{2,1,0:T(8,128)(2,1)}, u32[]{:S(2)}, u32[]{:S(2)}) collective-permute-start(bf16[2,128,1024]{2,1,0:T(8,128)(2,1)} %pad_maximum_fusion.3), channel_id=1, source_target_pairs={{0,2},{1,3},{2,0},{3,1},{4,6},{5,7},{6,4},{7,5},{8,10},{9,11},{10,... | collective-permute-start | bytes 1572872 | tf_op jit(solution)/shard_map/ppermute | solution.py:16
  16.8 22.0 %collective-permute-start.2 = (bf16[2,128,1024]{2,1,0:T(8,128)(2,1)}, bf16[2,128,1024]{2,1,0:T(8,128)(2,1)}, u32[]{:S(2)}, u32[]{:S(2)}) collective-permute-start(bf16[2,128,1024]{2,1,0:T(8,128)(2,1)} %pad_maximum_fusion.4), channel_id=1, source_target_pairs={{0,4},{1,5},{2,6},{3,7},{4,0},{5,1},{6,2},{7,3},{8,12},{9,13},{10,... | collective-permute-start | bytes 1572872 | tf_op jit(solution)/shard_map/ppermute | solution.py:16
  84.3 23.5 %collective-permute-start.5 = (bf16[2,128,1024]{2,1,0:T(8,128)(2,1)S(1)}, bf16[2,128,1024]{2,1,0:T(8,128)(2,1)S(1)}, u32[]{:S(2)}, u32[]{:S(2)}) collective-permute-start(bf16[2,128,1024]{2,1,0:T(8,128)(2,1)S(1)} %pad_maximum_fusion.7), channel_id=1, source_target_pairs={{0,4},{1,5},{2,6},{3,7},{4,0},{5,1},{6,2},{7,3},{8,12},{9,13},{10,... | collective-permute-start | bytes 1572872 | tf_op jit(solution)/shard_map/ppermute | solution.py:16
  86.5 20.0 %collective-permute-start.4 = (bf16[2,128,1024]{2,1,0:T(8,128)(2,1)S(1)}, bf16[2,128,1024]{2,1,0:T(8,128)(2,1)S(1)}, u32[]{:S(2)}, u32[]{:S(2)}) collective-permute-start(bf16[2,128,1024]{2,1,0:T(8,128)(2,1)S(1)} %pad_maximum_fusion.6), channel_id=1, source_target_pairs={{0,2},{1,3},{2,0},{3,1},{4,6},{5,7},{6,4},{7,5},{8,10},{9,11},{10,... | collective-permute-start | bytes 1572872 | tf_op jit(solution)/shard_map/ppermute | solution.py:16
  89.7 16.9 %collective-permute-start.3 = (bf16[2,128,1024]{2,1,0:T(8,128)(2,1)S(1)}, bf16[2,128,1024]{2,1,0:T(8,128)(2,1)S(1)}, u32[]{:S(2)}, u32[]{:S(2)}) collective-permute-start(bf16[2,128,1024]{2,1,0:T(8,128)(2,1)S(1)} %pad_maximum_fusion.5), channel_id=1, source_target_pairs={{0,1},{1,0},{2,3},{3,2},{4,5},{5,4},{6,7},{7,6},{8,9},{9,8},{10,11... | collective-permute-start | bytes 1572872 | tf_op jit(solution)/shard_map/ppermute | solution.py:16
  112.0 7.3 %collective-permute-start.18 = (bf16[1024,256]{1,0:T(8,128)(2,1)S(1)}, bf16[1024,256]{1,0:T(8,128)(2,1)S(1)}, u32[]{:S(2)}, u32[]{:S(2)}) collective-permute-start(bf16[1024,256]{1,0:T(8,128)(2,1)S(1)} %convolution_convert_fusion.11), channel_id=1, source_target_pairs={{0,8},{8,0},{16,24},{24,16},{1,9},{9,1},{17,25},{25,17},{2,10},{10... | collective-permute-start | bytes 1572872 | tf_op jit(solution)/shard_map/ppermute | solution.py:94
  118.1 28.6 %collective-permute-start.6 = (bf16[1024,640]{0,1:T(8,128)(2,1)}, bf16[1024,640]{0,1:T(8,128)(2,1)}, u32[]{:S(2)}, u32[]{:S(2)}) collective-permute-start(bf16[1024,640]{0,1:T(8,128)(2,1)} %fusion.3), channel_id=1, source_target_pairs={{0,8},{8,0},{16,24},{24,16},{1,9},{9,1},{17,25},{25,17},{2,10},{10... | collective-permute-start | bytes 3932168 | tf_op jit(solution)/shard_map/ppermute | solution.py:94
  118.8 10.3 %collective-permute-start.12 = (bf16[1024,384]{0,1:T(8,128)(2,1)S(1)}, bf16[1024,384]{0,1:T(8,128)(2,1)S(1)}, u32[]{:S(2)}, u32[]{:S(2)}) collective-permute-start(bf16[1024,384]{0,1:T(8,128)(2,1)S(1)} %fusion.7), channel_id=1, source_target_pairs={{0,8},{8,0},{16,24},{24,16},{1,9},{9,1},{17,25},{25,17},{2,10},{10... | collective-permute-start | bytes 2359304 | tf_op jit(solution)/shard_map/ppermute | solution.py:94
  120.0 8.0 %collective-permute-start.19 = (bf16[2,2,2,64,256]{4,3,0,2,1:T(8,128)(2,1)S(1)}, bf16[2,2,2,64,256]{4,3,0,2,1:T(8,128)(2,1)S(1)}, u32[]{:S(2)}, u32[]{:S(2)}) collective-permute-start(bf16[2,2,2,64,256]{4,3,0,2,1:T(8,128)(2,1)S(1)} %bitcast.229), channel_id=1, source_target_pairs={{0,16},{8,24},{16,0},{24,8},{1,17},{9,25},{17,1},{25,9},{2,18},{10... | collective-permute-start | bytes 786440 | tf_op jit(solution)/shard_map/ppermute | solution.py:94
  133.0 12.1 %collective-permute-start.13 = (bf16[2,2,2,64,384]{4,3,0,2,1:T(8,128)(2,1)S(1)}, bf16[2,2,2,64,384]{4,3,0,2,1:T(8,128)(2,1)S(1)}, u32[]{:S(2)}, u32[]{:S(2)}) collective-permute-start(bf16[2,2,2,64,384]{4,3,0,2,1:T(8,128)(2,1)S(1)} %bitcast.228), channel_id=1, source_target_pairs={{0,16},{8,24},{16,0},{24,8},{1,17},{9,25},{17,1},{25,9},{2,18},{10... | collective-permute-start | bytes 1179656 | tf_op jit(solution)/shard_map/ppermute | solution.py:94
  135.6 8.1 %collective-permute-start.22 = (bf16[64,256]{1,0:T(8,128)(2,1)S(1)}, bf16[64,256]{1,0:T(8,128)(2,1)S(1)}, u32[]{:S(2)}, u32[]{:S(2)}) collective-permute-start(bf16[64,256]{1,0:T(8,128)(2,1)S(1)} %dynamic-slice_bitcast_fusion.18), channel_id=1, source_target_pairs={{0,4},{1,5},{2,6},{3,7},{4,0},{5,1},{6,2},{7,3},{8,12},{9,13},{10,... | collective-permute-start | bytes 98312 | tf_op jit(solution)/shard_map/ppermute | solution.py:94
  140.7 15.5 %collective-permute-start.24 = (bf16[1024,768]{1,0:T(8,128)(2,1)}, bf16[1024,768]{1,0:T(8,128)(2,1)}, u32[]{:S(2)}, u32[]{:S(2)}) collective-permute-start(bf16[1024,768]{1,0:T(8,128)(2,1)} %convolution_convert_fusion), channel_id=1, source_target_pairs={{0,8},{8,0},{16,24},{24,16},{1,9},{9,1},{17,25},{25,17},{2,10},{10... | collective-permute-start | bytes 4718600 | tf_op jit(solution)/shard_map/ppermute | solution.py:94
  143.8 17.0 %collective-permute-start.23 = (bf16[64,256]{1,0:T(8,128)(2,1)S(1)}, bf16[64,256]{1,0:T(8,128)(2,1)S(1)}, u32[]{:S(2)}, u32[]{:S(2)}) collective-permute-start(bf16[64,256]{1,0:T(8,128)(2,1)S(1)} %fusion.50), channel_id=1, source_target_pairs={{0,16},{8,24},{16,0},{24,8},{1,17},{9,25},{17,1},{25,9},{2,18},{10... | collective-permute-start | bytes 98312 | tf_op jit(solution)/shard_map/ppermute | solution.py:94
  145.2 6.4 %collective-permute-start.14 = (bf16[2,2,64,384]{3,2,0,1:T(8,128)(2,1)S(1)}, bf16[2,2,64,384]{3,2,0,1:T(8,128)(2,1)}, u32[]{:S(2)}, u32[]{:S(2)}) collective-permute-start(bf16[2,2,64,384]{3,2,0,1:T(8,128)(2,1)S(1)} %dynamic-slice_bitcast_fusion.10), channel_id=1, source_target_pairs={{0,2},{1,3},{2,0},{3,1},{4,6},{5,7},{6,4},{7,5},{8,10},{9,11},{10,... | collective-permute-start | bytes 589832 | tf_op jit(solution)/shard_map/ppermute | solution.py:94
  153.0 22.9 %collective-permute-start.7 = (bf16[2,2,2,64,640]{4,3,2,1,0:T(8,128)(2,1)S(1)}, bf16[2,2,2,64,640]{4,3,2,1,0:T(8,128)(2,1)S(1)}, u32[]{:S(2)}, u32[]{:S(2)}) collective-permute-start(bf16[2,2,2,64,640]{4,3,2,1,0:T(8,128)(2,1)S(1)} %dynamic-slice_bitcast_fusion), channel_id=1, source_target_pairs={{0,1},{1,0},{2,3},{3,2},{4,5},{5,4},{6,7},{7,6},{8,9},{9,8},{10,11... | collective-permute-start | bytes 1966088 | tf_op jit(solution)/shard_map/ppermute | solution.py:94
  159.2 18.2 %collective-permute-start.25 = (bf16[2,2,2,64,768]{4,3,0,2,1:T(8,128)(2,1)S(1)}, bf16[2,2,2,64,768]{4,3,0,2,1:T(8,128)(2,1)S(1)}, u32[]{:S(2)}, u32[]{:S(2)}) collective-permute-start(bf16[2,2,2,64,768]{4,3,0,2,1:T(8,128)(2,1)S(1)} %bitcast.226), channel_id=1, source_target_pairs={{0,2},{1,3},{2,0},{3,1},{4,6},{5,7},{6,4},{7,5},{8,10},{9,11},{10,... | collective-permute-start | bytes 2359304 | tf_op jit(solution)/shard_map/ppermute | solution.py:94
  160.8 14.8 %collective-permute-start.16 = (bf16[64,384]{1,0:T(8,128)(2,1)S(1)}, bf16[64,384]{1,0:T(8,128)(2,1)S(1)}, u32[]{:S(2)}, u32[]{:S(2)}) collective-permute-start(bf16[64,384]{1,0:T(8,128)(2,1)S(1)} %dynamic-slice_bitcast_fusion.17), channel_id=1, source_target_pairs={{0,4},{1,5},{2,6},{3,7},{4,0},{5,1},{6,2},{7,3},{8,12},{9,13},{10,... | collective-permute-start | bytes 147464 | tf_op jit(solution)/shard_map/ppermute | solution.py:94
  176.2 6.0 %collective-permute-start.8 = (bf16[2,2,64,640]{3,2,1,0:T(8,128)(2,1)S(1)}, bf16[2,2,64,640]{3,2,1,0:T(8,128)(2,1)S(1)}, u32[]{:S(2)}, u32[]{:S(2)}) collective-permute-start(bf16[2,2,64,640]{3,2,1,0:T(8,128)(2,1)S(1)} %dynamic-slice_bitcast_fusion.2), channel_id=1, source_target_pairs={{0,16},{8,24},{16,0},{24,8},{1,17},{9,25},{17,1},{25,9},{2,18},{10... | collective-permute-start | bytes 983048 | tf_op jit(solution)/shard_map/ppermute | solution.py:94
  177.7 7.0 %collective-permute-start.26 = (bf16[2,2,64,768]{3,2,0,1:T(8,128)(2,1)S(1)}, bf16[2,2,64,768]{3,2,0,1:T(8,128)(2,1)S(1)}, u32[]{:S(2)}, u32[]{:S(2)}) collective-permute-start(bf16[2,2,64,768]{3,2,0,1:T(8,128)(2,1)S(1)} %dynamic-slice_bitcast_fusion.1), channel_id=1, source_target_pairs={{0,1},{1,0},{2,3},{3,2},{4,5},{5,4},{6,7},{7,6},{8,9},{9,8},{10,11... | collective-permute-start | bytes 1179656 | tf_op jit(solution)/shard_map/ppermute | solution.py:94
  184.8 4.9 %collective-permute-start.27 = (bf16[2,64,768]{2,1,0:T(8,128)(2,1)S(1)}, bf16[2,64,768]{2,1,0:T(8,128)(2,1)S(1)}, u32[]{:S(2)}, u32[]{:S(2)}) collective-permute-start(bf16[2,64,768]{2,1,0:T(8,128)(2,1)S(1)} %dynamic-slice_bitcast_fusion.9), channel_id=1, source_target_pairs={{0,16},{8,24},{16,0},{24,8},{1,17},{9,25},{17,1},{25,9},{2,18},{10... | collective-permute-start | bytes 589832 | tf_op jit(solution)/shard_map/ppermute | solution.py:94
  186.9 5.8 %collective-permute-start.10 = (bf16[64,640]{1,0:T(8,128)(2,1)S(1)}, bf16[64,640]{1,0:T(8,128)(2,1)S(1)}, u32[]{:S(2)}, u32[]{:S(2)}) collective-permute-start(bf16[64,640]{1,0:T(8,128)(2,1)S(1)} %dynamic-slice_bitcast_fusion.15), channel_id=1, source_target_pairs={{0,4},{1,5},{2,6},{3,7},{4,0},{5,1},{6,2},{7,3},{8,12},{9,13},{10,... | collective-permute-start | bytes 245768 | tf_op jit(solution)/shard_map/ppermute | solution.py:94
  189.8 5.0 %collective-permute-start.28 = (bf16[64,768]{1,0:T(8,128)(2,1)S(1)}, bf16[64,768]{1,0:T(8,128)(2,1)S(1)}, u32[]{:S(2)}, u32[]{:S(2)}) collective-permute-start(bf16[64,768]{1,0:T(8,128)(2,1)S(1)} %dynamic-slice_bitcast_fusion.13), channel_id=1, source_target_pairs={{0,4},{1,5},{2,6},{3,7},{4,0},{5,1},{6,2},{7,3},{8,12},{9,13},{10,... | collective-permute-start | bytes 294920 | tf_op jit(solution)/shard_map/ppermute | solution.py:94
  199.0 12.1 %collective-permute-start.30 = (bf16[128,2048]{1,0:T(8,128)(2,1)S(1)}, bf16[128,2048]{1,0:T(8,128)(2,1)S(1)}, u32[]{:S(2)}, u32[]{:S(2)}) collective-permute-start(bf16[128,2048]{1,0:T(8,128)(2,1)S(1)} %pad_maximum_fusion.8), channel_id=1, source_target_pairs={{0,8},{8,0},{16,24},{24,16},{1,9},{9,1},{17,25},{25,17},{2,10},{10... | collective-permute-start | bytes 1572872 | tf_op jit(solution)/shard_map/ppermute | solution.py:94
  (35 other events, 288.6 us)

commit v4 on v3

--- a/solution.py
+++ b/solution.py
@@ -125,28 +125,24 @@
         (sources[2][0], pick(sources[2][1], sources[0][1])),
         (pick(sources[3][0], sources[1][0]), pick(sources[3][1], sources[1][1])),
     ]
-    dims = [("seq", 0)] + [("dp", b) for b in range(1, dp_bits)] + [("seq", b) for b in range(1, seq_bits)]
-    first = dims[:3]
-    n_parts = len(first)
-    units = 2 * width // LANES
-    cuts = [units * p // n_parts * LANES for p in range(n_parts + 1)]
+    seq_dims = [("seq", b) for b in range(seq_bits)]
+    dp_dims = [("dp", b) for b in range(1, dp_bits)]
+    if seq_bits >= 2:
+        orders = [
+            seq_dims[:2] + dp_dims + seq_dims[2:],
+            seq_dims[1::-1] + seq_dims[2:] + dp_dims,
+        ]
+    else:
+        orders = [seq_dims + dp_dims] * 2
     shape = [2] * seq_bits + [2] * (dp_bits - 1) + [blk >> (dp_bits - 1)]
+    sends = [term(*send[g], 0, width) for g in range(2)]
+    keeps = [term(*keep[g], 0, width) for g in range(2)]
+    got = exchange(sends, "dp", 1)
     pieces = []
-    for p in range(n_parts):
-        order = first[p:] + first[:p] + dims[3:]
-        datas = []
-        spans = []
-        for g in range(2):
-            lo = max(cuts[p], g * width) - g * width
-            hi = min(cuts[p + 1], (g + 1) * width) - g * width
-            if hi > lo:
-                spans.append((g, lo, hi))
-        sends = [term(*send[g], lo, hi) for g, lo, hi in spans]
-        keeps = [term(*keep[g], lo, hi) for g, lo, hi in spans]
-        got = exchange(sends, "dp", 1)
-        datas = [add_bf16(k, r).reshape(shape + [k.shape[1]]) for k, r in zip(keeps, got)]
+    for g in range(2):
+        data = add_bf16(keeps[g], got[g]).reshape(shape + [width])
         removed = []
-        for axis, b in order:
+        for axis, b in orders[g]:
             if axis == "seq":
                 at = seq_bits - 1 - b
                 bit = (seq_i >> b) % 2
@@ -155,17 +151,16 @@
                 bit = (dp_i >> b) % 2
             at_now = at - sum(1 for r in removed if r < at)
             removed.append(at)
-            kept = [lax.dynamic_index_in_dim(d, bit, at_now, keepdims=False) for d in datas]
-            out = [lax.dynamic_index_in_dim(d, 1 - bit, at_now, keepdims=False) for d in datas]
-            datas = [add_bf16(k, r) for k, r in zip(kept, exchange(out, axis, 1 << b))]
-        for b in range(1, dp_bits):
-            got = exchange(datas, "dp", 1 << b)
-            first_half = (dp_i >> b) % 2 == 0
-            datas = [
-                jnp.where(first_half, jnp.concatenate([d, r], 0), jnp.concatenate([r, d], 0))
-                for d, r in zip(datas, got)
-            ]
-        pieces.extend(datas)
+            kept = lax.dynamic_index_in_dim(data, bit, at_now, keepdims=False)
+            out = lax.dynamic_index_in_dim(data, 1 - bit, at_now, keepdims=False)
+            data = add_bf16(kept, exchange(out, axis, 1 << b))
+        pieces.append(data)
+    data = jnp.concatenate(pieces, axis=1)
+    for b in range(1, dp_bits):
+        recv = exchange(data, "dp", 1 << b)
+        first_half = (dp_i >> b) % 2 == 0
+        data = jnp.where(first_half, jnp.concatenate([data, recv], 0), jnp.concatenate([recv, data], 0))
+    pieces = [data]
     part = jnp.concatenate(pieces, axis=1)
     back = exchange(part, "dp", 1)
     mine = [part[:, :width], part[:, width:]]

time: 213 us -> 207 us (0.972)
  starting transfers between devices: 52.7 us -> 25.4 us
  waiting for transfers between devices: 60.2 us -> 84.3 us
  local copies, waits for them, and re-layouts: 13.5 us -> 10.5 us
    ppermute x25 -> x12, starting transfers between devices: 41.4 us -> 16.7 us  [exchange(): lax.ppermute(array, axis, [(i, i ^ mask) for i in range(lax.axis_size(axi...]
    ppermute x6, waiting for transfers between devices: 23.1 us -> 36.5 us  [partner(): lax.ppermute(array, axis, [(i, i ^ 1 << apart) for i in range(lax.axis_si...]
    ppermute x25 -> x12, waiting for transfers between devices: 37.2 us -> 47.8 us  [exchange(): lax.ppermute(array, axis, [(i, i ^ mask) for i in range(lax.axis_size(axi...]
    unnamed x56 -> x52, local copies, waits for them, and re-layouts: 5.13 us -> 1.97 us
    dynamic_slice x6 -> x4, local copies, waits for them, and re-layouts: 0.35 us -> 3.46 us  [the longest x2 2.06 us: reduce_gradients(): out = lax.dynamic_index_in_dim(data, 1 - bit, at_now, keepdims=False)]
    squeeze x3, local copies, waits for them, and re-layouts: 3.19 us -> 0.11 us  [body(): piece[1]]
    ppermute x6, starting transfers between devices: 11.3 us -> 8.75 us  [partner(): lax.ppermute(array, axis, [(i, i ^ 1 << apart) for i in range(lax.axis_si...]
    another operation x3, other arithmetic: 2.52 us -> 0.15 us  [swap_blocks(): jnp.stack([lax.dynamic_slice_in_dim(keys_local, start, BLOCK, 0), lax.dyn...]
  transfers between devices with their start and end apart: 31 -> 18, of which waited for: 16 -> 13; matrix products, arithmetic and copies ran while one was open for 16% -> 17% of each run, Pallas kernels for 0% -> 0%
where the time goes in v4:
time: 207 us
  waiting for transfers between devices  84.3 us (41%)
  Pallas kernels  38.1 us (18%)
  matrix products  30.2 us (15%)
  starting transfers between devices  25.4 us (12%)
  other arithmetic  15.1 us (7%)
  local copies, waits for them, and re-layouts  10.5 us (5%)
  between operations  3.35 us (2%)
    ppermute x12, waiting for transfers between devices, exchange(): lax.ppermute(array, axis, [(i, i ^ mask) for i in range(lax.axis_size(axi...  47.8 us
    pallas_call x1, Pallas kernels, attention(): pl.pallas_call(functools.partial(attention_kernel, head=head, scale=head...  38.1 us
    ppermute x6, waiting for transfers between devices, partner(): lax.ppermute(array, axis, [(i, i ^ 1 << apart) for i in range(lax.axis_si...  36.5 us
    ppermute x12, starting transfers between devices, exchange(): lax.ppermute(array, axis, [(i, i ^ mask) for i in range(lax.axis_size(axi...  16.7 us
    dot_general x4, matrix products, term(): jnp.dot(left.T, right[:, lo:hi], preferred_element_type=jnp.float32)  11.8 us
    ppermute x6, starting transfers between devices, partner(): lax.ppermute(array, axis, [(i, i ^ 1 << apart) for i in range(lax.axis_si...  8.75 us
    dot_general x1, matrix products, body(): jnp.dot(rows, w_value, preferred_element_type=jnp.float32)  4.28 us
  transfers between devices with their start and end apart: 18, of which 13 were waited for; matrix products, arithmetic and copies ran while one was open for 17% of the time, Pallas kernels for 0%

profile of v4, /device:TPU:1, one launch (start us, length us, event | category | flops | bytes accessed | tf_op | source)
XLA Modules:
  0.0 206.8 jit_solution(6511993244893932910)
XLA Ops:
  4.0 4.3 %convolution_convert_fusion.3 = bf16[512,1024]{1,0:T(8,128)(2,1)} fusion(bf16[1024,1024]{1,0:T(8,128)(2,1)} %param.10, bf16[1,512,1024]{2,1,0:T(8,128)(2,1)} %param.7), kind=kOutput, calls=%fused_computation.14 | convolution fusion | flops 1074266112 | bytes 4194304 | tf_op jit(solution)/shard_map/dot_general | solution.py:185
  14.6 2.4 %collective-permute-start.2 = (bf16[2,128,1024]{2,1,0:T(8,128)(2,1)S(1)}, bf16[2,128,1024]{2,1,0:T(8,128)(2,1)S(1)}, u32[]{:S(2)}, u32[]{:S(2)}) collective-permute-start(bf16[2,128,1024]{2,1,0:T(8,128)(2,1)S(1)} %pad_maximum_fusion.4), channel_id=1, source_target_pairs={{0,4},{1,5},{2,6},{3,7},{4,0},{5,1},{6,2},{7,3},{8,12},{9,13},{10,... | collective-permute-start | bytes 1572872 | tf_op jit(solution)/shard_map/ppermute | solution.py:16
  19.2 2.3 %convolution_convert_fusion.2.do_ref = bf16[512,1024]{1,0:T(8,128)(2,1)} fusion(bf16[1024,1024]{1,0:T(8,128)(2,1)S(1)} %copy-done.11, bf16[1,512,1024]{2,1,0:T(8,128)(2,1)S(1)} %copy-done.19), kind=kOutput, calls=%fused_computation.13 | convolution fusion | flops 1074266112 | bytes 4194304 | tf_op jit(solution)/shard_map/dot_general | solution.py:189
  21.5 3.2 %collective-permute-done = bf16[2,128,1024]{2,1,0:T(8,128)(2,1)S(1)} collective-permute-done((bf16[2,128,1024]{2,1,0:T(8,128)(2,1)S(1)}, bf16[2,128,1024]{2,1,0:T(8,128)(2,1)S(1)}, u32[]{:S(2)}, u32[]{:S(2)}) %collective-permute-start) | collective-permute-done | bytes 524320 | tf_op jit(solution)/shard_map/ppermute | solution.py:16
  24.8 11.9 %collective-permute-done.1 = bf16[2,128,1024]{2,1,0:T(8,128)(2,1)S(1)} collective-permute-done((bf16[2,128,1024]{2,1,0:T(8,128)(2,1)S(1)}, bf16[2,128,1024]{2,1,0:T(8,128)(2,1)S(1)}, u32[]{:S(2)}, u32[]{:S(2)}) %collective-permute-start.1) | collective-permute-done | bytes 524320 | tf_op jit(solution)/shard_map/ppermute | solution.py:16
  39.6 38.1 %shard_map.118 = (bf16[512,1024]{1,0:T(8,128)(2,1)}, bf16[512,1024]{1,0:T(8,128)(2,1)}, f32[896,1024]{1,0:T(8,128)}, f32[896,1024]{1,0:T(8,128)}) custom-call(bf16[512,1024]{1,0:T(8,128)(2,1)} %convolution_convert_fusion.5.q_ref, bf16[896,1024]{1,0:T(8,128)(2,1)} %pad_maximum_fusion.k_ref, bf16[896,1024]{1,0:T(8,128)(2,1)} %pad_maximum_fusion.1.v_ref, ...), custom_call_target="tpu_custom_call" | custom-call | flops 11274289152 | bytes 13107200 | tf_op jit(solution)/shard_map/pallas_call | solution.py:73
  77.7 2.5 %convert.31 = bf16[896,1024]{1,0:T(8,128)(2,1)S(1)} convert(f32[896,1024]{1,0:T(8,128)} %get-tuple-element.12) | non-fusion elementwise | flops 917504 | bytes 5505024 | tf_op jit(solution)/shard_map/convert.26
  82.0 2.6 %collective-permute-start.4 = (bf16[2,128,1024]{2,1,0:T(8,128)(2,1)}, bf16[2,128,1024]{2,1,0:T(8,128)(2,1)S(1)}, u32[]{:S(2)}, u32[]{:S(2)}) collective-permute-start(bf16[2,128,1024]{2,1,0:T(8,128)(2,1)} %pad_maximum_fusion.6), channel_id=1, source_target_pairs={{0,2},{1,3},{2,0},{3,1},{4,6},{5,7},{6,4},{7,5},{8,10},{9,11},{10,... | collective-permute-start | bytes 1572872 | tf_op jit(solution)/shard_map/ppermute | solution.py:16
  88.6 8.8 %collective-permute-done.4 = bf16[2,128,1024]{2,1,0:T(8,128)(2,1)S(1)} collective-permute-done((bf16[2,128,1024]{2,1,0:T(8,128)(2,1)}, bf16[2,128,1024]{2,1,0:T(8,128)(2,1)S(1)}, u32[]{:S(2)}, u32[]{:S(2)}) %collective-permute-start.4) | collective-permute-done | bytes 524320 | tf_op jit(solution)/shard_map/ppermute | solution.py:16
  99.2 12.6 %collective-permute-done.5 = bf16[2,128,1024]{2,1,0:T(8,128)(2,1)S(1)} collective-permute-done((bf16[2,128,1024]{2,1,0:T(8,128)(2,1)S(1)}, bf16[2,128,1024]{2,1,0:T(8,128)(2,1)S(1)}, u32[]{:S(2)}, u32[]{:S(2)}) %collective-permute-start.5) | collective-permute-done | bytes 524320 | tf_op jit(solution)/shard_map/ppermute | solution.py:16
  112.2 2.6 %convert_bitcast_fusion = bf16[1024,1024]{1,0:T(8,128)(2,1)} fusion(bf16[1,512,1024]{2,1,0:T(8,128)(2,1)S(1)} %copy-done.17, bf16[512,1024]{1,0:T(8,128)(2,1)S(1)} %copy-done.22, pred[]{:T(512)S(6)} %eq.17, f32[512,1024]{1,0:T(8,128)S(1)} %get-tuple-element.28), kind=kOutput, calls=%fused_computation.7 | convolution fusion | flops 1075838976 | bytes 6291457 | tf_op jit(solution)/shard_map/dot_general | solution.py:102
  114.8 3.3 %collective-permute-start.6 = (bf16[1024,1024]{1,0:T(8,128)(2,1)}, bf16[1024,1024]{1,0:T(8,128)(2,1)}, u32[]{:S(2)}, u32[]{:S(2)}) collective-permute-start(bf16[1024,1024]{1,0:T(8,128)(2,1)} %convert_bitcast_fusion), channel_id=1, source_target_pairs={{0,8},{8,0},{16,24},{24,16},{1,9},{9,1},{17,25},{25,17},{2,10},{10... | collective-permute-start | bytes 6291464 | tf_op jit(solution)/shard_map/ppermute | solution.py:94
  118.1 2.7 %convolution_convert_fusion = bf16[1024,1024]{1,0:T(8,128)(2,1)} fusion(bf16[1,512,1024]{2,1,0:T(8,128)(2,1)S(1)} %copy-done.20, bf16[512,1024]{1,0:T(8,128)(2,1)S(1)} %copy-done.23, bf16[1,512,1024]{2,1,0:T(8,128)(2,1)S(1)} %copy-done.17, pred[]{:T(512)S(6)} %eq.17, f32[512,1024]{1,0:T(8,128)S(1)} %get-tuple-element.29), kind=kOutput, calls=%fused_computation.9 | convolution fusion | flops 1076363264 | bytes 7340033 | tf_op jit(solution)/shard_map/dot_general | solution.py:102
  122.3 3.5 %fusion = bf16[1024,1024]{1,0:T(8,128)(2,1)S(1)} fusion(bf16[1024,1024]{1,0:T(8,128)(2,1)} %collective-permute-done.6, bf16[1,512,1024]{2,1,0:T(8,128)(2,1)S(1)} %copy-done.17, bf16[512,1024]{1,0:T(8,128)(2,1)} %get-tuple-element.11, pred[]{:T(512)S(6)} %eq.17, f32[512,1024]{1,0:T(8,128)} %copy-done.1), kind=kOutput, calls=%fused_computation.1 | convolution fusion | flops 1080033280 | bytes 8388609 | tf_op jit(solution)/shard_map/dot_general | solution.py:102
  128.8 2.9 %add_convert_fusion = bf16[1024,1024]{1,0:T(8,128)(2,1)S(1)} fusion(bf16[1024,1024]{1,0:T(8,128)(2,1)} %collective-permute-done.11, bf16[1,512,1024]{2,1,0:T(8,128)(2,1)S(1)} %copy-done.21, bf16[512,1024]{1,0:T(8,128)(2,1)S(1)} %copy-done.24, bf16[1,512,1024]{2,1,0:T(8,128)(2,1)S(1)} %copy-done.18, pred[]{:T(512)S(6)} %eq.17, f32[512,1024]{1,0:T(8,128)S(1)} %copy-done.6), kind=kOutput, calls=%fused_computation.2 | convolution fusion | flops 1080557568 | bytes 9437185 | tf_op jit(solution)/shard_map/dot_general | solution.py:102
  133.9 2.5 %fusion.43 = f32[512,1024]{1,0:T(8,128)S(1)} fusion(bf16[512,1024]{1,0:T(8,128)(2,1)} %get-tuple-element.11, bf16[1024,1024]{1,0:T(8,128)(2,1)S(1)} %copy-done), kind=kOutput, calls=%fused_computation.117 | convolution fusion | flops 1073741824 | bytes 5242880 | tf_op jit(solution)/shard_map/dot_general | solution.py:210
  136.4 15.0 %collective-permute-done.7 = bf16[2,2,2,64,1024]{4,3,0,2,1:T(8,128)(2,1)} collective-permute-done((bf16[2,2,2,64,1024]{4,3,0,2,1:T(8,128)(2,1)}, bf16[2,2,2,64,1024]{4,3,0,2,1:T(8,128)(2,1)}, u32[]{:S(2)}, u32[]{:S(2)}) %collective-permute-start.7) | collective-permute-done | bytes 1048608 | tf_op jit(solution)/shard_map/ppermute | solution.py:94
  153.3 5.0 %collective-permute-done.12 = bf16[2,2,2,64,1024]{4,3,2,0,1:T(8,128)(2,1)} collective-permute-done((bf16[2,2,2,64,1024]{4,3,2,0,1:T(8,128)(2,1)}, bf16[2,2,2,64,1024]{4,3,2,0,1:T(8,128)(2,1)}, u32[]{:S(2)}, u32[]{:S(2)}) %collective-permute-start.12) | collective-permute-done | bytes 1048608 | tf_op jit(solution)/shard_map/ppermute | solution.py:94
  163.6 5.8 %collective-permute-done.8 = bf16[2,2,64,1024]{3,2,0,1:T(8,128)(2,1)S(1)} collective-permute-done((bf16[2,2,64,1024]{3,2,0,1:T(8,128)(2,1)S(1)}, bf16[2,2,64,1024]{3,2,0,1:T(8,128)(2,1)S(1)}, u32[]{:S(2)}, u32[]{:S(2)}) %collective-permute-start.8) | collective-permute-done | bytes 524320 | tf_op jit(solution)/shard_map/ppermute | solution.py:94
  172.0 3.9 %collective-permute-done.9 = bf16[2,64,1024]{2,1,0:T(8,128)(2,1)S(1)} collective-permute-done((bf16[2,64,1024]{2,1,0:T(8,128)(2,1)S(1)}, bf16[2,64,1024]{2,1,0:T(8,128)(2,1)S(1)}, u32[]{:S(2)}, u32[]{:S(2)}) %collective-permute-start.9) | collective-permute-done | bytes 262176 | tf_op jit(solution)/shard_map/ppermute | solution.py:94
  176.8 10.8 %collective-permute-done.14 = bf16[2,64,1024]{2,1,0:T(8,128)(2,1)S(1)} collective-permute-done((bf16[2,64,1024]{2,1,0:T(8,128)(2,1)S(1)}, bf16[2,64,1024]{2,1,0:T(8,128)(2,1)S(1)}, u32[]{:S(2)}, u32[]{:S(2)}) %collective-permute-start.14) | collective-permute-done | bytes 262176 | tf_op jit(solution)/shard_map/ppermute | solution.py:94
  194.3 3.5 %collective-permute-done.16 = bf16[64,2048]{1,0:T(8,128)(2,1)S(1)} collective-permute-done((bf16[64,2048]{1,0:T(8,128)(2,1)S(1)}, bf16[64,2048]{1,0:T(8,128)(2,1)S(1)}, u32[]{:S(2)}, u32[]{:S(2)}) %collective-permute-start.16) | collective-permute-done | bytes 262176 | tf_op jit(solution)/shard_map/ppermute | solution.py:94
  197.9 5.3 %collective-permute-start.17 = (bf16[128,2048]{1,0:T(8,128)(2,1)S(1)}, bf16[128,2048]{1,0:T(8,128)(2,1)S(1)}, u32[]{:S(2)}, u32[]{:S(2)}) collective-permute-start(bf16[128,2048]{1,0:T(8,128)(2,1)S(1)} %maximum_select_fusion), channel_id=1, source_target_pairs={{0,8},{8,0},{16,24},{24,16},{1,9},{9,1},{17,25},{25,17},{2,10},{10... | collective-permute-start | bytes 1572872 | tf_op jit(solution)/shard_map/ppermute | solution.py:94
  203.2 2.3 %fusion.4 = bf16[1,512,1024]{2,1,0:T(8,128)(2,1)} fusion(bf16[1024,1024]{1,0:T(8,128)(2,1)S(1)} %copy-done.10, f32[512,1024]{1,0:T(8,128)S(1)} %fusion.43, f32[512,1024]{1,0:T(8,128)S(1)} %fusion.40, f32[512,1024]{1,0:T(8,128)S(1)} %copy-done.2), kind=kOutput, calls=%fused_computation.18 | convolution fusion | flops 1075838976 | bytes 9437184 | tf_op jit(solution)/shard_map/dot_general | solution.py:212
  (123 shorter events, 45.9 us)
Async XLA Ops:
  0.6 16.3 %copy-start = (bf16[1024,1024]{1,0:T(8,128)(2,1)S(1)}, bf16[1024,1024]{1,0:T(8,128)(2,1)}, u32[]{:S(2)}) copy-start(bf16[1024,1024]{1,0:T(8,128)(2,1)} %param.8) | copy-start | bytes 6291460
  11.0 13.7 %collective-permute-start = (bf16[2,128,1024]{2,1,0:T(8,128)(2,1)S(1)}, bf16[2,128,1024]{2,1,0:T(8,128)(2,1)S(1)}, u32[]{:S(2)}, u32[]{:S(2)}) collective-permute-start(bf16[2,128,1024]{2,1,0:T(8,128)(2,1)S(1)} %pad_maximum_fusion.2), channel_id=1, source_target_pairs={{0,1},{1,0},{2,3},{3,2},{4,5},{5,4},{6,7},{7,6},{8,9},{9,8},{10,11... | collective-permute-start | bytes 1572872 | tf_op jit(solution)/shard_map/ppermute | solution.py:16
  13.1 23.5 %collective-permute-start.1 = (bf16[2,128,1024]{2,1,0:T(8,128)(2,1)S(1)}, bf16[2,128,1024]{2,1,0:T(8,128)(2,1)S(1)}, u32[]{:S(2)}, u32[]{:S(2)}) collective-permute-start(bf16[2,128,1024]{2,1,0:T(8,128)(2,1)S(1)} %pad_maximum_fusion.3), channel_id=1, source_target_pairs={{0,2},{1,3},{2,0},{3,1},{4,6},{5,7},{6,4},{7,5},{8,10},{9,11},{10,... | collective-permute-start | bytes 1572872 | tf_op jit(solution)/shard_map/ppermute | solution.py:16
  14.6 22.1 %collective-permute-start.2 = (bf16[2,128,1024]{2,1,0:T(8,128)(2,1)S(1)}, bf16[2,128,1024]{2,1,0:T(8,128)(2,1)S(1)}, u32[]{:S(2)}, u32[]{:S(2)}) collective-permute-start(bf16[2,128,1024]{2,1,0:T(8,128)(2,1)S(1)} %pad_maximum_fusion.4), channel_id=1, source_target_pairs={{0,4},{1,5},{2,6},{3,7},{4,0},{5,1},{6,2},{7,3},{8,12},{9,13},{10,... | collective-permute-start | bytes 1572872 | tf_op jit(solution)/shard_map/ppermute | solution.py:16
  21.5 15.2 %copy-start.9 = (bf16[512,1024]{1,0:T(8,128)(2,1)S(1)}, bf16[512,1024]{1,0:T(8,128)(2,1)}, u32[]{:S(2)}) copy-start(bf16[512,1024]{1,0:T(8,128)(2,1)} %convolution_convert_fusion.3) | copy-start | bytes 3145732
  82.0 15.4 %collective-permute-start.4 = (bf16[2,128,1024]{2,1,0:T(8,128)(2,1)}, bf16[2,128,1024]{2,1,0:T(8,128)(2,1)S(1)}, u32[]{:S(2)}, u32[]{:S(2)}) collective-permute-start(bf16[2,128,1024]{2,1,0:T(8,128)(2,1)} %pad_maximum_fusion.6), channel_id=1, source_target_pairs={{0,2},{1,3},{2,0},{3,1},{4,6},{5,7},{6,4},{7,5},{8,10},{9,11},{10,... | collective-permute-start | bytes 1572872 | tf_op jit(solution)/shard_map/ppermute | solution.py:16
  85.4 12.1 %collective-permute-start.3 = (bf16[2,128,1024]{2,1,0:T(8,128)(2,1)}, bf16[2,128,1024]{2,1,0:T(8,128)(2,1)}, u32[]{:S(2)}, u32[]{:S(2)}) collective-permute-start(bf16[2,128,1024]{2,1,0:T(8,128)(2,1)} %pad_maximum_fusion.5), channel_id=1, source_target_pairs={{0,1},{1,0},{2,3},{3,2},{4,5},{5,4},{6,7},{7,6},{8,9},{9,8},{10,11... | collective-permute-start | bytes 1572872 | tf_op jit(solution)/shard_map/ppermute | solution.py:16
  88.5 23.3 %collective-permute-start.5 = (bf16[2,128,1024]{2,1,0:T(8,128)(2,1)S(1)}, bf16[2,128,1024]{2,1,0:T(8,128)(2,1)S(1)}, u32[]{:S(2)}, u32[]{:S(2)}) collective-permute-start(bf16[2,128,1024]{2,1,0:T(8,128)(2,1)S(1)} %pad_maximum_fusion.7), channel_id=1, source_target_pairs={{0,4},{1,5},{2,6},{3,7},{4,0},{5,1},{6,2},{7,3},{8,12},{9,13},{10,... | collective-permute-start | bytes 1572872 | tf_op jit(solution)/shard_map/ppermute | solution.py:16
  99.1 13.0 %copy-start.17 = (bf16[1,512,1024]{2,1,0:T(8,128)(2,1)S(1)}, bf16[1,512,1024]{2,1,0:T(8,128)(2,1)}, u32[]{:S(2)}) copy-start(bf16[1,512,1024]{2,1,0:T(8,128)(2,1)} %param.7) | copy-start | bytes 3145732
  99.1 13.0 %copy-start.22 = (bf16[512,1024]{1,0:T(8,128)(2,1)S(1)}, bf16[512,1024]{1,0:T(8,128)(2,1)}, u32[]{:S(2)}) copy-start(bf16[512,1024]{1,0:T(8,128)(2,1)} %get-tuple-element.11) | copy-start | bytes 3145732
  114.8 7.5 %collective-permute-start.6 = (bf16[1024,1024]{1,0:T(8,128)(2,1)}, bf16[1024,1024]{1,0:T(8,128)(2,1)}, u32[]{:S(2)}, u32[]{:S(2)}) collective-permute-start(bf16[1024,1024]{1,0:T(8,128)(2,1)} %convert_bitcast_fusion), channel_id=1, source_target_pairs={{0,8},{8,0},{16,24},{24,16},{1,9},{9,1},{17,25},{25,17},{2,10},{10... | collective-permute-start | bytes 6291464 | tf_op jit(solution)/shard_map/ppermute | solution.py:94
  120.8 7.5 %collective-permute-start.11 = (bf16[1024,1024]{1,0:T(8,128)(2,1)}, bf16[1024,1024]{1,0:T(8,128)(2,1)}, u32[]{:S(2)}, u32[]{:S(2)}) collective-permute-start(bf16[1024,1024]{1,0:T(8,128)(2,1)} %convolution_convert_fusion), channel_id=1, source_target_pairs={{0,8},{8,0},{16,24},{24,16},{1,9},{9,1},{17,25},{25,17},{2,10},{10... | collective-permute-start | bytes 6291464 | tf_op jit(solution)/shard_map/ppermute | solution.py:94
  127.1 24.3 %collective-permute-start.7 = (bf16[2,2,2,64,1024]{4,3,0,2,1:T(8,128)(2,1)}, bf16[2,2,2,64,1024]{4,3,0,2,1:T(8,128)(2,1)}, u32[]{:S(2)}, u32[]{:S(2)}) collective-permute-start(bf16[2,2,2,64,1024]{4,3,0,2,1:T(8,128)(2,1)} %bitcast.164), channel_id=1, source_target_pairs={{0,1},{1,0},{2,3},{3,2},{4,5},{5,4},{6,7},{7,6},{8,9},{9,8},{10,11... | collective-permute-start | bytes 3145736 | tf_op jit(solution)/shard_map/ppermute | solution.py:94
  133.9 24.3 %collective-permute-start.12 = (bf16[2,2,2,64,1024]{4,3,2,0,1:T(8,128)(2,1)}, bf16[2,2,2,64,1024]{4,3,2,0,1:T(8,128)(2,1)}, u32[]{:S(2)}, u32[]{:S(2)}) collective-permute-start(bf16[2,2,2,64,1024]{4,3,2,0,1:T(8,128)(2,1)} %bitcast.163), channel_id=1, source_target_pairs={{0,2},{1,3},{2,0},{3,1},{4,6},{5,7},{6,4},{7,5},{8,10},{9,11},{10,... | collective-permute-start | bytes 3145736 | tf_op jit(solution)/shard_map/ppermute | solution.py:94
  153.2 16.2 %collective-permute-start.8 = (bf16[2,2,64,1024]{3,2,0,1:T(8,128)(2,1)S(1)}, bf16[2,2,64,1024]{3,2,0,1:T(8,128)(2,1)S(1)}, u32[]{:S(2)}, u32[]{:S(2)}) collective-permute-start(bf16[2,2,64,1024]{3,2,0,1:T(8,128)(2,1)S(1)} %dynamic-slice_bitcast_fusion.1), channel_id=1, source_target_pairs={{0,2},{1,3},{2,0},{3,1},{4,6},{5,7},{6,4},{7,5},{8,10},{9,11},{10,... | collective-permute-start | bytes 1572872 | tf_op jit(solution)/shard_map/ppermute | solution.py:94
  160.1 10.8 %collective-permute-start.13 = (bf16[2,2,64,1024]{3,2,1,0:T(8,128)(2,1)S(1)}, bf16[2,2,64,1024]{3,2,1,0:T(8,128)(2,1)S(1)}, u32[]{:S(2)}, u32[]{:S(2)}) collective-permute-start(bf16[2,2,64,1024]{3,2,1,0:T(8,128)(2,1)S(1)} %dynamic-slice_bitcast_fusion), channel_id=1, source_target_pairs={{0,1},{1,0},{2,3},{3,2},{4,5},{5,4},{6,7},{7,6},{8,9},{9,8},{10,11... | collective-permute-start | bytes 1572872 | tf_op jit(solution)/shard_map/ppermute | solution.py:94
  169.6 6.3 %collective-permute-start.9 = (bf16[2,64,1024]{2,1,0:T(8,128)(2,1)S(1)}, bf16[2,64,1024]{2,1,0:T(8,128)(2,1)S(1)}, u32[]{:S(2)}, u32[]{:S(2)}) collective-permute-start(bf16[2,64,1024]{2,1,0:T(8,128)(2,1)S(1)} %dynamic-slice_bitcast_fusion.3), channel_id=1, source_target_pairs={{0,16},{8,24},{16,0},{24,8},{1,17},{9,25},{17,1},{25,9},{2,18},{10... | collective-permute-start | bytes 786440 | tf_op jit(solution)/shard_map/ppermute | solution.py:94
  170.9 22.1 %copy-start.14 = (bf16[1024,1024]{1,0:T(8,128)(2,1)S(1)}, bf16[1024,1024]{1,0:T(8,128)(2,1)}, u32[]{:S(2)}) copy-start(bf16[1024,1024]{1,0:T(8,128)(2,1)} %param.9) | copy-start | bytes 6291460
  171.1 21.9 %copy-start.7 = (f32[512,1024]{1,0:T(8,128)S(1)}, f32[512,1024]{1,0:T(8,128)}, u32[]{:S(2)}) copy-start(f32[512,1024]{1,0:T(8,128)} %copy-done.5) | copy-start | bytes 6291460
  171.2 16.4 %collective-permute-start.14 = (bf16[2,64,1024]{2,1,0:T(8,128)(2,1)S(1)}, bf16[2,64,1024]{2,1,0:T(8,128)(2,1)S(1)}, u32[]{:S(2)}, u32[]{:S(2)}) collective-permute-start(bf16[2,64,1024]{2,1,0:T(8,128)(2,1)S(1)} %dynamic-slice_bitcast_fusion.2), channel_id=1, source_target_pairs={{0,4},{1,5},{2,6},{3,7},{4,0},{5,1},{6,2},{7,3},{8,12},{9,13},{10,... | collective-permute-start | bytes 786440 | tf_op jit(solution)/shard_map/ppermute | solution.py:94
  176.2 14.2 %collective-permute-start.10 = (bf16[64,1024]{1,0:T(8,128)(2,1)S(1)}, bf16[64,1024]{1,0:T(8,128)(2,1)S(1)}, u32[]{:S(2)}, u32[]{:S(2)}) collective-permute-start(bf16[64,1024]{1,0:T(8,128)(2,1)S(1)} %dynamic-slice_bitcast_fusion.11), channel_id=1, source_target_pairs={{0,4},{1,5},{2,6},{3,7},{4,0},{5,1},{6,2},{7,3},{8,12},{9,13},{10,... | collective-permute-start | bytes 393224 | tf_op jit(solution)/shard_map/ppermute | solution.py:94
  187.7 4.0 %collective-permute-start.15 = (bf16[64,1024]{1,0:T(8,128)(2,1)S(1)}, bf16[64,1024]{1,0:T(8,128)(2,1)S(1)}, u32[]{:S(2)}, u32[]{:S(2)}) collective-permute-start(bf16[64,1024]{1,0:T(8,128)(2,1)S(1)} %dynamic-slice_bitcast_fusion.10), channel_id=1, source_target_pairs={{0,16},{8,24},{16,0},{24,8},{1,17},{9,25},{17,1},{25,9},{2,18},{10... | collective-permute-start | bytes 393224 | tf_op jit(solution)/shard_map/ppermute | solution.py:94
  191.8 6.0 %collective-permute-start.16 = (bf16[64,2048]{1,0:T(8,128)(2,1)S(1)}, bf16[64,2048]{1,0:T(8,128)(2,1)S(1)}, u32[]{:S(2)}, u32[]{:S(2)}) collective-permute-start(bf16[64,2048]{1,0:T(8,128)(2,1)S(1)} %pad_maximum_fusion.8), channel_id=1, source_target_pairs={{0,16},{8,24},{16,0},{24,8},{1,17},{9,25},{17,1},{25,9},{2,18},{10... | collective-permute-start | bytes 786440 | tf_op jit(solution)/shard_map/ppermute | solution.py:94
  197.9 7.5 %collective-permute-start.17 = (bf16[128,2048]{1,0:T(8,128)(2,1)S(1)}, bf16[128,2048]{1,0:T(8,128)(2,1)S(1)}, u32[]{:S(2)}, u32[]{:S(2)}) collective-permute-start(bf16[128,2048]{1,0:T(8,128)(2,1)S(1)} %maximum_select_fusion), channel_id=1, source_target_pairs={{0,8},{8,0},{16,24},{24,16},{1,9},{9,1},{17,25},{25,17},{2,10},{10... | collective-permute-start | bytes 1572872 | tf_op jit(solution)/shard_map/ppermute | solution.py:94
  (20 other events, 96.7 us)

commit v5 on v4

--- a/solution.py
+++ b/solution.py
@@ -102,47 +102,36 @@
     return jnp.dot(left.T, right[:, lo:hi], preferred_element_type=jnp.float32).astype(jnp.bfloat16)
 
 
-def reduce_gradients(sources):
+def halving_orders(seq_bits, dp_bits):
+    seq_dims = [("seq", b) for b in range(seq_bits)]
+    dp_dims = [("dp", b) for b in range(1, dp_bits)]
+    if seq_bits >= 2:
+        return [seq_dims[:2] + dp_dims + seq_dims[2:], seq_dims[1::-1] + seq_dims[2:] + dp_dims]
+    return [seq_dims + dp_dims] * 2
+
+
+def reduce_pair(first, second):
     n_dp = lax.axis_size("dp")
     n_seq = lax.axis_size("seq")
     seq_bits = n_seq.bit_length() - 1
     dp_bits = n_dp.bit_length() - 1
-    width = sources[0][1].shape[1]
-    rows = sources[0][0].shape[1]
+    width = first[1].shape[1]
+    rows = first[0].shape[1]
     blk = rows // n_seq
     dp_i = lax.axis_index("dp")
     seq_i = lax.axis_index("seq")
     low = dp_i % 2 == 0
-
-    def pick(a, b):
-        return jnp.where(low, a, b)
-
-    keep = [
-        (sources[0][0], pick(sources[0][1], sources[2][1])),
-        (pick(sources[1][0], sources[3][0]), pick(sources[1][1], sources[3][1])),
-    ]
-    send = [
-        (sources[2][0], pick(sources[2][1], sources[0][1])),
-        (pick(sources[3][0], sources[1][0]), pick(sources[3][1], sources[1][1])),
-    ]
-    seq_dims = [("seq", b) for b in range(seq_bits)]
-    dp_dims = [("dp", b) for b in range(1, dp_bits)]
-    if seq_bits >= 2:
-        orders = [
-            seq_dims[:2] + dp_dims + seq_dims[2:],
-            seq_dims[1::-1] + seq_dims[2:] + dp_dims,
-        ]
-    else:
-        orders = [seq_dims + dp_dims] * 2
+    keep = (jnp.where(low, first[0], second[0]), jnp.where(low, first[1], second[1]))
+    send = (jnp.where(low, second[0], first[0]), jnp.where(low, second[1], first[1]))
+    got = exchange(term(*send, 0, width), "dp", 1)
     shape = [2] * seq_bits + [2] * (dp_bits - 1) + [blk >> (dp_bits - 1)]
-    sends = [term(*send[g], 0, width) for g in range(2)]
-    keeps = [term(*keep[g], 0, width) for g in range(2)]
-    got = exchange(sends, "dp", 1)
+    cut = (width // LANES) // 2 * LANES
+    spans = [(0, cut), (cut, width)]
     pieces = []
-    for g in range(2):
-        data = add_bf16(keeps[g], got[g]).reshape(shape + [width])
+    for order, (lo, hi) in zip(halving_orders(seq_bits, dp_bits), spans):
+        data = add_bf16(term(*keep, lo, hi), got[:, lo:hi]).reshape(shape + [hi - lo])
         removed = []
-        for axis, b in orders[g]:
+        for axis, b in order:
             if axis == "seq":
                 at = seq_bits - 1 - b
                 bit = (seq_i >> b) % 2
@@ -160,17 +149,21 @@
         recv = exchange(data, "dp", 1 << b)
         first_half = (dp_i >> b) % 2 == 0
         data = jnp.where(first_half, jnp.concatenate([data, recv], 0), jnp.concatenate([recv, data], 0))
-    pieces = [data]
-    part = jnp.concatenate(pieces, axis=1)
-    back = exchange(part, "dp", 1)
-    mine = [part[:, :width], part[:, width:]]
+    return data
+
+
+def gather_pairs(early, late):
+    width = early.shape[1]
+    both = jnp.concatenate([early, late], axis=1)
+    back = exchange(both, "dp", 1)
+    low = lax.axis_index("dp") % 2 == 0
+    mine = [both[:, :width], both[:, width:]]
     other = [back[:, :width], back[:, width:]]
-    return (
-        pick(mine[0], other[0]).astype(jnp.float32),
-        pick(mine[1], other[1]).astype(jnp.float32),
-        pick(other[0], mine[0]).astype(jnp.float32),
-        pick(other[1], mine[1]).astype(jnp.float32),
-    )
+    query = jnp.where(low, mine[0], other[0])
+    outw = jnp.where(low, other[0], mine[0])
+    key = jnp.where(low, mine[1], other[1])
+    value = jnp.where(low, other[1], mine[1])
+    return tuple(g.astype(jnp.float32) for g in (query, key, value, outw))
 
 
 def body(layer_input, w_query, w_key, w_value, w_out, offsets, grad_out):
@@ -211,8 +204,9 @@
     total = total + jnp.dot(dkey, w_key.T, preferred_element_type=jnp.float32)
     total = total + jnp.dot(dvalue, w_value.T, preferred_element_type=jnp.float32)
     grad_input = total.astype(jnp.bfloat16)
-    sources = ((rows, dquery), (rows, dkey), (rows, dvalue), (attended, cot))
-    grads = reduce_gradients(sources)
+    early = reduce_pair((rows, dquery), (attended, cot))
+    late = reduce_pair((rows, dkey), (rows, dvalue))
+    grads = gather_pairs(early, late)
     return (result[None], grad_input[None]) + grads
 
 

time: 207 us -> 210 us (1.014)
  waiting for transfers between devices: 84.3 us -> 62.8 us
  starting transfers between devices: 25.4 us -> 42 us
  local copies, waits for them, and re-layouts: 10.5 us -> 20.1 us
  matrix products: 30.2 us -> 28 us
    ppermute x12 -> x21, starting transfers between devices: 16.7 us -> 30.7 us  [exchange(): lax.ppermute(array, axis, [(i, i ^ mask) for i in range(lax.axis_size(axi...]
    ppermute x12 -> x21, waiting for transfers between devices: 47.8 us -> 36.9 us  [exchange(): lax.ppermute(array, axis, [(i, i ^ mask) for i in range(lax.axis_size(axi...]
    ppermute x6, waiting for transfers between devices: 36.5 us -> 25.9 us  [partner(): lax.ppermute(array, axis, [(i, i ^ 1 << apart) for i in range(lax.axis_si...]
    convert_element_type x0 -> x2, local copies, waits for them, and re-layouts: none -> 3.77 us  [add_bf16(): return (a.astype(jnp.float32) + b.astype(jnp.float32)).astype(jnp.bfloat16)]
    squeeze x3, local copies, waits for them, and re-layouts: 0.11 us -> 3.19 us  [body(): piece[1]]
    ppermute x6, starting transfers between devices: 8.75 us -> 11.3 us  [partner(): lax.ppermute(array, axis, [(i, i ^ 1 << apart) for i in range(lax.axis_si...]
    another operation x3, other arithmetic: 0.15 us -> 2.52 us  [swap_blocks(): jnp.stack([lax.dynamic_slice_in_dim(keys_local, start, BLOCK, 0), lax.dyn...]
    dot_general x4 -> x6, matrix products: 11.8 us -> 9.43 us  [term(): jnp.dot(left.T, right[:, lo:hi], preferred_element_type=jnp.float32)]
  transfers between devices with their start and end apart: 18 -> 27, of which waited for: 13 -> 14; matrix products, arithmetic and copies ran while one was open for 17% -> 20% of each run, Pallas kernels for 0% -> 0%
where the time goes in v5:
time: 210 us
  waiting for transfers between devices  62.8 us (30%)
  starting transfers between devices  42 us (20%)
  Pallas kernels  38.1 us (18%)
  matrix products  28 us (13%)
  local copies, waits for them, and re-layouts  20.1 us (10%)
  other arithmetic  15.6 us (7%)
  between operations  3.26 us (2%)
    pallas_call x1, Pallas kernels, attention(): pl.pallas_call(functools.partial(attention_kernel, head=head, scale=head...  38.1 us
    ppermute x21, waiting for transfers between devices, exchange(): lax.ppermute(array, axis, [(i, i ^ mask) for i in range(lax.axis_size(axi...  36.9 us
    ppermute x21, starting transfers between devices, exchange(): lax.ppermute(array, axis, [(i, i ^ mask) for i in range(lax.axis_size(axi...  30.7 us
    ppermute x6, waiting for transfers between devices, partner(): lax.ppermute(array, axis, [(i, i ^ 1 << apart) for i in range(lax.axis_si...  25.9 us
    ppermute x6, starting transfers between devices, partner(): lax.ppermute(array, axis, [(i, i ^ 1 << apart) for i in range(lax.axis_si...  11.3 us
    dot_general x6, matrix products, term(): jnp.dot(left.T, right[:, lo:hi], preferred_element_type=jnp.float32)  9.43 us
    dot_general x1, matrix products, body(): jnp.dot(rows, w_value, preferred_element_type=jnp.float32)  4.28 us
    convert_element_type x16, other arithmetic, add_bf16(): return (a.astype(jnp.float32) + b.astype(jnp.float32)).astype(jnp.bfloat16)  4.21 us
  transfers between devices with their start and end apart: 27, of which 14 were waited for; matrix products, arithmetic and copies ran while one was open for 20% of the time, Pallas kernels for 0%

profile of v5, /device:TPU:1, one launch (start us, length us, event | category | flops | bytes accessed | tf_op | source)
XLA Modules:
  0.0 209.9 jit_solution(9676918310793173126)
XLA Ops:
  4.0 4.3 %convolution_convert_fusion.3 = bf16[512,1024]{1,0:T(8,128)(2,1)} fusion(bf16[1024,1024]{1,0:T(8,128)(2,1)} %param.10, bf16[1,512,1024]{2,1,0:T(8,128)(2,1)} %param.7), kind=kOutput, calls=%fused_computation.13 | convolution fusion | flops 1074266112 | bytes 4194304 | tf_op jit(solution)/shard_map/dot_general | solution.py:178
  16.8 2.3 %collective-permute-start.2 = (bf16[2,128,1024]{2,1,0:T(8,128)(2,1)}, bf16[2,128,1024]{2,1,0:T(8,128)(2,1)}, u32[]{:S(2)}, u32[]{:S(2)}) collective-permute-start(bf16[2,128,1024]{2,1,0:T(8,128)(2,1)} %pad_maximum_fusion.4), channel_id=1, source_target_pairs={{0,4},{1,5},{2,6},{3,7},{4,0},{5,1},{6,2},{7,3},{8,12},{9,13},{10,... | collective-permute-start | bytes 1572872 | tf_op jit(solution)/shard_map/ppermute | solution.py:16
  21.3 2.3 %convolution_convert_fusion.2.do_ref = bf16[512,1024]{1,0:T(8,128)(2,1)} fusion(bf16[1024,1024]{1,0:T(8,128)(2,1)S(1)} %copy-done.19, bf16[1,512,1024]{2,1,0:T(8,128)(2,1)S(1)} %copy-done.12), kind=kOutput, calls=%fused_computation.12 | convolution fusion | flops 1074266112 | bytes 4194304 | tf_op jit(solution)/shard_map/dot_general | solution.py:182
  26.8 10.9 %collective-permute-done.1 = bf16[2,128,1024]{2,1,0:T(8,128)(2,1)} collective-permute-done((bf16[2,128,1024]{2,1,0:T(8,128)(2,1)}, bf16[2,128,1024]{2,1,0:T(8,128)(2,1)}, u32[]{:S(2)}, u32[]{:S(2)}) %collective-permute-start.1) | collective-permute-done | bytes 524320 | tf_op jit(solution)/shard_map/ppermute | solution.py:16
  42.7 38.1 %shard_map.118 = (bf16[512,1024]{1,0:T(8,128)(2,1)}, bf16[512,1024]{1,0:T(8,128)(2,1)}, f32[896,1024]{1,0:T(8,128)}, f32[896,1024]{1,0:T(8,128)}) custom-call(bf16[512,1024]{1,0:T(8,128)(2,1)} %convolution_convert_fusion.5.q_ref, bf16[896,1024]{1,0:T(8,128)(2,1)} %pad_maximum_fusion.k_ref, bf16[896,1024]{1,0:T(8,128)(2,1)} %pad_maximum_fusion.1.v_ref, ...), custom_call_target="tpu_custom_call" | custom-call | flops 11274289152 | bytes 13107200 | tf_op jit(solution)/shard_map/pallas_call | solution.py:73
  80.8 2.5 %convert.40 = bf16[896,1024]{1,0:T(8,128)(2,1)S(1)} convert(f32[896,1024]{1,0:T(8,128)} %get-tuple-element.12) | non-fusion elementwise | flops 917504 | bytes 5505024 | tf_op jit(solution)/shard_map/convert.35
  89.0 3.1 %collective-permute-start.4 = (bf16[2,128,1024]{2,1,0:T(8,128)(2,1)S(1)}, bf16[2,128,1024]{2,1,0:T(8,128)(2,1)S(1)}, u32[]{:S(2)}, u32[]{:S(2)}) collective-permute-start(bf16[2,128,1024]{2,1,0:T(8,128)(2,1)S(1)} %pad_maximum_fusion.6), channel_id=1, source_target_pairs={{0,2},{1,3},{2,0},{3,1},{4,6},{5,7},{6,4},{7,5},{8,10},{9,11},{10,... | collective-permute-start | bytes 1572872 | tf_op jit(solution)/shard_map/ppermute | solution.py:16
  93.8 3.0 %collective-permute-start.6 = (bf16[1024,1024]{1,0:T(8,128)(2,1)S(1)}, bf16[1024,1024]{1,0:T(8,128)(2,1)S(1)}, u32[]{:S(2)}, u32[]{:S(2)}) collective-permute-start(bf16[1024,1024]{1,0:T(8,128)(2,1)S(1)} %convolution_convert_fusion), channel_id=1, source_target_pairs={{0,8},{8,0},{16,24},{24,16},{1,9},{9,1},{17,25},{25,17},{2,10},{10... | collective-permute-start | bytes 6291464 | tf_op jit(solution)/shard_map/ppermute | solution.py:94
  97.0 6.0 %collective-permute-done.3 = bf16[2,128,1024]{2,1,0:T(8,128)(2,1)S(1)} collective-permute-done((bf16[2,128,1024]{2,1,0:T(8,128)(2,1)S(1)}, bf16[2,128,1024]{2,1,0:T(8,128)(2,1)S(1)}, u32[]{:S(2)}, u32[]{:S(2)}) %collective-permute-start.3) | collective-permute-done | bytes 524320 | tf_op jit(solution)/shard_map/ppermute | solution.py:16
  103.3 6.9 %collective-permute-done.5 = bf16[2,128,1024]{2,1,0:T(8,128)(2,1)S(1)} collective-permute-done((bf16[2,128,1024]{2,1,0:T(8,128)(2,1)S(1)}, bf16[2,128,1024]{2,1,0:T(8,128)(2,1)S(1)}, u32[]{:S(2)}, u32[]{:S(2)}) %collective-permute-start.5) | collective-permute-done | bytes 524320 | tf_op jit(solution)/shard_map/ppermute | solution.py:16
  112.4 3.3 %collective-permute-start.16 = (bf16[1024,1024]{0,1:T(8,128)(2,1)S(1)}, bf16[1024,1024]{0,1:T(8,128)(2,1)S(1)}, u32[]{:S(2)}, u32[]{:S(2)}) collective-permute-start(bf16[1024,1024]{0,1:T(8,128)(2,1)S(1)} %convert_bitcast_fusion), channel_id=1, source_target_pairs={{0,8},{8,0},{16,24},{24,16},{1,9},{9,1},{17,25},{25,17},{2,10},{10... | collective-permute-start | bytes 6291464 | tf_op jit(solution)/shard_map/ppermute | solution.py:94
  115.7 2.7 %fusion.60 = f32[512,1024]{1,0:T(8,128)} fusion(bf16[512,1024]{1,0:T(8,128)(2,1)S(1)} %copy-done.14, bf16[1024,1024]{1,0:T(8,128)(2,1)S(1)} %copy-done), kind=kOutput, calls=%fused_computation.155 | convolution fusion | flops 1073741824 | bytes 5242880 | tf_op jit(solution)/shard_map/dot_general | solution.py:203
  134.0 3.4 %fusion = bf16[1024,512]{0,1:T(8,128)(2,1)} fusion(bf16[1024,1024]{0,1:T(8,128)(2,1)} %copy-done.23, bf16[1,512,1024]{2,1,0:T(8,128)(2,1)} %param.7, bf16[512,1024]{1,0:T(8,128)(2,1)} %copy-done.15), kind=kOutput, calls=%fused_computation.1 | convolution fusion | flops 539492352 | bytes 3670016 | tf_op jit(solution)/shard_map/dot_general | solution.py:102
  137.4 2.3 %copy.26 = bf16[1024,512]{1,0:T(8,128)(2,1)} copy(bf16[1024,512]{0,1:T(8,128)(2,1)} %fusion) | data formatting | bytes 2097152 | tf_op jit(solution)/shard_map/convert_element_type | solution.py:98
  145.5 13.9 %collective-permute-done.8 = bf16[2,2,64,512]{3,2,0,1:T(8,128)(2,1)S(1)} collective-permute-done((bf16[2,2,64,512]{3,2,0,1:T(8,128)(2,1)S(1)}, bf16[2,2,64,512]{3,2,0,1:T(8,128)(2,1)S(1)}, u32[]{:S(2)}, u32[]{:S(2)}) %collective-permute-start.8) | collective-permute-done | bytes 262176 | tf_op jit(solution)/shard_map/ppermute | solution.py:94
  160.9 3.2 %collective-permute-start.13 = (bf16[2,64,512]{2,1,0:T(8,128)(2,1)S(1)}, bf16[2,64,512]{2,1,0:T(8,128)(2,1)S(1)}, u32[]{:S(2)}, u32[]{:S(2)}) collective-permute-start(bf16[2,64,512]{2,1,0:T(8,128)(2,1)S(1)} %dynamic-slice_bitcast_fusion.13), channel_id=1, source_target_pairs={{0,4},{1,5},{2,6},{3,7},{4,0},{5,1},{6,2},{7,3},{8,12},{9,13},{10,... | collective-permute-start | bytes 393224 | tf_op jit(solution)/shard_map/ppermute | solution.py:94
  164.2 2.5 %collective-permute-start.10 = (bf16[64,512]{1,0:T(8,128)(2,1)S(1)}, bf16[64,512]{1,0:T(8,128)(2,1)S(1)}, u32[]{:S(2)}, u32[]{:S(2)}) collective-permute-start(bf16[64,512]{1,0:T(8,128)(2,1)S(1)} %dynamic-slice_bitcast_fusion.18), channel_id=1, source_target_pairs={{0,4},{1,5},{2,6},{3,7},{4,0},{5,1},{6,2},{7,3},{8,12},{9,13},{10,... | collective-permute-start | bytes 196616 | tf_op jit(solution)/shard_map/ppermute | solution.py:94
  166.7 4.0 %collective-permute-done.13 = bf16[2,64,512]{2,1,0:T(8,128)(2,1)S(1)} collective-permute-done((bf16[2,64,512]{2,1,0:T(8,128)(2,1)S(1)}, bf16[2,64,512]{2,1,0:T(8,128)(2,1)S(1)}, u32[]{:S(2)}, u32[]{:S(2)}) %collective-permute-start.13) | collective-permute-done | bytes 131104 | tf_op jit(solution)/shard_map/ppermute | solution.py:94
  176.0 4.8 %collective-permute-done.18 = bf16[2,2,64,512]{3,2,1,0:T(8,128)(2,1)S(1)} collective-permute-done((bf16[2,2,64,512]{3,2,1,0:T(8,128)(2,1)S(1)}, bf16[2,2,64,512]{3,2,1,0:T(8,128)(2,1)S(1)}, u32[]{:S(2)}, u32[]{:S(2)}) %collective-permute-start.18) | collective-permute-done | bytes 262176 | tf_op jit(solution)/shard_map/ppermute | solution.py:94
  182.6 2.5 %collective-permute-done.19 = bf16[2,64,512]{2,1,0:T(8,128)(2,1)S(1)} collective-permute-done((bf16[2,64,512]{2,1,0:T(8,128)(2,1)S(1)}, bf16[2,64,512]{2,1,0:T(8,128)(2,1)S(1)}, u32[]{:S(2)}, u32[]{:S(2)}) %collective-permute-start.19) | collective-permute-done | bytes 131104 | tf_op jit(solution)/shard_map/ppermute | solution.py:94
  185.2 4.1 %collective-permute-done.23 = bf16[2,64,512]{2,1,0:T(8,128)(2,1)S(1)} collective-permute-done((bf16[2,64,512]{2,1,0:T(8,128)(2,1)S(1)}, bf16[2,64,512]{2,1,0:T(8,128)(2,1)S(1)}, u32[]{:S(2)}, u32[]{:S(2)}) %collective-permute-start.23) | collective-permute-done | bytes 131104 | tf_op jit(solution)/shard_map/ppermute | solution.py:94
  190.1 2.5 %collective-permute-done.24 = bf16[64,512]{1,0:T(8,128)(2,1)S(1)} collective-permute-done((bf16[64,512]{1,0:T(8,128)(2,1)S(1)}, bf16[64,512]{1,0:T(8,128)(2,1)S(1)}, u32[]{:S(2)}, u32[]{:S(2)}) %collective-permute-start.24) | collective-permute-done | bytes 65568 | tf_op jit(solution)/shard_map/ppermute | solution.py:94
  196.9 9.3 %collective-permute-start.26 = (bf16[128,2048]{1,0:T(8,128)(2,1)S(1)}, bf16[128,2048]{1,0:T(8,128)(2,1)S(1)}, u32[]{:S(2)}, u32[]{:S(2)}) collective-permute-start(bf16[128,2048]{1,0:T(8,128)(2,1)S(1)} %pad_maximum_fusion.8), channel_id=1, source_target_pairs={{0,8},{8,0},{16,24},{24,16},{1,9},{9,1},{17,25},{25,17},{2,10},{10... | collective-permute-start | bytes 1572872 | tf_op jit(solution)/shard_map/ppermute | solution.py:94
  206.2 2.3 %fusion.3 = bf16[1,512,1024]{2,1,0:T(8,128)(2,1)} fusion(bf16[1024,1024]{1,0:T(8,128)(2,1)S(1)} %copy-done.10, f32[512,1024]{1,0:T(8,128)S(1)} %copy-done.11, f32[512,1024]{1,0:T(8,128)S(1)} %fusion.57, f32[512,1024]{1,0:T(8,128)S(1)} %copy-done.2), kind=kOutput, calls=%fused_computation.21 | convolution fusion | flops 1075838976 | bytes 9437184 | tf_op jit(solution)/shard_map/dot_general | solution.py:205
  (165 shorter events, 66.6 us)
Async XLA Ops:
  11.8 14.0 %collective-permute-start = (bf16[2,128,1024]{2,1,0:T(8,128)(2,1)}, bf16[2,128,1024]{2,1,0:T(8,128)(2,1)}, u32[]{:S(2)}, u32[]{:S(2)}) collective-permute-start(bf16[2,128,1024]{2,1,0:T(8,128)(2,1)} %pad_maximum_fusion.2), channel_id=1, source_target_pairs={{0,1},{1,0},{2,3},{3,2},{4,5},{5,4},{6,7},{7,6},{8,9},{9,8},{10,11... | collective-permute-start | bytes 1572872 | tf_op jit(solution)/shard_map/ppermute | solution.py:16
  14.7 23.1 %collective-permute-start.1 = (bf16[2,128,1024]{2,1,0:T(8,128)(2,1)}, bf16[2,128,1024]{2,1,0:T(8,128)(2,1)}, u32[]{:S(2)}, u32[]{:S(2)}) collective-permute-start(bf16[2,128,1024]{2,1,0:T(8,128)(2,1)} %pad_maximum_fusion.3), channel_id=1, source_target_pairs={{0,2},{1,3},{2,0},{3,1},{4,6},{5,7},{6,4},{7,5},{8,10},{9,11},{10,... | collective-permute-start | bytes 1572872 | tf_op jit(solution)/shard_map/ppermute | solution.py:16
  16.8 22.0 %collective-permute-start.2 = (bf16[2,128,1024]{2,1,0:T(8,128)(2,1)}, bf16[2,128,1024]{2,1,0:T(8,128)(2,1)}, u32[]{:S(2)}, u32[]{:S(2)}) collective-permute-start(bf16[2,128,1024]{2,1,0:T(8,128)(2,1)} %pad_maximum_fusion.4), channel_id=1, source_target_pairs={{0,4},{1,5},{2,6},{3,7},{4,0},{5,1},{6,2},{7,3},{8,12},{9,13},{10,... | collective-permute-start | bytes 1572872 | tf_op jit(solution)/shard_map/ppermute | solution.py:16
  86.7 23.5 %collective-permute-start.5 = (bf16[2,128,1024]{2,1,0:T(8,128)(2,1)S(1)}, bf16[2,128,1024]{2,1,0:T(8,128)(2,1)S(1)}, u32[]{:S(2)}, u32[]{:S(2)}) collective-permute-start(bf16[2,128,1024]{2,1,0:T(8,128)(2,1)S(1)} %pad_maximum_fusion.7), channel_id=1, source_target_pairs={{0,4},{1,5},{2,6},{3,7},{4,0},{5,1},{6,2},{7,3},{8,12},{9,13},{10,... | collective-permute-start | bytes 1572872 | tf_op jit(solution)/shard_map/ppermute | solution.py:16
  89.0 21.3 %collective-permute-start.4 = (bf16[2,128,1024]{2,1,0:T(8,128)(2,1)S(1)}, bf16[2,128,1024]{2,1,0:T(8,128)(2,1)S(1)}, u32[]{:S(2)}, u32[]{:S(2)}) collective-permute-start(bf16[2,128,1024]{2,1,0:T(8,128)(2,1)S(1)} %pad_maximum_fusion.6), channel_id=1, source_target_pairs={{0,2},{1,3},{2,0},{3,1},{4,6},{5,7},{6,4},{7,5},{8,10},{9,11},{10,... | collective-permute-start | bytes 1572872 | tf_op jit(solution)/shard_map/ppermute | solution.py:16
  92.2 10.8 %collective-permute-start.3 = (bf16[2,128,1024]{2,1,0:T(8,128)(2,1)S(1)}, bf16[2,128,1024]{2,1,0:T(8,128)(2,1)S(1)}, u32[]{:S(2)}, u32[]{:S(2)}) collective-permute-start(bf16[2,128,1024]{2,1,0:T(8,128)(2,1)S(1)} %pad_maximum_fusion.5), channel_id=1, source_target_pairs={{0,1},{1,0},{2,3},{3,2},{4,5},{5,4},{6,7},{7,6},{8,9},{9,8},{10,11... | collective-permute-start | bytes 1572872 | tf_op jit(solution)/shard_map/ppermute | solution.py:16
  93.8 27.3 %collective-permute-start.6 = (bf16[1024,1024]{1,0:T(8,128)(2,1)S(1)}, bf16[1024,1024]{1,0:T(8,128)(2,1)S(1)}, u32[]{:S(2)}, u32[]{:S(2)}) collective-permute-start(bf16[1024,1024]{1,0:T(8,128)(2,1)S(1)} %convolution_convert_fusion), channel_id=1, source_target_pairs={{0,8},{8,0},{16,24},{24,16},{1,9},{9,1},{17,25},{25,17},{2,10},{10... | collective-permute-start | bytes 6291464 | tf_op jit(solution)/shard_map/ppermute | solution.py:94
  112.4 15.0 %collective-permute-start.16 = (bf16[1024,1024]{0,1:T(8,128)(2,1)S(1)}, bf16[1024,1024]{0,1:T(8,128)(2,1)S(1)}, u32[]{:S(2)}, u32[]{:S(2)}) collective-permute-start(bf16[1024,1024]{0,1:T(8,128)(2,1)S(1)} %convert_bitcast_fusion), channel_id=1, source_target_pairs={{0,8},{8,0},{16,24},{24,16},{1,9},{9,1},{17,25},{25,17},{2,10},{10... | collective-permute-start | bytes 6291464 | tf_op jit(solution)/shard_map/ppermute | solution.py:94
  123.6 18.0 %collective-permute-start.7 = (bf16[2,2,2,64,512]{4,3,0,2,1:T(8,128)(2,1)}, bf16[2,2,2,64,512]{4,3,0,2,1:T(8,128)(2,1)}, u32[]{:S(2)}, u32[]{:S(2)}) collective-permute-start(bf16[2,2,2,64,512]{4,3,0,2,1:T(8,128)(2,1)} %bitcast.219), channel_id=1, source_target_pairs={{0,1},{1,0},{2,3},{3,2},{4,5},{5,4},{6,7},{7,6},{8,9},{9,8},{10,11... | collective-permute-start | bytes 1572872 | tf_op jit(solution)/shard_map/ppermute | solution.py:94
  126.5 17.4 %collective-permute-start.11 = (bf16[2,2,2,64,512]{4,3,2,0,1:T(8,128)(2,1)}, bf16[2,2,2,64,512]{4,3,2,0,1:T(8,128)(2,1)}, u32[]{:S(2)}, u32[]{:S(2)}) collective-permute-start(bf16[2,2,2,64,512]{4,3,2,0,1:T(8,128)(2,1)} %bitcast.218), channel_id=1, source_target_pairs={{0,2},{1,3},{2,0},{3,1},{4,6},{5,7},{6,4},{7,5},{8,10},{9,11},{10,... | collective-permute-start | bytes 1572872 | tf_op jit(solution)/shard_map/ppermute | solution.py:94
  132.8 41.4 %collective-permute-start.17 = (bf16[2,2,2,64,512]{4,3,2,1,0:T(8,128)(2,1)}, bf16[2,2,2,64,512]{4,3,2,1,0:T(8,128)(2,1)}, u32[]{:S(2)}, u32[]{:S(2)}) collective-permute-start(bf16[2,2,2,64,512]{4,3,2,1,0:T(8,128)(2,1)} %dynamic-slice_bitcast_fusion), channel_id=1, source_target_pairs={{0,1},{1,0},{2,3},{3,2},{4,5},{5,4},{6,7},{7,6},{8,9},{9,8},{10,11... | collective-permute-start | bytes 1572872 | tf_op jit(solution)/shard_map/ppermute | solution.py:94
  141.1 34.4 %collective-permute-start.21 = (bf16[2,2,2,64,512]{4,3,2,0,1:T(8,128)(2,1)S(1)}, bf16[2,2,2,64,512]{4,3,2,0,1:T(8,128)(2,1)S(1)}, u32[]{:S(2)}, u32[]{:S(2)}) collective-permute-start(bf16[2,2,2,64,512]{4,3,2,0,1:T(8,128)(2,1)S(1)} %bitcast.225), channel_id=1, source_target_pairs={{0,2},{1,3},{2,0},{3,1},{4,6},{5,7},{6,4},{7,5},{8,10},{9,11},{10,... | collective-permute-start | bytes 1572872 | tf_op jit(solution)/shard_map/ppermute | solution.py:94
  142.9 16.5 %collective-permute-start.8 = (bf16[2,2,64,512]{3,2,0,1:T(8,128)(2,1)S(1)}, bf16[2,2,64,512]{3,2,0,1:T(8,128)(2,1)S(1)}, u32[]{:S(2)}, u32[]{:S(2)}) collective-permute-start(bf16[2,2,64,512]{3,2,0,1:T(8,128)(2,1)S(1)} %dynamic-slice_bitcast_fusion.4), channel_id=1, source_target_pairs={{0,2},{1,3},{2,0},{3,1},{4,6},{5,7},{6,4},{7,5},{8,10},{9,11},{10,... | collective-permute-start | bytes 786440 | tf_op jit(solution)/shard_map/ppermute | solution.py:94
  145.2 15.6 %collective-permute-start.12 = (bf16[2,2,64,512]{3,2,1,0:T(8,128)(2,1)S(1)}, bf16[2,2,64,512]{3,2,1,0:T(8,128)(2,1)S(1)}, u32[]{:S(2)}, u32[]{:S(2)}) collective-permute-start(bf16[2,2,64,512]{3,2,1,0:T(8,128)(2,1)S(1)} %dynamic-slice_bitcast_fusion.3), channel_id=1, source_target_pairs={{0,1},{1,0},{2,3},{3,2},{4,5},{5,4},{6,7},{7,6},{8,9},{9,8},{10,11... | collective-permute-start | bytes 786440 | tf_op jit(solution)/shard_map/ppermute | solution.py:94
  159.5 4.6 %collective-permute-start.9 = (bf16[2,64,512]{2,1,0:T(8,128)(2,1)S(1)}, bf16[2,64,512]{2,1,0:T(8,128)(2,1)S(1)}, u32[]{:S(2)}, u32[]{:S(2)}) collective-permute-start(bf16[2,64,512]{2,1,0:T(8,128)(2,1)S(1)} %dynamic-slice_bitcast_fusion.14), channel_id=1, source_target_pairs={{0,16},{8,24},{16,0},{24,8},{1,17},{9,25},{17,1},{25,9},{2,18},{10... | collective-permute-start | bytes 393224 | tf_op jit(solution)/shard_map/ppermute | solution.py:94
  160.9 9.8 %collective-permute-start.13 = (bf16[2,64,512]{2,1,0:T(8,128)(2,1)S(1)}, bf16[2,64,512]{2,1,0:T(8,128)(2,1)S(1)}, u32[]{:S(2)}, u32[]{:S(2)}) collective-permute-start(bf16[2,64,512]{2,1,0:T(8,128)(2,1)S(1)} %dynamic-slice_bitcast_fusion.13), channel_id=1, source_target_pairs={{0,4},{1,5},{2,6},{3,7},{4,0},{5,1},{6,2},{7,3},{8,12},{9,13},{10,... | collective-permute-start | bytes 393224 | tf_op jit(solution)/shard_map/ppermute | solution.py:94
  164.2 8.6 %collective-permute-start.10 = (bf16[64,512]{1,0:T(8,128)(2,1)S(1)}, bf16[64,512]{1,0:T(8,128)(2,1)S(1)}, u32[]{:S(2)}, u32[]{:S(2)}) collective-permute-start(bf16[64,512]{1,0:T(8,128)(2,1)S(1)} %dynamic-slice_bitcast_fusion.18), channel_id=1, source_target_pairs={{0,4},{1,5},{2,6},{3,7},{4,0},{5,1},{6,2},{7,3},{8,12},{9,13},{10,... | collective-permute-start | bytes 196616 | tf_op jit(solution)/shard_map/ppermute | solution.py:94
  173.9 21.1 %collective-permute-start.15 = (bf16[64,1024]{1,0:T(8,128)(2,1)S(1)}, bf16[64,1024]{1,0:T(8,128)(2,1)S(1)}, u32[]{:S(2)}, u32[]{:S(2)}) collective-permute-start(bf16[64,1024]{1,0:T(8,128)(2,1)S(1)} %pad_maximum_fusion.9), channel_id=1, source_target_pairs={{0,16},{8,24},{16,0},{24,8},{1,17},{9,25},{17,1},{25,9},{2,18},{10... | collective-permute-start | bytes 393224 | tf_op jit(solution)/shard_map/ppermute | solution.py:94
  175.5 5.3 %collective-permute-start.18 = (bf16[2,2,64,512]{3,2,1,0:T(8,128)(2,1)S(1)}, bf16[2,2,64,512]{3,2,1,0:T(8,128)(2,1)S(1)}, u32[]{:S(2)}, u32[]{:S(2)}) collective-permute-start(bf16[2,2,64,512]{3,2,1,0:T(8,128)(2,1)S(1)} %dynamic-slice_bitcast_fusion.2), channel_id=1, source_target_pairs={{0,2},{1,3},{2,0},{3,1},{4,6},{5,7},{6,4},{7,5},{8,10},{9,11},{10,... | collective-permute-start | bytes 786440 | tf_op jit(solution)/shard_map/ppermute | solution.py:94
  175.7 6.7 %collective-permute-start.22 = (bf16[2,2,64,512]{3,2,1,0:T(8,128)(2,1)S(1)}, bf16[2,2,64,512]{3,2,1,0:T(8,128)(2,1)S(1)}, u32[]{:S(2)}, u32[]{:S(2)}) collective-permute-start(bf16[2,2,64,512]{3,2,1,0:T(8,128)(2,1)S(1)} %dynamic-slice_bitcast_fusion.1), channel_id=1, source_target_pairs={{0,1},{1,0},{2,3},{3,2},{4,5},{5,4},{6,7},{7,6},{8,9},{9,8},{10,11... | collective-permute-start | bytes 786440 | tf_op jit(solution)/shard_map/ppermute | solution.py:94
  180.8 4.2 %collective-permute-start.19 = (bf16[2,64,512]{2,1,0:T(8,128)(2,1)S(1)}, bf16[2,64,512]{2,1,0:T(8,128)(2,1)S(1)}, u32[]{:S(2)}, u32[]{:S(2)}) collective-permute-start(bf16[2,64,512]{2,1,0:T(8,128)(2,1)S(1)} %dynamic-slice_bitcast_fusion.12), channel_id=1, source_target_pairs={{0,16},{8,24},{16,0},{24,8},{1,17},{9,25},{17,1},{25,9},{2,18},{10... | collective-permute-start | bytes 393224 | tf_op jit(solution)/shard_map/ppermute | solution.py:94
  182.5 6.8 %collective-permute-start.23 = (bf16[2,64,512]{2,1,0:T(8,128)(2,1)S(1)}, bf16[2,64,512]{2,1,0:T(8,128)(2,1)S(1)}, u32[]{:S(2)}, u32[]{:S(2)}) collective-permute-start(bf16[2,64,512]{2,1,0:T(8,128)(2,1)S(1)} %dynamic-slice_bitcast_fusion.11), channel_id=1, source_target_pairs={{0,4},{1,5},{2,6},{3,7},{4,0},{5,1},{6,2},{7,3},{8,12},{9,13},{10,... | collective-permute-start | bytes 393224 | tf_op jit(solution)/shard_map/ppermute | solution.py:94
  185.1 4.9 %collective-permute-start.20 = (bf16[64,512]{1,0:T(8,128)(2,1)S(1)}, bf16[64,512]{1,0:T(8,128)(2,1)S(1)}, u32[]{:S(2)}, u32[]{:S(2)}) collective-permute-start(bf16[64,512]{1,0:T(8,128)(2,1)S(1)} %dynamic-slice_bitcast_fusion.16), channel_id=1, source_target_pairs={{0,4},{1,5},{2,6},{3,7},{4,0},{5,1},{6,2},{7,3},{8,12},{9,13},{10,... | collective-permute-start | bytes 196616 | tf_op jit(solution)/shard_map/ppermute | solution.py:94
  196.9 11.6 %collective-permute-start.26 = (bf16[128,2048]{1,0:T(8,128)(2,1)S(1)}, bf16[128,2048]{1,0:T(8,128)(2,1)S(1)}, u32[]{:S(2)}, u32[]{:S(2)}) collective-permute-start(bf16[128,2048]{1,0:T(8,128)(2,1)S(1)} %pad_maximum_fusion.8), channel_id=1, source_target_pairs={{0,8},{8,0},{16,24},{24,16},{1,9},{9,1},{17,25},{25,17},{2,10},{10... | collective-permute-start | bytes 1572872 | tf_op jit(solution)/shard_map/ppermute | solution.py:94
  (28 other events, 210.1 us)

commit v6 on v4

--- a/solution.py
+++ b/solution.py
@@ -16,24 +16,26 @@
     return lax.ppermute(array, axis, [(i, i ^ 1 << apart) for i in range(lax.axis_size(axis))])
 
 
-def swap_blocks(keys_local, values_local, offsets, levels):
+def swap_blocks(rows, w_key, w_value, offsets, levels):
     remote = []
     for level in range(levels):
-        start = offsets[level] * BLOCK
+        block = lax.dynamic_slice_in_dim(rows, offsets[level] * BLOCK, BLOCK, 0)
         pair = jnp.stack(
             [
-                lax.dynamic_slice_in_dim(keys_local, start, BLOCK, 0),
-                lax.dynamic_slice_in_dim(values_local, start, BLOCK, 0),
+                jnp.dot(block, w_key, preferred_element_type=jnp.float32).astype(jnp.bfloat16),
+                jnp.dot(block, w_value, preferred_element_type=jnp.float32).astype(jnp.bfloat16),
             ]
         )
         remote.append(partner(pair, "seq", level))
     return remote
 
 
-def attention_kernel(q_ref, k_ref, v_ref, do_ref, att_ref, dq_ref, dk_ref, dv_ref, *, head, scale):
+def attention_kernel(q_ref, k_ref, v_ref, do_ref, *refs, head, scale):
+    remote = refs[:-4]
+    att_ref, dq_ref, dk_ref, dv_ref = refs[-4:]
     q = q_ref[...]
-    k = k_ref[...]
-    v = v_ref[...]
+    k = jnp.concatenate([k_ref[...]] + [r[0] for r in remote], axis=0)
+    v = jnp.concatenate([v_ref[...]] + [r[1] for r in remote], axis=0)
     do = do_ref[...]
     width = q.shape[1]
     lane = lax.broadcasted_iota(jnp.int32, (1, width), 1)
@@ -64,16 +66,17 @@
     dv_ref[...] = outs[3]
 
 
-def attention(query, keys, values, d_att, head):
+def attention(query, keys, values, d_att, remote, head):
     tok, width = query.shape
-    total = keys.shape[0]
+    total = tok + sum(r.shape[1] for r in remote)
     steps = width // LANES
     qspec = pl.BlockSpec((tok, LANES), lambda i: (0, i))
     kspec = pl.BlockSpec((total, LANES), lambda i: (0, i))
+    rspecs = [pl.BlockSpec((2, r.shape[1], LANES), lambda i: (0, 0, i)) for r in remote]
     return pl.pallas_call(
         functools.partial(attention_kernel, head=head, scale=head ** -0.5),
         grid=(steps,),
-        in_specs=[qspec, kspec, kspec, qspec],
+        in_specs=[qspec, qspec, qspec, qspec] + rspecs,
         out_specs=[qspec, qspec, kspec, kspec],
         out_shape=[
             jax.ShapeDtypeStruct((tok, width), jnp.bfloat16),
@@ -87,7 +90,7 @@
             transcendentals=tok * total * (width // head),
             bytes_accessed=4 * tok * width + 12 * total * width,
         ),
-    )(query, keys, values, d_att)
+    )(query, keys, values, d_att, *remote)
 
 
 def exchange(array, axis, mask):
@@ -180,14 +183,12 @@
     width = rows.shape[1]
     head = width // HEADS
     levels = lax.axis_size("seq").bit_length() - 1
+    remote = swap_blocks(rows, w_key, w_value, offsets, levels)
     query = jnp.dot(rows, w_query, preferred_element_type=jnp.float32).astype(jnp.bfloat16)
     keys_local = jnp.dot(rows, w_key, preferred_element_type=jnp.float32).astype(jnp.bfloat16)
     values_local = jnp.dot(rows, w_value, preferred_element_type=jnp.float32).astype(jnp.bfloat16)
-    remote = swap_blocks(keys_local, values_local, offsets, levels)
-    all_keys = jnp.concatenate([keys_local] + [piece[0] for piece in remote], 0)
-    all_values = jnp.concatenate([values_local] + [piece[1] for piece in remote], 0)
     d_att = jnp.dot(cot, w_out.T, preferred_element_type=jnp.float32).astype(jnp.bfloat16)
-    attended, dquery, dk_acc, dv_acc = attention(query, all_keys, all_values, d_att, head)
+    attended, dquery, dk_acc, dv_acc = attention(query, keys_local, values_local, d_att, remote, head)
     result = jnp.dot(attended, w_out, preferred_element_type=jnp.float32).astype(jnp.bfloat16)
     dkey_sum = dk_acc[:tok]
     dvalue_sum = dv_acc[:tok]

time: 207 us -> 210 us (1.014)
  waiting for transfers between devices: 84.3 us -> 76.2 us
  other arithmetic: 15.1 us -> 20 us
  matrix products: 30.2 us -> 33.7 us
    dot_general x0 -> x6, matrix products: none -> 5.97 us  [the longest x3 4.63 us: swap_blocks(): jnp.dot(block, w_key, preferred_element_type=jnp.float32)]
    ppermute x6, waiting for transfers between devices: 36.5 us -> 31.2 us  [partner(): lax.ppermute(array, axis, [(i, i ^ 1 << apart) for i in range(lax.axis_si...]
    convert_element_type x8 -> x10, other arithmetic: 4.09 us -> 9.19 us  [add_bf16(): return (a.astype(jnp.float32) + b.astype(jnp.float32)).astype(jnp.bfloat16)]
    concatenate x2 -> x0, other arithmetic: 2.83 us -> none  [the longest x1 1.45 us: body(): all_keys = jnp.concatenate([keys_local] + [piece[0] for piece in remote], 0)]
    ppermute x12, waiting for transfers between devices: 47.8 us -> 45 us  [exchange(): lax.ppermute(array, axis, [(i, i ^ mask) for i in range(lax.axis_size(axi...]
    unnamed x52 -> x48, local copies, waits for them, and re-layouts: 1.97 us -> 4.27 us
  transfers between devices with their start and end apart: 18 -> 18, of which waited for: 13 -> 13; matrix products, arithmetic and copies ran while one was open for 17% -> 23% of each run, Pallas kernels for 0% -> 0%
where the time goes in v6:
time: 210 us
  waiting for transfers between devices  76.2 us (36%)
  Pallas kernels  38 us (18%)
  matrix products  33.7 us (16%)
  starting transfers between devices  26.4 us (13%)
  other arithmetic  20 us (10%)
  local copies, waits for them, and re-layouts  12.5 us (6%)
  between operations  3.08 us (1%)
    ppermute x12, waiting for transfers between devices, exchange(): lax.ppermute(array, axis, [(i, i ^ mask) for i in range(lax.axis_size(axi...  45 us
    pallas_call x1, Pallas kernels, attention(): pl.pallas_call(functools.partial(attention_kernel, head=head, scale=head...  38 us
    ppermute x6, waiting for transfers between devices, partner(): lax.ppermute(array, axis, [(i, i ^ 1 << apart) for i in range(lax.axis_si...  31.2 us
    ppermute x12, starting transfers between devices, exchange(): lax.ppermute(array, axis, [(i, i ^ mask) for i in range(lax.axis_size(axi...  17.9 us
    dot_general x4, matrix products, term(): jnp.dot(left.T, right[:, lo:hi], preferred_element_type=jnp.float32)  9.7 us
    convert_element_type x10, other arithmetic, add_bf16(): return (a.astype(jnp.float32) + b.astype(jnp.float32)).astype(jnp.bfloat16)  9.19 us
    ppermute x6, starting transfers between devices, partner(): lax.ppermute(array, axis, [(i, i ^ 1 << apart) for i in range(lax.axis_si...  8.52 us
    dot_general x3, matrix products, swap_blocks(): jnp.dot(block, w_key, preferred_element_type=jnp.float32)  4.63 us
  transfers between devices with their start and end apart: 18, of which 13 were waited for; matrix products, arithmetic and copies ran while one was open for 23% of the time, Pallas kernels for 0%

profile of v6, /device:TPU:1, one launch (start us, length us, event | category | flops | bytes accessed | tf_op | source)
XLA Modules:
  0.0 209.9 jit_solution(5232353711460958230)
XLA Ops:
  16.3 2.4 %collective-permute-start.2 = (bf16[2,128,1024]{2,1,0:T(8,128)(2,1)S(1)}, bf16[2,128,1024]{2,1,0:T(8,128)(2,1)S(1)}, u32[]{:S(2)}, u32[]{:S(2)}) collective-permute-start(bf16[2,128,1024]{2,1,0:T(8,128)(2,1)S(1)} %pad_maximum_fusion.2), channel_id=1, source_target_pairs={{0,4},{1,5},{2,6},{3,7},{4,0},{5,1},{6,2},{7,3},{8,12},{9,13},{10,... | collective-permute-start | bytes 1572872 | tf_op jit(solution)/shard_map/ppermute | solution.py:16
  18.7 2.3 %convolution_convert_fusion.3.v_ref = bf16[512,1024]{1,0:T(8,128)(2,1)} fusion(bf16[1024,1024]{1,0:T(8,128)(2,1)S(1)} %copy-done, bf16[1,512,1024]{2,1,0:T(8,128)(2,1)S(1)} %copy-done.11), kind=kOutput, calls=%fused_computation.12 | convolution fusion | flops 1074266112 | bytes 4194304 | tf_op jit(solution)/shard_map/dot_general | solution.py:189
  27.7 5.8 %collective-permute-done.1.refs_1_ = bf16[2,128,1024]{2,1,0:T(8,128)(2,1)} collective-permute-done((bf16[2,128,1024]{2,1,0:T(8,128)(2,1)}, bf16[2,128,1024]{2,1,0:T(8,128)(2,1)}, u32[]{:S(2)}, u32[]{:S(2)}) %collective-permute-start.1) | collective-permute-done | bytes 524320 | tf_op jit(solution)/shard_map/ppermute | solution.py:16
  33.5 7.3 %collective-permute-done.2.refs_2_ = bf16[2,128,1024]{2,1,0:T(8,128)(2,1)S(1)} collective-permute-done((bf16[2,128,1024]{2,1,0:T(8,128)(2,1)S(1)}, bf16[2,128,1024]{2,1,0:T(8,128)(2,1)S(1)}, u32[]{:S(2)}, u32[]{:S(2)}) %collective-permute-start.2) | collective-permute-done | bytes 524320 | tf_op jit(solution)/shard_map/ppermute | solution.py:16
  41.6 38.0 %shard_map.118 = (bf16[512,1024]{1,0:T(8,128)(2,1)}, bf16[512,1024]{1,0:T(8,128)(2,1)}, f32[896,1024]{1,0:T(8,128)}, f32[896,1024]{1,0:T(8,128)}) custom-call(bf16[512,1024]{1,0:T(8,128)(2,1)} %convolution_convert_fusion.5.q_ref, bf16[512,1024]{1,0:T(8,128)(2,1)} %convolution_convert_fusion.4.k_ref, bf16[512,1024]{1,0:T(8,128)(2,1)} %convolution_convert_fusion.3.v_ref, ...), custom_call_target="tpu_custom_call" | custom-call | flops 11274289152 | bytes 13107200 | tf_op jit(solution)/shard_map/pallas_call | solution.py:76
  79.6 2.5 %convert.31 = bf16[896,1024]{1,0:T(8,128)(2,1)S(1)} convert(f32[896,1024]{1,0:T(8,128)} %get-tuple-element.12) | non-fusion elementwise | flops 917504 | bytes 5505024 | tf_op jit(solution)/shard_map/convert.26
  89.5 2.6 %collective-permute-start.5 = (bf16[2,128,1024]{2,1,0:T(8,128)(2,1)S(1)}, bf16[2,128,1024]{2,1,0:T(8,128)(2,1)S(1)}, u32[]{:S(2)}, u32[]{:S(2)}) collective-permute-start(bf16[2,128,1024]{2,1,0:T(8,128)(2,1)S(1)} %pad_maximum_fusion.5), channel_id=1, source_target_pairs={{0,4},{1,5},{2,6},{3,7},{4,0},{5,1},{6,2},{7,3},{8,12},{9,13},{10,... | collective-permute-start | bytes 1572872 | tf_op jit(solution)/shard_map/ppermute | solution.py:16
  92.0 10.6 %collective-permute-done.4 = bf16[2,128,1024]{2,1,0:T(8,128)(2,1)} collective-permute-done((bf16[2,128,1024]{2,1,0:T(8,128)(2,1)}, bf16[2,128,1024]{2,1,0:T(8,128)(2,1)}, u32[]{:S(2)}, u32[]{:S(2)}) %collective-permute-start.4) | collective-permute-done | bytes 524320 | tf_op jit(solution)/shard_map/ppermute | solution.py:16
  105.4 7.5 %collective-permute-done.5 = bf16[2,128,1024]{2,1,0:T(8,128)(2,1)S(1)} collective-permute-done((bf16[2,128,1024]{2,1,0:T(8,128)(2,1)S(1)}, bf16[2,128,1024]{2,1,0:T(8,128)(2,1)S(1)}, u32[]{:S(2)}, u32[]{:S(2)}) %collective-permute-start.5) | collective-permute-done | bytes 524320 | tf_op jit(solution)/shard_map/ppermute | solution.py:16
  113.3 2.6 %convert_bitcast_fusion = bf16[1024,1024]{1,0:T(8,128)(2,1)} fusion(bf16[1,512,1024]{2,1,0:T(8,128)(2,1)S(1)} %copy-done.11, bf16[512,1024]{1,0:T(8,128)(2,1)S(1)} %copy-done.20, pred[]{:T(512)S(6)} %eq.17, f32[512,1024]{1,0:T(8,128)S(1)} %get-tuple-element.29), kind=kOutput, calls=%fused_computation.7 | convolution fusion | flops 1075838976 | bytes 6291457 | tf_op jit(solution)/shard_map/dot_general | solution.py:105
  116.0 3.3 %collective-permute-start.6 = (bf16[1024,1024]{1,0:T(8,128)(2,1)}, bf16[1024,1024]{1,0:T(8,128)(2,1)}, u32[]{:S(2)}, u32[]{:S(2)}) collective-permute-start(bf16[1024,1024]{1,0:T(8,128)(2,1)} %convert_bitcast_fusion), channel_id=1, source_target_pairs={{0,8},{8,0},{16,24},{24,16},{1,9},{9,1},{17,25},{25,17},{2,10},{10... | collective-permute-start | bytes 6291464 | tf_op jit(solution)/shard_map/ppermute | solution.py:97
  119.2 2.7 %convolution_convert_fusion = bf16[1024,1024]{1,0:T(8,128)(2,1)} fusion(bf16[1,512,1024]{2,1,0:T(8,128)(2,1)S(1)} %copy-done.17, bf16[512,1024]{1,0:T(8,128)(2,1)S(1)} %copy-done.22, bf16[1,512,1024]{2,1,0:T(8,128)(2,1)S(1)} %copy-done.11, pred[]{:T(512)S(6)} %eq.17, f32[512,1024]{1,0:T(8,128)S(1)} %get-tuple-element.28), kind=kOutput, calls=%fused_computation.9 | convolution fusion | flops 1076363264 | bytes 7340033 | tf_op jit(solution)/shard_map/dot_general | solution.py:105
  122.3 3.0 %fusion.16 = bf16[1024,1024]{0,1:T(8,128)(2,1)S(1)} fusion(bf16[1,512,1024]{2,1,0:T(8,128)(2,1)S(1)} %copy-done.11, bf16[512,1024]{1,0:T(8,128)(2,1)} %get-tuple-element.11, pred[]{:T(512)S(6)} %eq.17, f32[512,1024]{1,0:T(8,128)} %copy-done.8), kind=kOutput, calls=%fused_computation.42 | convolution fusion | flops 1074790400 | bytes 6291457 | tf_op jit(solution)/shard_map/dot_general | solution.py:105
  126.8 2.5 %fusion = bf16[1024,1024]{1,0:T(8,128)(2,1)S(1)} fusion(bf16[1024,1024]{1,0:T(8,128)(2,1)} %collective-permute-done.6, bf16[1024,1024]{0,1:T(8,128)(2,1)S(1)} %fusion.16), kind=kLoop, calls=%fused_computation.1 | loop fusion | flops 4194304 | bytes 6291456 | tf_op jit(solution)/shard_map/convert_element_type | solution.py:101
  131.8 2.5 %add_convert_fusion = bf16[1024,1024]{1,0:T(8,128)(2,1)S(1)} fusion(bf16[1024,1024]{1,0:T(8,128)(2,1)} %collective-permute-done.11, bf16[1024,1024]{1,0:T(8,128)(2,1)S(1)} %fusion.14), kind=kLoop, calls=%fused_computation.2 | loop fusion | flops 4194304 | bytes 6291456 | tf_op jit(solution)/shard_map/convert_element_type | solution.py:101
  136.6 4.1 %fusion.3 = bf16[1,512,1024]{2,1,0:T(8,128)(2,1)} fusion(bf16[512,1024]{1,0:T(8,128)(2,1)} %get-tuple-element.10, bf16[1024,1024]{1,0:T(8,128)(2,1)} %param.11), kind=kOutput, calls=%fused_computation.15 | convolution fusion | flops 1074266112 | bytes 4194304 | tf_op jit(solution)/shard_map/dot_general | solution.py:192
  140.8 14.5 %collective-permute-done.7 = bf16[2,2,2,64,1024]{4,3,0,2,1:T(8,128)(2,1)} collective-permute-done((bf16[2,2,2,64,1024]{4,3,0,2,1:T(8,128)(2,1)}, bf16[2,2,2,64,1024]{4,3,0,2,1:T(8,128)(2,1)}, u32[]{:S(2)}, u32[]{:S(2)}) %collective-permute-start.7) | collective-permute-done | bytes 1048608 | tf_op jit(solution)/shard_map/ppermute | solution.py:97
  157.1 3.8 %collective-permute-done.12 = bf16[2,2,2,64,1024]{4,3,2,0,1:T(8,128)(2,1)} collective-permute-done((bf16[2,2,2,64,1024]{4,3,2,0,1:T(8,128)(2,1)}, bf16[2,2,2,64,1024]{4,3,2,0,1:T(8,128)(2,1)}, u32[]{:S(2)}, u32[]{:S(2)}) %collective-permute-start.12) | collective-permute-done | bytes 1048608 | tf_op jit(solution)/shard_map/ppermute | solution.py:97
  164.7 7.4 %collective-permute-done.8 = bf16[2,2,64,1024]{3,2,0,1:T(8,128)(2,1)S(1)} collective-permute-done((bf16[2,2,64,1024]{3,2,0,1:T(8,128)(2,1)S(1)}, bf16[2,2,64,1024]{3,2,0,1:T(8,128)(2,1)S(1)}, u32[]{:S(2)}, u32[]{:S(2)}) %collective-permute-start.8) | collective-permute-done | bytes 524320 | tf_op jit(solution)/shard_map/ppermute | solution.py:97
  176.0 2.7 %collective-permute-done.9 = bf16[2,64,1024]{2,1,0:T(8,128)(2,1)S(1)} collective-permute-done((bf16[2,64,1024]{2,1,0:T(8,128)(2,1)S(1)}, bf16[2,64,1024]{2,1,0:T(8,128)(2,1)S(1)}, u32[]{:S(2)}, u32[]{:S(2)}) %collective-permute-start.9) | collective-permute-done | bytes 262176 | tf_op jit(solution)/shard_map/ppermute | solution.py:97
  180.3 10.1 %collective-permute-done.14 = bf16[2,64,1024]{2,1,0:T(8,128)(2,1)S(1)} collective-permute-done((bf16[2,64,1024]{2,1,0:T(8,128)(2,1)S(1)}, bf16[2,64,1024]{2,1,0:T(8,128)(2,1)S(1)}, u32[]{:S(2)}, u32[]{:S(2)}) %collective-permute-start.14) | collective-permute-done | bytes 262176 | tf_op jit(solution)/shard_map/ppermute | solution.py:97
  197.2 3.6 %collective-permute-done.16 = bf16[64,2048]{1,0:T(8,128)(2,1)S(1)} collective-permute-done((bf16[64,2048]{1,0:T(8,128)(2,1)S(1)}, bf16[64,2048]{1,0:T(8,128)(2,1)S(1)}, u32[]{:S(2)}, u32[]{:S(2)}) %collective-permute-start.16) | collective-permute-done | bytes 262176 | tf_op jit(solution)/shard_map/ppermute | solution.py:97
  200.9 5.3 %collective-permute-start.17 = (bf16[128,2048]{1,0:T(8,128)(2,1)S(1)}, bf16[128,2048]{1,0:T(8,128)(2,1)S(1)}, u32[]{:S(2)}, u32[]{:S(2)}) collective-permute-start(bf16[128,2048]{1,0:T(8,128)(2,1)S(1)} %maximum_select_fusion), channel_id=1, source_target_pairs={{0,8},{8,0},{16,24},{24,16},{1,9},{9,1},{17,25},{25,17},{2,10},{10... | collective-permute-start | bytes 1572872 | tf_op jit(solution)/shard_map/ppermute | solution.py:97
  206.2 2.3 %fusion.4 = bf16[1,512,1024]{2,1,0:T(8,128)(2,1)} fusion(f32[512,1024]{1,0:T(8,128)S(1)} %fusion.63, f32[512,1024]{1,0:T(8,128)S(1)} %fusion.67, bf16[512,1024]{1,0:T(8,128)(2,1)S(1)} %copy-done.21, bf16[1024,1024]{1,0:T(8,128)(2,1)S(1)} %copy-done.15), kind=kOutput, calls=%fused_computation.16 | convolution fusion | flops 1075314688 | bytes 8388608 | tf_op jit(solution)/shard_map/dot_general | solution.py:211
  (120 shorter events, 57.4 us)
Async XLA Ops:
  6.2 21.5 %collective-permute-start = (bf16[2,128,1024]{2,1,0:T(8,128)(2,1)}, bf16[2,128,1024]{2,1,0:T(8,128)(2,1)}, u32[]{:S(2)}, u32[]{:S(2)}) collective-permute-start(bf16[2,128,1024]{2,1,0:T(8,128)(2,1)} %pad_maximum_fusion), channel_id=1, source_target_pairs={{0,1},{1,0},{2,3},{3,2},{4,5},{5,4},{6,7},{7,6},{8,9},{9,8},{10,11... | collective-permute-start | bytes 1572872 | tf_op jit(solution)/shard_map/ppermute | solution.py:16
  12.2 21.3 %collective-permute-start.1 = (bf16[2,128,1024]{2,1,0:T(8,128)(2,1)}, bf16[2,128,1024]{2,1,0:T(8,128)(2,1)}, u32[]{:S(2)}, u32[]{:S(2)}) collective-permute-start(bf16[2,128,1024]{2,1,0:T(8,128)(2,1)} %pad_maximum_fusion.1), channel_id=1, source_target_pairs={{0,2},{1,3},{2,0},{3,1},{4,6},{5,7},{6,4},{7,5},{8,10},{9,11},{10,... | collective-permute-start | bytes 1572872 | tf_op jit(solution)/shard_map/ppermute | solution.py:16
  16.3 24.5 %collective-permute-start.2 = (bf16[2,128,1024]{2,1,0:T(8,128)(2,1)S(1)}, bf16[2,128,1024]{2,1,0:T(8,128)(2,1)S(1)}, u32[]{:S(2)}, u32[]{:S(2)}) collective-permute-start(bf16[2,128,1024]{2,1,0:T(8,128)(2,1)S(1)} %pad_maximum_fusion.2), channel_id=1, source_target_pairs={{0,4},{1,5},{2,6},{3,7},{4,0},{5,1},{6,2},{7,3},{8,12},{9,13},{10,... | collective-permute-start | bytes 1572872 | tf_op jit(solution)/shard_map/ppermute | solution.py:16
  84.7 18.0 %collective-permute-start.4 = (bf16[2,128,1024]{2,1,0:T(8,128)(2,1)}, bf16[2,128,1024]{2,1,0:T(8,128)(2,1)}, u32[]{:S(2)}, u32[]{:S(2)}) collective-permute-start(bf16[2,128,1024]{2,1,0:T(8,128)(2,1)} %pad_maximum_fusion.4), channel_id=1, source_target_pairs={{0,2},{1,3},{2,0},{3,1},{4,6},{5,7},{6,4},{7,5},{8,10},{9,11},{10,... | collective-permute-start | bytes 1572872 | tf_op jit(solution)/shard_map/ppermute | solution.py:16
  85.5 18.3 %collective-permute-start.3 = (bf16[2,128,1024]{2,1,0:T(8,128)(2,1)}, bf16[2,128,1024]{2,1,0:T(8,128)(2,1)}, u32[]{:S(2)}, u32[]{:S(2)}) collective-permute-start(bf16[2,128,1024]{2,1,0:T(8,128)(2,1)} %pad_maximum_fusion.3), channel_id=1, source_target_pairs={{0,1},{1,0},{2,3},{3,2},{4,5},{5,4},{6,7},{7,6},{8,9},{9,8},{10,11... | collective-permute-start | bytes 1572872 | tf_op jit(solution)/shard_map/ppermute | solution.py:16
  89.5 23.5 %collective-permute-start.5 = (bf16[2,128,1024]{2,1,0:T(8,128)(2,1)S(1)}, bf16[2,128,1024]{2,1,0:T(8,128)(2,1)S(1)}, u32[]{:S(2)}, u32[]{:S(2)}) collective-permute-start(bf16[2,128,1024]{2,1,0:T(8,128)(2,1)S(1)} %pad_maximum_fusion.5), channel_id=1, source_target_pairs={{0,4},{1,5},{2,6},{3,7},{4,0},{5,1},{6,2},{7,3},{8,12},{9,13},{10,... | collective-permute-start | bytes 1572872 | tf_op jit(solution)/shard_map/ppermute | solution.py:16
  105.4 7.9 %copy-start.20 = (bf16[512,1024]{1,0:T(8,128)(2,1)S(1)}, bf16[512,1024]{1,0:T(8,128)(2,1)}, u32[]{:S(2)}) copy-start(bf16[512,1024]{1,0:T(8,128)(2,1)} %get-tuple-element.11) | copy-start | bytes 3145732
  113.3 5.9 %copy-start.5 = (f32[512,1024]{1,0:T(8,128)}, f32[512,1024]{1,0:T(8,128)S(1)}, u32[]{:S(2)}) copy-start(f32[512,1024]{1,0:T(8,128)S(1)} %get-tuple-element.28) | copy-start | bytes 6291460
  116.0 10.8 %collective-permute-start.6 = (bf16[1024,1024]{1,0:T(8,128)(2,1)}, bf16[1024,1024]{1,0:T(8,128)(2,1)}, u32[]{:S(2)}, u32[]{:S(2)}) collective-permute-start(bf16[1024,1024]{1,0:T(8,128)(2,1)} %convert_bitcast_fusion), channel_id=1, source_target_pairs={{0,8},{8,0},{16,24},{24,16},{1,9},{9,1},{17,25},{25,17},{2,10},{10... | collective-permute-start | bytes 6291464 | tf_op jit(solution)/shard_map/ppermute | solution.py:97
  121.9 9.9 %collective-permute-start.11 = (bf16[1024,1024]{1,0:T(8,128)(2,1)}, bf16[1024,1024]{1,0:T(8,128)(2,1)}, u32[]{:S(2)}, u32[]{:S(2)}) collective-permute-start(bf16[1024,1024]{1,0:T(8,128)(2,1)} %convolution_convert_fusion), channel_id=1, source_target_pairs={{0,8},{8,0},{16,24},{24,16},{1,9},{9,1},{17,25},{25,17},{2,10},{10... | collective-permute-start | bytes 6291464 | tf_op jit(solution)/shard_map/ppermute | solution.py:97
  130.6 24.6 %collective-permute-start.7 = (bf16[2,2,2,64,1024]{4,3,0,2,1:T(8,128)(2,1)}, bf16[2,2,2,64,1024]{4,3,0,2,1:T(8,128)(2,1)}, u32[]{:S(2)}, u32[]{:S(2)}) collective-permute-start(bf16[2,2,2,64,1024]{4,3,0,2,1:T(8,128)(2,1)} %bitcast.173), channel_id=1, source_target_pairs={{0,1},{1,0},{2,3},{3,2},{4,5},{5,4},{6,7},{7,6},{8,9},{9,8},{10,11... | collective-permute-start | bytes 3145736 | tf_op jit(solution)/shard_map/ppermute | solution.py:97
  136.6 24.3 %collective-permute-start.12 = (bf16[2,2,2,64,1024]{4,3,2,0,1:T(8,128)(2,1)}, bf16[2,2,2,64,1024]{4,3,2,0,1:T(8,128)(2,1)}, u32[]{:S(2)}, u32[]{:S(2)}) collective-permute-start(bf16[2,2,2,64,1024]{4,3,2,0,1:T(8,128)(2,1)} %bitcast.172), channel_id=1, source_target_pairs={{0,2},{1,3},{2,0},{3,1},{4,6},{5,7},{6,4},{7,5},{8,10},{9,11},{10,... | collective-permute-start | bytes 3145736 | tf_op jit(solution)/shard_map/ppermute | solution.py:97
  157.1 15.0 %collective-permute-start.8 = (bf16[2,2,64,1024]{3,2,0,1:T(8,128)(2,1)S(1)}, bf16[2,2,64,1024]{3,2,0,1:T(8,128)(2,1)S(1)}, u32[]{:S(2)}, u32[]{:S(2)}) collective-permute-start(bf16[2,2,64,1024]{3,2,0,1:T(8,128)(2,1)S(1)} %dynamic-slice_bitcast_fusion.1), channel_id=1, source_target_pairs={{0,2},{1,3},{2,0},{3,1},{4,6},{5,7},{6,4},{7,5},{8,10},{9,11},{10,... | collective-permute-start | bytes 1572872 | tf_op jit(solution)/shard_map/ppermute | solution.py:97
  163.0 10.8 %collective-permute-start.13 = (bf16[2,2,64,1024]{3,2,1,0:T(8,128)(2,1)S(1)}, bf16[2,2,64,1024]{3,2,1,0:T(8,128)(2,1)S(1)}, u32[]{:S(2)}, u32[]{:S(2)}) collective-permute-start(bf16[2,2,64,1024]{3,2,1,0:T(8,128)(2,1)S(1)} %dynamic-slice_bitcast_fusion), channel_id=1, source_target_pairs={{0,1},{1,0},{2,3},{3,2},{4,5},{5,4},{6,7},{7,6},{8,9},{9,8},{10,11... | collective-permute-start | bytes 1572872 | tf_op jit(solution)/shard_map/ppermute | solution.py:97
  172.3 6.3 %collective-permute-start.9 = (bf16[2,64,1024]{2,1,0:T(8,128)(2,1)S(1)}, bf16[2,64,1024]{2,1,0:T(8,128)(2,1)S(1)}, u32[]{:S(2)}, u32[]{:S(2)}) collective-permute-start(bf16[2,64,1024]{2,1,0:T(8,128)(2,1)S(1)} %dynamic-slice_bitcast_fusion.3), channel_id=1, source_target_pairs={{0,16},{8,24},{16,0},{24,8},{1,17},{9,25},{17,1},{25,9},{2,18},{10... | collective-permute-start | bytes 786440 | tf_op jit(solution)/shard_map/ppermute | solution.py:97
  173.8 22.1 %copy-start.7 = (f32[512,1024]{1,0:T(8,128)S(1)}, f32[512,1024]{1,0:T(8,128)}, u32[]{:S(2)}) copy-start(f32[512,1024]{1,0:T(8,128)} %copy-done.5) | copy-start | bytes 6291460
  174.0 21.9 %copy-start.2 = (bf16[1024,1024]{1,0:T(8,128)(2,1)S(1)}, bf16[1024,1024]{1,0:T(8,128)(2,1)}, u32[]{:S(2)}) copy-start(bf16[1024,1024]{1,0:T(8,128)(2,1)} %param.9) | copy-start | bytes 6291460
  174.0 16.4 %collective-permute-start.14 = (bf16[2,64,1024]{2,1,0:T(8,128)(2,1)S(1)}, bf16[2,64,1024]{2,1,0:T(8,128)(2,1)S(1)}, u32[]{:S(2)}, u32[]{:S(2)}) collective-permute-start(bf16[2,64,1024]{2,1,0:T(8,128)(2,1)S(1)} %dynamic-slice_bitcast_fusion.2), channel_id=1, source_target_pairs={{0,4},{1,5},{2,6},{3,7},{4,0},{5,1},{6,2},{7,3},{8,12},{9,13},{10,... | collective-permute-start | bytes 786440 | tf_op jit(solution)/shard_map/ppermute | solution.py:97
  178.7 14.5 %collective-permute-start.10 = (bf16[64,1024]{1,0:T(8,128)(2,1)S(1)}, bf16[64,1024]{1,0:T(8,128)(2,1)S(1)}, u32[]{:S(2)}, u32[]{:S(2)}) collective-permute-start(bf16[64,1024]{1,0:T(8,128)(2,1)S(1)} %dynamic-slice_bitcast_fusion.5), channel_id=1, source_target_pairs={{0,4},{1,5},{2,6},{3,7},{4,0},{5,1},{6,2},{7,3},{8,12},{9,13},{10,... | collective-permute-start | bytes 393224 | tf_op jit(solution)/shard_map/ppermute | solution.py:97
  190.5 4.1 %collective-permute-start.15 = (bf16[64,1024]{1,0:T(8,128)(2,1)S(1)}, bf16[64,1024]{1,0:T(8,128)(2,1)S(1)}, u32[]{:S(2)}, u32[]{:S(2)}) collective-permute-start(bf16[64,1024]{1,0:T(8,128)(2,1)S(1)} %dynamic-slice_bitcast_fusion.4), channel_id=1, source_target_pairs={{0,16},{8,24},{16,0},{24,8},{1,17},{9,25},{17,1},{25,9},{2,18},{10... | collective-permute-start | bytes 393224 | tf_op jit(solution)/shard_map/ppermute | solution.py:97
  194.6 11.6 %copy-start.15 = (bf16[1024,1024]{1,0:T(8,128)(2,1)S(1)}, bf16[1024,1024]{1,0:T(8,128)(2,1)}, u32[]{:S(2)}) copy-start(bf16[1024,1024]{1,0:T(8,128)(2,1)} %param.8) | copy-start | bytes 6291460
  194.6 11.6 %copy-start.21 = (bf16[512,1024]{1,0:T(8,128)(2,1)S(1)}, bf16[512,1024]{1,0:T(8,128)(2,1)}, u32[]{:S(2)}) copy-start(bf16[512,1024]{1,0:T(8,128)(2,1)} %get-tuple-element.11) | copy-start | bytes 3145732
  194.7 6.1 %collective-permute-start.16 = (bf16[64,2048]{1,0:T(8,128)(2,1)S(1)}, bf16[64,2048]{1,0:T(8,128)(2,1)S(1)}, u32[]{:S(2)}, u32[]{:S(2)}) collective-permute-start(bf16[64,2048]{1,0:T(8,128)(2,1)S(1)} %pad_maximum_fusion.6), channel_id=1, source_target_pairs={{0,16},{8,24},{16,0},{24,8},{1,17},{9,25},{17,1},{25,9},{2,18},{10... | collective-permute-start | bytes 786440 | tf_op jit(solution)/shard_map/ppermute | solution.py:97
  200.9 7.6 %collective-permute-start.17 = (bf16[128,2048]{1,0:T(8,128)(2,1)S(1)}, bf16[128,2048]{1,0:T(8,128)(2,1)S(1)}, u32[]{:S(2)}, u32[]{:S(2)}) collective-permute-start(bf16[128,2048]{1,0:T(8,128)(2,1)S(1)} %maximum_select_fusion), channel_id=1, source_target_pairs={{0,8},{8,0},{16,24},{24,16},{1,9},{9,1},{17,25},{25,17},{2,10},{10... | collective-permute-start | bytes 1572872 | tf_op jit(solution)/shard_map/ppermute | solution.py:97
  (18 other events, 56.2 us)

commit v7 on v4

--- a/solution.py
+++ b/solution.py
@@ -37,9 +37,13 @@
     do = do_ref[...]
     width = q.shape[1]
     lane = lax.broadcasted_iota(jnp.int32, (1, width), 1)
+    row = lax.broadcasted_iota(jnp.int32, (width, 1), 0)
+    q_t = q.T
+    do_t = do.T
     outs = None
     for j in range(width // head):
         inside = (lane >= j * head) & (lane < (j + 1) * head)
+        rows_in = (row >= j * head) & (row < (j + 1) * head)
         qm = jnp.where(inside, q * jnp.asarray(scale, q.dtype), jnp.zeros_like(q))
         dom = jnp.where(inside, do, jnp.zeros_like(do))
         s = lax.dot_general(qm, k, (((1,), (1,)), ((), ())), preferred_element_type=jnp.float32)
@@ -52,16 +56,21 @@
         delta = jnp.sum(p * dp, axis=-1, keepdims=True)
         ds = (p * (dp - delta) * scale).astype(jnp.bfloat16)
         dq = jnp.dot(ds, k, preferred_element_type=jnp.float32)
-        dk = lax.dot_general(ds, q, (((0,), (0,)), ((), ())), preferred_element_type=jnp.float32)
-        dv = lax.dot_general(pb, do, (((0,), (0,)), ((), ())), preferred_element_type=jnp.float32)
+        dk_t = jnp.dot(q_t, ds, preferred_element_type=jnp.float32)
+        dv_t = jnp.dot(do_t, pb, preferred_element_type=jnp.float32)
         if outs is None:
-            outs = [a, dq, dk, dv]
+            outs = [a, dq, dk_t, dv_t]
         else:
-            outs = [jnp.where(inside, new, old) for new, old in zip([a, dq, dk, dv], outs)]
+            outs = [
+                jnp.where(inside, a, outs[0]),
+                jnp.where(inside, dq, outs[1]),
+                jnp.where(rows_in, dk_t, outs[2]),
+                jnp.where(rows_in, dv_t, outs[3]),
+            ]
     att_ref[...] = outs[0].astype(att_ref.dtype)
     dq_ref[...] = outs[1].astype(dq_ref.dtype)
-    dk_ref[...] = outs[2]
-    dv_ref[...] = outs[3]
+    dk_ref[...] = outs[2].T
+    dv_ref[...] = outs[3].T
 
 
 def attention(query, keys, values, d_att, head):

time: 207 us -> 203 us (0.981)
  Pallas kernels: 38.1 us -> 33.4 us
    pallas_call x1, Pallas kernels: 38.1 us -> 33.4 us  [attention(): pl.pallas_call(functools.partial(attention_kernel, head=head, scale=head...]
where the time goes in v7:
time: 203 us; the launch traced here: 202 us
  waiting for transfers between devices  84.3 us (42%)
  Pallas kernels  33.4 us (16%)
  matrix products  30.2 us (15%)
  starting transfers between devices  25.4 us (13%)
  other arithmetic  15.1 us (7%)
  local copies, waits for them, and re-layouts  10.6 us (5%)
  between operations  3.35 us (2%)
    ppermute x12, waiting for transfers between devices, exchange(): lax.ppermute(array, axis, [(i, i ^ mask) for i in range(lax.axis_size(axi...  47.8 us
    ppermute x6, waiting for transfers between devices, partner(): lax.ppermute(array, axis, [(i, i ^ 1 << apart) for i in range(lax.axis_si...  36.5 us
    pallas_call x1, Pallas kernels, attention(): pl.pallas_call(functools.partial(attention_kernel, head=head, scale=head...  33.4 us
    ppermute x12, starting transfers between devices, exchange(): lax.ppermute(array, axis, [(i, i ^ mask) for i in range(lax.axis_size(axi...  16.6 us
    dot_general x4, matrix products, term(): jnp.dot(left.T, right[:, lo:hi], preferred_element_type=jnp.float32)  11.8 us
    ppermute x6, starting transfers between devices, partner(): lax.ppermute(array, axis, [(i, i ^ 1 << apart) for i in range(lax.axis_si...  8.75 us
    dot_general x1, matrix products, body(): jnp.dot(rows, w_value, preferred_element_type=jnp.float32)  4.28 us
    convert_element_type x8, other arithmetic, add_bf16(): return (a.astype(jnp.float32) + b.astype(jnp.float32)).astype(jnp.bfloat16)  4.09 us
  transfers between devices with their start and end apart: 18, of which 13 were waited for; matrix products, arithmetic and copies ran while one was open for 17% of the time, Pallas kernels for 0%

profile of v7, /device:TPU:1, one launch (start us, length us, event | category | flops | bytes accessed | tf_op | source)
XLA Modules:
  0.0 202.2 jit_solution(14591365507195871551)
XLA Ops:
  4.0 4.3 %convolution_convert_fusion.3 = bf16[512,1024]{1,0:T(8,128)(2,1)} fusion(bf16[1024,1024]{1,0:T(8,128)(2,1)} %param.10, bf16[1,512,1024]{2,1,0:T(8,128)(2,1)} %param.7), kind=kOutput, calls=%fused_computation.14 | convolution fusion | flops 1074266112 | bytes 4194304 | tf_op jit(solution)/shard_map/dot_general | solution.py:194
  14.6 2.4 %collective-permute-start.2 = (bf16[2,128,1024]{2,1,0:T(8,128)(2,1)S(1)}, bf16[2,128,1024]{2,1,0:T(8,128)(2,1)S(1)}, u32[]{:S(2)}, u32[]{:S(2)}) collective-permute-start(bf16[2,128,1024]{2,1,0:T(8,128)(2,1)S(1)} %pad_maximum_fusion.4), channel_id=1, source_target_pairs={{0,4},{1,5},{2,6},{3,7},{4,0},{5,1},{6,2},{7,3},{8,12},{9,13},{10,... | collective-permute-start | bytes 1572872 | tf_op jit(solution)/shard_map/ppermute | solution.py:16
  19.2 2.3 %convolution_convert_fusion.2.do_ref = bf16[512,1024]{1,0:T(8,128)(2,1)} fusion(bf16[1024,1024]{1,0:T(8,128)(2,1)S(1)} %copy-done.11, bf16[1,512,1024]{2,1,0:T(8,128)(2,1)S(1)} %copy-done.19), kind=kOutput, calls=%fused_computation.13 | convolution fusion | flops 1074266112 | bytes 4194304 | tf_op jit(solution)/shard_map/dot_general | solution.py:198
  21.5 3.2 %collective-permute-done = bf16[2,128,1024]{2,1,0:T(8,128)(2,1)S(1)} collective-permute-done((bf16[2,128,1024]{2,1,0:T(8,128)(2,1)S(1)}, bf16[2,128,1024]{2,1,0:T(8,128)(2,1)S(1)}, u32[]{:S(2)}, u32[]{:S(2)}) %collective-permute-start) | collective-permute-done | bytes 524320 | tf_op jit(solution)/shard_map/ppermute | solution.py:16
  24.8 11.9 %collective-permute-done.1 = bf16[2,128,1024]{2,1,0:T(8,128)(2,1)S(1)} collective-permute-done((bf16[2,128,1024]{2,1,0:T(8,128)(2,1)S(1)}, bf16[2,128,1024]{2,1,0:T(8,128)(2,1)S(1)}, u32[]{:S(2)}, u32[]{:S(2)}) %collective-permute-start.1) | collective-permute-done | bytes 524320 | tf_op jit(solution)/shard_map/ppermute | solution.py:16
  39.6 33.4 %shard_map.118 = (bf16[512,1024]{1,0:T(8,128)(2,1)}, bf16[512,1024]{1,0:T(8,128)(2,1)}, f32[896,1024]{1,0:T(8,128)}, f32[896,1024]{1,0:T(8,128)}) custom-call(bf16[512,1024]{1,0:T(8,128)(2,1)} %convolution_convert_fusion.5.q_ref, bf16[896,1024]{1,0:T(8,128)(2,1)} %pad_maximum_fusion.k_ref, bf16[896,1024]{1,0:T(8,128)(2,1)} %pad_maximum_fusion.1.v_ref, ...), custom_call_target="tpu_custom_call" | custom-call | flops 11274289152 | bytes 13107200 | tf_op jit(solution)/shard_map/pallas_call | solution.py:82
  73.0 2.5 %convert.31 = bf16[896,1024]{1,0:T(8,128)(2,1)S(1)} convert(f32[896,1024]{1,0:T(8,128)} %get-tuple-element.12) | non-fusion elementwise | flops 917504 | bytes 5505024 | tf_op jit(solution)/shard_map/convert.26
  77.3 2.6 %collective-permute-start.4 = (bf16[2,128,1024]{2,1,0:T(8,128)(2,1)}, bf16[2,128,1024]{2,1,0:T(8,128)(2,1)S(1)}, u32[]{:S(2)}, u32[]{:S(2)}) collective-permute-start(bf16[2,128,1024]{2,1,0:T(8,128)(2,1)} %pad_maximum_fusion.6), channel_id=1, source_target_pairs={{0,2},{1,3},{2,0},{3,1},{4,6},{5,7},{6,4},{7,5},{8,10},{9,11},{10,... | collective-permute-start | bytes 1572872 | tf_op jit(solution)/shard_map/ppermute | solution.py:16
  84.0 8.8 %collective-permute-done.4 = bf16[2,128,1024]{2,1,0:T(8,128)(2,1)S(1)} collective-permute-done((bf16[2,128,1024]{2,1,0:T(8,128)(2,1)}, bf16[2,128,1024]{2,1,0:T(8,128)(2,1)S(1)}, u32[]{:S(2)}, u32[]{:S(2)}) %collective-permute-start.4) | collective-permute-done | bytes 524320 | tf_op jit(solution)/shard_map/ppermute | solution.py:16
  94.5 12.7 %collective-permute-done.5 = bf16[2,128,1024]{2,1,0:T(8,128)(2,1)S(1)} collective-permute-done((bf16[2,128,1024]{2,1,0:T(8,128)(2,1)S(1)}, bf16[2,128,1024]{2,1,0:T(8,128)(2,1)S(1)}, u32[]{:S(2)}, u32[]{:S(2)}) %collective-permute-start.5) | collective-permute-done | bytes 524320 | tf_op jit(solution)/shard_map/ppermute | solution.py:16
  107.5 2.6 %convert_bitcast_fusion = bf16[1024,1024]{1,0:T(8,128)(2,1)} fusion(bf16[1,512,1024]{2,1,0:T(8,128)(2,1)S(1)} %copy-done.17, bf16[512,1024]{1,0:T(8,128)(2,1)S(1)} %copy-done.22, pred[]{:T(512)S(6)} %eq.17, f32[512,1024]{1,0:T(8,128)S(1)} %get-tuple-element.28), kind=kOutput, calls=%fused_computation.7 | convolution fusion | flops 1075838976 | bytes 6291457 | tf_op jit(solution)/shard_map/dot_general | solution.py:111
  110.2 3.3 %collective-permute-start.6 = (bf16[1024,1024]{1,0:T(8,128)(2,1)}, bf16[1024,1024]{1,0:T(8,128)(2,1)}, u32[]{:S(2)}, u32[]{:S(2)}) collective-permute-start(bf16[1024,1024]{1,0:T(8,128)(2,1)} %convert_bitcast_fusion), channel_id=1, source_target_pairs={{0,8},{8,0},{16,24},{24,16},{1,9},{9,1},{17,25},{25,17},{2,10},{10... | collective-permute-start | bytes 6291464 | tf_op jit(solution)/shard_map/ppermute | solution.py:103
  113.5 2.7 %convolution_convert_fusion = bf16[1024,1024]{1,0:T(8,128)(2,1)} fusion(bf16[1,512,1024]{2,1,0:T(8,128)(2,1)S(1)} %copy-done.20, bf16[512,1024]{1,0:T(8,128)(2,1)S(1)} %copy-done.23, bf16[1,512,1024]{2,1,0:T(8,128)(2,1)S(1)} %copy-done.17, pred[]{:T(512)S(6)} %eq.17, f32[512,1024]{1,0:T(8,128)S(1)} %get-tuple-element.29), kind=kOutput, calls=%fused_computation.9 | convolution fusion | flops 1076363264 | bytes 7340033 | tf_op jit(solution)/shard_map/dot_general | solution.py:111
  117.6 3.5 %fusion = bf16[1024,1024]{1,0:T(8,128)(2,1)S(1)} fusion(bf16[1024,1024]{1,0:T(8,128)(2,1)} %collective-permute-done.6, bf16[1,512,1024]{2,1,0:T(8,128)(2,1)S(1)} %copy-done.17, bf16[512,1024]{1,0:T(8,128)(2,1)} %get-tuple-element.11, pred[]{:T(512)S(6)} %eq.17, f32[512,1024]{1,0:T(8,128)} %copy-done.1), kind=kOutput, calls=%fused_computation.1 | convolution fusion | flops 1080033280 | bytes 8388609 | tf_op jit(solution)/shard_map/dot_general | solution.py:111
  124.2 2.9 %add_convert_fusion = bf16[1024,1024]{1,0:T(8,128)(2,1)S(1)} fusion(bf16[1024,1024]{1,0:T(8,128)(2,1)} %collective-permute-done.11, bf16[1,512,1024]{2,1,0:T(8,128)(2,1)S(1)} %copy-done.21, bf16[512,1024]{1,0:T(8,128)(2,1)S(1)} %copy-done.24, bf16[1,512,1024]{2,1,0:T(8,128)(2,1)S(1)} %copy-done.18, pred[]{:T(512)S(6)} %eq.17, f32[512,1024]{1,0:T(8,128)S(1)} %copy-done.6), kind=kOutput, calls=%fused_computation.2 | convolution fusion | flops 1080557568 | bytes 9437185 | tf_op jit(solution)/shard_map/dot_general | solution.py:111
  129.3 2.5 %fusion.43 = f32[512,1024]{1,0:T(8,128)S(1)} fusion(bf16[512,1024]{1,0:T(8,128)(2,1)} %get-tuple-element.11, bf16[1024,1024]{1,0:T(8,128)(2,1)S(1)} %copy-done), kind=kOutput, calls=%fused_computation.117 | convolution fusion | flops 1073741824 | bytes 5242880 | tf_op jit(solution)/shard_map/dot_general | solution.py:219
  131.8 15.0 %collective-permute-done.7 = bf16[2,2,2,64,1024]{4,3,0,2,1:T(8,128)(2,1)} collective-permute-done((bf16[2,2,2,64,1024]{4,3,0,2,1:T(8,128)(2,1)}, bf16[2,2,2,64,1024]{4,3,0,2,1:T(8,128)(2,1)}, u32[]{:S(2)}, u32[]{:S(2)}) %collective-permute-start.7) | collective-permute-done | bytes 1048608 | tf_op jit(solution)/shard_map/ppermute | solution.py:103
  148.6 5.0 %collective-permute-done.12 = bf16[2,2,2,64,1024]{4,3,2,0,1:T(8,128)(2,1)} collective-permute-done((bf16[2,2,2,64,1024]{4,3,2,0,1:T(8,128)(2,1)}, bf16[2,2,2,64,1024]{4,3,2,0,1:T(8,128)(2,1)}, u32[]{:S(2)}, u32[]{:S(2)}) %collective-permute-start.12) | collective-permute-done | bytes 1048608 | tf_op jit(solution)/shard_map/ppermute | solution.py:103
  159.0 5.8 %collective-permute-done.8 = bf16[2,2,64,1024]{3,2,0,1:T(8,128)(2,1)S(1)} collective-permute-done((bf16[2,2,64,1024]{3,2,0,1:T(8,128)(2,1)S(1)}, bf16[2,2,64,1024]{3,2,0,1:T(8,128)(2,1)S(1)}, u32[]{:S(2)}, u32[]{:S(2)}) %collective-permute-start.8) | collective-permute-done | bytes 524320 | tf_op jit(solution)/shard_map/ppermute | solution.py:103
  167.4 3.9 %collective-permute-done.9 = bf16[2,64,1024]{2,1,0:T(8,128)(2,1)S(1)} collective-permute-done((bf16[2,64,1024]{2,1,0:T(8,128)(2,1)S(1)}, bf16[2,64,1024]{2,1,0:T(8,128)(2,1)S(1)}, u32[]{:S(2)}, u32[]{:S(2)}) %collective-permute-start.9) | collective-permute-done | bytes 262176 | tf_op jit(solution)/shard_map/ppermute | solution.py:103
  172.2 10.8 %collective-permute-done.14 = bf16[2,64,1024]{2,1,0:T(8,128)(2,1)S(1)} collective-permute-done((bf16[2,64,1024]{2,1,0:T(8,128)(2,1)S(1)}, bf16[2,64,1024]{2,1,0:T(8,128)(2,1)S(1)}, u32[]{:S(2)}, u32[]{:S(2)}) %collective-permute-start.14) | collective-permute-done | bytes 262176 | tf_op jit(solution)/shard_map/ppermute | solution.py:103
  189.7 3.5 %collective-permute-done.16 = bf16[64,2048]{1,0:T(8,128)(2,1)S(1)} collective-permute-done((bf16[64,2048]{1,0:T(8,128)(2,1)S(1)}, bf16[64,2048]{1,0:T(8,128)(2,1)S(1)}, u32[]{:S(2)}, u32[]{:S(2)}) %collective-permute-start.16) | collective-permute-done | bytes 262176 | tf_op jit(solution)/shard_map/ppermute | solution.py:103
  193.3 5.3 %collective-permute-start.17 = (bf16[128,2048]{1,0:T(8,128)(2,1)S(1)}, bf16[128,2048]{1,0:T(8,128)(2,1)S(1)}, u32[]{:S(2)}, u32[]{:S(2)}) collective-permute-start(bf16[128,2048]{1,0:T(8,128)(2,1)S(1)} %maximum_select_fusion), channel_id=1, source_target_pairs={{0,8},{8,0},{16,24},{24,16},{1,9},{9,1},{17,25},{25,17},{2,10},{10... | collective-permute-start | bytes 1572872 | tf_op jit(solution)/shard_map/ppermute | solution.py:103
  198.6 2.3 %fusion.4 = bf16[1,512,1024]{2,1,0:T(8,128)(2,1)} fusion(bf16[1024,1024]{1,0:T(8,128)(2,1)S(1)} %copy-done.10, f32[512,1024]{1,0:T(8,128)S(1)} %fusion.43, f32[512,1024]{1,0:T(8,128)S(1)} %fusion.40, f32[512,1024]{1,0:T(8,128)S(1)} %copy-done.2), kind=kOutput, calls=%fused_computation.18 | convolution fusion | flops 1075838976 | bytes 9437184 | tf_op jit(solution)/shard_map/dot_general | solution.py:221
  (123 shorter events, 45.9 us)
Async XLA Ops:
  0.6 16.3 %copy-start = (bf16[1024,1024]{1,0:T(8,128)(2,1)S(1)}, bf16[1024,1024]{1,0:T(8,128)(2,1)}, u32[]{:S(2)}) copy-start(bf16[1024,1024]{1,0:T(8,128)(2,1)} %param.8) | copy-start | bytes 6291460
  11.0 13.7 %collective-permute-start = (bf16[2,128,1024]{2,1,0:T(8,128)(2,1)S(1)}, bf16[2,128,1024]{2,1,0:T(8,128)(2,1)S(1)}, u32[]{:S(2)}, u32[]{:S(2)}) collective-permute-start(bf16[2,128,1024]{2,1,0:T(8,128)(2,1)S(1)} %pad_maximum_fusion.2), channel_id=1, source_target_pairs={{0,1},{1,0},{2,3},{3,2},{4,5},{5,4},{6,7},{7,6},{8,9},{9,8},{10,11... | collective-permute-start | bytes 1572872 | tf_op jit(solution)/shard_map/ppermute | solution.py:16
  13.1 23.5 %collective-permute-start.1 = (bf16[2,128,1024]{2,1,0:T(8,128)(2,1)S(1)}, bf16[2,128,1024]{2,1,0:T(8,128)(2,1)S(1)}, u32[]{:S(2)}, u32[]{:S(2)}) collective-permute-start(bf16[2,128,1024]{2,1,0:T(8,128)(2,1)S(1)} %pad_maximum_fusion.3), channel_id=1, source_target_pairs={{0,2},{1,3},{2,0},{3,1},{4,6},{5,7},{6,4},{7,5},{8,10},{9,11},{10,... | collective-permute-start | bytes 1572872 | tf_op jit(solution)/shard_map/ppermute | solution.py:16
  14.6 22.1 %collective-permute-start.2 = (bf16[2,128,1024]{2,1,0:T(8,128)(2,1)S(1)}, bf16[2,128,1024]{2,1,0:T(8,128)(2,1)S(1)}, u32[]{:S(2)}, u32[]{:S(2)}) collective-permute-start(bf16[2,128,1024]{2,1,0:T(8,128)(2,1)S(1)} %pad_maximum_fusion.4), channel_id=1, source_target_pairs={{0,4},{1,5},{2,6},{3,7},{4,0},{5,1},{6,2},{7,3},{8,12},{9,13},{10,... | collective-permute-start | bytes 1572872 | tf_op jit(solution)/shard_map/ppermute | solution.py:16
  21.5 15.2 %copy-start.9 = (bf16[512,1024]{1,0:T(8,128)(2,1)S(1)}, bf16[512,1024]{1,0:T(8,128)(2,1)}, u32[]{:S(2)}) copy-start(bf16[512,1024]{1,0:T(8,128)(2,1)} %convolution_convert_fusion.3) | copy-start | bytes 3145732
  77.3 15.4 %collective-permute-start.4 = (bf16[2,128,1024]{2,1,0:T(8,128)(2,1)}, bf16[2,128,1024]{2,1,0:T(8,128)(2,1)S(1)}, u32[]{:S(2)}, u32[]{:S(2)}) collective-permute-start(bf16[2,128,1024]{2,1,0:T(8,128)(2,1)} %pad_maximum_fusion.6), channel_id=1, source_target_pairs={{0,2},{1,3},{2,0},{3,1},{4,6},{5,7},{6,4},{7,5},{8,10},{9,11},{10,... | collective-permute-start | bytes 1572872 | tf_op jit(solution)/shard_map/ppermute | solution.py:16
  80.7 12.1 %collective-permute-start.3 = (bf16[2,128,1024]{2,1,0:T(8,128)(2,1)}, bf16[2,128,1024]{2,1,0:T(8,128)(2,1)}, u32[]{:S(2)}, u32[]{:S(2)}) collective-permute-start(bf16[2,128,1024]{2,1,0:T(8,128)(2,1)} %pad_maximum_fusion.5), channel_id=1, source_target_pairs={{0,1},{1,0},{2,3},{3,2},{4,5},{5,4},{6,7},{7,6},{8,9},{9,8},{10,11... | collective-permute-start | bytes 1572872 | tf_op jit(solution)/shard_map/ppermute | solution.py:16
  83.9 23.3 %collective-permute-start.5 = (bf16[2,128,1024]{2,1,0:T(8,128)(2,1)S(1)}, bf16[2,128,1024]{2,1,0:T(8,128)(2,1)S(1)}, u32[]{:S(2)}, u32[]{:S(2)}) collective-permute-start(bf16[2,128,1024]{2,1,0:T(8,128)(2,1)S(1)} %pad_maximum_fusion.7), channel_id=1, source_target_pairs={{0,4},{1,5},{2,6},{3,7},{4,0},{5,1},{6,2},{7,3},{8,12},{9,13},{10,... | collective-permute-start | bytes 1572872 | tf_op jit(solution)/shard_map/ppermute | solution.py:16
  94.5 13.0 %copy-start.17 = (bf16[1,512,1024]{2,1,0:T(8,128)(2,1)S(1)}, bf16[1,512,1024]{2,1,0:T(8,128)(2,1)}, u32[]{:S(2)}) copy-start(bf16[1,512,1024]{2,1,0:T(8,128)(2,1)} %param.7) | copy-start | bytes 3145732
  94.5 13.0 %copy-start.22 = (bf16[512,1024]{1,0:T(8,128)(2,1)S(1)}, bf16[512,1024]{1,0:T(8,128)(2,1)}, u32[]{:S(2)}) copy-start(bf16[512,1024]{1,0:T(8,128)(2,1)} %get-tuple-element.11) | copy-start | bytes 3145732
  110.2 7.4 %collective-permute-start.6 = (bf16[1024,1024]{1,0:T(8,128)(2,1)}, bf16[1024,1024]{1,0:T(8,128)(2,1)}, u32[]{:S(2)}, u32[]{:S(2)}) collective-permute-start(bf16[1024,1024]{1,0:T(8,128)(2,1)} %convert_bitcast_fusion), channel_id=1, source_target_pairs={{0,8},{8,0},{16,24},{24,16},{1,9},{9,1},{17,25},{25,17},{2,10},{10... | collective-permute-start | bytes 6291464 | tf_op jit(solution)/shard_map/ppermute | solution.py:103
  116.2 7.5 %collective-permute-start.11 = (bf16[1024,1024]{1,0:T(8,128)(2,1)}, bf16[1024,1024]{1,0:T(8,128)(2,1)}, u32[]{:S(2)}, u32[]{:S(2)}) collective-permute-start(bf16[1024,1024]{1,0:T(8,128)(2,1)} %convolution_convert_fusion), channel_id=1, source_target_pairs={{0,8},{8,0},{16,24},{24,16},{1,9},{9,1},{17,25},{25,17},{2,10},{10... | collective-permute-start | bytes 6291464 | tf_op jit(solution)/shard_map/ppermute | solution.py:103
  122.5 24.3 %collective-permute-start.7 = (bf16[2,2,2,64,1024]{4,3,0,2,1:T(8,128)(2,1)}, bf16[2,2,2,64,1024]{4,3,0,2,1:T(8,128)(2,1)}, u32[]{:S(2)}, u32[]{:S(2)}) collective-permute-start(bf16[2,2,2,64,1024]{4,3,0,2,1:T(8,128)(2,1)} %bitcast.164), channel_id=1, source_target_pairs={{0,1},{1,0},{2,3},{3,2},{4,5},{5,4},{6,7},{7,6},{8,9},{9,8},{10,11... | collective-permute-start | bytes 3145736 | tf_op jit(solution)/shard_map/ppermute | solution.py:103
  129.3 24.3 %collective-permute-start.12 = (bf16[2,2,2,64,1024]{4,3,2,0,1:T(8,128)(2,1)}, bf16[2,2,2,64,1024]{4,3,2,0,1:T(8,128)(2,1)}, u32[]{:S(2)}, u32[]{:S(2)}) collective-permute-start(bf16[2,2,2,64,1024]{4,3,2,0,1:T(8,128)(2,1)} %bitcast.163), channel_id=1, source_target_pairs={{0,2},{1,3},{2,0},{3,1},{4,6},{5,7},{6,4},{7,5},{8,10},{9,11},{10,... | collective-permute-start | bytes 3145736 | tf_op jit(solution)/shard_map/ppermute | solution.py:103
  148.5 16.2 %collective-permute-start.8 = (bf16[2,2,64,1024]{3,2,0,1:T(8,128)(2,1)S(1)}, bf16[2,2,64,1024]{3,2,0,1:T(8,128)(2,1)S(1)}, u32[]{:S(2)}, u32[]{:S(2)}) collective-permute-start(bf16[2,2,64,1024]{3,2,0,1:T(8,128)(2,1)S(1)} %dynamic-slice_bitcast_fusion.1), channel_id=1, source_target_pairs={{0,2},{1,3},{2,0},{3,1},{4,6},{5,7},{6,4},{7,5},{8,10},{9,11},{10,... | collective-permute-start | bytes 1572872 | tf_op jit(solution)/shard_map/ppermute | solution.py:103
  155.5 10.8 %collective-permute-start.13 = (bf16[2,2,64,1024]{3,2,1,0:T(8,128)(2,1)S(1)}, bf16[2,2,64,1024]{3,2,1,0:T(8,128)(2,1)S(1)}, u32[]{:S(2)}, u32[]{:S(2)}) collective-permute-start(bf16[2,2,64,1024]{3,2,1,0:T(8,128)(2,1)S(1)} %dynamic-slice_bitcast_fusion), channel_id=1, source_target_pairs={{0,1},{1,0},{2,3},{3,2},{4,5},{5,4},{6,7},{7,6},{8,9},{9,8},{10,11... | collective-permute-start | bytes 1572872 | tf_op jit(solution)/shard_map/ppermute | solution.py:103
  165.0 6.3 %collective-permute-start.9 = (bf16[2,64,1024]{2,1,0:T(8,128)(2,1)S(1)}, bf16[2,64,1024]{2,1,0:T(8,128)(2,1)S(1)}, u32[]{:S(2)}, u32[]{:S(2)}) collective-permute-start(bf16[2,64,1024]{2,1,0:T(8,128)(2,1)S(1)} %dynamic-slice_bitcast_fusion.3), channel_id=1, source_target_pairs={{0,16},{8,24},{16,0},{24,8},{1,17},{9,25},{17,1},{25,9},{2,18},{10... | collective-permute-start | bytes 786440 | tf_op jit(solution)/shard_map/ppermute | solution.py:103
  166.3 22.1 %copy-start.14 = (bf16[1024,1024]{1,0:T(8,128)(2,1)S(1)}, bf16[1024,1024]{1,0:T(8,128)(2,1)}, u32[]{:S(2)}) copy-start(bf16[1024,1024]{1,0:T(8,128)(2,1)} %param.9) | copy-start | bytes 6291460
  166.5 21.9 %copy-start.7 = (f32[512,1024]{1,0:T(8,128)S(1)}, f32[512,1024]{1,0:T(8,128)}, u32[]{:S(2)}) copy-start(f32[512,1024]{1,0:T(8,128)} %copy-done.5) | copy-start | bytes 6291460
  166.6 16.4 %collective-permute-start.14 = (bf16[2,64,1024]{2,1,0:T(8,128)(2,1)S(1)}, bf16[2,64,1024]{2,1,0:T(8,128)(2,1)S(1)}, u32[]{:S(2)}, u32[]{:S(2)}) collective-permute-start(bf16[2,64,1024]{2,1,0:T(8,128)(2,1)S(1)} %dynamic-slice_bitcast_fusion.2), channel_id=1, source_target_pairs={{0,4},{1,5},{2,6},{3,7},{4,0},{5,1},{6,2},{7,3},{8,12},{9,13},{10,... | collective-permute-start | bytes 786440 | tf_op jit(solution)/shard_map/ppermute | solution.py:103
  171.6 14.2 %collective-permute-start.10 = (bf16[64,1024]{1,0:T(8,128)(2,1)S(1)}, bf16[64,1024]{1,0:T(8,128)(2,1)S(1)}, u32[]{:S(2)}, u32[]{:S(2)}) collective-permute-start(bf16[64,1024]{1,0:T(8,128)(2,1)S(1)} %dynamic-slice_bitcast_fusion.11), channel_id=1, source_target_pairs={{0,4},{1,5},{2,6},{3,7},{4,0},{5,1},{6,2},{7,3},{8,12},{9,13},{10,... | collective-permute-start | bytes 393224 | tf_op jit(solution)/shard_map/ppermute | solution.py:103
  183.1 4.0 %collective-permute-start.15 = (bf16[64,1024]{1,0:T(8,128)(2,1)S(1)}, bf16[64,1024]{1,0:T(8,128)(2,1)S(1)}, u32[]{:S(2)}, u32[]{:S(2)}) collective-permute-start(bf16[64,1024]{1,0:T(8,128)(2,1)S(1)} %dynamic-slice_bitcast_fusion.10), channel_id=1, source_target_pairs={{0,16},{8,24},{16,0},{24,8},{1,17},{9,25},{17,1},{25,9},{2,18},{10... | collective-permute-start | bytes 393224 | tf_op jit(solution)/shard_map/ppermute | solution.py:103
  187.2 6.0 %collective-permute-start.16 = (bf16[64,2048]{1,0:T(8,128)(2,1)S(1)}, bf16[64,2048]{1,0:T(8,128)(2,1)S(1)}, u32[]{:S(2)}, u32[]{:S(2)}) collective-permute-start(bf16[64,2048]{1,0:T(8,128)(2,1)S(1)} %pad_maximum_fusion.8), channel_id=1, source_target_pairs={{0,16},{8,24},{16,0},{24,8},{1,17},{9,25},{17,1},{25,9},{2,18},{10... | collective-permute-start | bytes 786440 | tf_op jit(solution)/shard_map/ppermute | solution.py:103
  193.3 7.5 %collective-permute-start.17 = (bf16[128,2048]{1,0:T(8,128)(2,1)S(1)}, bf16[128,2048]{1,0:T(8,128)(2,1)S(1)}, u32[]{:S(2)}, u32[]{:S(2)}) collective-permute-start(bf16[128,2048]{1,0:T(8,128)(2,1)S(1)} %maximum_select_fusion), channel_id=1, source_target_pairs={{0,8},{8,0},{16,24},{24,16},{1,9},{9,1},{17,25},{25,17},{2,10},{10... | collective-permute-start | bytes 1572872 | tf_op jit(solution)/shard_map/ppermute | solution.py:103
  (20 other events, 96.6 us)

commit v8 on v4

--- a/solution.py
+++ b/solution.py
@@ -37,31 +37,35 @@
     do = do_ref[...]
     width = q.shape[1]
     lane = lax.broadcasted_iota(jnp.int32, (1, width), 1)
-    outs = None
+    row = lax.broadcasted_iota(jnp.int32, (width, 1), 0)
+    q_t = q.T
+    do_t = do.T
+    probs, grads, v_parts, k_parts, q_parts, do_parts = [], [], [], [], [], []
     for j in range(width // head):
         inside = (lane >= j * head) & (lane < (j + 1) * head)
+        rows_in = (row >= j * head) & (row < (j + 1) * head)
         qm = jnp.where(inside, q * jnp.asarray(scale, q.dtype), jnp.zeros_like(q))
         dom = jnp.where(inside, do, jnp.zeros_like(do))
         s = lax.dot_general(qm, k, (((1,), (1,)), ((), ())), preferred_element_type=jnp.float32)
         top = jnp.max(s, axis=-1, keepdims=True)
         e = jnp.exp(s - top)
         p = e * (1.0 / jnp.sum(e, axis=-1, keepdims=True))
-        pb = p.astype(jnp.bfloat16)
-        a = jnp.dot(pb, v, preferred_element_type=jnp.float32)
         dp = lax.dot_general(dom, v, (((1,), (1,)), ((), ())), preferred_element_type=jnp.float32)
         delta = jnp.sum(p * dp, axis=-1, keepdims=True)
-        ds = (p * (dp - delta) * scale).astype(jnp.bfloat16)
-        dq = jnp.dot(ds, k, preferred_element_type=jnp.float32)
-        dk = lax.dot_general(ds, q, (((0,), (0,)), ((), ())), preferred_element_type=jnp.float32)
-        dv = lax.dot_general(pb, do, (((0,), (0,)), ((), ())), preferred_element_type=jnp.float32)
-        if outs is None:
-            outs = [a, dq, dk, dv]
-        else:
-            outs = [jnp.where(inside, new, old) for new, old in zip([a, dq, dk, dv], outs)]
-    att_ref[...] = outs[0].astype(att_ref.dtype)
-    dq_ref[...] = outs[1].astype(dq_ref.dtype)
-    dk_ref[...] = outs[2]
-    dv_ref[...] = outs[3]
+        probs.append(p.astype(jnp.bfloat16))
+        grads.append((p * (dp - delta) * scale).astype(jnp.bfloat16))
+        v_parts.append(jnp.where(inside, v, jnp.zeros_like(v)))
+        k_parts.append(jnp.where(inside, k, jnp.zeros_like(k)))
+        q_parts.append(jnp.where(rows_in, q_t, jnp.zeros_like(q_t)))
+        do_parts.append(jnp.where(rows_in, do_t, jnp.zeros_like(do_t)))
+    att = jnp.dot(jnp.concatenate(probs, 1), jnp.concatenate(v_parts, 0), preferred_element_type=jnp.float32)
+    dq = jnp.dot(jnp.concatenate(grads, 1), jnp.concatenate(k_parts, 0), preferred_element_type=jnp.float32)
+    dk_t = jnp.dot(jnp.concatenate(q_parts, 1), jnp.concatenate(grads, 0), preferred_element_type=jnp.float32)
+    dv_t = jnp.dot(jnp.concatenate(do_parts, 1), jnp.concatenate(probs, 0), preferred_element_type=jnp.float32)
+    att_ref[...] = att.astype(att_ref.dtype)
+    dq_ref[...] = dq.astype(dq_ref.dtype)
+    dk_ref[...] = dk_t.T
+    dv_ref[...] = dv_t.T
 
 
 def attention(query, keys, values, d_att, head):

time: 207 us -> 199 us (0.961)
  Pallas kernels: 38.1 us -> 29.6 us
    pallas_call x1, Pallas kernels: 38.1 us -> 29.6 us  [attention(): pl.pallas_call(functools.partial(attention_kernel, head=head, scale=head...]
where the time goes in v8:
time: 199 us; the launch traced here: 198 us
  waiting for transfers between devices  84.3 us (42%)
  matrix products  30.1 us (15%)
  Pallas kernels  29.6 us (15%)
  starting transfers between devices  25.3 us (13%)
  other arithmetic  15.1 us (8%)
  local copies, waits for them, and re-layouts  10.6 us (5%)
  between operations  3.35 us (2%)
    ppermute x12, waiting for transfers between devices, exchange(): lax.ppermute(array, axis, [(i, i ^ mask) for i in range(lax.axis_size(axi...  47.8 us
    ppermute x6, waiting for transfers between devices, partner(): lax.ppermute(array, axis, [(i, i ^ 1 << apart) for i in range(lax.axis_si...  36.5 us
    pallas_call x1, Pallas kernels, attention(): pl.pallas_call(functools.partial(attention_kernel, head=head, scale=head...  29.6 us
    ppermute x12, starting transfers between devices, exchange(): lax.ppermute(array, axis, [(i, i ^ mask) for i in range(lax.axis_size(axi...  16.6 us
    dot_general x4, matrix products, term(): jnp.dot(left.T, right[:, lo:hi], preferred_element_type=jnp.float32)  11.8 us
    ppermute x6, starting transfers between devices, partner(): lax.ppermute(array, axis, [(i, i ^ 1 << apart) for i in range(lax.axis_si...  8.75 us
    dot_general x1, matrix products, body(): jnp.dot(rows, w_value, preferred_element_type=jnp.float32)  4.28 us
    convert_element_type x8, other arithmetic, add_bf16(): return (a.astype(jnp.float32) + b.astype(jnp.float32)).astype(jnp.bfloat16)  4.09 us
  transfers between devices with their start and end apart: 18, of which 13 were waited for; matrix products, arithmetic and copies ran while one was open for 17% of the time, Pallas kernels for 0%

profile of v8, /device:TPU:1, one launch (start us, length us, event | category | flops | bytes accessed | tf_op | source)
XLA Modules:
  0.0 198.5 jit_solution(3636501663036034905)
XLA Ops:
  4.0 4.3 %convolution_convert_fusion.3 = bf16[512,1024]{1,0:T(8,128)(2,1)} fusion(bf16[1024,1024]{1,0:T(8,128)(2,1)} %param.10, bf16[1,512,1024]{2,1,0:T(8,128)(2,1)} %param.7), kind=kOutput, calls=%fused_computation.14 | convolution fusion | flops 1074266112 | bytes 4194304 | tf_op jit(solution)/shard_map/dot_general | solution.py:189
  14.6 2.4 %collective-permute-start.2 = (bf16[2,128,1024]{2,1,0:T(8,128)(2,1)S(1)}, bf16[2,128,1024]{2,1,0:T(8,128)(2,1)S(1)}, u32[]{:S(2)}, u32[]{:S(2)}) collective-permute-start(bf16[2,128,1024]{2,1,0:T(8,128)(2,1)S(1)} %pad_maximum_fusion.4), channel_id=1, source_target_pairs={{0,4},{1,5},{2,6},{3,7},{4,0},{5,1},{6,2},{7,3},{8,12},{9,13},{10,... | collective-permute-start | bytes 1572872 | tf_op jit(solution)/shard_map/ppermute | solution.py:16
  19.2 2.3 %convolution_convert_fusion.2.do_ref = bf16[512,1024]{1,0:T(8,128)(2,1)} fusion(bf16[1024,1024]{1,0:T(8,128)(2,1)S(1)} %copy-done.11, bf16[1,512,1024]{2,1,0:T(8,128)(2,1)S(1)} %copy-done.19), kind=kOutput, calls=%fused_computation.13 | convolution fusion | flops 1074266112 | bytes 4194304 | tf_op jit(solution)/shard_map/dot_general | solution.py:193
  21.5 3.2 %collective-permute-done = bf16[2,128,1024]{2,1,0:T(8,128)(2,1)S(1)} collective-permute-done((bf16[2,128,1024]{2,1,0:T(8,128)(2,1)S(1)}, bf16[2,128,1024]{2,1,0:T(8,128)(2,1)S(1)}, u32[]{:S(2)}, u32[]{:S(2)}) %collective-permute-start) | collective-permute-done | bytes 524320 | tf_op jit(solution)/shard_map/ppermute | solution.py:16
  24.8 11.9 %collective-permute-done.1 = bf16[2,128,1024]{2,1,0:T(8,128)(2,1)S(1)} collective-permute-done((bf16[2,128,1024]{2,1,0:T(8,128)(2,1)S(1)}, bf16[2,128,1024]{2,1,0:T(8,128)(2,1)S(1)}, u32[]{:S(2)}, u32[]{:S(2)}) %collective-permute-start.1) | collective-permute-done | bytes 524320 | tf_op jit(solution)/shard_map/ppermute | solution.py:16
  39.6 29.6 %shard_map.118 = (bf16[512,1024]{1,0:T(8,128)(2,1)}, bf16[512,1024]{1,0:T(8,128)(2,1)}, f32[896,1024]{1,0:T(8,128)}, f32[896,1024]{1,0:T(8,128)}) custom-call(bf16[512,1024]{1,0:T(8,128)(2,1)} %convolution_convert_fusion.5.q_ref, bf16[896,1024]{1,0:T(8,128)(2,1)} %pad_maximum_fusion.k_ref, bf16[896,1024]{1,0:T(8,128)(2,1)} %pad_maximum_fusion.1.v_ref, ...), custom_call_target="tpu_custom_call" | custom-call | flops 11274289152 | bytes 13107200 | tf_op jit(solution)/shard_map/pallas_call | solution.py:77
  69.2 2.5 %convert.31 = bf16[896,1024]{1,0:T(8,128)(2,1)S(1)} convert(f32[896,1024]{1,0:T(8,128)} %get-tuple-element.12) | non-fusion elementwise | flops 917504 | bytes 5505024 | tf_op jit(solution)/shard_map/convert.26
  73.6 2.6 %collective-permute-start.4 = (bf16[2,128,1024]{2,1,0:T(8,128)(2,1)}, bf16[2,128,1024]{2,1,0:T(8,128)(2,1)S(1)}, u32[]{:S(2)}, u32[]{:S(2)}) collective-permute-start(bf16[2,128,1024]{2,1,0:T(8,128)(2,1)} %pad_maximum_fusion.6), channel_id=1, source_target_pairs={{0,2},{1,3},{2,0},{3,1},{4,6},{5,7},{6,4},{7,5},{8,10},{9,11},{10,... | collective-permute-start | bytes 1572872 | tf_op jit(solution)/shard_map/ppermute | solution.py:16
  80.2 8.8 %collective-permute-done.4 = bf16[2,128,1024]{2,1,0:T(8,128)(2,1)S(1)} collective-permute-done((bf16[2,128,1024]{2,1,0:T(8,128)(2,1)}, bf16[2,128,1024]{2,1,0:T(8,128)(2,1)S(1)}, u32[]{:S(2)}, u32[]{:S(2)}) %collective-permute-start.4) | collective-permute-done | bytes 524320 | tf_op jit(solution)/shard_map/ppermute | solution.py:16
  90.7 12.6 %collective-permute-done.5 = bf16[2,128,1024]{2,1,0:T(8,128)(2,1)S(1)} collective-permute-done((bf16[2,128,1024]{2,1,0:T(8,128)(2,1)S(1)}, bf16[2,128,1024]{2,1,0:T(8,128)(2,1)S(1)}, u32[]{:S(2)}, u32[]{:S(2)}) %collective-permute-start.5) | collective-permute-done | bytes 524320 | tf_op jit(solution)/shard_map/ppermute | solution.py:16
  103.8 2.6 %convert_bitcast_fusion = bf16[1024,1024]{1,0:T(8,128)(2,1)} fusion(bf16[1,512,1024]{2,1,0:T(8,128)(2,1)S(1)} %copy-done.17, bf16[512,1024]{1,0:T(8,128)(2,1)S(1)} %copy-done.22, pred[]{:T(512)S(6)} %eq.17, f32[512,1024]{1,0:T(8,128)S(1)} %get-tuple-element.28), kind=kOutput, calls=%fused_computation.7 | convolution fusion | flops 1075838976 | bytes 6291457 | tf_op jit(solution)/shard_map/dot_general | solution.py:106
  106.4 3.3 %collective-permute-start.6 = (bf16[1024,1024]{1,0:T(8,128)(2,1)}, bf16[1024,1024]{1,0:T(8,128)(2,1)}, u32[]{:S(2)}, u32[]{:S(2)}) collective-permute-start(bf16[1024,1024]{1,0:T(8,128)(2,1)} %convert_bitcast_fusion), channel_id=1, source_target_pairs={{0,8},{8,0},{16,24},{24,16},{1,9},{9,1},{17,25},{25,17},{2,10},{10... | collective-permute-start | bytes 6291464 | tf_op jit(solution)/shard_map/ppermute | solution.py:98
  109.7 2.7 %convolution_convert_fusion = bf16[1024,1024]{1,0:T(8,128)(2,1)} fusion(bf16[1,512,1024]{2,1,0:T(8,128)(2,1)S(1)} %copy-done.20, bf16[512,1024]{1,0:T(8,128)(2,1)S(1)} %copy-done.23, bf16[1,512,1024]{2,1,0:T(8,128)(2,1)S(1)} %copy-done.17, pred[]{:T(512)S(6)} %eq.17, f32[512,1024]{1,0:T(8,128)S(1)} %get-tuple-element.29), kind=kOutput, calls=%fused_computation.9 | convolution fusion | flops 1076363264 | bytes 7340033 | tf_op jit(solution)/shard_map/dot_general | solution.py:106
  113.9 3.5 %fusion = bf16[1024,1024]{1,0:T(8,128)(2,1)S(1)} fusion(bf16[1024,1024]{1,0:T(8,128)(2,1)} %collective-permute-done.6, bf16[1,512,1024]{2,1,0:T(8,128)(2,1)S(1)} %copy-done.17, bf16[512,1024]{1,0:T(8,128)(2,1)} %get-tuple-element.11, pred[]{:T(512)S(6)} %eq.17, f32[512,1024]{1,0:T(8,128)} %copy-done.1), kind=kOutput, calls=%fused_computation.1 | convolution fusion | flops 1080033280 | bytes 8388609 | tf_op jit(solution)/shard_map/dot_general | solution.py:106
  120.4 2.9 %add_convert_fusion = bf16[1024,1024]{1,0:T(8,128)(2,1)S(1)} fusion(bf16[1024,1024]{1,0:T(8,128)(2,1)} %collective-permute-done.11, bf16[1,512,1024]{2,1,0:T(8,128)(2,1)S(1)} %copy-done.21, bf16[512,1024]{1,0:T(8,128)(2,1)S(1)} %copy-done.24, bf16[1,512,1024]{2,1,0:T(8,128)(2,1)S(1)} %copy-done.18, pred[]{:T(512)S(6)} %eq.17, f32[512,1024]{1,0:T(8,128)S(1)} %copy-done.6), kind=kOutput, calls=%fused_computation.2 | convolution fusion | flops 1080557568 | bytes 9437185 | tf_op jit(solution)/shard_map/dot_general | solution.py:106
  125.5 2.5 %fusion.43 = f32[512,1024]{1,0:T(8,128)S(1)} fusion(bf16[512,1024]{1,0:T(8,128)(2,1)} %get-tuple-element.11, bf16[1024,1024]{1,0:T(8,128)(2,1)S(1)} %copy-done), kind=kOutput, calls=%fused_computation.117 | convolution fusion | flops 1073741824 | bytes 5242880 | tf_op jit(solution)/shard_map/dot_general | solution.py:214
  128.0 15.0 %collective-permute-done.7 = bf16[2,2,2,64,1024]{4,3,0,2,1:T(8,128)(2,1)} collective-permute-done((bf16[2,2,2,64,1024]{4,3,0,2,1:T(8,128)(2,1)}, bf16[2,2,2,64,1024]{4,3,0,2,1:T(8,128)(2,1)}, u32[]{:S(2)}, u32[]{:S(2)}) %collective-permute-start.7) | collective-permute-done | bytes 1048608 | tf_op jit(solution)/shard_map/ppermute | solution.py:98
  144.9 5.0 %collective-permute-done.12 = bf16[2,2,2,64,1024]{4,3,2,0,1:T(8,128)(2,1)} collective-permute-done((bf16[2,2,2,64,1024]{4,3,2,0,1:T(8,128)(2,1)}, bf16[2,2,2,64,1024]{4,3,2,0,1:T(8,128)(2,1)}, u32[]{:S(2)}, u32[]{:S(2)}) %collective-permute-start.12) | collective-permute-done | bytes 1048608 | tf_op jit(solution)/shard_map/ppermute | solution.py:98
  155.2 5.8 %collective-permute-done.8 = bf16[2,2,64,1024]{3,2,0,1:T(8,128)(2,1)S(1)} collective-permute-done((bf16[2,2,64,1024]{3,2,0,1:T(8,128)(2,1)S(1)}, bf16[2,2,64,1024]{3,2,0,1:T(8,128)(2,1)S(1)}, u32[]{:S(2)}, u32[]{:S(2)}) %collective-permute-start.8) | collective-permute-done | bytes 524320 | tf_op jit(solution)/shard_map/ppermute | solution.py:98
  163.6 3.9 %collective-permute-done.9 = bf16[2,64,1024]{2,1,0:T(8,128)(2,1)S(1)} collective-permute-done((bf16[2,64,1024]{2,1,0:T(8,128)(2,1)S(1)}, bf16[2,64,1024]{2,1,0:T(8,128)(2,1)S(1)}, u32[]{:S(2)}, u32[]{:S(2)}) %collective-permute-start.9) | collective-permute-done | bytes 262176 | tf_op jit(solution)/shard_map/ppermute | solution.py:98
  168.4 10.8 %collective-permute-done.14 = bf16[2,64,1024]{2,1,0:T(8,128)(2,1)S(1)} collective-permute-done((bf16[2,64,1024]{2,1,0:T(8,128)(2,1)S(1)}, bf16[2,64,1024]{2,1,0:T(8,128)(2,1)S(1)}, u32[]{:S(2)}, u32[]{:S(2)}) %collective-permute-start.14) | collective-permute-done | bytes 262176 | tf_op jit(solution)/shard_map/ppermute | solution.py:98
  185.9 3.5 %collective-permute-done.16 = bf16[64,2048]{1,0:T(8,128)(2,1)S(1)} collective-permute-done((bf16[64,2048]{1,0:T(8,128)(2,1)S(1)}, bf16[64,2048]{1,0:T(8,128)(2,1)S(1)}, u32[]{:S(2)}, u32[]{:S(2)}) %collective-permute-start.16) | collective-permute-done | bytes 262176 | tf_op jit(solution)/shard_map/ppermute | solution.py:98
  189.5 5.3 %collective-permute-start.17 = (bf16[128,2048]{1,0:T(8,128)(2,1)S(1)}, bf16[128,2048]{1,0:T(8,128)(2,1)S(1)}, u32[]{:S(2)}, u32[]{:S(2)}) collective-permute-start(bf16[128,2048]{1,0:T(8,128)(2,1)S(1)} %maximum_select_fusion), channel_id=1, source_target_pairs={{0,8},{8,0},{16,24},{24,16},{1,9},{9,1},{17,25},{25,17},{2,10},{10... | collective-permute-start | bytes 1572872 | tf_op jit(solution)/shard_map/ppermute | solution.py:98
  194.8 2.3 %fusion.4 = bf16[1,512,1024]{2,1,0:T(8,128)(2,1)} fusion(bf16[1024,1024]{1,0:T(8,128)(2,1)S(1)} %copy-done.10, f32[512,1024]{1,0:T(8,128)S(1)} %fusion.43, f32[512,1024]{1,0:T(8,128)S(1)} %fusion.40, f32[512,1024]{1,0:T(8,128)S(1)} %copy-done.2), kind=kOutput, calls=%fused_computation.18 | convolution fusion | flops 1075838976 | bytes 9437184 | tf_op jit(solution)/shard_map/dot_general | solution.py:216
  (123 shorter events, 45.9 us)
Async XLA Ops:
  0.6 16.3 %copy-start = (bf16[1024,1024]{1,0:T(8,128)(2,1)S(1)}, bf16[1024,1024]{1,0:T(8,128)(2,1)}, u32[]{:S(2)}) copy-start(bf16[1024,1024]{1,0:T(8,128)(2,1)} %param.8) | copy-start | bytes 6291460
  11.0 13.7 %collective-permute-start = (bf16[2,128,1024]{2,1,0:T(8,128)(2,1)S(1)}, bf16[2,128,1024]{2,1,0:T(8,128)(2,1)S(1)}, u32[]{:S(2)}, u32[]{:S(2)}) collective-permute-start(bf16[2,128,1024]{2,1,0:T(8,128)(2,1)S(1)} %pad_maximum_fusion.2), channel_id=1, source_target_pairs={{0,1},{1,0},{2,3},{3,2},{4,5},{5,4},{6,7},{7,6},{8,9},{9,8},{10,11... | collective-permute-start | bytes 1572872 | tf_op jit(solution)/shard_map/ppermute | solution.py:16
  13.1 23.5 %collective-permute-start.1 = (bf16[2,128,1024]{2,1,0:T(8,128)(2,1)S(1)}, bf16[2,128,1024]{2,1,0:T(8,128)(2,1)S(1)}, u32[]{:S(2)}, u32[]{:S(2)}) collective-permute-start(bf16[2,128,1024]{2,1,0:T(8,128)(2,1)S(1)} %pad_maximum_fusion.3), channel_id=1, source_target_pairs={{0,2},{1,3},{2,0},{3,1},{4,6},{5,7},{6,4},{7,5},{8,10},{9,11},{10,... | collective-permute-start | bytes 1572872 | tf_op jit(solution)/shard_map/ppermute | solution.py:16
  14.6 22.1 %collective-permute-start.2 = (bf16[2,128,1024]{2,1,0:T(8,128)(2,1)S(1)}, bf16[2,128,1024]{2,1,0:T(8,128)(2,1)S(1)}, u32[]{:S(2)}, u32[]{:S(2)}) collective-permute-start(bf16[2,128,1024]{2,1,0:T(8,128)(2,1)S(1)} %pad_maximum_fusion.4), channel_id=1, source_target_pairs={{0,4},{1,5},{2,6},{3,7},{4,0},{5,1},{6,2},{7,3},{8,12},{9,13},{10,... | collective-permute-start | bytes 1572872 | tf_op jit(solution)/shard_map/ppermute | solution.py:16
  21.5 15.2 %copy-start.9 = (bf16[512,1024]{1,0:T(8,128)(2,1)S(1)}, bf16[512,1024]{1,0:T(8,128)(2,1)}, u32[]{:S(2)}) copy-start(bf16[512,1024]{1,0:T(8,128)(2,1)} %convolution_convert_fusion.3) | copy-start | bytes 3145732
  73.6 15.4 %collective-permute-start.4 = (bf16[2,128,1024]{2,1,0:T(8,128)(2,1)}, bf16[2,128,1024]{2,1,0:T(8,128)(2,1)S(1)}, u32[]{:S(2)}, u32[]{:S(2)}) collective-permute-start(bf16[2,128,1024]{2,1,0:T(8,128)(2,1)} %pad_maximum_fusion.6), channel_id=1, source_target_pairs={{0,2},{1,3},{2,0},{3,1},{4,6},{5,7},{6,4},{7,5},{8,10},{9,11},{10,... | collective-permute-start | bytes 1572872 | tf_op jit(solution)/shard_map/ppermute | solution.py:16
  77.0 12.1 %collective-permute-start.3 = (bf16[2,128,1024]{2,1,0:T(8,128)(2,1)}, bf16[2,128,1024]{2,1,0:T(8,128)(2,1)}, u32[]{:S(2)}, u32[]{:S(2)}) collective-permute-start(bf16[2,128,1024]{2,1,0:T(8,128)(2,1)} %pad_maximum_fusion.5), channel_id=1, source_target_pairs={{0,1},{1,0},{2,3},{3,2},{4,5},{5,4},{6,7},{7,6},{8,9},{9,8},{10,11... | collective-permute-start | bytes 1572872 | tf_op jit(solution)/shard_map/ppermute | solution.py:16
  80.1 23.3 %collective-permute-start.5 = (bf16[2,128,1024]{2,1,0:T(8,128)(2,1)S(1)}, bf16[2,128,1024]{2,1,0:T(8,128)(2,1)S(1)}, u32[]{:S(2)}, u32[]{:S(2)}) collective-permute-start(bf16[2,128,1024]{2,1,0:T(8,128)(2,1)S(1)} %pad_maximum_fusion.7), channel_id=1, source_target_pairs={{0,4},{1,5},{2,6},{3,7},{4,0},{5,1},{6,2},{7,3},{8,12},{9,13},{10,... | collective-permute-start | bytes 1572872 | tf_op jit(solution)/shard_map/ppermute | solution.py:16
  90.7 13.0 %copy-start.17 = (bf16[1,512,1024]{2,1,0:T(8,128)(2,1)S(1)}, bf16[1,512,1024]{2,1,0:T(8,128)(2,1)}, u32[]{:S(2)}) copy-start(bf16[1,512,1024]{2,1,0:T(8,128)(2,1)} %param.7) | copy-start | bytes 3145732
  90.7 13.0 %copy-start.22 = (bf16[512,1024]{1,0:T(8,128)(2,1)S(1)}, bf16[512,1024]{1,0:T(8,128)(2,1)}, u32[]{:S(2)}) copy-start(bf16[512,1024]{1,0:T(8,128)(2,1)} %get-tuple-element.11) | copy-start | bytes 3145732
  106.4 7.4 %collective-permute-start.6 = (bf16[1024,1024]{1,0:T(8,128)(2,1)}, bf16[1024,1024]{1,0:T(8,128)(2,1)}, u32[]{:S(2)}, u32[]{:S(2)}) collective-permute-start(bf16[1024,1024]{1,0:T(8,128)(2,1)} %convert_bitcast_fusion), channel_id=1, source_target_pairs={{0,8},{8,0},{16,24},{24,16},{1,9},{9,1},{17,25},{25,17},{2,10},{10... | collective-permute-start | bytes 6291464 | tf_op jit(solution)/shard_map/ppermute | solution.py:98
  112.4 7.5 %collective-permute-start.11 = (bf16[1024,1024]{1,0:T(8,128)(2,1)}, bf16[1024,1024]{1,0:T(8,128)(2,1)}, u32[]{:S(2)}, u32[]{:S(2)}) collective-permute-start(bf16[1024,1024]{1,0:T(8,128)(2,1)} %convolution_convert_fusion), channel_id=1, source_target_pairs={{0,8},{8,0},{16,24},{24,16},{1,9},{9,1},{17,25},{25,17},{2,10},{10... | collective-permute-start | bytes 6291464 | tf_op jit(solution)/shard_map/ppermute | solution.py:98
  118.7 24.3 %collective-permute-start.7 = (bf16[2,2,2,64,1024]{4,3,0,2,1:T(8,128)(2,1)}, bf16[2,2,2,64,1024]{4,3,0,2,1:T(8,128)(2,1)}, u32[]{:S(2)}, u32[]{:S(2)}) collective-permute-start(bf16[2,2,2,64,1024]{4,3,0,2,1:T(8,128)(2,1)} %bitcast.164), channel_id=1, source_target_pairs={{0,1},{1,0},{2,3},{3,2},{4,5},{5,4},{6,7},{7,6},{8,9},{9,8},{10,11... | collective-permute-start | bytes 3145736 | tf_op jit(solution)/shard_map/ppermute | solution.py:98
  125.5 24.3 %collective-permute-start.12 = (bf16[2,2,2,64,1024]{4,3,2,0,1:T(8,128)(2,1)}, bf16[2,2,2,64,1024]{4,3,2,0,1:T(8,128)(2,1)}, u32[]{:S(2)}, u32[]{:S(2)}) collective-permute-start(bf16[2,2,2,64,1024]{4,3,2,0,1:T(8,128)(2,1)} %bitcast.163), channel_id=1, source_target_pairs={{0,2},{1,3},{2,0},{3,1},{4,6},{5,7},{6,4},{7,5},{8,10},{9,11},{10,... | collective-permute-start | bytes 3145736 | tf_op jit(solution)/shard_map/ppermute | solution.py:98
  144.8 16.2 %collective-permute-start.8 = (bf16[2,2,64,1024]{3,2,0,1:T(8,128)(2,1)S(1)}, bf16[2,2,64,1024]{3,2,0,1:T(8,128)(2,1)S(1)}, u32[]{:S(2)}, u32[]{:S(2)}) collective-permute-start(bf16[2,2,64,1024]{3,2,0,1:T(8,128)(2,1)S(1)} %dynamic-slice_bitcast_fusion.1), channel_id=1, source_target_pairs={{0,2},{1,3},{2,0},{3,1},{4,6},{5,7},{6,4},{7,5},{8,10},{9,11},{10,... | collective-permute-start | bytes 1572872 | tf_op jit(solution)/shard_map/ppermute | solution.py:98
  151.7 10.8 %collective-permute-start.13 = (bf16[2,2,64,1024]{3,2,1,0:T(8,128)(2,1)S(1)}, bf16[2,2,64,1024]{3,2,1,0:T(8,128)(2,1)S(1)}, u32[]{:S(2)}, u32[]{:S(2)}) collective-permute-start(bf16[2,2,64,1024]{3,2,1,0:T(8,128)(2,1)S(1)} %dynamic-slice_bitcast_fusion), channel_id=1, source_target_pairs={{0,1},{1,0},{2,3},{3,2},{4,5},{5,4},{6,7},{7,6},{8,9},{9,8},{10,11... | collective-permute-start | bytes 1572872 | tf_op jit(solution)/shard_map/ppermute | solution.py:98
  161.2 6.3 %collective-permute-start.9 = (bf16[2,64,1024]{2,1,0:T(8,128)(2,1)S(1)}, bf16[2,64,1024]{2,1,0:T(8,128)(2,1)S(1)}, u32[]{:S(2)}, u32[]{:S(2)}) collective-permute-start(bf16[2,64,1024]{2,1,0:T(8,128)(2,1)S(1)} %dynamic-slice_bitcast_fusion.3), channel_id=1, source_target_pairs={{0,16},{8,24},{16,0},{24,8},{1,17},{9,25},{17,1},{25,9},{2,18},{10... | collective-permute-start | bytes 786440 | tf_op jit(solution)/shard_map/ppermute | solution.py:98
  162.5 22.1 %copy-start.14 = (bf16[1024,1024]{1,0:T(8,128)(2,1)S(1)}, bf16[1024,1024]{1,0:T(8,128)(2,1)}, u32[]{:S(2)}) copy-start(bf16[1024,1024]{1,0:T(8,128)(2,1)} %param.9) | copy-start | bytes 6291460
  162.7 21.9 %copy-start.7 = (f32[512,1024]{1,0:T(8,128)S(1)}, f32[512,1024]{1,0:T(8,128)}, u32[]{:S(2)}) copy-start(f32[512,1024]{1,0:T(8,128)} %copy-done.5) | copy-start | bytes 6291460
  162.8 16.4 %collective-permute-start.14 = (bf16[2,64,1024]{2,1,0:T(8,128)(2,1)S(1)}, bf16[2,64,1024]{2,1,0:T(8,128)(2,1)S(1)}, u32[]{:S(2)}, u32[]{:S(2)}) collective-permute-start(bf16[2,64,1024]{2,1,0:T(8,128)(2,1)S(1)} %dynamic-slice_bitcast_fusion.2), channel_id=1, source_target_pairs={{0,4},{1,5},{2,6},{3,7},{4,0},{5,1},{6,2},{7,3},{8,12},{9,13},{10,... | collective-permute-start | bytes 786440 | tf_op jit(solution)/shard_map/ppermute | solution.py:98
  167.8 14.2 %collective-permute-start.10 = (bf16[64,1024]{1,0:T(8,128)(2,1)S(1)}, bf16[64,1024]{1,0:T(8,128)(2,1)S(1)}, u32[]{:S(2)}, u32[]{:S(2)}) collective-permute-start(bf16[64,1024]{1,0:T(8,128)(2,1)S(1)} %dynamic-slice_bitcast_fusion.11), channel_id=1, source_target_pairs={{0,4},{1,5},{2,6},{3,7},{4,0},{5,1},{6,2},{7,3},{8,12},{9,13},{10,... | collective-permute-start | bytes 393224 | tf_op jit(solution)/shard_map/ppermute | solution.py:98
  179.3 4.0 %collective-permute-start.15 = (bf16[64,1024]{1,0:T(8,128)(2,1)S(1)}, bf16[64,1024]{1,0:T(8,128)(2,1)S(1)}, u32[]{:S(2)}, u32[]{:S(2)}) collective-permute-start(bf16[64,1024]{1,0:T(8,128)(2,1)S(1)} %dynamic-slice_bitcast_fusion.10), channel_id=1, source_target_pairs={{0,16},{8,24},{16,0},{24,8},{1,17},{9,25},{17,1},{25,9},{2,18},{10... | collective-permute-start | bytes 393224 | tf_op jit(solution)/shard_map/ppermute | solution.py:98
  183.4 6.0 %collective-permute-start.16 = (bf16[64,2048]{1,0:T(8,128)(2,1)S(1)}, bf16[64,2048]{1,0:T(8,128)(2,1)S(1)}, u32[]{:S(2)}, u32[]{:S(2)}) collective-permute-start(bf16[64,2048]{1,0:T(8,128)(2,1)S(1)} %pad_maximum_fusion.8), channel_id=1, source_target_pairs={{0,16},{8,24},{16,0},{24,8},{1,17},{9,25},{17,1},{25,9},{2,18},{10... | collective-permute-start | bytes 786440 | tf_op jit(solution)/shard_map/ppermute | solution.py:98
  189.5 7.5 %collective-permute-start.17 = (bf16[128,2048]{1,0:T(8,128)(2,1)S(1)}, bf16[128,2048]{1,0:T(8,128)(2,1)S(1)}, u32[]{:S(2)}, u32[]{:S(2)}) collective-permute-start(bf16[128,2048]{1,0:T(8,128)(2,1)S(1)} %maximum_select_fusion), channel_id=1, source_target_pairs={{0,8},{8,0},{16,24},{24,16},{1,9},{9,1},{17,25},{25,17},{2,10},{10... | collective-permute-start | bytes 1572872 | tf_op jit(solution)/shard_map/ppermute | solution.py:98
  (20 other events, 96.6 us)

commit v9 on v8

--- a/solution.py
+++ b/solution.py
@@ -30,10 +30,12 @@
     return remote
 
 
-def attention_kernel(q_ref, k_ref, v_ref, do_ref, att_ref, dq_ref, dk_ref, dv_ref, *, head, scale):
+def attention_kernel(q_ref, k_ref, v_ref, do_ref, *refs, head, scale):
+    remote = refs[:-5]
+    att_ref, dq_ref, dk_ref, dv_ref, back_ref = refs[-5:]
     q = q_ref[...]
-    k = k_ref[...]
-    v = v_ref[...]
+    k = jnp.concatenate([k_ref[...]] + [r[0] for r in remote], axis=0)
+    v = jnp.concatenate([v_ref[...]] + [r[1] for r in remote], axis=0)
     do = do_ref[...]
     width = q.shape[1]
     lane = lax.broadcasted_iota(jnp.int32, (1, width), 1)
@@ -64,26 +66,39 @@
     dv_t = jnp.dot(jnp.concatenate(do_parts, 1), jnp.concatenate(probs, 0), preferred_element_type=jnp.float32)
     att_ref[...] = att.astype(att_ref.dtype)
     dq_ref[...] = dq.astype(dq_ref.dtype)
-    dk_ref[...] = dk_t.T
-    dv_ref[...] = dv_t.T
-
-
-def attention(query, keys, values, d_att, head):
+    dk = dk_t.T
+    dv = dv_t.T
+    tok = q.shape[0]
+    dk_ref[...] = dk[:tok]
+    dv_ref[...] = dv[:tok]
+    low = tok
+    for level, r in enumerate(remote):
+        high = low + r.shape[1]
+        back_ref[level, 0] = dk[low:high].astype(back_ref.dtype)
+        back_ref[level, 1] = dv[low:high].astype(back_ref.dtype)
+        low = high
+
+
+def attention(query, keys, values, d_att, remote, head):
     tok, width = query.shape
-    total = keys.shape[0]
+    levels = len(remote)
+    block = remote[0].shape[1]
+    total = tok + levels * block
     steps = width // LANES
     qspec = pl.BlockSpec((tok, LANES), lambda i: (0, i))
-    kspec = pl.BlockSpec((total, LANES), lambda i: (0, i))
+    rspec = pl.BlockSpec((2, block, LANES), lambda i: (0, 0, i))
+    bspec = pl.BlockSpec((levels, 2, block, LANES), lambda i: (0, 0, 0, i))
     return pl.pallas_call(
         functools.partial(attention_kernel, head=head, scale=head ** -0.5),
         grid=(steps,),
-        in_specs=[qspec, kspec, kspec, qspec],
-        out_specs=[qspec, qspec, kspec, kspec],
+        in_specs=[qspec] * 4 + [rspec] * levels,
+        out_specs=[qspec] * 4 + [bspec],
         out_shape=[
             jax.ShapeDtypeStruct((tok, width), jnp.bfloat16),
             jax.ShapeDtypeStruct((tok, width), jnp.bfloat16),
-            jax.ShapeDtypeStruct((total, width), jnp.float32),
-            jax.ShapeDtypeStruct((total, width), jnp.float32),
+            jax.ShapeDtypeStruct((tok, width), jnp.float32),
+            jax.ShapeDtypeStruct((tok, width), jnp.float32),
+            jax.ShapeDtypeStruct((levels, 2, block, width), jnp.bfloat16),
         ],
         compiler_params=pltpu.CompilerParams(vmem_limit_bytes=60 * 1024 * 1024),
         cost_estimate=pl.CostEstimate(
@@ -91,7 +106,7 @@
             transcendentals=tok * total * (width // head),
             bytes_accessed=4 * tok * width + 12 * total * width,
         ),
-    )(query, keys, values, d_att)
+    )(query, keys, values, d_att, *remote)
 
 
 def exchange(array, axis, mask):
@@ -188,17 +203,11 @@
     keys_local = jnp.dot(rows, w_key, preferred_element_type=jnp.float32).astype(jnp.bfloat16)
     values_local = jnp.dot(rows, w_value, preferred_element_type=jnp.float32).astype(jnp.bfloat16)
     remote = swap_blocks(keys_local, values_local, offsets, levels)
-    all_keys = jnp.concatenate([keys_local] + [piece[0] for piece in remote], 0)
-    all_values = jnp.concatenate([values_local] + [piece[1] for piece in remote], 0)
     d_att = jnp.dot(cot, w_out.T, preferred_element_type=jnp.float32).astype(jnp.bfloat16)
-    attended, dquery, dk_acc, dv_acc = attention(query, all_keys, all_values, d_att, head)
+    attended, dquery, dkey_sum, dvalue_sum, back = attention(query, keys_local, values_local, d_att, remote, head)
     result = jnp.dot(attended, w_out, preferred_element_type=jnp.float32).astype(jnp.bfloat16)
-    dkey_sum = dk_acc[:tok]
-    dvalue_sum = dv_acc[:tok]
     for level in range(levels):
-        low = tok + level * BLOCK
-        piece = jnp.stack([dk_acc[low : low + BLOCK], dv_acc[low : low + BLOCK]])
-        returned = partner(piece.astype(jnp.bfloat16), "seq", level).astype(piece.dtype)
+        returned = partner(back[level], "seq", level).astype(jnp.float32)
         start = offsets[level] * BLOCK
         dkey_sum = lax.dynamic_update_slice_in_dim(
             dkey_sum, lax.dynamic_slice_in_dim(dkey_sum, start, BLOCK, 0) + returned[0], start, 0

time: 199 us -> 198 us (level)
  waiting for transfers between devices: 84.3 us -> 80.3 us
  other arithmetic: 15.1 us -> 17.3 us
    dynamic_update_slice x3, other arithmetic: 0.68 us -> 6.14 us  [body(): lax.dynamic_update_slice_in_dim(dkey_sum, lax.dynamic_slice_in_dim(dkey_s...]
    convert_element_type x8 -> x10, other arithmetic: 4.09 us -> 9.18 us  [add_bf16(): return (a.astype(jnp.float32) + b.astype(jnp.float32)).astype(jnp.bfloat16)]
    another operation x5 -> x0, other arithmetic: 4.48 us -> none
    ppermute x6, waiting for transfers between devices: 36.5 us -> 33.6 us  [partner(): lax.ppermute(array, axis, [(i, i ^ 1 << apart) for i in range(lax.axis_si...]
    concatenate x2 -> x0, other arithmetic: 2.83 us -> none  [the longest x1 1.45 us: body(): all_keys = jnp.concatenate([keys_local] + [piece[0] for piece in remote], 0)]
    ppermute x6, starting transfers between devices: 8.75 us -> 11.3 us  [partner(): lax.ppermute(array, axis, [(i, i ^ 1 << apart) for i in range(lax.axis_si...]
    squeeze x3 -> x1, local copies, waits for them, and re-layouts: 0.11 us -> 2.53 us  [body(): returned = partner(back[level], 'seq', level).astype(jnp.float32)]
    slice x2 -> x0, local copies, waits for them, and re-layouts: 2.01 us -> none  [the longest x1 1.88 us: body(): dvalue_sum = dv_acc[:tok]]
  transfers between devices with their start and end apart: 18 -> 18, of which waited for: 13 -> 11; matrix products, arithmetic and copies ran while one was open for 17% -> 19% of each run, Pallas kernels for 0% -> 0%
where the time goes in v9:
time: 198 us; the launch traced here: 197 us
  waiting for transfers between devices  80.3 us (41%)
  matrix products  30.7 us (16%)
  Pallas kernels  29.3 us (15%)
  starting transfers between devices  26.1 us (13%)
  other arithmetic  17.3 us (9%)
  local copies, waits for them, and re-layouts  10.8 us (5%)
  between operations  3.03 us (2%)
    ppermute x12, waiting for transfers between devices, exchange(): lax.ppermute(array, axis, [(i, i ^ mask) for i in range(lax.axis_size(axi...  46.7 us
    ppermute x6, waiting for transfers between devices, partner(): lax.ppermute(array, axis, [(i, i ^ 1 << apart) for i in range(lax.axis_si...  33.6 us
    pallas_call x1, Pallas kernels, attention(): pl.pallas_call(functools.partial(attention_kernel, head=head, scale=head...  29.3 us
    ppermute x12, starting transfers between devices, exchange(): lax.ppermute(array, axis, [(i, i ^ mask) for i in range(lax.axis_size(axi...  14.8 us
    dot_general x4, matrix products, term(): jnp.dot(left.T, right[:, lo:hi], preferred_element_type=jnp.float32)  12.1 us
    ppermute x6, starting transfers between devices, partner(): lax.ppermute(array, axis, [(i, i ^ 1 << apart) for i in range(lax.axis_si...  11.3 us
    convert_element_type x10, other arithmetic, add_bf16(): return (a.astype(jnp.float32) + b.astype(jnp.float32)).astype(jnp.bfloat16)  9.18 us
    dynamic_update_slice x3, other arithmetic, body(): lax.dynamic_update_slice_in_dim(dkey_sum, lax.dynamic_slice_in_dim(dkey_s...  6.14 us
  transfers between devices with their start and end apart: 18, of which 11 were waited for; matrix products, arithmetic and copies ran while one was open for 19% of the time, Pallas kernels for 0%

profile of v9, /device:TPU:1, one launch (start us, length us, event | category | flops | bytes accessed | tf_op | source)
XLA Modules:
  0.0 197.5 jit_solution(2928041059993030936)
XLA Ops:
  4.0 3.3 %convolution_convert_fusion.3.v_ref = bf16[512,1024]{1,0:T(8,128)(2,1)S(1)} fusion(bf16[1024,1024]{1,0:T(8,128)(2,1)} %param.10, bf16[1,512,1024]{2,1,0:T(8,128)(2,1)} %param.7), kind=kOutput, calls=%fused_computation.12 | convolution fusion | flops 1074266112 | bytes 4194304 | tf_op jit(solution)/shard_map/dot_general | solution.py:204
  11.0 3.2 %collective-permute-start.2 = (bf16[2,128,1024]{2,1,0:T(8,128)(2,1)S(1)}, bf16[2,128,1024]{2,1,0:T(8,128)(2,1)S(1)}, u32[]{:S(2)}, u32[]{:S(2)}) collective-permute-start(bf16[2,128,1024]{2,1,0:T(8,128)(2,1)S(1)} %pad_maximum_fusion.2), channel_id=1, source_target_pairs={{0,4},{1,5},{2,6},{3,7},{4,0},{5,1},{6,2},{7,3},{8,12},{9,13},{10,... | collective-permute-start | bytes 1572872 | tf_op jit(solution)/shard_map/ppermute | solution.py:16
  19.2 2.3 %convolution_convert_fusion.2.do_ref = bf16[512,1024]{1,0:T(8,128)(2,1)} fusion(bf16[1024,1024]{1,0:T(8,128)(2,1)S(1)} %copy-done, bf16[1,512,1024]{2,1,0:T(8,128)(2,1)S(1)} %copy-done.16), kind=kOutput, calls=%fused_computation.11 | convolution fusion | flops 1074266112 | bytes 4194304 | tf_op jit(solution)/shard_map/dot_general | solution.py:206
  21.5 15.6 %collective-permute-done.2.refs_2_ = bf16[2,128,1024]{2,1,0:T(8,128)(2,1)S(1)} collective-permute-done((bf16[2,128,1024]{2,1,0:T(8,128)(2,1)S(1)}, bf16[2,128,1024]{2,1,0:T(8,128)(2,1)S(1)}, u32[]{:S(2)}, u32[]{:S(2)}) %collective-permute-start.2) | collective-permute-done | bytes 524320 | tf_op jit(solution)/shard_map/ppermute | solution.py:16
  38.9 29.3 %shard_map.118 = (bf16[512,1024]{1,0:T(8,128)(2,1)}, bf16[512,1024]{1,0:T(8,128)(2,1)}, f32[512,1024]{1,0:T(8,128)}, f32[512,1024]{1,0:T(8,128)}, bf16[3,2,128,1024]{3,2,1,0:T(8,128)(2,1)}) custom-call(bf16[512,1024]{1,0:T(8,128)(2,1)} %convolution_convert_fusion.5.q_ref, bf16[512,1024]{1,0:T(8,128)(2,1)} %convolution_convert_fusion.4.k_ref, ...), custom_call_target="tpu_custom_call" | custom-call | flops 11274289152 | bytes 13107200 | tf_op jit(solution)/shard_map/pallas_call | solution.py:91
  68.1 2.5 %slice_bitcast_fusion.6 = (bf16[2,128,1024]{2,1,0:T(8,128)(2,1)}, bf16[2,128,1024]{2,1,0:T(8,128)(2,1)}, bf16[2,128,1024]{2,1,0:T(8,128)(2,1)}) fusion(bf16[3,2,128,1024]{3,2,1,0:T(8,128)(2,1)} %get-tuple-element.14), kind=kLoop, calls=%fused_computation.71 | loop fusion | bytes 3145728 | tf_op jit(solution)/shard_map/squeeze | solution.py:210
  73.0 3.1 %collective-permute-start.5 = (bf16[2,128,1024]{2,1,0:T(8,128)(2,1)}, bf16[2,128,1024]{2,1,0:T(8,128)(2,1)S(1)}, u32[]{:S(2)}, u32[]{:S(2)}) collective-permute-start(bf16[2,128,1024]{2,1,0:T(8,128)(2,1)} %get-tuple-element.20), channel_id=1, source_target_pairs={{0,4},{1,5},{2,6},{3,7},{4,0},{5,1},{6,2},{7,3},{8,12},{9,13},{10,... | collective-permute-start | bytes 1572872 | tf_op jit(solution)/shard_map/ppermute | solution.py:16
  76.1 6.8 %collective-permute-done.3 = bf16[2,128,1024]{2,1,0:T(8,128)(2,1)S(1)} collective-permute-done((bf16[2,128,1024]{2,1,0:T(8,128)(2,1)}, bf16[2,128,1024]{2,1,0:T(8,128)(2,1)S(1)}, u32[]{:S(2)}, u32[]{:S(2)}) %collective-permute-start.3) | collective-permute-done | bytes 524320 | tf_op jit(solution)/shard_map/ppermute | solution.py:16
  83.0 11.3 %collective-permute-done.4 = bf16[2,128,1024]{2,1,0:T(8,128)(2,1)S(1)} collective-permute-done((bf16[2,128,1024]{2,1,0:T(8,128)(2,1)}, bf16[2,128,1024]{2,1,0:T(8,128)(2,1)S(1)}, u32[]{:S(2)}, u32[]{:S(2)}) %collective-permute-start.4) | collective-permute-done | bytes 524320 | tf_op jit(solution)/shard_map/ppermute | solution.py:16
  100.6 5.0 %convert_bitcast_fusion = bf16[1024,1024]{1,0:T(8,128)(2,1)} fusion(bf16[1,512,1024]{2,1,0:T(8,128)(2,1)S(1)} %copy-done.15, bf16[512,1024]{1,0:T(8,128)(2,1)S(1)} %copy-done.22, pred[]{:T(512)S(6)} %eq.17, f32[512,1024]{1,0:T(8,128)} %get-tuple-element.28), kind=kOutput, calls=%fused_computation.7 | convolution fusion | flops 1075838976 | bytes 6291457 | tf_op jit(solution)/shard_map/dot_general | solution.py:121
  105.7 2.9 %collective-permute-start.6 = (bf16[1024,1024]{1,0:T(8,128)(2,1)}, bf16[1024,1024]{1,0:T(8,128)(2,1)}, u32[]{:S(2)}, u32[]{:S(2)}) collective-permute-start(bf16[1024,1024]{1,0:T(8,128)(2,1)} %convert_bitcast_fusion), channel_id=1, source_target_pairs={{0,8},{8,0},{16,24},{24,16},{1,9},{9,1},{17,25},{25,17},{2,10},{10... | collective-permute-start | bytes 6291464 | tf_op jit(solution)/shard_map/ppermute | solution.py:113
  108.6 2.7 %convolution_convert_fusion = bf16[1024,1024]{1,0:T(8,128)(2,1)} fusion(bf16[1,512,1024]{2,1,0:T(8,128)(2,1)S(1)} %copy-done.17, bf16[512,1024]{1,0:T(8,128)(2,1)S(1)} %copy-done.24, bf16[1,512,1024]{2,1,0:T(8,128)(2,1)S(1)} %copy-done.15, pred[]{:T(512)S(6)} %eq.17, f32[512,1024]{1,0:T(8,128)S(1)} %get-tuple-element.27), kind=kOutput, calls=%fused_computation.9 | convolution fusion | flops 1076363264 | bytes 7340033 | tf_op jit(solution)/shard_map/dot_general | solution.py:121
  111.3 3.0 %fusion.10 = bf16[1024,1024]{0,1:T(8,128)(2,1)S(1)} fusion(bf16[1,512,1024]{2,1,0:T(8,128)(2,1)S(1)} %copy-done.15, bf16[512,1024]{1,0:T(8,128)(2,1)} %get-tuple-element.12, pred[]{:T(512)S(6)} %eq.17, f32[512,1024]{1,0:T(8,128)} %get-tuple-element.28), kind=kOutput, calls=%fused_computation.30 | convolution fusion | flops 1074790400 | bytes 6291457 | tf_op jit(solution)/shard_map/dot_general | solution.py:121
  115.7 2.5 %fusion = bf16[1024,1024]{1,0:T(8,128)(2,1)S(1)} fusion(bf16[1024,1024]{1,0:T(8,128)(2,1)} %collective-permute-done.6, bf16[1024,1024]{0,1:T(8,128)(2,1)S(1)} %fusion.10), kind=kLoop, calls=%fused_computation.1 | loop fusion | flops 4194304 | bytes 6291456 | tf_op jit(solution)/shard_map/convert_element_type | solution.py:117
  120.1 2.5 %add_convert_fusion = bf16[1024,1024]{1,0:T(8,128)(2,1)S(1)} fusion(bf16[1024,1024]{1,0:T(8,128)(2,1)} %collective-permute-done.11, bf16[1024,1024]{1,0:T(8,128)(2,1)S(1)} %fusion.8), kind=kLoop, calls=%fused_computation.2 | loop fusion | flops 4194304 | bytes 6291456 | tf_op jit(solution)/shard_map/convert_element_type | solution.py:117
  124.9 3.4 %fusion.3 = bf16[1,512,1024]{2,1,0:T(8,128)(2,1)} fusion(bf16[512,1024]{1,0:T(8,128)(2,1)} %get-tuple-element.11, bf16[1024,1024]{1,0:T(8,128)(2,1)S(1)} %copy-done), kind=kOutput, calls=%fused_computation.15 | convolution fusion | flops 1074266112 | bytes 4194304 | tf_op jit(solution)/shard_map/dot_general | solution.py:208
  128.4 15.4 %collective-permute-done.7 = bf16[2,2,2,64,1024]{4,3,0,2,1:T(8,128)(2,1)} collective-permute-done((bf16[2,2,2,64,1024]{4,3,0,2,1:T(8,128)(2,1)}, bf16[2,2,2,64,1024]{4,3,0,2,1:T(8,128)(2,1)}, u32[]{:S(2)}, u32[]{:S(2)}) %collective-permute-start.7) | collective-permute-done | bytes 1048608 | tf_op jit(solution)/shard_map/ppermute | solution.py:113
  145.6 3.1 %collective-permute-done.12 = bf16[2,2,2,64,1024]{4,3,2,0,1:T(8,128)(2,1)} collective-permute-done((bf16[2,2,2,64,1024]{4,3,2,0,1:T(8,128)(2,1)}, bf16[2,2,2,64,1024]{4,3,2,0,1:T(8,128)(2,1)}, u32[]{:S(2)}, u32[]{:S(2)}) %collective-permute-start.12) | collective-permute-done | bytes 1048608 | tf_op jit(solution)/shard_map/ppermute | solution.py:113
  153.2 6.8 %collective-permute-done.8 = bf16[2,2,64,1024]{3,2,0,1:T(8,128)(2,1)S(1)} collective-permute-done((bf16[2,2,64,1024]{3,2,0,1:T(8,128)(2,1)S(1)}, bf16[2,2,64,1024]{3,2,0,1:T(8,128)(2,1)S(1)}, u32[]{:S(2)}, u32[]{:S(2)}) %collective-permute-start.8) | collective-permute-done | bytes 524320 | tf_op jit(solution)/shard_map/ppermute | solution.py:113
  163.2 2.8 %collective-permute-done.9 = bf16[2,64,1024]{2,1,0:T(8,128)(2,1)S(1)} collective-permute-done((bf16[2,64,1024]{2,1,0:T(8,128)(2,1)S(1)}, bf16[2,64,1024]{2,1,0:T(8,128)(2,1)S(1)}, u32[]{:S(2)}, u32[]{:S(2)}) %collective-permute-start.9) | collective-permute-done | bytes 262176 | tf_op jit(solution)/shard_map/ppermute | solution.py:113
  168.0 9.7 %collective-permute-done.14 = bf16[2,64,1024]{2,1,0:T(8,128)(2,1)S(1)} collective-permute-done((bf16[2,64,1024]{2,1,0:T(8,128)(2,1)S(1)}, bf16[2,64,1024]{2,1,0:T(8,128)(2,1)S(1)}, u32[]{:S(2)}, u32[]{:S(2)}) %collective-permute-start.14) | collective-permute-done | bytes 262176 | tf_op jit(solution)/shard_map/ppermute | solution.py:113
  177.8 2.6 %collective-permute-done.10 = bf16[64,1024]{1,0:T(8,128)(2,1)S(1)} collective-permute-done((bf16[64,1024]{1,0:T(8,128)(2,1)S(1)}, bf16[64,1024]{1,0:T(8,128)(2,1)S(1)}, u32[]{:S(2)}, u32[]{:S(2)}) %collective-permute-start.10) | collective-permute-done | bytes 131104 | tf_op jit(solution)/shard_map/ppermute | solution.py:113
  183.4 4.8 %collective-permute-done.16 = bf16[64,2048]{1,0:T(8,128)(2,1)S(1)} collective-permute-done((bf16[64,2048]{1,0:T(8,128)(2,1)S(1)}, bf16[64,2048]{1,0:T(8,128)(2,1)S(1)}, u32[]{:S(2)}, u32[]{:S(2)}) %collective-permute-start.16) | collective-permute-done | bytes 262176 | tf_op jit(solution)/shard_map/ppermute | solution.py:113
  188.4 5.5 %collective-permute-start.17 = (bf16[128,2048]{1,0:T(8,128)(2,1)S(1)}, bf16[128,2048]{1,0:T(8,128)(2,1)S(1)}, u32[]{:S(2)}, u32[]{:S(2)}) collective-permute-start(bf16[128,2048]{1,0:T(8,128)(2,1)S(1)} %maximum_select_fusion), channel_id=1, source_target_pairs={{0,8},{8,0},{16,24},{24,16},{1,9},{9,1},{17,25},{25,17},{2,10},{10... | collective-permute-start | bytes 1572872 | tf_op jit(solution)/shard_map/ppermute | solution.py:113
  (112 shorter events, 44.1 us)
Async XLA Ops:
  0.6 18.5 %copy-start = (bf16[1024,1024]{1,0:T(8,128)(2,1)S(1)}, bf16[1024,1024]{1,0:T(8,128)(2,1)}, u32[]{:S(2)}) copy-start(bf16[1024,1024]{1,0:T(8,128)(2,1)} %param.11) | copy-start | bytes 6291460
  11.0 26.1 %collective-permute-start.2 = (bf16[2,128,1024]{2,1,0:T(8,128)(2,1)S(1)}, bf16[2,128,1024]{2,1,0:T(8,128)(2,1)S(1)}, u32[]{:S(2)}, u32[]{:S(2)}) collective-permute-start(bf16[2,128,1024]{2,1,0:T(8,128)(2,1)S(1)} %pad_maximum_fusion.2), channel_id=1, source_target_pairs={{0,4},{1,5},{2,6},{3,7},{4,0},{5,1},{6,2},{7,3},{8,12},{9,13},{10,... | collective-permute-start | bytes 1572872 | tf_op jit(solution)/shard_map/ppermute | solution.py:16
  14.2 22.9 %collective-permute-start.1 = (bf16[2,128,1024]{2,1,0:T(8,128)(2,1)S(1)}, bf16[2,128,1024]{2,1,0:T(8,128)(2,1)S(1)}, u32[]{:S(2)}, u32[]{:S(2)}) collective-permute-start(bf16[2,128,1024]{2,1,0:T(8,128)(2,1)S(1)} %pad_maximum_fusion.1), channel_id=1, source_target_pairs={{0,2},{1,3},{2,0},{3,1},{4,6},{5,7},{6,4},{7,5},{8,10},{9,11},{10,... | collective-permute-start | bytes 1572872 | tf_op jit(solution)/shard_map/ppermute | solution.py:16
  15.6 21.5 %collective-permute-start = (bf16[2,128,1024]{2,1,0:T(8,128)(2,1)S(1)}, bf16[2,128,1024]{2,1,0:T(8,128)(2,1)S(1)}, u32[]{:S(2)}, u32[]{:S(2)}) collective-permute-start(bf16[2,128,1024]{2,1,0:T(8,128)(2,1)S(1)} %pad_maximum_fusion), channel_id=1, source_target_pairs={{0,1},{1,0},{2,3},{3,2},{4,5},{5,4},{6,7},{7,6},{8,9},{9,8},{10,11... | collective-permute-start | bytes 1572872 | tf_op jit(solution)/shard_map/ppermute | solution.py:16
  70.6 12.2 %collective-permute-start.3 = (bf16[2,128,1024]{2,1,0:T(8,128)(2,1)}, bf16[2,128,1024]{2,1,0:T(8,128)(2,1)S(1)}, u32[]{:S(2)}, u32[]{:S(2)}) collective-permute-start(bf16[2,128,1024]{2,1,0:T(8,128)(2,1)} %get-tuple-element.22), channel_id=1, source_target_pairs={{0,1},{1,0},{2,3},{3,2},{4,5},{5,4},{6,7},{7,6},{8,9},{9,8},{10,11... | collective-permute-start | bytes 1572872 | tf_op jit(solution)/shard_map/ppermute | solution.py:16
  71.6 22.6 %collective-permute-start.4 = (bf16[2,128,1024]{2,1,0:T(8,128)(2,1)}, bf16[2,128,1024]{2,1,0:T(8,128)(2,1)S(1)}, u32[]{:S(2)}, u32[]{:S(2)}) collective-permute-start(bf16[2,128,1024]{2,1,0:T(8,128)(2,1)} %get-tuple-element.21), channel_id=1, source_target_pairs={{0,2},{1,3},{2,0},{3,1},{4,6},{5,7},{6,4},{7,5},{8,10},{9,11},{10,... | collective-permute-start | bytes 1572872 | tf_op jit(solution)/shard_map/ppermute | solution.py:16
  73.0 21.4 %copy-start.2 = (f32[512,1024]{1,0:T(8,128)S(1)}, f32[512,1024]{1,0:T(8,128)}, u32[]{:S(2)}) copy-start(f32[512,1024]{1,0:T(8,128)} %get-tuple-element.13) | copy-start | bytes 6291460
  73.0 25.4 %collective-permute-start.5 = (bf16[2,128,1024]{2,1,0:T(8,128)(2,1)}, bf16[2,128,1024]{2,1,0:T(8,128)(2,1)S(1)}, u32[]{:S(2)}, u32[]{:S(2)}) collective-permute-start(bf16[2,128,1024]{2,1,0:T(8,128)(2,1)} %get-tuple-element.20), channel_id=1, source_target_pairs={{0,4},{1,5},{2,6},{3,7},{4,0},{5,1},{6,2},{7,3},{8,12},{9,13},{10,... | collective-permute-start | bytes 1572872 | tf_op jit(solution)/shard_map/ppermute | solution.py:16
  105.7 10.1 %collective-permute-start.6 = (bf16[1024,1024]{1,0:T(8,128)(2,1)}, bf16[1024,1024]{1,0:T(8,128)(2,1)}, u32[]{:S(2)}, u32[]{:S(2)}) collective-permute-start(bf16[1024,1024]{1,0:T(8,128)(2,1)} %convert_bitcast_fusion), channel_id=1, source_target_pairs={{0,8},{8,0},{16,24},{24,16},{1,9},{9,1},{17,25},{25,17},{2,10},{10... | collective-permute-start | bytes 6291464 | tf_op jit(solution)/shard_map/ppermute | solution.py:113
  111.3 8.8 %collective-permute-start.11 = (bf16[1024,1024]{1,0:T(8,128)(2,1)}, bf16[1024,1024]{1,0:T(8,128)(2,1)}, u32[]{:S(2)}, u32[]{:S(2)}) collective-permute-start(bf16[1024,1024]{1,0:T(8,128)(2,1)} %convolution_convert_fusion), channel_id=1, source_target_pairs={{0,8},{8,0},{16,24},{24,16},{1,9},{9,1},{17,25},{25,17},{2,10},{10... | collective-permute-start | bytes 6291464 | tf_op jit(solution)/shard_map/ppermute | solution.py:113
  119.6 24.2 %collective-permute-start.7 = (bf16[2,2,2,64,1024]{4,3,0,2,1:T(8,128)(2,1)}, bf16[2,2,2,64,1024]{4,3,0,2,1:T(8,128)(2,1)}, u32[]{:S(2)}, u32[]{:S(2)}) collective-permute-start(bf16[2,2,2,64,1024]{4,3,0,2,1:T(8,128)(2,1)} %bitcast.146), channel_id=1, source_target_pairs={{0,1},{1,0},{2,3},{3,2},{4,5},{5,4},{6,7},{7,6},{8,9},{9,8},{10,11... | collective-permute-start | bytes 3145736 | tf_op jit(solution)/shard_map/ppermute | solution.py:113
  124.9 23.9 %collective-permute-start.12 = (bf16[2,2,2,64,1024]{4,3,2,0,1:T(8,128)(2,1)}, bf16[2,2,2,64,1024]{4,3,2,0,1:T(8,128)(2,1)}, u32[]{:S(2)}, u32[]{:S(2)}) collective-permute-start(bf16[2,2,2,64,1024]{4,3,2,0,1:T(8,128)(2,1)} %bitcast.145), channel_id=1, source_target_pairs={{0,2},{1,3},{2,0},{3,1},{4,6},{5,7},{6,4},{7,5},{8,10},{9,11},{10,... | collective-permute-start | bytes 3145736 | tf_op jit(solution)/shard_map/ppermute | solution.py:113
  145.6 14.4 %collective-permute-start.8 = (bf16[2,2,64,1024]{3,2,0,1:T(8,128)(2,1)S(1)}, bf16[2,2,64,1024]{3,2,0,1:T(8,128)(2,1)S(1)}, u32[]{:S(2)}, u32[]{:S(2)}) collective-permute-start(bf16[2,2,64,1024]{3,2,0,1:T(8,128)(2,1)S(1)} %dynamic-slice_bitcast_fusion.1), channel_id=1, source_target_pairs={{0,2},{1,3},{2,0},{3,1},{4,6},{5,7},{6,4},{7,5},{8,10},{9,11},{10,... | collective-permute-start | bytes 1572872 | tf_op jit(solution)/shard_map/ppermute | solution.py:113
  150.6 10.6 %collective-permute-start.13 = (bf16[2,2,64,1024]{3,2,1,0:T(8,128)(2,1)S(1)}, bf16[2,2,64,1024]{3,2,1,0:T(8,128)(2,1)S(1)}, u32[]{:S(2)}, u32[]{:S(2)}) collective-permute-start(bf16[2,2,64,1024]{3,2,1,0:T(8,128)(2,1)S(1)} %dynamic-slice_bitcast_fusion), channel_id=1, source_target_pairs={{0,1},{1,0},{2,3},{3,2},{4,5},{5,4},{6,7},{7,6},{8,9},{9,8},{10,11... | collective-permute-start | bytes 1572872 | tf_op jit(solution)/shard_map/ppermute | solution.py:113
  160.2 5.9 %collective-permute-start.9 = (bf16[2,64,1024]{2,1,0:T(8,128)(2,1)S(1)}, bf16[2,64,1024]{2,1,0:T(8,128)(2,1)S(1)}, u32[]{:S(2)}, u32[]{:S(2)}) collective-permute-start(bf16[2,64,1024]{2,1,0:T(8,128)(2,1)S(1)} %dynamic-slice_bitcast_fusion.3), channel_id=1, source_target_pairs={{0,16},{8,24},{16,0},{24,8},{1,17},{9,25},{17,1},{25,9},{2,18},{10... | collective-permute-start | bytes 786440 | tf_op jit(solution)/shard_map/ppermute | solution.py:113
  161.2 20.9 %copy-start.10 = (bf16[1024,1024]{1,0:T(8,128)(2,1)S(1)}, bf16[1024,1024]{1,0:T(8,128)(2,1)}, u32[]{:S(2)}) copy-start(bf16[1024,1024]{1,0:T(8,128)(2,1)} %param.9) | copy-start | bytes 6291460
  161.4 20.7 %copy-start.5 = (f32[512,1024]{1,0:T(8,128)S(1)}, f32[512,1024]{1,0:T(8,128)}, u32[]{:S(2)}) copy-start(f32[512,1024]{1,0:T(8,128)} %copy-done.3) | copy-start | bytes 6291460
  161.5 16.2 %collective-permute-start.14 = (bf16[2,64,1024]{2,1,0:T(8,128)(2,1)S(1)}, bf16[2,64,1024]{2,1,0:T(8,128)(2,1)S(1)}, u32[]{:S(2)}, u32[]{:S(2)}) collective-permute-start(bf16[2,64,1024]{2,1,0:T(8,128)(2,1)S(1)} %dynamic-slice_bitcast_fusion.2), channel_id=1, source_target_pairs={{0,4},{1,5},{2,6},{3,7},{4,0},{5,1},{6,2},{7,3},{8,12},{9,13},{10,... | collective-permute-start | bytes 786440 | tf_op jit(solution)/shard_map/ppermute | solution.py:113
  166.1 14.4 %collective-permute-start.10 = (bf16[64,1024]{1,0:T(8,128)(2,1)S(1)}, bf16[64,1024]{1,0:T(8,128)(2,1)S(1)}, u32[]{:S(2)}, u32[]{:S(2)}) collective-permute-start(bf16[64,1024]{1,0:T(8,128)(2,1)S(1)} %dynamic-slice_bitcast_fusion.11), channel_id=1, source_target_pairs={{0,4},{1,5},{2,6},{3,7},{4,0},{5,1},{6,2},{7,3},{8,12},{9,13},{10,... | collective-permute-start | bytes 393224 | tf_op jit(solution)/shard_map/ppermute | solution.py:113
  177.8 4.2 %collective-permute-start.15 = (bf16[64,1024]{1,0:T(8,128)(2,1)S(1)}, bf16[64,1024]{1,0:T(8,128)(2,1)S(1)}, u32[]{:S(2)}, u32[]{:S(2)}) collective-permute-start(bf16[64,1024]{1,0:T(8,128)(2,1)S(1)} %dynamic-slice_bitcast_fusion.10), channel_id=1, source_target_pairs={{0,16},{8,24},{16,0},{24,8},{1,17},{9,25},{17,1},{25,9},{2,18},{10... | collective-permute-start | bytes 393224 | tf_op jit(solution)/shard_map/ppermute | solution.py:113
  182.0 11.8 %copy-start.12 = (bf16[1024,1024]{1,0:T(8,128)(2,1)S(1)}, bf16[1024,1024]{1,0:T(8,128)(2,1)}, u32[]{:S(2)}) copy-start(bf16[1024,1024]{1,0:T(8,128)(2,1)} %param.8) | copy-start | bytes 6291460
  182.0 11.8 %copy-start.23 = (bf16[512,1024]{1,0:T(8,128)(2,1)S(1)}, bf16[512,1024]{1,0:T(8,128)(2,1)}, u32[]{:S(2)}) copy-start(bf16[512,1024]{1,0:T(8,128)(2,1)} %get-tuple-element.12) | copy-start | bytes 3145732
  182.0 6.2 %collective-permute-start.16 = (bf16[64,2048]{1,0:T(8,128)(2,1)S(1)}, bf16[64,2048]{1,0:T(8,128)(2,1)S(1)}, u32[]{:S(2)}, u32[]{:S(2)}) collective-permute-start(bf16[64,2048]{1,0:T(8,128)(2,1)S(1)} %pad_maximum_fusion.3), channel_id=1, source_target_pairs={{0,16},{8,24},{16,0},{24,8},{1,17},{9,25},{17,1},{25,9},{2,18},{10... | collective-permute-start | bytes 786440 | tf_op jit(solution)/shard_map/ppermute | solution.py:113
  188.4 7.8 %collective-permute-start.17 = (bf16[128,2048]{1,0:T(8,128)(2,1)S(1)}, bf16[128,2048]{1,0:T(8,128)(2,1)S(1)}, u32[]{:S(2)}, u32[]{:S(2)}) collective-permute-start(bf16[128,2048]{1,0:T(8,128)(2,1)S(1)} %maximum_select_fusion), channel_id=1, source_target_pairs={{0,8},{8,0},{16,24},{24,16},{1,9},{9,1},{17,25},{25,17},{2,10},{10... | collective-permute-start | bytes 1572872 | tf_op jit(solution)/shard_map/ppermute | solution.py:113
  (20 other events, 75.4 us)

commit v10 on v9

--- a/solution.py
+++ b/solution.py
@@ -16,14 +16,14 @@
     return lax.ppermute(array, axis, [(i, i ^ 1 << apart) for i in range(lax.axis_size(axis))])
 
 
-def swap_blocks(keys_local, values_local, offsets, levels):
+def swap_blocks(keys_local, values_local, offsets, levels, lo, hi):
     remote = []
     for level in range(levels):
         start = offsets[level] * BLOCK
         pair = jnp.stack(
             [
-                lax.dynamic_slice_in_dim(keys_local, start, BLOCK, 0),
-                lax.dynamic_slice_in_dim(values_local, start, BLOCK, 0),
+                lax.dynamic_slice_in_dim(keys_local[:, lo:hi], start, BLOCK, 0),
+                lax.dynamic_slice_in_dim(values_local[:, lo:hi], start, BLOCK, 0),
             ]
         )
         remote.append(partner(pair, "seq", level))
@@ -79,19 +79,22 @@
         low = high
 
 
-def attention(query, keys, values, d_att, remote, head):
-    tok, width = query.shape
+def attention(query, keys, values, d_att, remote, head, lo, hi):
+    tok = query.shape[0]
+    width = hi - lo
     levels = len(remote)
     block = remote[0].shape[1]
     total = tok + levels * block
     steps = width // LANES
+    base = lo // LANES
+    fspec = pl.BlockSpec((tok, LANES), lambda i: (0, i + base))
     qspec = pl.BlockSpec((tok, LANES), lambda i: (0, i))
     rspec = pl.BlockSpec((2, block, LANES), lambda i: (0, 0, i))
     bspec = pl.BlockSpec((levels, 2, block, LANES), lambda i: (0, 0, 0, i))
     return pl.pallas_call(
         functools.partial(attention_kernel, head=head, scale=head ** -0.5),
         grid=(steps,),
-        in_specs=[qspec] * 4 + [rspec] * levels,
+        in_specs=[fspec] * 4 + [rspec] * levels,
         out_specs=[qspec] * 4 + [bspec],
         out_shape=[
             jax.ShapeDtypeStruct((tok, width), jnp.bfloat16),
@@ -202,24 +205,36 @@
     query = jnp.dot(rows, w_query, preferred_element_type=jnp.float32).astype(jnp.bfloat16)
     keys_local = jnp.dot(rows, w_key, preferred_element_type=jnp.float32).astype(jnp.bfloat16)
     values_local = jnp.dot(rows, w_value, preferred_element_type=jnp.float32).astype(jnp.bfloat16)
-    remote = swap_blocks(keys_local, values_local, offsets, levels)
+    half = (width // LANES) // 2 * LANES
+    spans = [(0, half), (half, width)]
+    remotes = [swap_blocks(keys_local, values_local, offsets, levels, lo, hi) for lo, hi in spans]
     d_att = jnp.dot(cot, w_out.T, preferred_element_type=jnp.float32).astype(jnp.bfloat16)
-    attended, dquery, dkey_sum, dvalue_sum, back = attention(query, keys_local, values_local, d_att, remote, head)
+    outs = [
+        attention(query, keys_local, values_local, d_att, remote, head, lo, hi)
+        for remote, (lo, hi) in zip(remotes, spans)
+    ]
+    attended = jnp.concatenate([o[0] for o in outs], axis=1)
+    dquery = jnp.concatenate([o[1] for o in outs], axis=1)
     result = jnp.dot(attended, w_out, preferred_element_type=jnp.float32).astype(jnp.bfloat16)
-    for level in range(levels):
-        returned = partner(back[level], "seq", level).astype(jnp.float32)
-        start = offsets[level] * BLOCK
-        dkey_sum = lax.dynamic_update_slice_in_dim(
-            dkey_sum, lax.dynamic_slice_in_dim(dkey_sum, start, BLOCK, 0) + returned[0], start, 0
-        )
-        dvalue_sum = lax.dynamic_update_slice_in_dim(
-            dvalue_sum,
-            lax.dynamic_slice_in_dim(dvalue_sum, start, BLOCK, 0) + returned[1],
-            start,
-            0,
-        )
-    dkey = dkey_sum.astype(jnp.bfloat16)
-    dvalue = dvalue_sum.astype(jnp.bfloat16)
+    dkeys = []
+    dvalues = []
+    for _, _, dkey_sum, dvalue_sum, back in outs:
+        for level in range(levels):
+            returned = partner(back[level], "seq", level).astype(jnp.float32)
+            start = offsets[level] * BLOCK
+            dkey_sum = lax.dynamic_update_slice_in_dim(
+                dkey_sum, lax.dynamic_slice_in_dim(dkey_sum, start, BLOCK, 0) + returned[0], start, 0
+            )
+            dvalue_sum = lax.dynamic_update_slice_in_dim(
+                dvalue_sum,
+                lax.dynamic_slice_in_dim(dvalue_sum, start, BLOCK, 0) + returned[1],
+                start,
+                0,
+            )
+        dkeys.append(dkey_sum.astype(jnp.bfloat16))
+        dvalues.append(dvalue_sum.astype(jnp.bfloat16))
+    dkey = jnp.concatenate(dkeys, axis=1)
+    dvalue = jnp.concatenate(dvalues, axis=1)
     total = jnp.dot(dquery, w_query.T, preferred_element_type=jnp.float32)
     total = total + jnp.dot(dkey, w_key.T, preferred_element_type=jnp.float32)
     total = total + jnp.dot(dvalue, w_value.T, preferred_element_type=jnp.float32)

time: 198 us -> 185 us (0.934)
  waiting for transfers between devices: 80.3 us -> 52.4 us
  starting transfers between devices: 26.1 us -> 36.8 us
  other arithmetic: 17.3 us -> 10.7 us
  local copies, waits for them, and re-layouts: 10.8 us -> 17.3 us
    ppermute x6 -> x12, waiting for transfers between devices: 33.6 us -> 5.68 us  [partner(): lax.ppermute(array, axis, [(i, i ^ 1 << apart) for i in range(lax.axis_si...]
    ppermute x6 -> x12, starting transfers between devices: 11.3 us -> 17.3 us  [partner(): lax.ppermute(array, axis, [(i, i ^ 1 << apart) for i in range(lax.axis_si...]
    dynamic_update_slice x3 -> x6, other arithmetic: 6.14 us -> 0.76 us  [body(): lax.dynamic_update_slice_in_dim(dkey_sum, lax.dynamic_slice_in_dim(dkey_s...]
    convert_element_type x10 -> x8, other arithmetic: 9.18 us -> 4.1 us  [add_bf16(): return (a.astype(jnp.float32) + b.astype(jnp.float32)).astype(jnp.bfloat16)]
    ppermute x12, starting transfers between devices: 14.8 us -> 19.5 us  [exchange(): lax.ppermute(array, axis, [(i, i ^ mask) for i in range(lax.axis_size(axi...]
    unnamed x52 -> x75, local copies, waits for them, and re-layouts: 1.85 us -> 5.17 us
    convert_element_type x3 -> x6, other arithmetic: 0.31 us -> 2.39 us  [body(): returned = partner(back[level], 'seq', level).astype(jnp.float32)]
    pallas_call x1 -> x2, Pallas kernels: 29.3 us -> 31.2 us  [attention(): pl.pallas_call(functools.partial(attention_kernel, head=head, scale=head...]
  transfers between devices with their start and end apart: 18 -> 24, of which waited for: 11 -> 12; matrix products, arithmetic and copies ran while one was open for 19% -> 23% of each run, Pallas kernels for 0% -> 17%
where the time goes in v10:
time: 185 us; the launch traced here: 184 us
  waiting for transfers between devices  52.4 us (28%)
  starting transfers between devices  36.8 us (20%)
  matrix products  32.4 us (18%)
  Pallas kernels  31.2 us (17%)
  local copies, waits for them, and re-layouts  17.3 us (9%)
  other arithmetic  10.7 us (6%)
  between operations  3.31 us (2%)
    ppermute x12, waiting for transfers between devices, exchange(): lax.ppermute(array, axis, [(i, i ^ mask) for i in range(lax.axis_size(axi...  46.7 us
    pallas_call x2, Pallas kernels, attention(): pl.pallas_call(functools.partial(attention_kernel, head=head, scale=head...  31.2 us
    ppermute x12, starting transfers between devices, exchange(): lax.ppermute(array, axis, [(i, i ^ mask) for i in range(lax.axis_size(axi...  19.5 us
    ppermute x12, starting transfers between devices, partner(): lax.ppermute(array, axis, [(i, i ^ 1 << apart) for i in range(lax.axis_si...  17.3 us
    dot_general x4, matrix products, term(): jnp.dot(left.T, right[:, lo:hi], preferred_element_type=jnp.float32)  11.9 us
    ppermute x12, waiting for transfers between devices, partner(): lax.ppermute(array, axis, [(i, i ^ 1 << apart) for i in range(lax.axis_si...  5.68 us
    unnamed x75, local copies, waits for them, and re-layouts  5.17 us
    dot_general x1, matrix products, body(): jnp.dot(rows, w_query, preferred_element_type=jnp.float32)  4.14 us
  transfers between devices with their start and end apart: 24, of which 12 were waited for; matrix products, arithmetic and copies ran while one was open for 23% of the time, Pallas kernels for 17%

profile of v10, /device:TPU:1, one launch (start us, length us, event | category | flops | bytes accessed | tf_op | source)
XLA Modules:
  0.0 184.1 jit_solution(11647433056470820827)
XLA Ops:
  4.0 3.2 %convolution_convert_fusion.3.v_ref = bf16[512,1024]{1,0:T(8,128)(2,1)S(1)} fusion(bf16[1024,1024]{1,0:T(8,128)(2,1)} %param.10, bf16[1,512,1024]{2,1,0:T(8,128)(2,1)} %param.7), kind=kOutput, calls=%fused_computation.12 | convolution fusion | flops 1074266112 | bytes 4194304 | tf_op jit(solution)/shard_map/dot_general | solution.py:207
  17.6 2.3 %collective-permute-start.2 = (bf16[2,128,512]{2,1,0:T(8,128)(2,1)}, bf16[2,128,512]{2,1,0:T(8,128)(2,1)}, u32[]{:S(2)}, u32[]{:S(2)}) collective-permute-start(bf16[2,128,512]{2,1,0:T(8,128)(2,1)} %pad_maximum_fusion.12), channel_id=1, source_target_pairs={{0,4},{1,5},{2,6},{3,7},{4,0},{5,1},{6,2},{7,3},{8,12},{9,13},{10,... | collective-permute-start | bytes 786440 | tf_op jit(solution)/shard_map/ppermute | solution.py:16
  20.3 4.1 %convolution_convert_fusion.5.q_ref = bf16[512,1024]{1,0:T(8,128)(2,1)} fusion(bf16[1024,1024]{1,0:T(8,128)(2,1)} %param.8, bf16[1,512,1024]{2,1,0:T(8,128)(2,1)} %param.7), kind=kOutput, calls=%fused_computation.14 | convolution fusion | flops 1074266112 | bytes 4194304 | tf_op jit(solution)/shard_map/dot_general | solution.py:205
  25.2 3.5 %convolution_convert_fusion.2.do_ref = bf16[512,1024]{1,0:T(8,128)(2,1)} fusion(bf16[1024,1024]{1,0:T(8,128)(2,1)S(1)} %copy-done, bf16[1,512,1024]{2,1,0:T(8,128)(2,1)} %param.13), kind=kOutput, calls=%fused_computation.11 | convolution fusion | flops 1074266112 | bytes 4194304 | tf_op jit(solution)/shard_map/dot_general | solution.py:211
  28.9 15.6 %shard_map.118 = (bf16[512,512]{1,0:T(8,128)(2,1)}, bf16[512,512]{1,0:T(8,128)(2,1)}, f32[512,512]{1,0:T(8,128)}, f32[512,512]{1,0:T(8,128)}, bf16[3,2,128,512]{3,2,1,0:T(8,128)(2,1)}) custom-call(bf16[512,1024]{1,0:T(8,128)(2,1)} %convolution_convert_fusion.5.q_ref, bf16[512,1024]{1,0:T(8,128)(2,1)} %copy-done.10, bf16[512,1024]{1,0:T(8,128)(2,1)} %copy-done.9, ...), custom_call_target="tpu_custom_call" | custom-call | flops 5637144576 | bytes 6553600 | tf_op jit(solution)/shard_map/pallas_call | solution.py:94
  47.9 4.7 %collective-permute-start.7 = (bf16[2,128,512]{2,1,0:T(8,128)(2,1)}, bf16[2,128,512]{2,1,0:T(8,128)(2,1)}, u32[]{:S(2)}, u32[]{:S(2)}) collective-permute-start(bf16[2,128,512]{2,1,0:T(8,128)(2,1)} %get-tuple-element.39), channel_id=1, source_target_pairs={{0,2},{1,3},{2,0},{3,1},{4,6},{5,7},{6,4},{7,5},{8,10},{9,11},{10,... | collective-permute-start | bytes 786440 | tf_op jit(solution)/shard_map/ppermute | solution.py:16
  52.6 3.6 %collective-permute-start.8 = (bf16[2,128,512]{2,1,0:T(8,128)(2,1)}, bf16[2,128,512]{2,1,0:T(8,128)(2,1)S(1)}, u32[]{:S(2)}, u32[]{:S(2)}) collective-permute-start(bf16[2,128,512]{2,1,0:T(8,128)(2,1)} %get-tuple-element.38), channel_id=1, source_target_pairs={{0,4},{1,5},{2,6},{3,7},{4,0},{5,1},{6,2},{7,3},{8,12},{9,13},{10,... | collective-permute-start | bytes 786440 | tf_op jit(solution)/shard_map/ppermute | solution.py:16
  56.9 15.6 %shard_map.119 = (bf16[512,512]{1,0:T(8,128)(2,1)}, bf16[512,512]{1,0:T(8,128)(2,1)}, f32[512,512]{1,0:T(8,128)}, f32[512,512]{1,0:T(8,128)}, bf16[3,2,128,512]{3,2,1,0:T(8,128)(2,1)}) custom-call(bf16[512,1024]{1,0:T(8,128)(2,1)} %convolution_convert_fusion.5.q_ref, bf16[512,1024]{1,0:T(8,128)(2,1)} %copy-done.10, bf16[512,1024]{1,0:T(8,128)(2,1)} %copy-done.9, ...), custom_call_target="tpu_custom_call" | custom-call | flops 5637144576 | bytes 6553600 | tf_op jit(solution)/shard_map/pallas_call | solution.py:94
  79.6 2.2 %collective-permute-done.10 = bf16[2,128,512]{2,1,0:T(8,128)(2,1)S(1)} collective-permute-done((bf16[2,128,512]{2,1,0:T(8,128)(2,1)S(1)}, bf16[2,128,512]{2,1,0:T(8,128)(2,1)S(1)}, u32[]{:S(2)}, u32[]{:S(2)}) %collective-permute-start.10) | collective-permute-done | bytes 262176 | tf_op jit(solution)/shard_map/ppermute | solution.py:16
  82.0 2.5 %collective-permute-done.11 = bf16[2,128,512]{2,1,0:T(8,128)(2,1)S(1)} collective-permute-done((bf16[2,128,512]{2,1,0:T(8,128)(2,1)S(1)}, bf16[2,128,512]{2,1,0:T(8,128)(2,1)S(1)}, u32[]{:S(2)}, u32[]{:S(2)}) %collective-permute-start.11) | collective-permute-done | bytes 262176 | tf_op jit(solution)/shard_map/ppermute | solution.py:16
  84.8 2.7 %convert_bitcast_fusion = bf16[1024,1024]{1,0:T(8,128)(2,1)} fusion(bf16[1,512,1024]{2,1,0:T(8,128)(2,1)S(1)} %copy-done.28, bf16[512,1024]{1,0:T(8,128)(2,1)S(1)} %constant_dynamic-update-slice_fusion, pred[]{:T(512)S(6)} %eq.17, bf16[512,512]{1,0:T(8,128)(2,1)S(1)} %convert_element_type.207, bf16[512,512]{1,0:T(8,128)(2,1)S(1)} %convert_element_type.206), kind=kOutput, calls=%fused_computation.7 | convolution fusion | flops 1077411840 | bytes 5242881 | tf_op jit(solution)/shard_map/dot_general | solution.py:124
  87.5 7.1 %collective-permute-start.12 = (bf16[1024,1024]{1,0:T(8,128)(2,1)}, bf16[1024,1024]{1,0:T(8,128)(2,1)}, u32[]{:S(2)}, u32[]{:S(2)}) collective-permute-start(bf16[1024,1024]{1,0:T(8,128)(2,1)} %convert_bitcast_fusion), channel_id=1, source_target_pairs={{0,8},{8,0},{16,24},{24,16},{1,9},{9,1},{17,25},{25,17},{2,10},{10... | collective-permute-start | bytes 6291464 | tf_op jit(solution)/shard_map/ppermute | solution.py:116
  94.7 2.7 %convolution_convert_fusion = bf16[1024,1024]{1,0:T(8,128)(2,1)} fusion(bf16[1,512,1024]{2,1,0:T(8,128)(2,1)S(1)} %copy-done.30, bf16[1,512,1024]{2,1,0:T(8,128)(2,1)S(1)} %copy-done.28, pred[]{:T(512)S(6)} %eq.17, bf16[1,512,512]{2,1,0:T(8,128)(2,1)S(1)} %convert_bitcast_fusion.2, bf16[1,512,512]{2,1,0:T(8,128)(2,1)S(1)} %convert_bitcast_fusion.1, ...), kind=kOutput, calls=%fused_computation.9 | convolution fusion | flops 1080033280 | bytes 6291457 | tf_op jit(solution)/shard_map/dot_general | solution.py:124
  99.1 3.5 %fusion = bf16[1024,1024]{1,0:T(8,128)(2,1)S(1)} fusion(bf16[1024,1024]{1,0:T(8,128)(2,1)} %collective-permute-done.12, bf16[1,512,1024]{2,1,0:T(8,128)(2,1)} %param.7, bf16[512,1024]{1,0:T(8,128)(2,1)} %copy-done.21, pred[]{:T(512)S(6)} %eq.17, bf16[512,512]{1,0:T(8,128)(2,1)} %copy-done.13, bf16[512,512]{1,0:T(8,128)(2,1)} %copy-done.11), kind=kOutput, calls=%fused_computation.1 | convolution fusion | flops 1081606144 | bytes 7340033 | tf_op jit(solution)/shard_map/dot_general | solution.py:124
  105.9 2.9 %add_convert_fusion = bf16[1024,1024]{1,0:T(8,128)(2,1)S(1)} fusion(bf16[1024,1024]{1,0:T(8,128)(2,1)} %collective-permute-done.17, bf16[1,512,1024]{2,1,0:T(8,128)(2,1)S(1)} %copy-done.31, bf16[1,512,1024]{2,1,0:T(8,128)(2,1)S(1)} %copy-done.29, pred[]{:T(512)S(6)} %eq.17, bf16[1,512,512]{2,1,0:T(8,128)(2,1)S(1)} %copy-done.18, ...), kind=kOutput, calls=%fused_computation.2 | convolution fusion | flops 1084227584 | bytes 8388609 | tf_op jit(solution)/shard_map/dot_general | solution.py:124
  111.2 3.5 %fusion.3 = bf16[1,512,1024]{2,1,0:T(8,128)(2,1)} fusion(bf16[1024,1024]{1,0:T(8,128)(2,1)S(1)} %copy-done, bf16[512,512]{1,0:T(8,128)(2,1)} %get-tuple-element.17, bf16[512,512]{1,0:T(8,128)(2,1)} %get-tuple-element.16), kind=kOutput, calls=%fused_computation.15 | convolution fusion | flops 1076363264 | bytes 4194304 | tf_op jit(solution)/shard_map/dot_general | solution.py:218
  114.7 15.0 %collective-permute-done.13 = bf16[2,2,2,64,1024]{4,3,0,2,1:T(8,128)(2,1)} collective-permute-done((bf16[2,2,2,64,1024]{4,3,0,2,1:T(8,128)(2,1)}, bf16[2,2,2,64,1024]{4,3,0,2,1:T(8,128)(2,1)}, u32[]{:S(2)}, u32[]{:S(2)}) %collective-permute-start.13) | collective-permute-done | bytes 1048608 | tf_op jit(solution)/shard_map/ppermute | solution.py:116
  131.5 4.3 %collective-permute-done.18 = bf16[2,2,2,64,1024]{4,3,2,0,1:T(8,128)(2,1)} collective-permute-done((bf16[2,2,2,64,1024]{4,3,2,0,1:T(8,128)(2,1)}, bf16[2,2,2,64,1024]{4,3,2,0,1:T(8,128)(2,1)}, u32[]{:S(2)}, u32[]{:S(2)}) %collective-permute-start.18) | collective-permute-done | bytes 1048608 | tf_op jit(solution)/shard_map/ppermute | solution.py:116
  140.7 6.3 %collective-permute-done.14 = bf16[2,2,64,1024]{3,2,0,1:T(8,128)(2,1)S(1)} collective-permute-done((bf16[2,2,64,1024]{3,2,0,1:T(8,128)(2,1)S(1)}, bf16[2,2,64,1024]{3,2,0,1:T(8,128)(2,1)S(1)}, u32[]{:S(2)}, u32[]{:S(2)}) %collective-permute-start.14) | collective-permute-done | bytes 524320 | tf_op jit(solution)/shard_map/ppermute | solution.py:116
  150.4 3.5 %collective-permute-done.15 = bf16[2,64,1024]{2,1,0:T(8,128)(2,1)S(1)} collective-permute-done((bf16[2,64,1024]{2,1,0:T(8,128)(2,1)S(1)}, bf16[2,64,1024]{2,1,0:T(8,128)(2,1)S(1)}, u32[]{:S(2)}, u32[]{:S(2)}) %collective-permute-start.15) | collective-permute-done | bytes 262176 | tf_op jit(solution)/shard_map/ppermute | solution.py:116
  154.7 11.7 %collective-permute-done.20 = bf16[2,64,1024]{2,1,0:T(8,128)(2,1)S(1)} collective-permute-done((bf16[2,64,1024]{2,1,0:T(8,128)(2,1)S(1)}, bf16[2,64,1024]{2,1,0:T(8,128)(2,1)S(1)}, u32[]{:S(2)}, u32[]{:S(2)}) %collective-permute-start.20) | collective-permute-done | bytes 262176 | tf_op jit(solution)/shard_map/ppermute | solution.py:116
  173.2 2.7 %collective-permute-done.22 = bf16[64,2048]{1,0:T(8,128)(2,1)S(1)} collective-permute-done((bf16[64,2048]{1,0:T(8,128)(2,1)S(1)}, bf16[64,2048]{1,0:T(8,128)(2,1)S(1)}, u32[]{:S(2)}, u32[]{:S(2)}) %collective-permute-start.22) | collective-permute-done | bytes 262176 | tf_op jit(solution)/shard_map/ppermute | solution.py:116
  176.0 4.4 %collective-permute-start.23 = (bf16[128,2048]{1,0:T(8,128)(2,1)S(1)}, bf16[128,2048]{1,0:T(8,128)(2,1)S(1)}, u32[]{:S(2)}, u32[]{:S(2)}) collective-permute-start(bf16[128,2048]{1,0:T(8,128)(2,1)S(1)} %maximum_select_fusion), channel_id=1, source_target_pairs={{0,8},{8,0},{16,24},{24,16},{1,9},{9,1},{17,25},{25,17},{2,10},{10... | collective-permute-start | bytes 1572872 | tf_op jit(solution)/shard_map/ppermute | solution.py:116
  180.5 2.3 %fusion.4 = bf16[1,512,1024]{2,1,0:T(8,128)(2,1)} fusion(f32[512,1024]{1,0:T(8,128)S(1)} %fusion.36, f32[512,1024]{1,0:T(8,128)S(1)} %fusion.8, bf16[512,1024]{1,0:T(8,128)(2,1)S(1)} %copy-done.22, bf16[1024,1024]{1,0:T(8,128)(2,1)S(1)} %copy-done.26), kind=kOutput, calls=%fused_computation.16 | convolution fusion | flops 1075314688 | bytes 8388608 | tf_op jit(solution)/shard_map/dot_general | solution.py:238
  (166 shorter events, 50.8 us)
Async XLA Ops:
  13.4 15.3 %collective-permute-start = (bf16[2,128,512]{2,1,0:T(8,128)(2,1)S(1)}, bf16[2,128,512]{2,1,0:T(8,128)(2,1)}, u32[]{:S(2)}, u32[]{:S(2)}) collective-permute-start(bf16[2,128,512]{2,1,0:T(8,128)(2,1)S(1)} %pad_maximum_fusion.10), channel_id=1, source_target_pairs={{0,1},{1,0},{2,3},{3,2},{4,5},{5,4},{6,7},{7,6},{8,9},{9,8},{10,11... | collective-permute-start | bytes 786440 | tf_op jit(solution)/shard_map/ppermute | solution.py:16
  15.5 13.4 %collective-permute-start.1 = (bf16[2,128,512]{2,1,0:T(8,128)(2,1)S(1)}, bf16[2,128,512]{2,1,0:T(8,128)(2,1)}, u32[]{:S(2)}, u32[]{:S(2)}) collective-permute-start(bf16[2,128,512]{2,1,0:T(8,128)(2,1)S(1)} %pad_maximum_fusion.11), channel_id=1, source_target_pairs={{0,2},{1,3},{2,0},{3,1},{4,6},{5,7},{6,4},{7,5},{8,10},{9,11},{10,... | collective-permute-start | bytes 786440 | tf_op jit(solution)/shard_map/ppermute | solution.py:16
  17.6 11.3 %collective-permute-start.2 = (bf16[2,128,512]{2,1,0:T(8,128)(2,1)}, bf16[2,128,512]{2,1,0:T(8,128)(2,1)}, u32[]{:S(2)}, u32[]{:S(2)}) collective-permute-start(bf16[2,128,512]{2,1,0:T(8,128)(2,1)} %pad_maximum_fusion.12), channel_id=1, source_target_pairs={{0,4},{1,5},{2,6},{3,7},{4,0},{5,1},{6,2},{7,3},{8,12},{9,13},{10,... | collective-permute-start | bytes 786440 | tf_op jit(solution)/shard_map/ppermute | solution.py:16
  20.0 32.6 %collective-permute-start.5 = (bf16[2,128,512]{2,1,0:T(8,128)(2,1)S(1)}, bf16[2,128,512]{2,1,0:T(8,128)(2,1)}, u32[]{:S(2)}, u32[]{:S(2)}) collective-permute-start(bf16[2,128,512]{2,1,0:T(8,128)(2,1)S(1)} %pad_maximum_fusion.15), channel_id=1, source_target_pairs={{0,4},{1,5},{2,6},{3,7},{4,0},{5,1},{6,2},{7,3},{8,12},{9,13},{10,... | collective-permute-start | bytes 786440 | tf_op jit(solution)/shard_map/ppermute | solution.py:16
  20.1 36.1 %collective-permute-start.4 = (bf16[2,128,512]{2,1,0:T(8,128)(2,1)S(1)}, bf16[2,128,512]{2,1,0:T(8,128)(2,1)}, u32[]{:S(2)}, u32[]{:S(2)}) collective-permute-start(bf16[2,128,512]{2,1,0:T(8,128)(2,1)S(1)} %pad_maximum_fusion.14), channel_id=1, source_target_pairs={{0,2},{1,3},{2,0},{3,1},{4,6},{5,7},{6,4},{7,5},{8,10},{9,11},{10,... | collective-permute-start | bytes 786440 | tf_op jit(solution)/shard_map/ppermute | solution.py:16
  28.7 27.5 %collective-permute-start.3 = (bf16[2,128,512]{2,1,0:T(8,128)(2,1)}, bf16[2,128,512]{2,1,0:T(8,128)(2,1)S(1)}, u32[]{:S(2)}, u32[]{:S(2)}) collective-permute-start(bf16[2,128,512]{2,1,0:T(8,128)(2,1)} %pad_maximum_fusion.13), channel_id=1, source_target_pairs={{0,1},{1,0},{2,3},{3,2},{4,5},{5,4},{6,7},{7,6},{8,9},{9,8},{10,11... | collective-permute-start | bytes 786440 | tf_op jit(solution)/shard_map/ppermute | solution.py:16
  46.6 28.8 %collective-permute-start.6 = (bf16[2,128,512]{2,1,0:T(8,128)(2,1)}, bf16[2,128,512]{2,1,0:T(8,128)(2,1)}, u32[]{:S(2)}, u32[]{:S(2)}) collective-permute-start(bf16[2,128,512]{2,1,0:T(8,128)(2,1)} %get-tuple-element.40), channel_id=1, source_target_pairs={{0,1},{1,0},{2,3},{3,2},{4,5},{5,4},{6,7},{7,6},{8,9},{9,8},{10,11... | collective-permute-start | bytes 786440 | tf_op jit(solution)/shard_map/ppermute | solution.py:16
  47.9 28.9 %collective-permute-start.7 = (bf16[2,128,512]{2,1,0:T(8,128)(2,1)}, bf16[2,128,512]{2,1,0:T(8,128)(2,1)}, u32[]{:S(2)}, u32[]{:S(2)}) collective-permute-start(bf16[2,128,512]{2,1,0:T(8,128)(2,1)} %get-tuple-element.39), channel_id=1, source_target_pairs={{0,2},{1,3},{2,0},{3,1},{4,6},{5,7},{6,4},{7,5},{8,10},{9,11},{10,... | collective-permute-start | bytes 786440 | tf_op jit(solution)/shard_map/ppermute | solution.py:16
  52.6 25.4 %collective-permute-start.8 = (bf16[2,128,512]{2,1,0:T(8,128)(2,1)}, bf16[2,128,512]{2,1,0:T(8,128)(2,1)S(1)}, u32[]{:S(2)}, u32[]{:S(2)}) collective-permute-start(bf16[2,128,512]{2,1,0:T(8,128)(2,1)} %get-tuple-element.38), channel_id=1, source_target_pairs={{0,4},{1,5},{2,6},{3,7},{4,0},{5,1},{6,2},{7,3},{8,12},{9,13},{10,... | collective-permute-start | bytes 786440 | tf_op jit(solution)/shard_map/ppermute | solution.py:16
  73.9 5.3 %collective-permute-start.9 = (bf16[2,128,512]{2,1,0:T(8,128)(2,1)S(1)}, bf16[2,128,512]{2,1,0:T(8,128)(2,1)S(1)}, u32[]{:S(2)}, u32[]{:S(2)}) collective-permute-start(bf16[2,128,512]{2,1,0:T(8,128)(2,1)S(1)} %get-tuple-element.43), channel_id=1, source_target_pairs={{0,1},{1,0},{2,3},{3,2},{4,5},{5,4},{6,7},{7,6},{8,9},{9,8},{10,11... | collective-permute-start | bytes 786440 | tf_op jit(solution)/shard_map/ppermute | solution.py:16
  75.1 6.6 %collective-permute-start.10 = (bf16[2,128,512]{2,1,0:T(8,128)(2,1)S(1)}, bf16[2,128,512]{2,1,0:T(8,128)(2,1)S(1)}, u32[]{:S(2)}, u32[]{:S(2)}) collective-permute-start(bf16[2,128,512]{2,1,0:T(8,128)(2,1)S(1)} %get-tuple-element.42), channel_id=1, source_target_pairs={{0,2},{1,3},{2,0},{3,1},{4,6},{5,7},{6,4},{7,5},{8,10},{9,11},{10,... | collective-permute-start | bytes 786440 | tf_op jit(solution)/shard_map/ppermute | solution.py:16
  75.4 9.1 %collective-permute-start.11 = (bf16[2,128,512]{2,1,0:T(8,128)(2,1)S(1)}, bf16[2,128,512]{2,1,0:T(8,128)(2,1)S(1)}, u32[]{:S(2)}, u32[]{:S(2)}) collective-permute-start(bf16[2,128,512]{2,1,0:T(8,128)(2,1)S(1)} %get-tuple-element.41), channel_id=1, source_target_pairs={{0,4},{1,5},{2,6},{3,7},{4,0},{5,1},{6,2},{7,3},{8,12},{9,13},{10,... | collective-permute-start | bytes 786440 | tf_op jit(solution)/shard_map/ppermute | solution.py:16
  87.5 11.6 %collective-permute-start.12 = (bf16[1024,1024]{1,0:T(8,128)(2,1)}, bf16[1024,1024]{1,0:T(8,128)(2,1)}, u32[]{:S(2)}, u32[]{:S(2)}) collective-permute-start(bf16[1024,1024]{1,0:T(8,128)(2,1)} %convert_bitcast_fusion), channel_id=1, source_target_pairs={{0,8},{8,0},{16,24},{24,16},{1,9},{9,1},{17,25},{25,17},{2,10},{10... | collective-permute-start | bytes 6291464 | tf_op jit(solution)/shard_map/ppermute | solution.py:116
  97.5 7.8 %collective-permute-start.17 = (bf16[1024,1024]{1,0:T(8,128)(2,1)}, bf16[1024,1024]{1,0:T(8,128)(2,1)}, u32[]{:S(2)}, u32[]{:S(2)}) collective-permute-start(bf16[1024,1024]{1,0:T(8,128)(2,1)} %convolution_convert_fusion), channel_id=1, source_target_pairs={{0,8},{8,0},{16,24},{24,16},{1,9},{9,1},{17,25},{25,17},{2,10},{10... | collective-permute-start | bytes 6291464 | tf_op jit(solution)/shard_map/ppermute | solution.py:116
  105.0 24.7 %collective-permute-start.13 = (bf16[2,2,2,64,1024]{4,3,0,2,1:T(8,128)(2,1)}, bf16[2,2,2,64,1024]{4,3,0,2,1:T(8,128)(2,1)}, u32[]{:S(2)}, u32[]{:S(2)}) collective-permute-start(bf16[2,2,2,64,1024]{4,3,0,2,1:T(8,128)(2,1)} %bitcast.209), channel_id=1, source_target_pairs={{0,1},{1,0},{2,3},{3,2},{4,5},{5,4},{6,7},{7,6},{8,9},{9,8},{10,11... | collective-permute-start | bytes 3145736 | tf_op jit(solution)/shard_map/ppermute | solution.py:116
  111.2 24.7 %collective-permute-start.18 = (bf16[2,2,2,64,1024]{4,3,2,0,1:T(8,128)(2,1)}, bf16[2,2,2,64,1024]{4,3,2,0,1:T(8,128)(2,1)}, u32[]{:S(2)}, u32[]{:S(2)}) collective-permute-start(bf16[2,2,2,64,1024]{4,3,2,0,1:T(8,128)(2,1)} %bitcast.208), channel_id=1, source_target_pairs={{0,2},{1,3},{2,0},{3,1},{4,6},{5,7},{6,4},{7,5},{8,10},{9,11},{10,... | collective-permute-start | bytes 3145736 | tf_op jit(solution)/shard_map/ppermute | solution.py:116
  131.5 15.5 %collective-permute-start.14 = (bf16[2,2,64,1024]{3,2,0,1:T(8,128)(2,1)S(1)}, bf16[2,2,64,1024]{3,2,0,1:T(8,128)(2,1)S(1)}, u32[]{:S(2)}, u32[]{:S(2)}) collective-permute-start(bf16[2,2,64,1024]{3,2,0,1:T(8,128)(2,1)S(1)} %dynamic-slice_bitcast_fusion.1), channel_id=1, source_target_pairs={{0,2},{1,3},{2,0},{3,1},{4,6},{5,7},{6,4},{7,5},{8,10},{9,11},{10,... | collective-permute-start | bytes 1572872 | tf_op jit(solution)/shard_map/ppermute | solution.py:116
  137.7 11.5 %collective-permute-start.19 = (bf16[2,2,64,1024]{3,2,1,0:T(8,128)(2,1)S(1)}, bf16[2,2,64,1024]{3,2,1,0:T(8,128)(2,1)S(1)}, u32[]{:S(2)}, u32[]{:S(2)}) collective-permute-start(bf16[2,2,64,1024]{3,2,1,0:T(8,128)(2,1)S(1)} %dynamic-slice_bitcast_fusion), channel_id=1, source_target_pairs={{0,1},{1,0},{2,3},{3,2},{4,5},{5,4},{6,7},{7,6},{8,9},{9,8},{10,11... | collective-permute-start | bytes 1572872 | tf_op jit(solution)/shard_map/ppermute | solution.py:116
  147.3 6.7 %collective-permute-start.15 = (bf16[2,64,1024]{2,1,0:T(8,128)(2,1)S(1)}, bf16[2,64,1024]{2,1,0:T(8,128)(2,1)S(1)}, u32[]{:S(2)}, u32[]{:S(2)}) collective-permute-start(bf16[2,64,1024]{2,1,0:T(8,128)(2,1)S(1)} %dynamic-slice_bitcast_fusion.3), channel_id=1, source_target_pairs={{0,16},{8,24},{16,0},{24,8},{1,17},{9,25},{17,1},{25,9},{2,18},{10... | collective-permute-start | bytes 786440 | tf_op jit(solution)/shard_map/ppermute | solution.py:116
  149.5 16.9 %collective-permute-start.20 = (bf16[2,64,1024]{2,1,0:T(8,128)(2,1)S(1)}, bf16[2,64,1024]{2,1,0:T(8,128)(2,1)S(1)}, u32[]{:S(2)}, u32[]{:S(2)}) collective-permute-start(bf16[2,64,1024]{2,1,0:T(8,128)(2,1)S(1)} %dynamic-slice_bitcast_fusion.2), channel_id=1, source_target_pairs={{0,4},{1,5},{2,6},{3,7},{4,0},{5,1},{6,2},{7,3},{8,12},{9,13},{10,... | collective-permute-start | bytes 786440 | tf_op jit(solution)/shard_map/ppermute | solution.py:116
  154.0 15.1 %collective-permute-start.16 = (bf16[64,1024]{1,0:T(8,128)(2,1)S(1)}, bf16[64,1024]{1,0:T(8,128)(2,1)S(1)}, u32[]{:S(2)}, u32[]{:S(2)}) collective-permute-start(bf16[64,1024]{1,0:T(8,128)(2,1)S(1)} %dynamic-slice_bitcast_fusion.5), channel_id=1, source_target_pairs={{0,4},{1,5},{2,6},{3,7},{4,0},{5,1},{6,2},{7,3},{8,12},{9,13},{10,... | collective-permute-start | bytes 393224 | tf_op jit(solution)/shard_map/ppermute | solution.py:116
  166.4 4.1 %collective-permute-start.21 = (bf16[64,1024]{1,0:T(8,128)(2,1)S(1)}, bf16[64,1024]{1,0:T(8,128)(2,1)S(1)}, u32[]{:S(2)}, u32[]{:S(2)}) collective-permute-start(bf16[64,1024]{1,0:T(8,128)(2,1)S(1)} %dynamic-slice_bitcast_fusion.4), channel_id=1, source_target_pairs={{0,16},{8,24},{16,0},{24,8},{1,17},{9,25},{17,1},{25,9},{2,18},{10... | collective-permute-start | bytes 393224 | tf_op jit(solution)/shard_map/ppermute | solution.py:116
  170.6 5.3 %collective-permute-start.22 = (bf16[64,2048]{1,0:T(8,128)(2,1)S(1)}, bf16[64,2048]{1,0:T(8,128)(2,1)S(1)}, u32[]{:S(2)}, u32[]{:S(2)}) collective-permute-start(bf16[64,2048]{1,0:T(8,128)(2,1)S(1)} %pad_maximum_fusion.16), channel_id=1, source_target_pairs={{0,16},{8,24},{16,0},{24,8},{1,17},{9,25},{17,1},{25,9},{2,18},{10... | collective-permute-start | bytes 786440 | tf_op jit(solution)/shard_map/ppermute | solution.py:116
  176.0 6.7 %collective-permute-start.23 = (bf16[128,2048]{1,0:T(8,128)(2,1)S(1)}, bf16[128,2048]{1,0:T(8,128)(2,1)S(1)}, u32[]{:S(2)}, u32[]{:S(2)}) collective-permute-start(bf16[128,2048]{1,0:T(8,128)(2,1)S(1)} %maximum_select_fusion), channel_id=1, source_target_pairs={{0,8},{8,0},{16,24},{24,16},{1,9},{9,1},{17,25},{25,17},{2,10},{10... | collective-permute-start | bytes 1572872 | tf_op jit(solution)/shard_map/ppermute | solution.py:116
  (37 other events, 216.1 us)

commit v11 on v10

--- a/solution.py
+++ b/solution.py
@@ -10,6 +10,7 @@
 HEADS = 16
 BLOCK = 128
 LANES = 128
+SPLIT = 4
 
 
 def partner(array, axis, apart):
@@ -205,8 +206,9 @@
     query = jnp.dot(rows, w_query, preferred_element_type=jnp.float32).astype(jnp.bfloat16)
     keys_local = jnp.dot(rows, w_key, preferred_element_type=jnp.float32).astype(jnp.bfloat16)
     values_local = jnp.dot(rows, w_value, preferred_element_type=jnp.float32).astype(jnp.bfloat16)
-    half = (width // LANES) // 2 * LANES
-    spans = [(0, half), (half, width)]
+    units = width // LANES
+    cuts = [units * c // SPLIT * LANES for c in range(SPLIT + 1)]
+    spans = list(zip(cuts[:-1], cuts[1:]))
     remotes = [swap_blocks(keys_local, values_local, offsets, levels, lo, hi) for lo, hi in spans]
     d_att = jnp.dot(cot, w_out.T, preferred_element_type=jnp.float32).astype(jnp.bfloat16)
     outs = [

time: 185 us -> 193 us (1.043)
  waiting for transfers between devices: 52.4 us -> 59.3 us
  Pallas kernels: 31.2 us -> 35.1 us
    ppermute x12, starting transfers between devices: 19.5 us -> 12.7 us  [exchange(): lax.ppermute(array, axis, [(i, i ^ mask) for i in range(lax.axis_size(axi...]
    ppermute x12 -> x24, starting transfers between devices: 17.3 us -> 22.9 us  [partner(): lax.ppermute(array, axis, [(i, i ^ 1 << apart) for i in range(lax.axis_si...]
    ppermute x12 -> x24, waiting for transfers between devices: 5.68 us -> 9.9 us  [partner(): lax.ppermute(array, axis, [(i, i ^ 1 << apart) for i in range(lax.axis_si...]
    pallas_call x2 -> x4, Pallas kernels: 31.2 us -> 35.1 us  [attention(): pl.pallas_call(functools.partial(attention_kernel, head=head, scale=head...]
    squeeze x2 -> x4, local copies, waits for them, and re-layouts: 3.38 us -> 6.49 us  [body(): returned = partner(back[level], 'seq', level).astype(jnp.float32)]
    ppermute x12, waiting for transfers between devices: 46.7 us -> 49.5 us  [exchange(): lax.ppermute(array, axis, [(i, i ^ mask) for i in range(lax.axis_size(axi...]
    convert_element_type x6 -> x12, other arithmetic: 2.39 us -> 0.23 us  [body(): returned = partner(back[level], 'seq', level).astype(jnp.float32)]
    dot_general x1, matrix products: 1.26 us -> 3.31 us  [body(): jnp.dot(rows, w_key, preferred_element_type=jnp.float32)]
  transfers between devices with their start and end apart: 24 -> 36, of which waited for: 12 -> 14; matrix products, arithmetic and copies ran while one was open for 23% -> 21% of each run, Pallas kernels for 17% -> 18%
where the time goes in v11:
time: 193 us
  waiting for transfers between devices  59.3 us (31%)
  starting transfers between devices  35.6 us (18%)
  Pallas kernels  35.1 us (18%)
  matrix products  30.6 us (16%)
  local copies, waits for them, and re-layouts  18.7 us (10%)
  other arithmetic  9.15 us (5%)
  between operations  3.92 us (2%)
    ppermute x12, waiting for transfers between devices, exchange(): lax.ppermute(array, axis, [(i, i ^ mask) for i in range(lax.axis_size(axi...  49.5 us
    pallas_call x4, Pallas kernels, attention(): pl.pallas_call(functools.partial(attention_kernel, head=head, scale=head...  35.1 us
    ppermute x24, starting transfers between devices, partner(): lax.ppermute(array, axis, [(i, i ^ 1 << apart) for i in range(lax.axis_si...  22.9 us
    ppermute x12, starting transfers between devices, exchange(): lax.ppermute(array, axis, [(i, i ^ mask) for i in range(lax.axis_size(axi...  12.7 us
    dot_general x4, matrix products, term(): jnp.dot(left.T, right[:, lo:hi], preferred_element_type=jnp.float32)  12 us
    ppermute x24, waiting for transfers between devices, partner(): lax.ppermute(array, axis, [(i, i ^ 1 << apart) for i in range(lax.axis_si...  9.9 us
    squeeze x4, local copies, waits for them, and re-layouts, body(): returned = partner(back[level], 'seq', level).astype(jnp.float32)  6.49 us
    unnamed x131, local copies, waits for them, and re-layouts  5.27 us
  transfers between devices with their start and end apart: 36, of which 14 were waited for; matrix products, arithmetic and copies ran while one was open for 21% of the time, Pallas kernels for 18%

profile of v11, /device:TPU:1, one launch (start us, length us, event | category | flops | bytes accessed | tf_op | source)
XLA Modules:
  0.0 192.5 jit_solution(16925323733447039058)
XLA Ops:
  4.0 3.3 %convolution_convert_fusion.4.k_ref = bf16[512,1024]{1,0:T(8,128)(2,1)S(1)} fusion(bf16[1024,1024]{1,0:T(8,128)(2,1)} %param.9, bf16[1,512,1024]{2,1,0:T(8,128)(2,1)} %param.7), kind=kOutput, calls=%fused_computation.13 | convolution fusion | flops 1074266112 | bytes 4194304 | tf_op jit(solution)/shard_map/dot_general | solution.py:207
  16.7 2.3 %collective-permute-start.11 = (bf16[2,128,256]{2,1,0:T(8,128)(2,1)}, bf16[2,128,256]{2,1,0:T(8,128)(2,1)}, u32[]{:S(2)}, u32[]{:S(2)}) collective-permute-start(bf16[2,128,256]{2,1,0:T(8,128)(2,1)} %pad_maximum_fusion.19), channel_id=1, source_target_pairs={{0,4},{1,5},{2,6},{3,7},{4,0},{5,1},{6,2},{7,3},{8,12},{9,13},{10,... | collective-permute-start | bytes 393224 | tf_op jit(solution)/shard_map/ppermute | solution.py:17
  19.6 3.5 %convolution_convert_fusion.5.q_ref = bf16[512,1024]{1,0:T(8,128)(2,1)} fusion(bf16[1024,1024]{1,0:T(8,128)(2,1)S(1)} %copy-done.46, bf16[1,512,1024]{2,1,0:T(8,128)(2,1)} %param.7), kind=kOutput, calls=%fused_computation.14 | convolution fusion | flops 1074266112 | bytes 4194304 | tf_op jit(solution)/shard_map/dot_general | solution.py:206
  28.4 8.7 %shard_map.121 = (bf16[512,256]{1,0:T(8,128)(2,1)}, bf16[512,256]{1,0:T(8,128)(2,1)}, f32[512,256]{1,0:T(8,128)}, f32[512,256]{1,0:T(8,128)}, bf16[3,2,128,256]{3,2,1,0:T(8,128)(2,1)}) custom-call(bf16[512,1024]{1,0:T(8,128)(2,1)} %convolution_convert_fusion.5.q_ref, bf16[512,1024]{1,0:T(8,128)(2,1)} %copy-done.18, bf16[512,1024]{1,0:T(8,128)(2,1)} %copy-done.19, ...), custom_call_target="tpu_custom_call" | custom-call | flops 2818572288 | bytes 3276800 | tf_op jit(solution)/shard_map/pallas_call | solution.py:95
  42.1 8.8 %shard_map.120 = (bf16[512,256]{1,0:T(8,128)(2,1)}, bf16[512,256]{1,0:T(8,128)(2,1)}, f32[512,256]{1,0:T(8,128)}, f32[512,256]{1,0:T(8,128)}, bf16[3,2,128,256]{3,2,1,0:T(8,128)(2,1)}) custom-call(bf16[512,1024]{1,0:T(8,128)(2,1)} %convolution_convert_fusion.5.q_ref, bf16[512,1024]{1,0:T(8,128)(2,1)} %copy-done.18, bf16[512,1024]{1,0:T(8,128)(2,1)} %copy-done.19, ...), custom_call_target="tpu_custom_call" | custom-call | flops 2818572288 | bytes 3276800 | tf_op jit(solution)/shard_map/pallas_call | solution.py:95
  54.9 8.8 %shard_map.119 = (bf16[512,256]{1,0:T(8,128)(2,1)}, bf16[512,256]{1,0:T(8,128)(2,1)}, f32[512,256]{1,0:T(8,128)}, f32[512,256]{1,0:T(8,128)}, bf16[3,2,128,256]{3,2,1,0:T(8,128)(2,1)}) custom-call(bf16[512,1024]{1,0:T(8,128)(2,1)} %convolution_convert_fusion.5.q_ref, bf16[512,1024]{1,0:T(8,128)(2,1)} %copy-done.18, bf16[512,1024]{1,0:T(8,128)(2,1)} %copy-done.19, ...), custom_call_target="tpu_custom_call" | custom-call | flops 2818572288 | bytes 3276800 | tf_op jit(solution)/shard_map/pallas_call | solution.py:95
  65.5 2.3 %collective-permute-start.23 = (bf16[2,128,256]{2,1,0:T(8,128)(2,1)}, bf16[2,128,256]{2,1,0:T(8,128)(2,1)S(1)}, u32[]{:S(2)}, u32[]{:S(2)}) collective-permute-start(bf16[2,128,256]{2,1,0:T(8,128)(2,1)} %get-tuple-element.71), channel_id=1, source_target_pairs={{0,4},{1,5},{2,6},{3,7},{4,0},{5,1},{6,2},{7,3},{8,12},{9,13},{10,... | collective-permute-start | bytes 393224 | tf_op jit(solution)/shard_map/ppermute | solution.py:17
  69.9 8.8 %shard_map.118 = (bf16[512,256]{1,0:T(8,128)(2,1)}, bf16[512,256]{1,0:T(8,128)(2,1)}, f32[512,256]{1,0:T(8,128)}, f32[512,256]{1,0:T(8,128)}, bf16[3,2,128,256]{3,2,1,0:T(8,128)(2,1)}) custom-call(bf16[512,1024]{1,0:T(8,128)(2,1)} %convolution_convert_fusion.5.q_ref, bf16[512,1024]{1,0:T(8,128)(2,1)} %copy-done.18, bf16[512,1024]{1,0:T(8,128)(2,1)} %copy-done.19, ...), custom_call_target="tpu_custom_call" | custom-call | flops 2818572288 | bytes 3276800 | tf_op jit(solution)/shard_map/pallas_call | solution.py:95
  82.6 2.3 %collective-permute-start.17 = (bf16[2,128,256]{2,1,0:T(8,128)(2,1)S(1)}, bf16[2,128,256]{2,1,0:T(8,128)(2,1)S(1)}, u32[]{:S(2)}, u32[]{:S(2)}) collective-permute-start(bf16[2,128,256]{2,1,0:T(8,128)(2,1)S(1)} %get-tuple-element.65), channel_id=1, source_target_pairs={{0,4},{1,5},{2,6},{3,7},{4,0},{5,1},{6,2},{7,3},{8,12},{9,13},{10,... | collective-permute-start | bytes 393224 | tf_op jit(solution)/shard_map/ppermute | solution.py:17
  89.6 3.0 %collective-permute-done.13 = bf16[2,128,256]{2,1,0:T(8,128)(2,1)S(1)} collective-permute-done((bf16[2,128,256]{2,1,0:T(8,128)(2,1)S(1)}, bf16[2,128,256]{2,1,0:T(8,128)(2,1)S(1)}, u32[]{:S(2)}, u32[]{:S(2)}) %collective-permute-start.13) | collective-permute-done | bytes 131104 | tf_op jit(solution)/shard_map/ppermute | solution.py:17
  92.6 4.4 %collective-permute-done.14 = bf16[2,128,256]{2,1,0:T(8,128)(2,1)S(1)} collective-permute-done((bf16[2,128,256]{2,1,0:T(8,128)(2,1)S(1)}, bf16[2,128,256]{2,1,0:T(8,128)(2,1)S(1)}, u32[]{:S(2)}, u32[]{:S(2)}) %collective-permute-start.14) | collective-permute-done | bytes 131104 | tf_op jit(solution)/shard_map/ppermute | solution.py:17
  98.0 2.7 %convolution_convert_fusion = bf16[1024,1024]{1,0:T(8,128)(2,1)} fusion(bf16[1,512,1024]{2,1,0:T(8,128)(2,1)S(1)} %copy-done.49, bf16[1,512,1024]{2,1,0:T(8,128)(2,1)S(1)} %copy-done.51, pred[]{:T(512)S(6)} %eq.17, bf16[1,512,256]{2,1,0:T(8,128)(2,1)S(1)} %convert_bitcast_fusion.4, bf16[1,512,256]{2,1,0:T(8,128)(2,1)S(1)} %convert_bitcast_fusion.3, ...), kind=kOutput, calls=%fused_computation.9 | convolution fusion | flops 1084227584 | bytes 6291457 | tf_op jit(solution)/shard_map/dot_general | solution.py:125
  100.7 5.2 %collective-permute-start.29 = (bf16[1024,1024]{1,0:T(8,128)(2,1)}, bf16[1024,1024]{1,0:T(8,128)(2,1)}, u32[]{:S(2)}, u32[]{:S(2)}) collective-permute-start(bf16[1024,1024]{1,0:T(8,128)(2,1)} %convolution_convert_fusion), channel_id=1, source_target_pairs={{0,8},{8,0},{16,24},{24,16},{1,9},{9,1},{17,25},{25,17},{2,10},{10... | collective-permute-start | bytes 6291464 | tf_op jit(solution)/shard_map/ppermute | solution.py:117
  106.2 2.7 %convert_bitcast_fusion = bf16[1024,1024]{1,0:T(8,128)(2,1)} fusion(bf16[1,512,1024]{2,1,0:T(8,128)(2,1)S(1)} %copy-done.51, bf16[512,1024]{1,0:T(8,128)(2,1)S(1)} %constant_dynamic-update-slice_fusion, pred[]{:T(512)S(6)} %eq.17, bf16[512,256]{1,0:T(8,128)(2,1)S(1)} %convert_element_type.247, bf16[512,256]{1,0:T(8,128)(2,1)S(1)} %convert_element_type.246, ...), kind=kOutput, calls=%fused_computation.7 | convolution fusion | flops 1079508992 | bytes 5242881 | tf_op jit(solution)/shard_map/dot_general | solution.py:125
  110.0 3.7 %add_convert_fusion = bf16[1024,1024]{1,0:T(8,128)(2,1)S(1)} fusion(bf16[1024,1024]{1,0:T(8,128)(2,1)} %collective-permute-done.29, bf16[1,512,1024]{2,1,0:T(8,128)(2,1)} %param.13, bf16[1,512,1024]{2,1,0:T(8,128)(2,1)} %param.7, pred[]{:T(512)S(6)} %eq.17, bf16[1,512,256]{2,1,0:T(8,128)(2,1)S(1)} %convert_bitcast_fusion.4, ...), kind=kOutput, calls=%fused_computation.2 | convolution fusion | flops 1088421888 | bytes 8388609 | tf_op jit(solution)/shard_map/dot_general | solution.py:125
  116.0 2.9 %fusion = bf16[1024,1024]{1,0:T(8,128)(2,1)S(1)} fusion(bf16[1024,1024]{1,0:T(8,128)(2,1)} %collective-permute-done.24, bf16[1,512,1024]{2,1,0:T(8,128)(2,1)S(1)} %copy-done.52, bf16[512,1024]{1,0:T(8,128)(2,1)S(1)} %copy-done.41, pred[]{:T(512)S(6)} %eq.17, bf16[512,256]{1,0:T(8,128)(2,1)S(1)} %convert_element_type.247, ...), kind=kOutput, calls=%fused_computation.1 | convolution fusion | flops 1083703296 | bytes 7340033 | tf_op jit(solution)/shard_map/dot_general | solution.py:125
  121.6 3.4 %fusion.3 = bf16[1,512,1024]{2,1,0:T(8,128)(2,1)} fusion(bf16[1024,1024]{1,0:T(8,128)(2,1)S(1)} %copy-done, bf16[512,256]{1,0:T(8,128)(2,1)} %get-tuple-element.29, bf16[512,256]{1,0:T(8,128)(2,1)} %get-tuple-element.28, bf16[512,256]{1,0:T(8,128)(2,1)} %get-tuple-element.27, bf16[512,256]{1,0:T(8,128)(2,1)} %get-tuple-element.26), kind=kOutput, calls=%fused_computation.15 | convolution fusion | flops 1078460416 | bytes 4194304 | tf_op jit(solution)/shard_map/dot_general | solution.py:220
  125.0 14.8 %collective-permute-done.30 = bf16[2,2,2,64,1024]{4,3,2,0,1:T(8,128)(2,1)} collective-permute-done((bf16[2,2,2,64,1024]{4,3,2,0,1:T(8,128)(2,1)}, bf16[2,2,2,64,1024]{4,3,2,0,1:T(8,128)(2,1)}, u32[]{:S(2)}, u32[]{:S(2)}) %collective-permute-start.30) | collective-permute-done | bytes 1048608 | tf_op jit(solution)/shard_map/ppermute | solution.py:117
  141.7 4.2 %collective-permute-done.25 = bf16[2,2,2,64,1024]{4,3,0,2,1:T(8,128)(2,1)} collective-permute-done((bf16[2,2,2,64,1024]{4,3,0,2,1:T(8,128)(2,1)}, bf16[2,2,2,64,1024]{4,3,0,2,1:T(8,128)(2,1)}, u32[]{:S(2)}, u32[]{:S(2)}) %collective-permute-start.25) | collective-permute-done | bytes 1048608 | tf_op jit(solution)/shard_map/ppermute | solution.py:117
  150.5 6.5 %collective-permute-done.31 = bf16[2,2,64,1024]{3,2,1,0:T(8,128)(2,1)S(1)} collective-permute-done((bf16[2,2,64,1024]{3,2,1,0:T(8,128)(2,1)S(1)}, bf16[2,2,64,1024]{3,2,1,0:T(8,128)(2,1)S(1)}, u32[]{:S(2)}, u32[]{:S(2)}) %collective-permute-start.31) | collective-permute-done | bytes 524320 | tf_op jit(solution)/shard_map/ppermute | solution.py:117
  161.1 10.2 %collective-permute-done.32 = bf16[2,64,1024]{2,1,0:T(8,128)(2,1)S(1)} collective-permute-done((bf16[2,64,1024]{2,1,0:T(8,128)(2,1)S(1)}, bf16[2,64,1024]{2,1,0:T(8,128)(2,1)S(1)}, u32[]{:S(2)}, u32[]{:S(2)}) %collective-permute-start.32) | collective-permute-done | bytes 262176 | tf_op jit(solution)/shard_map/ppermute | solution.py:117
  172.8 2.4 %collective-permute-done.33 = bf16[64,1024]{1,0:T(8,128)(2,1)S(1)} collective-permute-done((bf16[64,1024]{1,0:T(8,128)(2,1)S(1)}, bf16[64,1024]{1,0:T(8,128)(2,1)S(1)}, u32[]{:S(2)}, u32[]{:S(2)}) %collective-permute-start.33) | collective-permute-done | bytes 131104 | tf_op jit(solution)/shard_map/ppermute | solution.py:117
  175.2 4.5 %collective-permute-done.28 = bf16[64,1024]{1,0:T(8,128)(2,1)S(1)} collective-permute-done((bf16[64,1024]{1,0:T(8,128)(2,1)S(1)}, bf16[64,1024]{1,0:T(8,128)(2,1)S(1)}, u32[]{:S(2)}, u32[]{:S(2)}) %collective-permute-start.28) | collective-permute-done | bytes 131104 | tf_op jit(solution)/shard_map/ppermute | solution.py:117
  181.5 5.1 %collective-permute-done.34 = bf16[64,2048]{1,0:T(8,128)(2,1)S(1)} collective-permute-done((bf16[64,2048]{1,0:T(8,128)(2,1)S(1)}, bf16[64,2048]{1,0:T(8,128)(2,1)S(1)}, u32[]{:S(2)}, u32[]{:S(2)}) %collective-permute-start.34) | collective-permute-done | bytes 262176 | tf_op jit(solution)/shard_map/ppermute | solution.py:117
  (276 shorter events, 64.1 us)
Async XLA Ops:
  12.0 13.7 %collective-permute-start.9 = (bf16[2,128,256]{2,1,0:T(8,128)(2,1)}, bf16[2,128,256]{2,1,0:T(8,128)(2,1)}, u32[]{:S(2)}, u32[]{:S(2)}) collective-permute-start(bf16[2,128,256]{2,1,0:T(8,128)(2,1)} %pad_maximum_fusion.17), channel_id=1, source_target_pairs={{0,1},{1,0},{2,3},{3,2},{4,5},{5,4},{6,7},{7,6},{8,9},{9,8},{10,11... | collective-permute-start | bytes 393224 | tf_op jit(solution)/shard_map/ppermute | solution.py:17
  14.7 11.1 %collective-permute-start.10 = (bf16[2,128,256]{2,1,0:T(8,128)(2,1)}, bf16[2,128,256]{2,1,0:T(8,128)(2,1)}, u32[]{:S(2)}, u32[]{:S(2)}) collective-permute-start(bf16[2,128,256]{2,1,0:T(8,128)(2,1)} %pad_maximum_fusion.18), channel_id=1, source_target_pairs={{0,2},{1,3},{2,0},{3,1},{4,6},{5,7},{6,4},{7,5},{8,10},{9,11},{10,... | collective-permute-start | bytes 393224 | tf_op jit(solution)/shard_map/ppermute | solution.py:17
  16.7 10.4 %collective-permute-start.11 = (bf16[2,128,256]{2,1,0:T(8,128)(2,1)}, bf16[2,128,256]{2,1,0:T(8,128)(2,1)}, u32[]{:S(2)}, u32[]{:S(2)}) collective-permute-start(bf16[2,128,256]{2,1,0:T(8,128)(2,1)} %pad_maximum_fusion.19), channel_id=1, source_target_pairs={{0,4},{1,5},{2,6},{3,7},{4,0},{5,1},{6,2},{7,3},{8,12},{9,13},{10,... | collective-permute-start | bytes 393224 | tf_op jit(solution)/shard_map/ppermute | solution.py:17
  19.0 19.9 %collective-permute-start.6 = (bf16[2,128,256]{2,1,0:T(8,128)(2,1)S(1)}, bf16[2,128,256]{2,1,0:T(8,128)(2,1)}, u32[]{:S(2)}, u32[]{:S(2)}) collective-permute-start(bf16[2,128,256]{2,1,0:T(8,128)(2,1)S(1)} %pad_maximum_fusion.14), channel_id=1, source_target_pairs={{0,1},{1,0},{2,3},{3,2},{4,5},{5,4},{6,7},{7,6},{8,9},{9,8},{10,11... | collective-permute-start | bytes 393224 | tf_op jit(solution)/shard_map/ppermute | solution.py:17
  19.4 21.8 %collective-permute-start.7 = (bf16[2,128,256]{2,1,0:T(8,128)(2,1)S(1)}, bf16[2,128,256]{2,1,0:T(8,128)(2,1)}, u32[]{:S(2)}, u32[]{:S(2)}) collective-permute-start(bf16[2,128,256]{2,1,0:T(8,128)(2,1)S(1)} %pad_maximum_fusion.15), channel_id=1, source_target_pairs={{0,2},{1,3},{2,0},{3,1},{4,6},{5,7},{6,4},{7,5},{8,10},{9,11},{10,... | collective-permute-start | bytes 393224 | tf_op jit(solution)/shard_map/ppermute | solution.py:17
  25.8 15.7 %collective-permute-start.8 = (bf16[2,128,256]{2,1,0:T(8,128)(2,1)S(1)}, bf16[2,128,256]{2,1,0:T(8,128)(2,1)S(1)}, u32[]{:S(2)}, u32[]{:S(2)}) collective-permute-start(bf16[2,128,256]{2,1,0:T(8,128)(2,1)S(1)} %pad_maximum_fusion.16), channel_id=1, source_target_pairs={{0,4},{1,5},{2,6},{3,7},{4,0},{5,1},{6,2},{7,3},{8,12},{9,13},{10,... | collective-permute-start | bytes 393224 | tf_op jit(solution)/shard_map/ppermute | solution.py:17
  25.9 26.8 %collective-permute-start.3 = (bf16[2,128,256]{2,1,0:T(8,128)(2,1)S(1)}, bf16[2,128,256]{2,1,0:T(8,128)(2,1)S(1)}, u32[]{:S(2)}, u32[]{:S(2)}) collective-permute-start(bf16[2,128,256]{2,1,0:T(8,128)(2,1)S(1)} %pad_maximum_fusion.11), channel_id=1, source_target_pairs={{0,1},{1,0},{2,3},{3,2},{4,5},{5,4},{6,7},{7,6},{8,9},{9,8},{10,11... | collective-permute-start | bytes 393224 | tf_op jit(solution)/shard_map/ppermute | solution.py:17
  27.1 25.7 %collective-permute-start.4 = (bf16[2,128,256]{2,1,0:T(8,128)(2,1)S(1)}, bf16[2,128,256]{2,1,0:T(8,128)(2,1)S(1)}, u32[]{:S(2)}, u32[]{:S(2)}) collective-permute-start(bf16[2,128,256]{2,1,0:T(8,128)(2,1)S(1)} %pad_maximum_fusion.12), channel_id=1, source_target_pairs={{0,2},{1,3},{2,0},{3,1},{4,6},{5,7},{6,4},{7,5},{8,10},{9,11},{10,... | collective-permute-start | bytes 393224 | tf_op jit(solution)/shard_map/ppermute | solution.py:17
  38.9 15.1 %collective-permute-start.5 = (bf16[2,128,256]{2,1,0:T(8,128)(2,1)S(1)}, bf16[2,128,256]{2,1,0:T(8,128)(2,1)S(1)}, u32[]{:S(2)}, u32[]{:S(2)}) collective-permute-start(bf16[2,128,256]{2,1,0:T(8,128)(2,1)S(1)} %pad_maximum_fusion.13), channel_id=1, source_target_pairs={{0,4},{1,5},{2,6},{3,7},{4,0},{5,1},{6,2},{7,3},{8,12},{9,13},{10,... | collective-permute-start | bytes 393224 | tf_op jit(solution)/shard_map/ppermute | solution.py:17
  41.2 24.3 %collective-permute-start = (bf16[2,128,256]{2,1,0:T(8,128)(2,1)S(1)}, bf16[2,128,256]{2,1,0:T(8,128)(2,1)S(1)}, u32[]{:S(2)}, u32[]{:S(2)}) collective-permute-start(bf16[2,128,256]{2,1,0:T(8,128)(2,1)S(1)} %pad_maximum_fusion.8), channel_id=1, source_target_pairs={{0,1},{1,0},{2,3},{3,2},{4,5},{5,4},{6,7},{7,6},{8,9},{9,8},{10,11... | collective-permute-start | bytes 393224 | tf_op jit(solution)/shard_map/ppermute | solution.py:17
  41.4 26.3 %collective-permute-start.1 = (bf16[2,128,256]{2,1,0:T(8,128)(2,1)S(1)}, bf16[2,128,256]{2,1,0:T(8,128)(2,1)S(1)}, u32[]{:S(2)}, u32[]{:S(2)}) collective-permute-start(bf16[2,128,256]{2,1,0:T(8,128)(2,1)S(1)} %pad_maximum_fusion.9), channel_id=1, source_target_pairs={{0,2},{1,3},{2,0},{3,1},{4,6},{5,7},{6,4},{7,5},{8,10},{9,11},{10,... | collective-permute-start | bytes 393224 | tf_op jit(solution)/shard_map/ppermute | solution.py:17
  52.7 16.0 %collective-permute-start.2 = (bf16[2,128,256]{2,1,0:T(8,128)(2,1)S(1)}, bf16[2,128,256]{2,1,0:T(8,128)(2,1)S(1)}, u32[]{:S(2)}, u32[]{:S(2)}) collective-permute-start(bf16[2,128,256]{2,1,0:T(8,128)(2,1)S(1)} %pad_maximum_fusion.10), channel_id=1, source_target_pairs={{0,4},{1,5},{2,6},{3,7},{4,0},{5,1},{6,2},{7,3},{8,12},{9,13},{10,... | collective-permute-start | bytes 393224 | tf_op jit(solution)/shard_map/ppermute | solution.py:17
  52.8 27.1 %collective-permute-start.21 = (bf16[2,128,256]{2,1,0:T(8,128)(2,1)}, bf16[2,128,256]{2,1,0:T(8,128)(2,1)S(1)}, u32[]{:S(2)}, u32[]{:S(2)}) collective-permute-start(bf16[2,128,256]{2,1,0:T(8,128)(2,1)} %get-tuple-element.73), channel_id=1, source_target_pairs={{0,1},{1,0},{2,3},{3,2},{4,5},{5,4},{6,7},{7,6},{8,9},{9,8},{10,11... | collective-permute-start | bytes 393224 | tf_op jit(solution)/shard_map/ppermute | solution.py:17
  54.0 26.2 %collective-permute-start.22 = (bf16[2,128,256]{2,1,0:T(8,128)(2,1)}, bf16[2,128,256]{2,1,0:T(8,128)(2,1)S(1)}, u32[]{:S(2)}, u32[]{:S(2)}) collective-permute-start(bf16[2,128,256]{2,1,0:T(8,128)(2,1)} %get-tuple-element.72), channel_id=1, source_target_pairs={{0,2},{1,3},{2,0},{3,1},{4,6},{5,7},{6,4},{7,5},{8,10},{9,11},{10,... | collective-permute-start | bytes 393224 | tf_op jit(solution)/shard_map/ppermute | solution.py:17
  65.5 16.1 %collective-permute-start.23 = (bf16[2,128,256]{2,1,0:T(8,128)(2,1)}, bf16[2,128,256]{2,1,0:T(8,128)(2,1)S(1)}, u32[]{:S(2)}, u32[]{:S(2)}) collective-permute-start(bf16[2,128,256]{2,1,0:T(8,128)(2,1)} %get-tuple-element.71), channel_id=1, source_target_pairs={{0,4},{1,5},{2,6},{3,7},{4,0},{5,1},{6,2},{7,3},{8,12},{9,13},{10,... | collective-permute-start | bytes 393224 | tf_op jit(solution)/shard_map/ppermute | solution.py:17
  68.4 14.2 %collective-permute-start.18 = (bf16[2,128,256]{2,1,0:T(8,128)(2,1)}, bf16[2,128,256]{2,1,0:T(8,128)(2,1)S(1)}, u32[]{:S(2)}, u32[]{:S(2)}) collective-permute-start(bf16[2,128,256]{2,1,0:T(8,128)(2,1)} %get-tuple-element.70), channel_id=1, source_target_pairs={{0,1},{1,0},{2,3},{3,2},{4,5},{5,4},{6,7},{7,6},{8,9},{9,8},{10,11... | collective-permute-start | bytes 393224 | tf_op jit(solution)/shard_map/ppermute | solution.py:17
  69.3 15.8 %collective-permute-start.19 = (bf16[2,128,256]{2,1,0:T(8,128)(2,1)}, bf16[2,128,256]{2,1,0:T(8,128)(2,1)S(1)}, u32[]{:S(2)}, u32[]{:S(2)}) collective-permute-start(bf16[2,128,256]{2,1,0:T(8,128)(2,1)} %get-tuple-element.69), channel_id=1, source_target_pairs={{0,2},{1,3},{2,0},{3,1},{4,6},{5,7},{6,4},{7,5},{8,10},{9,11},{10,... | collective-permute-start | bytes 393224 | tf_op jit(solution)/shard_map/ppermute | solution.py:17
  86.3 10.7 %collective-permute-start.14 = (bf16[2,128,256]{2,1,0:T(8,128)(2,1)S(1)}, bf16[2,128,256]{2,1,0:T(8,128)(2,1)S(1)}, u32[]{:S(2)}, u32[]{:S(2)}) collective-permute-start(bf16[2,128,256]{2,1,0:T(8,128)(2,1)S(1)} %get-tuple-element.62), channel_id=1, source_target_pairs={{0,4},{1,5},{2,6},{3,7},{4,0},{5,1},{6,2},{7,3},{8,12},{9,13},{10,... | collective-permute-start | bytes 393224 | tf_op jit(solution)/shard_map/ppermute | solution.py:17
  115.1 24.7 %collective-permute-start.30 = (bf16[2,2,2,64,1024]{4,3,2,0,1:T(8,128)(2,1)}, bf16[2,2,2,64,1024]{4,3,2,0,1:T(8,128)(2,1)}, u32[]{:S(2)}, u32[]{:S(2)}) collective-permute-start(bf16[2,2,2,64,1024]{4,3,2,0,1:T(8,128)(2,1)} %bitcast.322), channel_id=1, source_target_pairs={{0,2},{1,3},{2,0},{3,1},{4,6},{5,7},{6,4},{7,5},{8,10},{9,11},{10,... | collective-permute-start | bytes 3145736 | tf_op jit(solution)/shard_map/ppermute | solution.py:117
  121.2 24.7 %collective-permute-start.25 = (bf16[2,2,2,64,1024]{4,3,0,2,1:T(8,128)(2,1)}, bf16[2,2,2,64,1024]{4,3,0,2,1:T(8,128)(2,1)}, u32[]{:S(2)}, u32[]{:S(2)}) collective-permute-start(bf16[2,2,2,64,1024]{4,3,0,2,1:T(8,128)(2,1)} %bitcast.323), channel_id=1, source_target_pairs={{0,1},{1,0},{2,3},{3,2},{4,5},{5,4},{6,7},{7,6},{8,9},{9,8},{10,11... | collective-permute-start | bytes 3145736 | tf_op jit(solution)/shard_map/ppermute | solution.py:117
  141.6 15.4 %collective-permute-start.31 = (bf16[2,2,64,1024]{3,2,1,0:T(8,128)(2,1)S(1)}, bf16[2,2,64,1024]{3,2,1,0:T(8,128)(2,1)S(1)}, u32[]{:S(2)}, u32[]{:S(2)}) collective-permute-start(bf16[2,2,64,1024]{3,2,1,0:T(8,128)(2,1)S(1)} %dynamic-slice_bitcast_fusion), channel_id=1, source_target_pairs={{0,1},{1,0},{2,3},{3,2},{4,5},{5,4},{6,7},{7,6},{8,9},{9,8},{10,11... | collective-permute-start | bytes 1572872 | tf_op jit(solution)/shard_map/ppermute | solution.py:117
  147.8 11.5 %collective-permute-start.26 = (bf16[2,2,64,1024]{3,2,0,1:T(8,128)(2,1)S(1)}, bf16[2,2,64,1024]{3,2,0,1:T(8,128)(2,1)S(1)}, u32[]{:S(2)}, u32[]{:S(2)}) collective-permute-start(bf16[2,2,64,1024]{3,2,0,1:T(8,128)(2,1)S(1)} %dynamic-slice_bitcast_fusion.1), channel_id=1, source_target_pairs={{0,2},{1,3},{2,0},{3,1},{4,6},{5,7},{6,4},{7,5},{8,10},{9,11},{10,... | collective-permute-start | bytes 1572872 | tf_op jit(solution)/shard_map/ppermute | solution.py:117
  157.3 14.0 %collective-permute-start.32 = (bf16[2,64,1024]{2,1,0:T(8,128)(2,1)S(1)}, bf16[2,64,1024]{2,1,0:T(8,128)(2,1)S(1)}, u32[]{:S(2)}, u32[]{:S(2)}) collective-permute-start(bf16[2,64,1024]{2,1,0:T(8,128)(2,1)S(1)} %dynamic-slice_bitcast_fusion.2), channel_id=1, source_target_pairs={{0,4},{1,5},{2,6},{3,7},{4,0},{5,1},{6,2},{7,3},{8,12},{9,13},{10,... | collective-permute-start | bytes 786440 | tf_op jit(solution)/shard_map/ppermute | solution.py:117
  159.8 12.8 %collective-permute-start.27 = (bf16[2,64,1024]{2,1,0:T(8,128)(2,1)S(1)}, bf16[2,64,1024]{2,1,0:T(8,128)(2,1)S(1)}, u32[]{:S(2)}, u32[]{:S(2)}) collective-permute-start(bf16[2,64,1024]{2,1,0:T(8,128)(2,1)S(1)} %dynamic-slice_bitcast_fusion.3), channel_id=1, source_target_pairs={{0,16},{8,24},{16,0},{24,8},{1,17},{9,25},{17,1},{25,9},{2,18},{10... | collective-permute-start | bytes 786440 | tf_op jit(solution)/shard_map/ppermute | solution.py:117
  (76 other events, 389.8 us)

commit v12 on v10

--- a/solution.py
+++ b/solution.py
@@ -207,7 +207,9 @@
     values_local = jnp.dot(rows, w_value, preferred_element_type=jnp.float32).astype(jnp.bfloat16)
     half = (width // LANES) // 2 * LANES
     spans = [(0, half), (half, width)]
-    remotes = [swap_blocks(keys_local, values_local, offsets, levels, lo, hi) for lo, hi in spans]
+    remotes = [swap_blocks(keys_local, values_local, offsets, levels, *spans[0])]
+    later_keys, later_values, _ = lax.optimization_barrier((keys_local, values_local, remotes[0]))
+    remotes.append(swap_blocks(later_keys, later_values, offsets, levels, *spans[1]))
     d_att = jnp.dot(cot, w_out.T, preferred_element_type=jnp.float32).astype(jnp.bfloat16)
     outs = [
         attention(query, keys_local, values_local, d_att, remote, head, lo, hi)

time: 185 us -> 181 us (0.978)
  other arithmetic: 10.7 us -> 7.24 us
    ppermute x12, waiting for transfers between devices: 5.68 us -> 9.13 us  [partner(): lax.ppermute(array, axis, [(i, i ^ 1 << apart) for i in range(lax.axis_si...]
    ppermute x12, starting transfers between devices: 17.3 us -> 14.3 us  [partner(): lax.ppermute(array, axis, [(i, i ^ 1 << apart) for i in range(lax.axis_si...]
    unnamed x75 -> x77, local copies, waits for them, and re-layouts: 5.17 us -> 7.5 us
    ppermute x12, waiting for transfers between devices: 46.7 us -> 44.6 us  [exchange(): lax.ppermute(array, axis, [(i, i ^ mask) for i in range(lax.axis_size(axi...]
    convert_element_type x6, other arithmetic: 2.39 us -> 0.3 us  [body(): returned = partner(back[level], 'seq', level).astype(jnp.float32)]
    dot_general x1, matrix products: 1.26 us -> 3.31 us  [body(): jnp.dot(rows, w_key, preferred_element_type=jnp.float32)]
    dot_general x1, matrix products: 3.25 us -> 1.26 us  [body(): jnp.dot(rows, w_value, preferred_element_type=jnp.float32)]
  transfers between devices with their start and end apart: 24 -> 24, of which waited for: 12 -> 12; matrix products, arithmetic and copies ran while one was open for 23% -> 22% of each run, Pallas kernels for 17% -> 17%
where the time goes in v12:
time: 181 us
  waiting for transfers between devices  53.7 us (30%)
  starting transfers between devices  35.4 us (20%)
  matrix products  32.5 us (18%)
  Pallas kernels  31.2 us (17%)
  local copies, waits for them, and re-layouts  17.4 us (10%)
  other arithmetic  7.24 us (4%)
  between operations  3.36 us (2%)
    ppermute x12, waiting for transfers between devices, exchange(): lax.ppermute(array, axis, [(i, i ^ mask) for i in range(lax.axis_size(axi...  44.6 us
    pallas_call x2, Pallas kernels, attention(): pl.pallas_call(functools.partial(attention_kernel, head=head, scale=head...  31.2 us
    ppermute x12, starting transfers between devices, exchange(): lax.ppermute(array, axis, [(i, i ^ mask) for i in range(lax.axis_size(axi...  21.1 us
    ppermute x12, starting transfers between devices, partner(): lax.ppermute(array, axis, [(i, i ^ 1 << apart) for i in range(lax.axis_si...  14.3 us
    dot_general x4, matrix products, term(): jnp.dot(left.T, right[:, lo:hi], preferred_element_type=jnp.float32)  11.9 us
    ppermute x12, waiting for transfers between devices, partner(): lax.ppermute(array, axis, [(i, i ^ 1 << apart) for i in range(lax.axis_si...  9.13 us
    unnamed x77, local copies, waits for them, and re-layouts  7.5 us
    dot_general x1, matrix products, body(): jnp.dot(rows, w_query, preferred_element_type=jnp.float32)  4.14 us
  transfers between devices with their start and end apart: 24, of which 12 were waited for; matrix products, arithmetic and copies ran while one was open for 22% of the time, Pallas kernels for 17%

profile of v12, /device:TPU:1, one launch (start us, length us, event | category | flops | bytes accessed | tf_op | source)
XLA Modules:
  0.0 180.8 jit_solution(8381048904855359061)
XLA Ops:
  4.1 3.3 %convolution_convert_fusion.4.k_ref = bf16[512,1024]{1,0:T(8,128)(2,1)S(1)} fusion(bf16[1024,1024]{1,0:T(8,128)(2,1)} %param.9, bf16[1,512,1024]{2,1,0:T(8,128)(2,1)} %param.7), kind=kOutput, calls=%fused_computation.13 | convolution fusion | flops 1074266112 | bytes 4194304 | tf_op jit(solution)/shard_map/dot_general | solution.py:206
  9.9 2.1 %collective-permute-start = (bf16[2,128,512]{2,1,0:T(8,128)(2,1)S(1)}, bf16[2,128,512]{2,1,0:T(8,128)(2,1)}, u32[]{:S(2)}, u32[]{:S(2)}) collective-permute-start(bf16[2,128,512]{2,1,0:T(8,128)(2,1)S(1)} %pad_maximum_fusion.10), channel_id=1, source_target_pairs={{0,1},{1,0},{2,3},{3,2},{4,5},{5,4},{6,7},{7,6},{8,9},{9,8},{10,11... | collective-permute-start | bytes 786440 | tf_op jit(solution)/shard_map/ppermute | solution.py:16
  13.4 2.4 %collective-permute-start.2 = (bf16[2,128,512]{2,1,0:T(8,128)(2,1)S(1)}, bf16[2,128,512]{2,1,0:T(8,128)(2,1)}, u32[]{:S(2)}, u32[]{:S(2)}) collective-permute-start(bf16[2,128,512]{2,1,0:T(8,128)(2,1)S(1)} %pad_maximum_fusion.12), channel_id=1, source_target_pairs={{0,4},{1,5},{2,6},{3,7},{4,0},{5,1},{6,2},{7,3},{8,12},{9,13},{10,... | collective-permute-start | bytes 786440 | tf_op jit(solution)/shard_map/ppermute | solution.py:16
  15.8 4.1 %convolution_convert_fusion.5.q_ref = bf16[512,1024]{1,0:T(8,128)(2,1)} fusion(bf16[1024,1024]{1,0:T(8,128)(2,1)} %param.8, bf16[1,512,1024]{2,1,0:T(8,128)(2,1)} %param.7), kind=kOutput, calls=%fused_computation.14 | convolution fusion | flops 1074266112 | bytes 4194304 | tf_op jit(solution)/shard_map/dot_general | solution.py:205
  19.9 3.5 %convolution_convert_fusion.2.do_ref = bf16[512,1024]{1,0:T(8,128)(2,1)} fusion(bf16[1024,1024]{1,0:T(8,128)(2,1)S(1)} %copy-done, bf16[1,512,1024]{2,1,0:T(8,128)(2,1)} %param.13), kind=kOutput, calls=%fused_computation.11 | convolution fusion | flops 1074266112 | bytes 4194304 | tf_op jit(solution)/shard_map/dot_general | solution.py:213
  24.6 2.5 %collective-permute-start.5 = (bf16[2,128,512]{2,1,0:T(8,128)(2,1)S(1)}, bf16[2,128,512]{2,1,0:T(8,128)(2,1)S(1)}, u32[]{:S(2)}, u32[]{:S(2)}) collective-permute-start(bf16[2,128,512]{2,1,0:T(8,128)(2,1)S(1)} %pad_maximum_fusion.15), channel_id=1, source_target_pairs={{0,4},{1,5},{2,6},{3,7},{4,0},{5,1},{6,2},{7,3},{8,12},{9,13},{10,... | collective-permute-start | bytes 786440 | tf_op jit(solution)/shard_map/ppermute | solution.py:16
  27.7 15.6 %shard_map.118 = (bf16[512,512]{1,0:T(8,128)(2,1)}, bf16[512,512]{1,0:T(8,128)(2,1)}, f32[512,512]{1,0:T(8,128)}, f32[512,512]{1,0:T(8,128)}, bf16[3,2,128,512]{3,2,1,0:T(8,128)(2,1)}) custom-call(bf16[512,1024]{1,0:T(8,128)(2,1)} %convolution_convert_fusion.5.q_ref, bf16[512,1024]{1,0:T(8,128)(2,1)} %copy-done.9, bf16[512,1024]{1,0:T(8,128)(2,1)} %copy-done.10, ...), custom_call_target="tpu_custom_call" | custom-call | flops 5637144576 | bytes 6553600 | tf_op jit(solution)/shard_map/pallas_call | solution.py:94
  43.3 2.1 %slice_bitcast_fusion.15 = (bf16[2,128,512]{2,1,0:T(8,128)(2,1)}, bf16[2,128,512]{2,1,0:T(8,128)(2,1)}, bf16[2,128,512]{2,1,0:T(8,128)(2,1)}) fusion(bf16[3,2,128,512]{3,2,1,0:T(8,128)(2,1)} %get-tuple-element.25), kind=kLoop, calls=%fused_computation.119 | loop fusion | bytes 1572864 | tf_op jit(solution)/shard_map/squeeze | solution.py:225
  51.5 15.6 %shard_map.119 = (bf16[512,512]{1,0:T(8,128)(2,1)}, bf16[512,512]{1,0:T(8,128)(2,1)}, f32[512,512]{1,0:T(8,128)}, f32[512,512]{1,0:T(8,128)}, bf16[3,2,128,512]{3,2,1,0:T(8,128)(2,1)}) custom-call(bf16[512,1024]{1,0:T(8,128)(2,1)} %convolution_convert_fusion.5.q_ref, bf16[512,1024]{1,0:T(8,128)(2,1)} %copy-done.9, bf16[512,1024]{1,0:T(8,128)(2,1)} %copy-done.10, ...), custom_call_target="tpu_custom_call" | custom-call | flops 5637144576 | bytes 6553600 | tf_op jit(solution)/shard_map/pallas_call | solution.py:94
  75.8 4.7 %collective-permute-done.11 = bf16[2,128,512]{2,1,0:T(8,128)(2,1)S(1)} collective-permute-done((bf16[2,128,512]{2,1,0:T(8,128)(2,1)S(1)}, bf16[2,128,512]{2,1,0:T(8,128)(2,1)S(1)}, u32[]{:S(2)}, u32[]{:S(2)}) %collective-permute-start.11) | collective-permute-done | bytes 262176 | tf_op jit(solution)/shard_map/ppermute | solution.py:16
  82.6 2.7 %convert_bitcast_fusion = bf16[1024,1024]{1,0:T(8,128)(2,1)} fusion(bf16[1,512,1024]{2,1,0:T(8,128)(2,1)S(1)} %copy-done.28, bf16[512,1024]{1,0:T(8,128)(2,1)S(1)} %constant_dynamic-update-slice_fusion, pred[]{:T(512)S(6)} %eq.17, bf16[512,512]{1,0:T(8,128)(2,1)S(1)} %convert_element_type.207, bf16[512,512]{1,0:T(8,128)(2,1)S(1)} %convert_element_type.206), kind=kOutput, calls=%fused_computation.7 | convolution fusion | flops 1077411840 | bytes 5242881 | tf_op jit(solution)/shard_map/dot_general | solution.py:124
  85.3 5.2 %collective-permute-start.12 = (bf16[1024,1024]{1,0:T(8,128)(2,1)}, bf16[1024,1024]{1,0:T(8,128)(2,1)}, u32[]{:S(2)}, u32[]{:S(2)}) collective-permute-start(bf16[1024,1024]{1,0:T(8,128)(2,1)} %convert_bitcast_fusion), channel_id=1, source_target_pairs={{0,8},{8,0},{16,24},{24,16},{1,9},{9,1},{17,25},{25,17},{2,10},{10... | collective-permute-start | bytes 6291464 | tf_op jit(solution)/shard_map/ppermute | solution.py:116
  90.7 2.7 %convolution_convert_fusion = bf16[1024,1024]{1,0:T(8,128)(2,1)} fusion(bf16[1,512,1024]{2,1,0:T(8,128)(2,1)S(1)} %copy-done.30, bf16[1,512,1024]{2,1,0:T(8,128)(2,1)S(1)} %copy-done.28, pred[]{:T(512)S(6)} %eq.17, bf16[1,512,512]{2,1,0:T(8,128)(2,1)S(1)} %convert_bitcast_fusion.2, bf16[1,512,512]{2,1,0:T(8,128)(2,1)S(1)} %convert_bitcast_fusion.1, ...), kind=kOutput, calls=%fused_computation.9 | convolution fusion | flops 1080033280 | bytes 6291457 | tf_op jit(solution)/shard_map/dot_general | solution.py:124
  95.0 3.5 %fusion = bf16[1024,1024]{1,0:T(8,128)(2,1)S(1)} fusion(bf16[1024,1024]{1,0:T(8,128)(2,1)} %collective-permute-done.12, bf16[1,512,1024]{2,1,0:T(8,128)(2,1)} %param.7, bf16[512,1024]{1,0:T(8,128)(2,1)} %copy-done.21, pred[]{:T(512)S(6)} %eq.17, bf16[512,512]{1,0:T(8,128)(2,1)} %copy-done.13, bf16[512,512]{1,0:T(8,128)(2,1)} %copy-done.11), kind=kOutput, calls=%fused_computation.1 | convolution fusion | flops 1081606144 | bytes 7340033 | tf_op jit(solution)/shard_map/dot_general | solution.py:124
  102.2 3.0 %add_convert_fusion = bf16[1024,1024]{1,0:T(8,128)(2,1)S(1)} fusion(bf16[1024,1024]{1,0:T(8,128)(2,1)} %collective-permute-done.17, bf16[1,512,1024]{2,1,0:T(8,128)(2,1)S(1)} %copy-done.31, bf16[1,512,1024]{2,1,0:T(8,128)(2,1)S(1)} %copy-done.29, pred[]{:T(512)S(6)} %eq.17, bf16[1,512,512]{2,1,0:T(8,128)(2,1)S(1)} %copy-done.18, ...), kind=kOutput, calls=%fused_computation.2 | convolution fusion | flops 1084227584 | bytes 8388609 | tf_op jit(solution)/shard_map/dot_general | solution.py:124
  107.5 3.5 %fusion.3 = bf16[1,512,1024]{2,1,0:T(8,128)(2,1)} fusion(bf16[1024,1024]{1,0:T(8,128)(2,1)S(1)} %copy-done, bf16[512,512]{1,0:T(8,128)(2,1)} %get-tuple-element.21, bf16[512,512]{1,0:T(8,128)(2,1)} %get-tuple-element.18), kind=kOutput, calls=%fused_computation.15 | convolution fusion | flops 1076363264 | bytes 4194304 | tf_op jit(solution)/shard_map/dot_general | solution.py:220
  111.0 14.6 %collective-permute-done.13 = bf16[2,2,2,64,1024]{4,3,0,2,1:T(8,128)(2,1)} collective-permute-done((bf16[2,2,2,64,1024]{4,3,0,2,1:T(8,128)(2,1)}, bf16[2,2,2,64,1024]{4,3,0,2,1:T(8,128)(2,1)}, u32[]{:S(2)}, u32[]{:S(2)}) %collective-permute-start.13) | collective-permute-done | bytes 1048608 | tf_op jit(solution)/shard_map/ppermute | solution.py:116
  127.5 4.3 %collective-permute-done.18 = bf16[2,2,2,64,1024]{4,3,2,0,1:T(8,128)(2,1)} collective-permute-done((bf16[2,2,2,64,1024]{4,3,2,0,1:T(8,128)(2,1)}, bf16[2,2,2,64,1024]{4,3,2,0,1:T(8,128)(2,1)}, u32[]{:S(2)}, u32[]{:S(2)}) %collective-permute-start.18) | collective-permute-done | bytes 1048608 | tf_op jit(solution)/shard_map/ppermute | solution.py:116
  137.5 5.5 %collective-permute-done.14 = bf16[2,2,64,1024]{3,2,0,1:T(8,128)(2,1)S(1)} collective-permute-done((bf16[2,2,64,1024]{3,2,0,1:T(8,128)(2,1)S(1)}, bf16[2,2,64,1024]{3,2,0,1:T(8,128)(2,1)S(1)}, u32[]{:S(2)}, u32[]{:S(2)}) %collective-permute-start.14) | collective-permute-done | bytes 524320 | tf_op jit(solution)/shard_map/ppermute | solution.py:116
  146.1 3.5 %collective-permute-done.15 = bf16[2,64,1024]{2,1,0:T(8,128)(2,1)S(1)} collective-permute-done((bf16[2,64,1024]{2,1,0:T(8,128)(2,1)S(1)}, bf16[2,64,1024]{2,1,0:T(8,128)(2,1)S(1)}, u32[]{:S(2)}, u32[]{:S(2)}) %collective-permute-start.15) | collective-permute-done | bytes 262176 | tf_op jit(solution)/shard_map/ppermute | solution.py:116
  150.6 10.6 %collective-permute-done.20 = bf16[2,64,1024]{2,1,0:T(8,128)(2,1)S(1)} collective-permute-done((bf16[2,64,1024]{2,1,0:T(8,128)(2,1)S(1)}, bf16[2,64,1024]{2,1,0:T(8,128)(2,1)S(1)}, u32[]{:S(2)}, u32[]{:S(2)}) %collective-permute-start.20) | collective-permute-done | bytes 262176 | tf_op jit(solution)/shard_map/ppermute | solution.py:116
  168.2 3.5 %collective-permute-done.22 = bf16[64,2048]{1,0:T(8,128)(2,1)S(1)} collective-permute-done((bf16[64,2048]{1,0:T(8,128)(2,1)S(1)}, bf16[64,2048]{1,0:T(8,128)(2,1)S(1)}, u32[]{:S(2)}, u32[]{:S(2)}) %collective-permute-start.22) | collective-permute-done | bytes 262176 | tf_op jit(solution)/shard_map/ppermute | solution.py:116
  171.8 5.4 %collective-permute-start.23 = (bf16[128,2048]{1,0:T(8,128)(2,1)S(1)}, bf16[128,2048]{1,0:T(8,128)(2,1)S(1)}, u32[]{:S(2)}, u32[]{:S(2)}) collective-permute-start(bf16[128,2048]{1,0:T(8,128)(2,1)S(1)} %maximum_select_fusion), channel_id=1, source_target_pairs={{0,8},{8,0},{16,24},{24,16},{1,9},{9,1},{17,25},{25,17},{2,10},{10... | collective-permute-start | bytes 1572872 | tf_op jit(solution)/shard_map/ppermute | solution.py:116
  177.1 2.3 %fusion.4 = bf16[1,512,1024]{2,1,0:T(8,128)(2,1)} fusion(f32[512,1024]{1,0:T(8,128)S(1)} %fusion.36, f32[512,1024]{1,0:T(8,128)S(1)} %fusion.8, bf16[512,1024]{1,0:T(8,128)(2,1)S(1)} %copy-done.22, bf16[1024,1024]{1,0:T(8,128)(2,1)S(1)} %copy-done.26), kind=kOutput, calls=%fused_computation.16 | convolution fusion | flops 1075314688 | bytes 8388608 | tf_op jit(solution)/shard_map/dot_general | solution.py:240
  (173 shorter events, 51.2 us)
Async XLA Ops:
  9.9 13.6 %collective-permute-start = (bf16[2,128,512]{2,1,0:T(8,128)(2,1)S(1)}, bf16[2,128,512]{2,1,0:T(8,128)(2,1)}, u32[]{:S(2)}, u32[]{:S(2)}) collective-permute-start(bf16[2,128,512]{2,1,0:T(8,128)(2,1)S(1)} %pad_maximum_fusion.10), channel_id=1, source_target_pairs={{0,1},{1,0},{2,3},{3,2},{4,5},{5,4},{6,7},{7,6},{8,9},{9,8},{10,11... | collective-permute-start | bytes 786440 | tf_op jit(solution)/shard_map/ppermute | solution.py:16
  12.0 12.4 %collective-permute-start.1 = (bf16[2,128,512]{2,1,0:T(8,128)(2,1)S(1)}, bf16[2,128,512]{2,1,0:T(8,128)(2,1)}, u32[]{:S(2)}, u32[]{:S(2)}) collective-permute-start(bf16[2,128,512]{2,1,0:T(8,128)(2,1)S(1)} %pad_maximum_fusion.11), channel_id=1, source_target_pairs={{0,2},{1,3},{2,0},{3,1},{4,6},{5,7},{6,4},{7,5},{8,10},{9,11},{10,... | collective-permute-start | bytes 786440 | tf_op jit(solution)/shard_map/ppermute | solution.py:16
  13.4 11.0 %collective-permute-start.2 = (bf16[2,128,512]{2,1,0:T(8,128)(2,1)S(1)}, bf16[2,128,512]{2,1,0:T(8,128)(2,1)}, u32[]{:S(2)}, u32[]{:S(2)}) collective-permute-start(bf16[2,128,512]{2,1,0:T(8,128)(2,1)S(1)} %pad_maximum_fusion.12), channel_id=1, source_target_pairs={{0,4},{1,5},{2,6},{3,7},{4,0},{5,1},{6,2},{7,3},{8,12},{9,13},{10,... | collective-permute-start | bytes 786440 | tf_op jit(solution)/shard_map/ppermute | solution.py:16
  24.6 25.2 %collective-permute-start.5 = (bf16[2,128,512]{2,1,0:T(8,128)(2,1)S(1)}, bf16[2,128,512]{2,1,0:T(8,128)(2,1)S(1)}, u32[]{:S(2)}, u32[]{:S(2)}) collective-permute-start(bf16[2,128,512]{2,1,0:T(8,128)(2,1)S(1)} %pad_maximum_fusion.15), channel_id=1, source_target_pairs={{0,4},{1,5},{2,6},{3,7},{4,0},{5,1},{6,2},{7,3},{8,12},{9,13},{10,... | collective-permute-start | bytes 786440 | tf_op jit(solution)/shard_map/ppermute | solution.py:16
  27.1 23.7 %collective-permute-start.4 = (bf16[2,128,512]{2,1,0:T(8,128)(2,1)S(1)}, bf16[2,128,512]{2,1,0:T(8,128)(2,1)S(1)}, u32[]{:S(2)}, u32[]{:S(2)}) collective-permute-start(bf16[2,128,512]{2,1,0:T(8,128)(2,1)S(1)} %pad_maximum_fusion.14), channel_id=1, source_target_pairs={{0,2},{1,3},{2,0},{3,1},{4,6},{5,7},{6,4},{7,5},{8,10},{9,11},{10,... | collective-permute-start | bytes 786440 | tf_op jit(solution)/shard_map/ppermute | solution.py:16
  27.4 23.4 %collective-permute-start.3 = (bf16[2,128,512]{2,1,0:T(8,128)(2,1)S(1)}, bf16[2,128,512]{2,1,0:T(8,128)(2,1)}, u32[]{:S(2)}, u32[]{:S(2)}) collective-permute-start(bf16[2,128,512]{2,1,0:T(8,128)(2,1)S(1)} %pad_maximum_fusion.13), channel_id=1, source_target_pairs={{0,1},{1,0},{2,3},{3,2},{4,5},{5,4},{6,7},{7,6},{8,9},{9,8},{10,11... | collective-permute-start | bytes 786440 | tf_op jit(solution)/shard_map/ppermute | solution.py:16
  45.4 24.9 %collective-permute-start.6 = (bf16[2,128,512]{2,1,0:T(8,128)(2,1)}, bf16[2,128,512]{2,1,0:T(8,128)(2,1)S(1)}, u32[]{:S(2)}, u32[]{:S(2)}) collective-permute-start(bf16[2,128,512]{2,1,0:T(8,128)(2,1)} %get-tuple-element.40), channel_id=1, source_target_pairs={{0,1},{1,0},{2,3},{3,2},{4,5},{5,4},{6,7},{7,6},{8,9},{9,8},{10,11... | collective-permute-start | bytes 786440 | tf_op jit(solution)/shard_map/ppermute | solution.py:16
  46.6 24.0 %collective-permute-start.7 = (bf16[2,128,512]{2,1,0:T(8,128)(2,1)}, bf16[2,128,512]{2,1,0:T(8,128)(2,1)S(1)}, u32[]{:S(2)}, u32[]{:S(2)}) collective-permute-start(bf16[2,128,512]{2,1,0:T(8,128)(2,1)} %get-tuple-element.39), channel_id=1, source_target_pairs={{0,2},{1,3},{2,0},{3,1},{4,6},{5,7},{6,4},{7,5},{8,10},{9,11},{10,... | collective-permute-start | bytes 786440 | tf_op jit(solution)/shard_map/ppermute | solution.py:16
  49.8 22.1 %collective-permute-start.8 = (bf16[2,128,512]{2,1,0:T(8,128)(2,1)}, bf16[2,128,512]{2,1,0:T(8,128)(2,1)S(1)}, u32[]{:S(2)}, u32[]{:S(2)}) collective-permute-start(bf16[2,128,512]{2,1,0:T(8,128)(2,1)} %get-tuple-element.38), channel_id=1, source_target_pairs={{0,4},{1,5},{2,6},{3,7},{4,0},{5,1},{6,2},{7,3},{8,12},{9,13},{10,... | collective-permute-start | bytes 786440 | tf_op jit(solution)/shard_map/ppermute | solution.py:16
  68.5 5.3 %collective-permute-start.9 = (bf16[2,128,512]{2,1,0:T(8,128)(2,1)S(1)}, bf16[2,128,512]{2,1,0:T(8,128)(2,1)S(1)}, u32[]{:S(2)}, u32[]{:S(2)}) collective-permute-start(bf16[2,128,512]{2,1,0:T(8,128)(2,1)S(1)} %get-tuple-element.43), channel_id=1, source_target_pairs={{0,1},{1,0},{2,3},{3,2},{4,5},{5,4},{6,7},{7,6},{8,9},{9,8},{10,11... | collective-permute-start | bytes 786440 | tf_op jit(solution)/shard_map/ppermute | solution.py:16
  68.8 6.8 %collective-permute-start.10 = (bf16[2,128,512]{2,1,0:T(8,128)(2,1)S(1)}, bf16[2,128,512]{2,1,0:T(8,128)(2,1)S(1)}, u32[]{:S(2)}, u32[]{:S(2)}) collective-permute-start(bf16[2,128,512]{2,1,0:T(8,128)(2,1)S(1)} %get-tuple-element.42), channel_id=1, source_target_pairs={{0,2},{1,3},{2,0},{3,1},{4,6},{5,7},{6,4},{7,5},{8,10},{9,11},{10,... | collective-permute-start | bytes 786440 | tf_op jit(solution)/shard_map/ppermute | solution.py:16
  70.3 10.2 %collective-permute-start.11 = (bf16[2,128,512]{2,1,0:T(8,128)(2,1)S(1)}, bf16[2,128,512]{2,1,0:T(8,128)(2,1)S(1)}, u32[]{:S(2)}, u32[]{:S(2)}) collective-permute-start(bf16[2,128,512]{2,1,0:T(8,128)(2,1)S(1)} %get-tuple-element.41), channel_id=1, source_target_pairs={{0,4},{1,5},{2,6},{3,7},{4,0},{5,1},{6,2},{7,3},{8,12},{9,13},{10,... | collective-permute-start | bytes 786440 | tf_op jit(solution)/shard_map/ppermute | solution.py:16
  85.3 9.7 %collective-permute-start.12 = (bf16[1024,1024]{1,0:T(8,128)(2,1)}, bf16[1024,1024]{1,0:T(8,128)(2,1)}, u32[]{:S(2)}, u32[]{:S(2)}) collective-permute-start(bf16[1024,1024]{1,0:T(8,128)(2,1)} %convert_bitcast_fusion), channel_id=1, source_target_pairs={{0,8},{8,0},{16,24},{24,16},{1,9},{9,1},{17,25},{25,17},{2,10},{10... | collective-permute-start | bytes 6291464 | tf_op jit(solution)/shard_map/ppermute | solution.py:116
  93.4 8.8 %collective-permute-start.17 = (bf16[1024,1024]{1,0:T(8,128)(2,1)}, bf16[1024,1024]{1,0:T(8,128)(2,1)}, u32[]{:S(2)}, u32[]{:S(2)}) collective-permute-start(bf16[1024,1024]{1,0:T(8,128)(2,1)} %convolution_convert_fusion), channel_id=1, source_target_pairs={{0,8},{8,0},{16,24},{24,16},{1,9},{9,1},{17,25},{25,17},{2,10},{10... | collective-permute-start | bytes 6291464 | tf_op jit(solution)/shard_map/ppermute | solution.py:116
  101.0 24.7 %collective-permute-start.13 = (bf16[2,2,2,64,1024]{4,3,0,2,1:T(8,128)(2,1)}, bf16[2,2,2,64,1024]{4,3,0,2,1:T(8,128)(2,1)}, u32[]{:S(2)}, u32[]{:S(2)}) collective-permute-start(bf16[2,2,2,64,1024]{4,3,0,2,1:T(8,128)(2,1)} %bitcast.209), channel_id=1, source_target_pairs={{0,1},{1,0},{2,3},{3,2},{4,5},{5,4},{6,7},{7,6},{8,9},{9,8},{10,11... | collective-permute-start | bytes 3145736 | tf_op jit(solution)/shard_map/ppermute | solution.py:116
  107.5 24.4 %collective-permute-start.18 = (bf16[2,2,2,64,1024]{4,3,2,0,1:T(8,128)(2,1)}, bf16[2,2,2,64,1024]{4,3,2,0,1:T(8,128)(2,1)}, u32[]{:S(2)}, u32[]{:S(2)}) collective-permute-start(bf16[2,2,2,64,1024]{4,3,2,0,1:T(8,128)(2,1)} %bitcast.208), channel_id=1, source_target_pairs={{0,2},{1,3},{2,0},{3,1},{4,6},{5,7},{6,4},{7,5},{8,10},{9,11},{10,... | collective-permute-start | bytes 3145736 | tf_op jit(solution)/shard_map/ppermute | solution.py:116
  127.4 15.6 %collective-permute-start.14 = (bf16[2,2,64,1024]{3,2,0,1:T(8,128)(2,1)S(1)}, bf16[2,2,64,1024]{3,2,0,1:T(8,128)(2,1)S(1)}, u32[]{:S(2)}, u32[]{:S(2)}) collective-permute-start(bf16[2,2,64,1024]{3,2,0,1:T(8,128)(2,1)S(1)} %dynamic-slice_bitcast_fusion.1), channel_id=1, source_target_pairs={{0,2},{1,3},{2,0},{3,1},{4,6},{5,7},{6,4},{7,5},{8,10},{9,11},{10,... | collective-permute-start | bytes 1572872 | tf_op jit(solution)/shard_map/ppermute | solution.py:116
  133.7 10.8 %collective-permute-start.19 = (bf16[2,2,64,1024]{3,2,1,0:T(8,128)(2,1)S(1)}, bf16[2,2,64,1024]{3,2,1,0:T(8,128)(2,1)S(1)}, u32[]{:S(2)}, u32[]{:S(2)}) collective-permute-start(bf16[2,2,64,1024]{3,2,1,0:T(8,128)(2,1)S(1)} %dynamic-slice_bitcast_fusion), channel_id=1, source_target_pairs={{0,1},{1,0},{2,3},{3,2},{4,5},{5,4},{6,7},{7,6},{8,9},{9,8},{10,11... | collective-permute-start | bytes 1572872 | tf_op jit(solution)/shard_map/ppermute | solution.py:116
  143.2 6.3 %collective-permute-start.15 = (bf16[2,64,1024]{2,1,0:T(8,128)(2,1)S(1)}, bf16[2,64,1024]{2,1,0:T(8,128)(2,1)S(1)}, u32[]{:S(2)}, u32[]{:S(2)}) collective-permute-start(bf16[2,64,1024]{2,1,0:T(8,128)(2,1)S(1)} %dynamic-slice_bitcast_fusion.3), channel_id=1, source_target_pairs={{0,16},{8,24},{16,0},{24,8},{1,17},{9,25},{17,1},{25,9},{2,18},{10... | collective-permute-start | bytes 786440 | tf_op jit(solution)/shard_map/ppermute | solution.py:116
  144.8 16.4 %collective-permute-start.20 = (bf16[2,64,1024]{2,1,0:T(8,128)(2,1)S(1)}, bf16[2,64,1024]{2,1,0:T(8,128)(2,1)S(1)}, u32[]{:S(2)}, u32[]{:S(2)}) collective-permute-start(bf16[2,64,1024]{2,1,0:T(8,128)(2,1)S(1)} %dynamic-slice_bitcast_fusion.2), channel_id=1, source_target_pairs={{0,4},{1,5},{2,6},{3,7},{4,0},{5,1},{6,2},{7,3},{8,12},{9,13},{10,... | collective-permute-start | bytes 786440 | tf_op jit(solution)/shard_map/ppermute | solution.py:116
  149.7 14.4 %collective-permute-start.16 = (bf16[64,1024]{1,0:T(8,128)(2,1)S(1)}, bf16[64,1024]{1,0:T(8,128)(2,1)S(1)}, u32[]{:S(2)}, u32[]{:S(2)}) collective-permute-start(bf16[64,1024]{1,0:T(8,128)(2,1)S(1)} %dynamic-slice_bitcast_fusion.5), channel_id=1, source_target_pairs={{0,4},{1,5},{2,6},{3,7},{4,0},{5,1},{6,2},{7,3},{8,12},{9,13},{10,... | collective-permute-start | bytes 393224 | tf_op jit(solution)/shard_map/ppermute | solution.py:116
  161.3 4.1 %collective-permute-start.21 = (bf16[64,1024]{1,0:T(8,128)(2,1)S(1)}, bf16[64,1024]{1,0:T(8,128)(2,1)S(1)}, u32[]{:S(2)}, u32[]{:S(2)}) collective-permute-start(bf16[64,1024]{1,0:T(8,128)(2,1)S(1)} %dynamic-slice_bitcast_fusion.4), channel_id=1, source_target_pairs={{0,16},{8,24},{16,0},{24,8},{1,17},{9,25},{17,1},{25,9},{2,18},{10... | collective-permute-start | bytes 393224 | tf_op jit(solution)/shard_map/ppermute | solution.py:116
  165.5 6.1 %collective-permute-start.22 = (bf16[64,2048]{1,0:T(8,128)(2,1)S(1)}, bf16[64,2048]{1,0:T(8,128)(2,1)S(1)}, u32[]{:S(2)}, u32[]{:S(2)}) collective-permute-start(bf16[64,2048]{1,0:T(8,128)(2,1)S(1)} %pad_maximum_fusion.16), channel_id=1, source_target_pairs={{0,16},{8,24},{16,0},{24,8},{1,17},{9,25},{17,1},{25,9},{2,18},{10... | collective-permute-start | bytes 786440 | tf_op jit(solution)/shard_map/ppermute | solution.py:116
  171.8 7.7 %collective-permute-start.23 = (bf16[128,2048]{1,0:T(8,128)(2,1)S(1)}, bf16[128,2048]{1,0:T(8,128)(2,1)S(1)}, u32[]{:S(2)}, u32[]{:S(2)}) collective-permute-start(bf16[128,2048]{1,0:T(8,128)(2,1)S(1)} %maximum_select_fusion), channel_id=1, source_target_pairs={{0,8},{8,0},{16,24},{24,16},{1,9},{9,1},{17,25},{25,17},{2,10},{10... | collective-permute-start | bytes 1572872 | tf_op jit(solution)/shard_map/ppermute | solution.py:116
  (40 other events, 198.7 us)

commit v13 on v12

--- a/solution.py
+++ b/solution.py
@@ -124,14 +124,13 @@
     return jnp.dot(left.T, right[:, lo:hi], preferred_element_type=jnp.float32).astype(jnp.bfloat16)
 
 
-def reduce_gradients(sources):
+def reduce_gradients(rows, dquery, attended, cot, late_fn, hold):
     n_dp = lax.axis_size("dp")
     n_seq = lax.axis_size("seq")
     seq_bits = n_seq.bit_length() - 1
     dp_bits = n_dp.bit_length() - 1
-    width = sources[0][1].shape[1]
-    rows = sources[0][0].shape[1]
-    blk = rows // n_seq
+    width = dquery.shape[1]
+    blk = rows.shape[1] // n_seq
     dp_i = lax.axis_index("dp")
     seq_i = lax.axis_index("seq")
     low = dp_i % 2 == 0
@@ -139,14 +138,6 @@
     def pick(a, b):
         return jnp.where(low, a, b)
 
-    keep = [
-        (sources[0][0], pick(sources[0][1], sources[2][1])),
-        (pick(sources[1][0], sources[3][0]), pick(sources[1][1], sources[3][1])),
-    ]
-    send = [
-        (sources[2][0], pick(sources[2][1], sources[0][1])),
-        (pick(sources[3][0], sources[1][0]), pick(sources[3][1], sources[1][1])),
-    ]
     seq_dims = [("seq", b) for b in range(seq_bits)]
     dp_dims = [("dp", b) for b in range(1, dp_bits)]
     if seq_bits >= 2:
@@ -157,14 +148,13 @@
     else:
         orders = [seq_dims + dp_dims] * 2
     shape = [2] * seq_bits + [2] * (dp_bits - 1) + [blk >> (dp_bits - 1)]
-    sends = [term(*send[g], 0, width) for g in range(2)]
-    keeps = [term(*keep[g], 0, width) for g in range(2)]
-    got = exchange(sends, "dp", 1)
-    pieces = []
-    for g in range(2):
-        data = add_bf16(keeps[g], got[g]).reshape(shape + [width])
-        removed = []
-        for axis, b in orders[g]:
+
+    def start(keep, send):
+        got = exchange(term(*send, 0, width), "dp", 1)
+        return add_bf16(term(*keep, 0, width), got).reshape(shape + [width])
+
+    def steps(data, order, removed):
+        for axis, b in order:
             if axis == "seq":
                 at = seq_bits - 1 - b
                 bit = (seq_i >> b) % 2
@@ -176,23 +166,30 @@
             kept = lax.dynamic_index_in_dim(data, bit, at_now, keepdims=False)
             out = lax.dynamic_index_in_dim(data, 1 - bit, at_now, keepdims=False)
             data = add_bf16(kept, exchange(out, axis, 1 << b))
-        pieces.append(data)
-    data = jnp.concatenate(pieces, axis=1)
+        return data
+
+    early = start((pick(rows, attended), pick(dquery, cot)), (pick(attended, rows), pick(cot, dquery)))
+    removed_early = []
+    early = steps(early, orders[0][:1], removed_early)
+    early, hold = lax.optimization_barrier((early, hold))
+    dkey, dvalue = late_fn(hold)
+    late = start((rows, pick(dkey, dvalue)), (rows, pick(dvalue, dkey)))
+    late = steps(late, orders[1], [])
+    early = steps(early, orders[0][1:], removed_early)
+    data = jnp.concatenate([early, late], axis=1)
     for b in range(1, dp_bits):
         recv = exchange(data, "dp", 1 << b)
         first_half = (dp_i >> b) % 2 == 0
         data = jnp.where(first_half, jnp.concatenate([data, recv], 0), jnp.concatenate([recv, data], 0))
-    pieces = [data]
-    part = jnp.concatenate(pieces, axis=1)
-    back = exchange(part, "dp", 1)
-    mine = [part[:, :width], part[:, width:]]
+    back = exchange(data, "dp", 1)
+    mine = [data[:, :width], data[:, width:]]
     other = [back[:, :width], back[:, width:]]
-    return (
-        pick(mine[0], other[0]).astype(jnp.float32),
-        pick(mine[1], other[1]).astype(jnp.float32),
-        pick(other[0], mine[0]).astype(jnp.float32),
-        pick(other[1], mine[1]).astype(jnp.float32),
-    )
+    query = pick(mine[0], other[0])
+    outw = pick(other[0], mine[0])
+    key = pick(mine[1], other[1])
+    value = pick(other[1], mine[1])
+    grads = tuple(g.astype(jnp.float32) for g in (query, key, value, outw))
+    return grads, dkey, dvalue
 
 
 def body(layer_input, w_query, w_key, w_value, w_out, offsets, grad_out):
@@ -218,31 +215,35 @@
     attended = jnp.concatenate([o[0] for o in outs], axis=1)
     dquery = jnp.concatenate([o[1] for o in outs], axis=1)
     result = jnp.dot(attended, w_out, preferred_element_type=jnp.float32).astype(jnp.bfloat16)
-    dkeys = []
-    dvalues = []
-    for _, _, dkey_sum, dvalue_sum, back in outs:
-        for level in range(levels):
-            returned = partner(back[level], "seq", level).astype(jnp.float32)
-            start = offsets[level] * BLOCK
-            dkey_sum = lax.dynamic_update_slice_in_dim(
-                dkey_sum, lax.dynamic_slice_in_dim(dkey_sum, start, BLOCK, 0) + returned[0], start, 0
-            )
-            dvalue_sum = lax.dynamic_update_slice_in_dim(
-                dvalue_sum,
-                lax.dynamic_slice_in_dim(dvalue_sum, start, BLOCK, 0) + returned[1],
-                start,
-                0,
-            )
-        dkeys.append(dkey_sum.astype(jnp.bfloat16))
-        dvalues.append(dvalue_sum.astype(jnp.bfloat16))
-    dkey = jnp.concatenate(dkeys, axis=1)
-    dvalue = jnp.concatenate(dvalues, axis=1)
+    returned_all = [
+        [partner(back[level], "seq", level) for level in range(levels)] for _, _, _, _, back in outs
+    ]
+
+    def late_fn(returned_all):
+        dkeys = []
+        dvalues = []
+        for (_, _, dkey_sum, dvalue_sum, _), returned_list in zip(outs, returned_all):
+            for level in range(levels):
+                returned = returned_list[level].astype(jnp.float32)
+                start = offsets[level] * BLOCK
+                dkey_sum = lax.dynamic_update_slice_in_dim(
+                    dkey_sum, lax.dynamic_slice_in_dim(dkey_sum, start, BLOCK, 0) + returned[0], start, 0
+                )
+                dvalue_sum = lax.dynamic_update_slice_in_dim(
+                    dvalue_sum,
+                    lax.dynamic_slice_in_dim(dvalue_sum, start, BLOCK, 0) + returned[1],
+                    start,
+                    0,
+                )
+            dkeys.append(dkey_sum.astype(jnp.bfloat16))
+            dvalues.append(dvalue_sum.astype(jnp.bfloat16))
+        return jnp.concatenate(dkeys, axis=1), jnp.concatenate(dvalues, axis=1)
+
+    grads, dkey, dvalue = reduce_gradients(rows, dquery, attended, cot, late_fn, returned_all)
     total = jnp.dot(dquery, w_query.T, preferred_element_type=jnp.float32)
     total = total + jnp.dot(dkey, w_key.T, preferred_element_type=jnp.float32)
     total = total + jnp.dot(dvalue, w_value.T, preferred_element_type=jnp.float32)
     grad_input = total.astype(jnp.bfloat16)
-    sources = ((rows, dquery), (rows, dkey), (rows, dvalue), (attended, cot))
-    grads = reduce_gradients(sources)
     return (result[None], grad_input[None]) + grads
 
 

time: 181 us -> 206 us (1.14)
  waiting for transfers between devices: 53.7 us -> 89.4 us
  local copies, waits for them, and re-layouts: 17.4 us -> 8.9 us
  starting transfers between devices: 35.4 us -> 32.1 us
    ppermute x12, waiting for transfers between devices: 44.6 us -> 64.7 us  [exchange(): lax.ppermute(array, axis, [(i, i ^ mask) for i in range(lax.axis_size(axi...]
    ppermute x12, waiting for transfers between devices: 9.13 us -> 24.7 us  [partner(): lax.ppermute(array, axis, [(i, i ^ 1 << apart) for i in range(lax.axis_si...]
    unnamed x77 -> x60, local copies, waits for them, and re-layouts: 7.5 us -> 4.32 us
    dynamic_slice x4, local copies, waits for them, and re-layouts: 4.63 us -> 1.56 us  [the longest x2 1.11 us: steps(): out = lax.dynamic_index_in_dim(data, 1 - bit, at_now, keepdims=False)]
    ppermute x12, starting transfers between devices: 14.3 us -> 11.8 us  [partner(): lax.ppermute(array, axis, [(i, i ^ 1 << apart) for i in range(lax.axis_si...]
    dot_general x4, matrix products: 11.9 us -> 14.2 us  [term(): jnp.dot(left.T, right[:, lo:hi], preferred_element_type=jnp.float32)]
    squeeze x8, local copies, waits for them, and re-layouts: 3.55 us -> 1.35 us  [the longest x6 1.21 us: steps(): out = lax.dynamic_index_in_dim(data, 1 - bit, at_now, keepdims=False)]
  transfers between devices with their start and end apart: 24 -> 24, of which waited for: 12 -> 16; matrix products, arithmetic and copies ran while one was open for 22% -> 10% of each run, Pallas kernels for 17% -> 8%
where the time goes in v13:
time: 206 us
  waiting for transfers between devices  89.4 us (43%)
  matrix products  33.7 us (16%)
  starting transfers between devices  32.1 us (16%)
  Pallas kernels  31.3 us (15%)
  local copies, waits for them, and re-layouts  8.9 us (4%)
  other arithmetic  6.71 us (3%)
  between operations  3.3 us (2%)
    ppermute x12, waiting for transfers between devices, exchange(): lax.ppermute(array, axis, [(i, i ^ mask) for i in range(lax.axis_size(axi...  64.7 us
    pallas_call x2, Pallas kernels, attention(): pl.pallas_call(functools.partial(attention_kernel, head=head, scale=head...  31.3 us
    ppermute x12, waiting for transfers between devices, partner(): lax.ppermute(array, axis, [(i, i ^ 1 << apart) for i in range(lax.axis_si...  24.7 us
    ppermute x12, starting transfers between devices, exchange(): lax.ppermute(array, axis, [(i, i ^ mask) for i in range(lax.axis_size(axi...  20.3 us
    dot_general x4, matrix products, term(): jnp.dot(left.T, right[:, lo:hi], preferred_element_type=jnp.float32)  14.2 us
    ppermute x12, starting transfers between devices, partner(): lax.ppermute(array, axis, [(i, i ^ 1 << apart) for i in range(lax.axis_si...  11.8 us
    unnamed x60, local copies, waits for them, and re-layouts  4.32 us
    dot_general x1, matrix products, body(): jnp.dot(rows, w_query, preferred_element_type=jnp.float32)  4.14 us
  transfers between devices with their start and end apart: 24, of which 16 were waited for; matrix products, arithmetic and copies ran while one was open for 10% of the time, Pallas kernels for 8%

profile of v13, /device:TPU:1, one launch (start us, length us, event | category | flops | bytes accessed | tf_op | source)
XLA Modules:
  0.0 205.5 jit_solution(10817650748294638025)
XLA Ops:
  4.1 3.3 %convolution_convert_fusion.4.k_ref = bf16[512,1024]{1,0:T(8,128)(2,1)S(1)} fusion(bf16[1024,1024]{1,0:T(8,128)(2,1)} %param.9, bf16[1,512,1024]{2,1,0:T(8,128)(2,1)} %param.7), kind=kOutput, calls=%fused_computation.13 | convolution fusion | flops 1074266112 | bytes 4194304 | tf_op jit(solution)/shard_map/dot_general | solution.py:203
  15.8 4.1 %convolution_convert_fusion.5.q_ref = bf16[512,1024]{1,0:T(8,128)(2,1)} fusion(bf16[1024,1024]{1,0:T(8,128)(2,1)} %param.8, bf16[1,512,1024]{2,1,0:T(8,128)(2,1)} %param.7), kind=kOutput, calls=%fused_computation.14 | convolution fusion | flops 1074266112 | bytes 4194304 | tf_op jit(solution)/shard_map/dot_general | solution.py:202
  20.0 3.6 %convolution_convert_fusion.2.do_ref = bf16[512,1024]{1,0:T(8,128)(2,1)} fusion(bf16[1024,1024]{1,0:T(8,128)(2,1)S(1)} %copy-done, bf16[1,512,1024]{2,1,0:T(8,128)(2,1)} %param.13), kind=kOutput, calls=%fused_computation.11 | convolution fusion | flops 1074266112 | bytes 4194304 | tf_op jit(solution)/shard_map/dot_general | solution.py:210
  24.6 2.5 %collective-permute-start.5 = (bf16[2,128,512]{2,1,0:T(8,128)(2,1)S(1)}, bf16[2,128,512]{2,1,0:T(8,128)(2,1)}, u32[]{:S(2)}, u32[]{:S(2)}) collective-permute-start(bf16[2,128,512]{2,1,0:T(8,128)(2,1)S(1)} %pad_maximum_fusion.19), channel_id=1, source_target_pairs={{0,4},{1,5},{2,6},{3,7},{4,0},{5,1},{6,2},{7,3},{8,12},{9,13},{10,... | collective-permute-start | bytes 786440 | tf_op jit(solution)/shard_map/ppermute | solution.py:16
  27.8 15.6 %shard_map.118 = (bf16[512,512]{1,0:T(8,128)(2,1)}, bf16[512,512]{1,0:T(8,128)(2,1)}, f32[512,512]{1,0:T(8,128)}, f32[512,512]{1,0:T(8,128)}, bf16[3,2,128,512]{3,2,1,0:T(8,128)(2,1)}) custom-call(bf16[512,1024]{1,0:T(8,128)(2,1)} %convolution_convert_fusion.5.q_ref, bf16[512,1024]{1,0:T(8,128)(2,1)} %copy-done.6, bf16[512,1024]{1,0:T(8,128)(2,1)} %copy-done.7, ...), custom_call_target="tpu_custom_call" | custom-call | flops 5637144576 | bytes 6553600 | tf_op jit(solution)/shard_map/pallas_call | solution.py:94
  43.4 15.7 %shard_map.119 = (bf16[512,512]{1,0:T(8,128)(2,1)}, bf16[512,512]{1,0:T(8,128)(2,1)}, f32[512,512]{1,0:T(8,128)}, f32[512,512]{1,0:T(8,128)}, bf16[3,2,128,512]{3,2,1,0:T(8,128)(2,1)}) custom-call(bf16[512,1024]{1,0:T(8,128)(2,1)} %convolution_convert_fusion.5.q_ref, bf16[512,1024]{1,0:T(8,128)(2,1)} %copy-done.6, bf16[512,1024]{1,0:T(8,128)(2,1)} %copy-done.7, ...), custom_call_target="tpu_custom_call" | custom-call | flops 5637144576 | bytes 6553600 | tf_op jit(solution)/shard_map/pallas_call | solution.py:94
  59.1 4.4 %convolution_convert_fusion = bf16[1024,1024]{1,0:T(8,128)(2,1)} fusion(bf16[1,512,1024]{2,1,0:T(8,128)(2,1)S(1)} %copy-done.22, bf16[1,512,1024]{2,1,0:T(8,128)(2,1)} %param.7, pred[]{:T(512)S(6)} %eq.17, bf16[1,512,512]{2,1,0:T(8,128)(2,1)} %bitcast.212, bf16[1,512,512]{2,1,0:T(8,128)(2,1)S(1)} %bitcast.211, bf16[1,512,512]{2,1,0:T(8,128)(2,1)} %bitcast.216, ...), kind=kOutput, calls=%fused_computation.9 | convolution fusion | flops 1080033280 | bytes 6291457 | tf_op jit(solution)/shard_map/dot_general | solution.py:124
  63.5 4.8 %collective-permute-start.6 = (bf16[1024,1024]{1,0:T(8,128)(2,1)}, bf16[1024,1024]{1,0:T(8,128)(2,1)}, u32[]{:S(2)}, u32[]{:S(2)}) collective-permute-start(bf16[1024,1024]{1,0:T(8,128)(2,1)} %convolution_convert_fusion), channel_id=1, source_target_pairs={{0,8},{8,0},{16,24},{24,16},{1,9},{9,1},{17,25},{25,17},{2,10},{10... | collective-permute-start | bytes 6291464 | tf_op jit(solution)/shard_map/ppermute | solution.py:116
  68.3 4.1 %collective-permute-done.6 = bf16[1024,1024]{1,0:T(8,128)(2,1)} collective-permute-done((bf16[1024,1024]{1,0:T(8,128)(2,1)}, bf16[1024,1024]{1,0:T(8,128)(2,1)}, u32[]{:S(2)}, u32[]{:S(2)}) %collective-permute-start.6) | collective-permute-done | bytes 2097184 | tf_op jit(solution)/shard_map/ppermute | solution.py:116
  72.4 3.6 %add_convert_fusion = bf16[1024,1024]{1,0:T(8,128)(2,1)S(1)} fusion(bf16[1024,1024]{1,0:T(8,128)(2,1)} %collective-permute-done.6, bf16[1,512,1024]{2,1,0:T(8,128)(2,1)S(1)} %copy-done.22, bf16[1,512,1024]{2,1,0:T(8,128)(2,1)} %param.7, pred[]{:T(512)S(6)} %eq.17, bf16[1,512,512]{2,1,0:T(8,128)(2,1)} %bitcast.213, bf16[1,512,512]{2,1,0:T(8,128)(2,1)} %bitcast.210, ...), kind=kOutput, calls=%fused_computation.2 | convolution fusion | flops 1084227584 | bytes 8388609 | tf_op jit(solution)/shard_map/dot_general | solution.py:124
  80.8 11.3 %collective-permute-done.10 = bf16[2,128,512]{2,1,0:T(8,128)(2,1)S(1)} collective-permute-done((bf16[2,128,512]{2,1,0:T(8,128)(2,1)S(1)}, bf16[2,128,512]{2,1,0:T(8,128)(2,1)S(1)}, u32[]{:S(2)}, u32[]{:S(2)}) %collective-permute-start.10) | collective-permute-done | bytes 262176 | tf_op jit(solution)/shard_map/ppermute | solution.py:16
  92.0 8.4 %collective-permute-done.7 = bf16[2,2,2,64,1024]{4,3,0,2,1:T(8,128)(2,1)S(1)} collective-permute-done((bf16[2,2,2,64,1024]{4,3,0,2,1:T(8,128)(2,1)S(1)}, bf16[2,2,2,64,1024]{4,3,0,2,1:T(8,128)(2,1)S(1)}, u32[]{:S(2)}, u32[]{:S(2)}) %collective-permute-start.7) | collective-permute-done | bytes 1048608 | tf_op jit(solution)/shard_map/ppermute | solution.py:116
  101.8 4.2 %collective-permute-done.8 = bf16[2,128,512]{2,1,0:T(8,128)(2,1)S(1)} collective-permute-done((bf16[2,128,512]{2,1,0:T(8,128)(2,1)S(1)}, bf16[2,128,512]{2,1,0:T(8,128)(2,1)S(1)}, u32[]{:S(2)}, u32[]{:S(2)}) %collective-permute-start.8) | collective-permute-done | bytes 262176 | tf_op jit(solution)/shard_map/ppermute | solution.py:16
  106.1 5.6 %collective-permute-done.11 = bf16[2,128,512]{2,1,0:T(8,128)(2,1)S(1)} collective-permute-done((bf16[2,128,512]{2,1,0:T(8,128)(2,1)S(1)}, bf16[2,128,512]{2,1,0:T(8,128)(2,1)S(1)}, u32[]{:S(2)}, u32[]{:S(2)}) %collective-permute-start.11) | collective-permute-done | bytes 262176 | tf_op jit(solution)/shard_map/ppermute | solution.py:16
  111.7 2.6 %collective-permute-done.13 = bf16[2,128,512]{2,1,0:T(8,128)(2,1)S(1)} collective-permute-done((bf16[2,128,512]{2,1,0:T(8,128)(2,1)S(1)}, bf16[2,128,512]{2,1,0:T(8,128)(2,1)S(1)}, u32[]{:S(2)}, u32[]{:S(2)}) %collective-permute-start.13) | collective-permute-done | bytes 262176 | tf_op jit(solution)/shard_map/ppermute | solution.py:16
  119.0 2.6 %convert_bitcast_fusion = bf16[1024,1024]{1,0:T(8,128)(2,1)} fusion(bf16[1,512,1024]{2,1,0:T(8,128)(2,1)S(1)} %copy-done.24, pred[]{:T(512)S(6)} %eq.17, bf16[512,512]{1,0:T(8,128)(2,1)S(1)} %convert_element_type.216, bf16[512,512]{1,0:T(8,128)(2,1)S(1)} %convert_element_type.215, bf16[512,512]{1,0:T(8,128)(2,1)S(1)} %convert_element_type.214, ...), kind=kOutput, calls=%fused_computation.7 | convolution fusion | flops 1079508992 | bytes 5242881 | tf_op jit(solution)/shard_map/dot_general | solution.py:124
  122.5 4.1 %collective-permute-done.17 = bf16[1024,1024]{1,0:T(8,128)(2,1)} collective-permute-done((bf16[1024,1024]{1,0:T(8,128)(2,1)}, bf16[1024,1024]{1,0:T(8,128)(2,1)}, u32[]{:S(2)}, u32[]{:S(2)}) %collective-permute-start.17) | collective-permute-done | bytes 2097184 | tf_op jit(solution)/shard_map/ppermute | solution.py:116
  126.6 3.6 %fusion = bf16[1024,1024]{1,0:T(8,128)(2,1)S(1)} fusion(bf16[1024,1024]{1,0:T(8,128)(2,1)} %collective-permute-done.17, bf16[1,512,1024]{2,1,0:T(8,128)(2,1)} %param.7, pred[]{:T(512)S(6)} %eq.17, bf16[512,512]{1,0:T(8,128)(2,1)S(1)} %convert_element_type.216, bf16[512,512]{1,0:T(8,128)(2,1)S(1)} %convert_element_type.215, bf16[512,512]{1,0:T(8,128)(2,1)} %copy-done.16, ...), kind=kOutput, calls=%fused_computation.1 | convolution fusion | flops 1083703296 | bytes 7340033 | tf_op jit(solution)/shard_map/dot_general | solution.py:124
  134.1 22.1 %collective-permute-done.18 = bf16[2,2,2,64,1024]{4,3,2,0,1:T(8,128)(2,1)} collective-permute-done((bf16[2,2,2,64,1024]{4,3,2,0,1:T(8,128)(2,1)}, bf16[2,2,2,64,1024]{4,3,2,0,1:T(8,128)(2,1)}, u32[]{:S(2)}, u32[]{:S(2)}) %collective-permute-start.18) | collective-permute-done | bytes 1048608 | tf_op jit(solution)/shard_map/ppermute | solution.py:116
  161.5 5.8 %collective-permute-done.14 = bf16[2,2,64,1024]{3,2,0,1:T(8,128)(2,1)S(1)} collective-permute-done((bf16[2,2,64,1024]{3,2,0,1:T(8,128)(2,1)S(1)}, bf16[2,2,64,1024]{3,2,0,1:T(8,128)(2,1)S(1)}, u32[]{:S(2)}, u32[]{:S(2)}) %collective-permute-start.14) | collective-permute-done | bytes 524320 | tf_op jit(solution)/shard_map/ppermute | solution.py:116
  171.0 3.2 %collective-permute-done.15 = bf16[2,64,1024]{2,1,0:T(8,128)(2,1)S(1)} collective-permute-done((bf16[2,64,1024]{2,1,0:T(8,128)(2,1)S(1)}, bf16[2,64,1024]{2,1,0:T(8,128)(2,1)S(1)}, u32[]{:S(2)}, u32[]{:S(2)}) %collective-permute-start.15) | collective-permute-done | bytes 262176 | tf_op jit(solution)/shard_map/ppermute | solution.py:116
  175.3 11.3 %collective-permute-done.20 = bf16[2,64,1024]{2,1,0:T(8,128)(2,1)S(1)} collective-permute-done((bf16[2,64,1024]{2,1,0:T(8,128)(2,1)S(1)}, bf16[2,64,1024]{2,1,0:T(8,128)(2,1)S(1)}, u32[]{:S(2)}, u32[]{:S(2)}) %collective-permute-start.20) | collective-permute-done | bytes 262176 | tf_op jit(solution)/shard_map/ppermute | solution.py:116
  193.5 2.5 %collective-permute-done.22 = bf16[64,2048]{1,0:T(8,128)(2,1)S(1)} collective-permute-done((bf16[64,2048]{1,0:T(8,128)(2,1)S(1)}, bf16[64,2048]{1,0:T(8,128)(2,1)S(1)}, u32[]{:S(2)}, u32[]{:S(2)}) %collective-permute-start.22) | collective-permute-done | bytes 262176 | tf_op jit(solution)/shard_map/ppermute | solution.py:116
  196.1 4.4 %collective-permute-start.23 = (bf16[128,2048]{1,0:T(8,128)(2,1)S(1)}, bf16[128,2048]{1,0:T(8,128)(2,1)S(1)}, u32[]{:S(2)}, u32[]{:S(2)}) collective-permute-start(bf16[128,2048]{1,0:T(8,128)(2,1)S(1)} %maximum_select_fusion), channel_id=1, source_target_pairs={{0,8},{8,0},{16,24},{24,16},{1,9},{9,1},{17,25},{25,17},{2,10},{10... | collective-permute-start | bytes 1572872 | tf_op jit(solution)/shard_map/ppermute | solution.py:116
  (153 shorter events, 48.7 us)
Async XLA Ops:
  9.9 13.6 %collective-permute-start = (bf16[2,128,512]{2,1,0:T(8,128)(2,1)S(1)}, bf16[2,128,512]{2,1,0:T(8,128)(2,1)}, u32[]{:S(2)}, u32[]{:S(2)}) collective-permute-start(bf16[2,128,512]{2,1,0:T(8,128)(2,1)S(1)} %pad_maximum_fusion.14), channel_id=1, source_target_pairs={{0,1},{1,0},{2,3},{3,2},{4,5},{5,4},{6,7},{7,6},{8,9},{9,8},{10,11... | collective-permute-start | bytes 786440 | tf_op jit(solution)/shard_map/ppermute | solution.py:16
  12.1 12.4 %collective-permute-start.1 = (bf16[2,128,512]{2,1,0:T(8,128)(2,1)S(1)}, bf16[2,128,512]{2,1,0:T(8,128)(2,1)}, u32[]{:S(2)}, u32[]{:S(2)}) collective-permute-start(bf16[2,128,512]{2,1,0:T(8,128)(2,1)S(1)} %pad_maximum_fusion.15), channel_id=1, source_target_pairs={{0,2},{1,3},{2,0},{3,1},{4,6},{5,7},{6,4},{7,5},{8,10},{9,11},{10,... | collective-permute-start | bytes 786440 | tf_op jit(solution)/shard_map/ppermute | solution.py:16
  13.4 11.0 %collective-permute-start.2 = (bf16[2,128,512]{2,1,0:T(8,128)(2,1)S(1)}, bf16[2,128,512]{2,1,0:T(8,128)(2,1)}, u32[]{:S(2)}, u32[]{:S(2)}) collective-permute-start(bf16[2,128,512]{2,1,0:T(8,128)(2,1)S(1)} %pad_maximum_fusion.16), channel_id=1, source_target_pairs={{0,4},{1,5},{2,6},{3,7},{4,0},{5,1},{6,2},{7,3},{8,12},{9,13},{10,... | collective-permute-start | bytes 786440 | tf_op jit(solution)/shard_map/ppermute | solution.py:16
  24.6 18.7 %collective-permute-start.5 = (bf16[2,128,512]{2,1,0:T(8,128)(2,1)S(1)}, bf16[2,128,512]{2,1,0:T(8,128)(2,1)}, u32[]{:S(2)}, u32[]{:S(2)}) collective-permute-start(bf16[2,128,512]{2,1,0:T(8,128)(2,1)S(1)} %pad_maximum_fusion.19), channel_id=1, source_target_pairs={{0,4},{1,5},{2,6},{3,7},{4,0},{5,1},{6,2},{7,3},{8,12},{9,13},{10,... | collective-permute-start | bytes 786440 | tf_op jit(solution)/shard_map/ppermute | solution.py:16
  27.2 16.2 %collective-permute-start.4 = (bf16[2,128,512]{2,1,0:T(8,128)(2,1)S(1)}, bf16[2,128,512]{2,1,0:T(8,128)(2,1)}, u32[]{:S(2)}, u32[]{:S(2)}) collective-permute-start(bf16[2,128,512]{2,1,0:T(8,128)(2,1)S(1)} %pad_maximum_fusion.18), channel_id=1, source_target_pairs={{0,2},{1,3},{2,0},{3,1},{4,6},{5,7},{6,4},{7,5},{8,10},{9,11},{10,... | collective-permute-start | bytes 786440 | tf_op jit(solution)/shard_map/ppermute | solution.py:16
  27.4 15.9 %collective-permute-start.3 = (bf16[2,128,512]{2,1,0:T(8,128)(2,1)S(1)}, bf16[2,128,512]{2,1,0:T(8,128)(2,1)}, u32[]{:S(2)}, u32[]{:S(2)}) collective-permute-start(bf16[2,128,512]{2,1,0:T(8,128)(2,1)S(1)} %pad_maximum_fusion.17), channel_id=1, source_target_pairs={{0,1},{1,0},{2,3},{3,2},{4,5},{5,4},{6,7},{7,6},{8,9},{9,8},{10,11... | collective-permute-start | bytes 786440 | tf_op jit(solution)/shard_map/ppermute | solution.py:16
  63.5 8.9 %collective-permute-start.6 = (bf16[1024,1024]{1,0:T(8,128)(2,1)}, bf16[1024,1024]{1,0:T(8,128)(2,1)}, u32[]{:S(2)}, u32[]{:S(2)}) collective-permute-start(bf16[1024,1024]{1,0:T(8,128)(2,1)} %convolution_convert_fusion), channel_id=1, source_target_pairs={{0,8},{8,0},{16,24},{24,16},{1,9},{9,1},{17,25},{25,17},{2,10},{10... | collective-permute-start | bytes 6291464 | tf_op jit(solution)/shard_map/ppermute | solution.py:116
  76.4 24.1 %collective-permute-start.7 = (bf16[2,2,2,64,1024]{4,3,0,2,1:T(8,128)(2,1)S(1)}, bf16[2,2,2,64,1024]{4,3,0,2,1:T(8,128)(2,1)S(1)}, u32[]{:S(2)}, u32[]{:S(2)}) collective-permute-start(bf16[2,2,2,64,1024]{4,3,0,2,1:T(8,128)(2,1)S(1)} %bitcast.209), channel_id=1, source_target_pairs={{0,1},{1,0},{2,3},{3,2},{4,5},{5,4},{6,7},{7,6},{8,9},{9,8},{10,11... | collective-permute-start | bytes 3145736 | tf_op jit(solution)/shard_map/ppermute | solution.py:116
  77.7 14.3 %collective-permute-start.10 = (bf16[2,128,512]{2,1,0:T(8,128)(2,1)S(1)}, bf16[2,128,512]{2,1,0:T(8,128)(2,1)S(1)}, u32[]{:S(2)}, u32[]{:S(2)}) collective-permute-start(bf16[2,128,512]{2,1,0:T(8,128)(2,1)S(1)} %get-tuple-element.55), channel_id=1, source_target_pairs={{0,4},{1,5},{2,6},{3,7},{4,0},{5,1},{6,2},{7,3},{8,12},{9,13},{10,... | collective-permute-start | bytes 786440 | tf_op jit(solution)/shard_map/ppermute | solution.py:16
  77.8 28.2 %collective-permute-start.8 = (bf16[2,128,512]{2,1,0:T(8,128)(2,1)S(1)}, bf16[2,128,512]{2,1,0:T(8,128)(2,1)S(1)}, u32[]{:S(2)}, u32[]{:S(2)}) collective-permute-start(bf16[2,128,512]{2,1,0:T(8,128)(2,1)S(1)} %get-tuple-element.57), channel_id=1, source_target_pairs={{0,1},{1,0},{2,3},{3,2},{4,5},{5,4},{6,7},{7,6},{8,9},{9,8},{10,11... | collective-permute-start | bytes 786440 | tf_op jit(solution)/shard_map/ppermute | solution.py:16
  78.9 27.2 %collective-permute-start.9 = (bf16[2,128,512]{2,1,0:T(8,128)(2,1)S(1)}, bf16[2,128,512]{2,1,0:T(8,128)(2,1)S(1)}, u32[]{:S(2)}, u32[]{:S(2)}) collective-permute-start(bf16[2,128,512]{2,1,0:T(8,128)(2,1)S(1)} %get-tuple-element.56), channel_id=1, source_target_pairs={{0,2},{1,3},{2,0},{3,1},{4,6},{5,7},{6,4},{7,5},{8,10},{9,11},{10,... | collective-permute-start | bytes 786440 | tf_op jit(solution)/shard_map/ppermute | solution.py:16
  80.2 31.5 %collective-permute-start.11 = (bf16[2,128,512]{2,1,0:T(8,128)(2,1)S(1)}, bf16[2,128,512]{2,1,0:T(8,128)(2,1)S(1)}, u32[]{:S(2)}, u32[]{:S(2)}) collective-permute-start(bf16[2,128,512]{2,1,0:T(8,128)(2,1)S(1)} %get-tuple-element.54), channel_id=1, source_target_pairs={{0,1},{1,0},{2,3},{3,2},{4,5},{5,4},{6,7},{7,6},{8,9},{9,8},{10,11... | collective-permute-start | bytes 786440 | tf_op jit(solution)/shard_map/ppermute | solution.py:16
  92.0 19.6 %collective-permute-start.12 = (bf16[2,128,512]{2,1,0:T(8,128)(2,1)S(1)}, bf16[2,128,512]{2,1,0:T(8,128)(2,1)S(1)}, u32[]{:S(2)}, u32[]{:S(2)}) collective-permute-start(bf16[2,128,512]{2,1,0:T(8,128)(2,1)S(1)} %get-tuple-element.53), channel_id=1, source_target_pairs={{0,2},{1,3},{2,0},{3,1},{4,6},{5,7},{6,4},{7,5},{8,10},{9,11},{10,... | collective-permute-start | bytes 786440 | tf_op jit(solution)/shard_map/ppermute | solution.py:16
  100.4 13.9 %collective-permute-start.13 = (bf16[2,128,512]{2,1,0:T(8,128)(2,1)S(1)}, bf16[2,128,512]{2,1,0:T(8,128)(2,1)S(1)}, u32[]{:S(2)}, u32[]{:S(2)}) collective-permute-start(bf16[2,128,512]{2,1,0:T(8,128)(2,1)S(1)} %get-tuple-element.52), channel_id=1, source_target_pairs={{0,4},{1,5},{2,6},{3,7},{4,0},{5,1},{6,2},{7,3},{8,12},{9,13},{10,... | collective-permute-start | bytes 786440 | tf_op jit(solution)/shard_map/ppermute | solution.py:16
  121.7 5.0 %collective-permute-start.17 = (bf16[1024,1024]{1,0:T(8,128)(2,1)}, bf16[1024,1024]{1,0:T(8,128)(2,1)}, u32[]{:S(2)}, u32[]{:S(2)}) collective-permute-start(bf16[1024,1024]{1,0:T(8,128)(2,1)} %convert_bitcast_fusion), channel_id=1, source_target_pairs={{0,8},{8,0},{16,24},{24,16},{1,9},{9,1},{17,25},{25,17},{2,10},{10... | collective-permute-start | bytes 6291464 | tf_op jit(solution)/shard_map/ppermute | solution.py:116
  131.5 24.7 %collective-permute-start.18 = (bf16[2,2,2,64,1024]{4,3,2,0,1:T(8,128)(2,1)}, bf16[2,2,2,64,1024]{4,3,2,0,1:T(8,128)(2,1)}, u32[]{:S(2)}, u32[]{:S(2)}) collective-permute-start(bf16[2,2,2,64,1024]{4,3,2,0,1:T(8,128)(2,1)} %bitcast.205), channel_id=1, source_target_pairs={{0,2},{1,3},{2,0},{3,1},{4,6},{5,7},{6,4},{7,5},{8,10},{9,11},{10,... | collective-permute-start | bytes 3145736 | tf_op jit(solution)/shard_map/ppermute | solution.py:116
  132.5 34.7 %collective-permute-start.14 = (bf16[2,2,64,1024]{3,2,0,1:T(8,128)(2,1)S(1)}, bf16[2,2,64,1024]{3,2,0,1:T(8,128)(2,1)S(1)}, u32[]{:S(2)}, u32[]{:S(2)}) collective-permute-start(bf16[2,2,64,1024]{3,2,0,1:T(8,128)(2,1)S(1)} %dynamic-slice_bitcast_fusion.1), channel_id=1, source_target_pairs={{0,2},{1,3},{2,0},{3,1},{4,6},{5,7},{6,4},{7,5},{8,10},{9,11},{10,... | collective-permute-start | bytes 1572872 | tf_op jit(solution)/shard_map/ppermute | solution.py:116
  157.9 11.5 %collective-permute-start.19 = (bf16[2,2,64,1024]{3,2,1,0:T(8,128)(2,1)S(1)}, bf16[2,2,64,1024]{3,2,1,0:T(8,128)(2,1)S(1)}, u32[]{:S(2)}, u32[]{:S(2)}) collective-permute-start(bf16[2,2,64,1024]{3,2,1,0:T(8,128)(2,1)S(1)} %dynamic-slice_bitcast_fusion), channel_id=1, source_target_pairs={{0,1},{1,0},{2,3},{3,2},{4,5},{5,4},{6,7},{7,6},{8,9},{9,8},{10,11... | collective-permute-start | bytes 1572872 | tf_op jit(solution)/shard_map/ppermute | solution.py:116
  167.5 6.7 %collective-permute-start.15 = (bf16[2,64,1024]{2,1,0:T(8,128)(2,1)S(1)}, bf16[2,64,1024]{2,1,0:T(8,128)(2,1)S(1)}, u32[]{:S(2)}, u32[]{:S(2)}) collective-permute-start(bf16[2,64,1024]{2,1,0:T(8,128)(2,1)S(1)} %dynamic-slice_bitcast_fusion.3), channel_id=1, source_target_pairs={{0,16},{8,24},{16,0},{24,8},{1,17},{9,25},{17,1},{25,9},{2,18},{10... | collective-permute-start | bytes 786440 | tf_op jit(solution)/shard_map/ppermute | solution.py:116
  169.7 16.9 %collective-permute-start.20 = (bf16[2,64,1024]{2,1,0:T(8,128)(2,1)S(1)}, bf16[2,64,1024]{2,1,0:T(8,128)(2,1)S(1)}, u32[]{:S(2)}, u32[]{:S(2)}) collective-permute-start(bf16[2,64,1024]{2,1,0:T(8,128)(2,1)S(1)} %dynamic-slice_bitcast_fusion.2), channel_id=1, source_target_pairs={{0,4},{1,5},{2,6},{3,7},{4,0},{5,1},{6,2},{7,3},{8,12},{9,13},{10,... | collective-permute-start | bytes 786440 | tf_op jit(solution)/shard_map/ppermute | solution.py:116
  174.3 15.1 %collective-permute-start.16 = (bf16[64,1024]{1,0:T(8,128)(2,1)S(1)}, bf16[64,1024]{1,0:T(8,128)(2,1)S(1)}, u32[]{:S(2)}, u32[]{:S(2)}) collective-permute-start(bf16[64,1024]{1,0:T(8,128)(2,1)S(1)} %dynamic-slice_bitcast_fusion.5), channel_id=1, source_target_pairs={{0,4},{1,5},{2,6},{3,7},{4,0},{5,1},{6,2},{7,3},{8,12},{9,13},{10,... | collective-permute-start | bytes 393224 | tf_op jit(solution)/shard_map/ppermute | solution.py:116
  186.7 3.9 %collective-permute-start.21 = (bf16[64,1024]{1,0:T(8,128)(2,1)S(1)}, bf16[64,1024]{1,0:T(8,128)(2,1)S(1)}, u32[]{:S(2)}, u32[]{:S(2)}) collective-permute-start(bf16[64,1024]{1,0:T(8,128)(2,1)S(1)} %dynamic-slice_bitcast_fusion.4), channel_id=1, source_target_pairs={{0,16},{8,24},{16,0},{24,8},{1,17},{9,25},{17,1},{25,9},{2,18},{10... | collective-permute-start | bytes 393224 | tf_op jit(solution)/shard_map/ppermute | solution.py:116
  190.7 5.3 %collective-permute-start.22 = (bf16[64,2048]{1,0:T(8,128)(2,1)S(1)}, bf16[64,2048]{1,0:T(8,128)(2,1)S(1)}, u32[]{:S(2)}, u32[]{:S(2)}) collective-permute-start(bf16[64,2048]{1,0:T(8,128)(2,1)S(1)} %pad_maximum_fusion.20), channel_id=1, source_target_pairs={{0,16},{8,24},{16,0},{24,8},{1,17},{9,25},{17,1},{25,9},{2,18},{10... | collective-permute-start | bytes 786440 | tf_op jit(solution)/shard_map/ppermute | solution.py:116
  196.1 8.0 %collective-permute-start.23 = (bf16[128,2048]{1,0:T(8,128)(2,1)S(1)}, bf16[128,2048]{1,0:T(8,128)(2,1)S(1)}, u32[]{:S(2)}, u32[]{:S(2)}) collective-permute-start(bf16[128,2048]{1,0:T(8,128)(2,1)S(1)} %maximum_select_fusion), channel_id=1, source_target_pairs={{0,8},{8,0},{16,24},{24,16},{1,9},{9,1},{17,25},{25,17},{2,10},{10... | collective-permute-start | bytes 1572872 | tf_op jit(solution)/shard_map/ppermute | solution.py:116
  (32 other events, 230.5 us)

commit v14 on v12

--- a/solution.py
+++ b/solution.py
@@ -152,7 +152,7 @@
     if seq_bits >= 2:
         orders = [
             seq_dims[:2] + dp_dims + seq_dims[2:],
-            seq_dims[1::-1] + seq_dims[2:] + dp_dims,
+            dp_dims + seq_dims,
         ]
     else:
         orders = [seq_dims + dp_dims] * 2

time: 181 us -> 177 us (0.978)
  starting transfers between devices: 35.4 us -> 32 us
    ppermute x12, starting transfers between devices: 21.1 us -> 17.7 us  [exchange(): lax.ppermute(array, axis, [(i, i ^ mask) for i in range(lax.axis_size(axi...]
  transfers between devices with their start and end apart: 24 -> 24, of which waited for: 12 -> 11; matrix products, arithmetic and copies ran while one was open for 22% -> 23% of each run, Pallas kernels for 17% -> 18%
where the time goes in v14:
time: 177 us; the launch traced here: 176 us
  waiting for transfers between devices  52.1 us (29%)
  matrix products  32.5 us (18%)
  starting transfers between devices  32 us (18%)
  Pallas kernels  31.2 us (18%)
  local copies, waits for them, and re-layouts  17.4 us (10%)
  other arithmetic  7.25 us (4%)
  between operations  3.39 us (2%)
    ppermute x12, waiting for transfers between devices, exchange(): lax.ppermute(array, axis, [(i, i ^ mask) for i in range(lax.axis_size(axi...  43 us
    pallas_call x2, Pallas kernels, attention(): pl.pallas_call(functools.partial(attention_kernel, head=head, scale=head...  31.2 us
    ppermute x12, starting transfers between devices, exchange(): lax.ppermute(array, axis, [(i, i ^ mask) for i in range(lax.axis_size(axi...  17.7 us
    ppermute x12, starting transfers between devices, partner(): lax.ppermute(array, axis, [(i, i ^ 1 << apart) for i in range(lax.axis_si...  14.3 us
    dot_general x4, matrix products, term(): jnp.dot(left.T, right[:, lo:hi], preferred_element_type=jnp.float32)  11.9 us
    ppermute x12, waiting for transfers between devices, partner(): lax.ppermute(array, axis, [(i, i ^ 1 << apart) for i in range(lax.axis_si...  9.13 us
    unnamed x77, local copies, waits for them, and re-layouts  7.5 us
    dot_general x1, matrix products, body(): jnp.dot(rows, w_query, preferred_element_type=jnp.float32)  4.14 us
  transfers between devices with their start and end apart: 24, of which 11 were waited for; matrix products, arithmetic and copies ran while one was open for 23% of the time, Pallas kernels for 18%

profile of v14, /device:TPU:1, one launch (start us, length us, event | category | flops | bytes accessed | tf_op | source)
XLA Modules:
  0.0 175.9 jit_solution(2070066974105403356)
XLA Ops:
  4.1 3.3 %convolution_convert_fusion.4.k_ref = bf16[512,1024]{1,0:T(8,128)(2,1)S(1)} fusion(bf16[1024,1024]{1,0:T(8,128)(2,1)} %param.9, bf16[1,512,1024]{2,1,0:T(8,128)(2,1)} %param.7), kind=kOutput, calls=%fused_computation.13 | convolution fusion | flops 1074266112 | bytes 4194304 | tf_op jit(solution)/shard_map/dot_general | solution.py:206
  9.9 2.1 %collective-permute-start = (bf16[2,128,512]{2,1,0:T(8,128)(2,1)S(1)}, bf16[2,128,512]{2,1,0:T(8,128)(2,1)}, u32[]{:S(2)}, u32[]{:S(2)}) collective-permute-start(bf16[2,128,512]{2,1,0:T(8,128)(2,1)S(1)} %pad_maximum_fusion.10), channel_id=1, source_target_pairs={{0,1},{1,0},{2,3},{3,2},{4,5},{5,4},{6,7},{7,6},{8,9},{9,8},{10,11... | collective-permute-start | bytes 786440 | tf_op jit(solution)/shard_map/ppermute | solution.py:16
  13.4 2.4 %collective-permute-start.2 = (bf16[2,128,512]{2,1,0:T(8,128)(2,1)S(1)}, bf16[2,128,512]{2,1,0:T(8,128)(2,1)}, u32[]{:S(2)}, u32[]{:S(2)}) collective-permute-start(bf16[2,128,512]{2,1,0:T(8,128)(2,1)S(1)} %pad_maximum_fusion.12), channel_id=1, source_target_pairs={{0,4},{1,5},{2,6},{3,7},{4,0},{5,1},{6,2},{7,3},{8,12},{9,13},{10,... | collective-permute-start | bytes 786440 | tf_op jit(solution)/shard_map/ppermute | solution.py:16
  15.8 4.1 %convolution_convert_fusion.5.q_ref = bf16[512,1024]{1,0:T(8,128)(2,1)} fusion(bf16[1024,1024]{1,0:T(8,128)(2,1)} %param.8, bf16[1,512,1024]{2,1,0:T(8,128)(2,1)} %param.7), kind=kOutput, calls=%fused_computation.14 | convolution fusion | flops 1074266112 | bytes 4194304 | tf_op jit(solution)/shard_map/dot_general | solution.py:205
  19.9 3.5 %convolution_convert_fusion.2.do_ref = bf16[512,1024]{1,0:T(8,128)(2,1)} fusion(bf16[1024,1024]{1,0:T(8,128)(2,1)S(1)} %copy-done, bf16[1,512,1024]{2,1,0:T(8,128)(2,1)} %param.13), kind=kOutput, calls=%fused_computation.11 | convolution fusion | flops 1074266112 | bytes 4194304 | tf_op jit(solution)/shard_map/dot_general | solution.py:213
  24.6 2.5 %collective-permute-start.5 = (bf16[2,128,512]{2,1,0:T(8,128)(2,1)S(1)}, bf16[2,128,512]{2,1,0:T(8,128)(2,1)S(1)}, u32[]{:S(2)}, u32[]{:S(2)}) collective-permute-start(bf16[2,128,512]{2,1,0:T(8,128)(2,1)S(1)} %pad_maximum_fusion.15), channel_id=1, source_target_pairs={{0,4},{1,5},{2,6},{3,7},{4,0},{5,1},{6,2},{7,3},{8,12},{9,13},{10,... | collective-permute-start | bytes 786440 | tf_op jit(solution)/shard_map/ppermute | solution.py:16
  27.7 15.6 %shard_map.118 = (bf16[512,512]{1,0:T(8,128)(2,1)}, bf16[512,512]{1,0:T(8,128)(2,1)}, f32[512,512]{1,0:T(8,128)}, f32[512,512]{1,0:T(8,128)}, bf16[3,2,128,512]{3,2,1,0:T(8,128)(2,1)}) custom-call(bf16[512,1024]{1,0:T(8,128)(2,1)} %convolution_convert_fusion.5.q_ref, bf16[512,1024]{1,0:T(8,128)(2,1)} %copy-done.9, bf16[512,1024]{1,0:T(8,128)(2,1)} %copy-done.10, ...), custom_call_target="tpu_custom_call" | custom-call | flops 5637144576 | bytes 6553600 | tf_op jit(solution)/shard_map/pallas_call | solution.py:94
  51.5 15.6 %shard_map.119 = (bf16[512,512]{1,0:T(8,128)(2,1)}, bf16[512,512]{1,0:T(8,128)(2,1)}, f32[512,512]{1,0:T(8,128)}, f32[512,512]{1,0:T(8,128)}, bf16[3,2,128,512]{3,2,1,0:T(8,128)(2,1)}) custom-call(bf16[512,1024]{1,0:T(8,128)(2,1)} %convolution_convert_fusion.5.q_ref, bf16[512,1024]{1,0:T(8,128)(2,1)} %copy-done.9, bf16[512,1024]{1,0:T(8,128)(2,1)} %copy-done.10, ...), custom_call_target="tpu_custom_call" | custom-call | flops 5637144576 | bytes 6553600 | tf_op jit(solution)/shard_map/pallas_call | solution.py:94
  75.8 4.7 %collective-permute-done.11 = bf16[2,128,512]{2,1,0:T(8,128)(2,1)S(1)} collective-permute-done((bf16[2,128,512]{2,1,0:T(8,128)(2,1)S(1)}, bf16[2,128,512]{2,1,0:T(8,128)(2,1)S(1)}, u32[]{:S(2)}, u32[]{:S(2)}) %collective-permute-start.11) | collective-permute-done | bytes 262176 | tf_op jit(solution)/shard_map/ppermute | solution.py:16
  82.6 2.7 %convert_bitcast_fusion = bf16[1024,1024]{1,0:T(8,128)(2,1)} fusion(bf16[1,512,1024]{2,1,0:T(8,128)(2,1)S(1)} %copy-done.28, bf16[512,1024]{1,0:T(8,128)(2,1)S(1)} %constant_dynamic-update-slice_fusion, pred[]{:T(512)S(6)} %eq.17, bf16[512,512]{1,0:T(8,128)(2,1)S(1)} %convert_element_type.207, bf16[512,512]{1,0:T(8,128)(2,1)S(1)} %convert_element_type.206), kind=kOutput, calls=%fused_computation.7 | convolution fusion | flops 1077411840 | bytes 5242881 | tf_op jit(solution)/shard_map/dot_general | solution.py:124
  85.3 5.2 %collective-permute-start.12 = (bf16[1024,1024]{1,0:T(8,128)(2,1)}, bf16[1024,1024]{1,0:T(8,128)(2,1)}, u32[]{:S(2)}, u32[]{:S(2)}) collective-permute-start(bf16[1024,1024]{1,0:T(8,128)(2,1)} %convert_bitcast_fusion), channel_id=1, source_target_pairs={{0,8},{8,0},{16,24},{24,16},{1,9},{9,1},{17,25},{25,17},{2,10},{10... | collective-permute-start | bytes 6291464 | tf_op jit(solution)/shard_map/ppermute | solution.py:116
  90.7 2.7 %convolution_convert_fusion = bf16[1024,1024]{1,0:T(8,128)(2,1)} fusion(bf16[1,512,1024]{2,1,0:T(8,128)(2,1)S(1)} %copy-done.30, bf16[1,512,1024]{2,1,0:T(8,128)(2,1)S(1)} %copy-done.28, pred[]{:T(512)S(6)} %eq.17, bf16[1,512,512]{2,1,0:T(8,128)(2,1)S(1)} %convert_bitcast_fusion.2, bf16[1,512,512]{2,1,0:T(8,128)(2,1)S(1)} %convert_bitcast_fusion.1, ...), kind=kOutput, calls=%fused_computation.9 | convolution fusion | flops 1080033280 | bytes 6291457 | tf_op jit(solution)/shard_map/dot_general | solution.py:124
  95.0 3.5 %fusion = bf16[1024,1024]{1,0:T(8,128)(2,1)S(1)} fusion(bf16[1024,1024]{1,0:T(8,128)(2,1)} %collective-permute-done.12, bf16[1,512,1024]{2,1,0:T(8,128)(2,1)} %param.7, bf16[512,1024]{1,0:T(8,128)(2,1)} %copy-done.21, pred[]{:T(512)S(6)} %eq.17, bf16[512,512]{1,0:T(8,128)(2,1)} %copy-done.13, bf16[512,512]{1,0:T(8,128)(2,1)} %copy-done.11), kind=kOutput, calls=%fused_computation.1 | convolution fusion | flops 1081606144 | bytes 7340033 | tf_op jit(solution)/shard_map/dot_general | solution.py:124
  102.2 3.0 %add_convert_fusion = bf16[1024,1024]{1,0:T(8,128)(2,1)S(1)} fusion(bf16[1024,1024]{1,0:T(8,128)(2,1)} %collective-permute-done.17, bf16[1,512,1024]{2,1,0:T(8,128)(2,1)S(1)} %copy-done.31, bf16[1,512,1024]{2,1,0:T(8,128)(2,1)S(1)} %copy-done.29, pred[]{:T(512)S(6)} %eq.17, bf16[1,512,512]{2,1,0:T(8,128)(2,1)S(1)} %copy-done.18, ...), kind=kOutput, calls=%fused_computation.2 | convolution fusion | flops 1084227584 | bytes 8388609 | tf_op jit(solution)/shard_map/dot_general | solution.py:124
  108.7 3.5 %fusion.3 = bf16[1,512,1024]{2,1,0:T(8,128)(2,1)} fusion(bf16[1024,1024]{1,0:T(8,128)(2,1)S(1)} %copy-done, bf16[512,512]{1,0:T(8,128)(2,1)} %get-tuple-element.21, bf16[512,512]{1,0:T(8,128)(2,1)} %get-tuple-element.18), kind=kOutput, calls=%fused_computation.15 | convolution fusion | flops 1076363264 | bytes 4194304 | tf_op jit(solution)/shard_map/dot_general | solution.py:220
  112.2 13.4 %collective-permute-done.13 = bf16[2,2,2,64,1024]{4,3,0,2,1:T(8,128)(2,1)} collective-permute-done((bf16[2,2,2,64,1024]{4,3,0,2,1:T(8,128)(2,1)}, bf16[2,2,2,64,1024]{4,3,0,2,1:T(8,128)(2,1)}, u32[]{:S(2)}, u32[]{:S(2)}) %collective-permute-start.13) | collective-permute-done | bytes 1048608 | tf_op jit(solution)/shard_map/ppermute | solution.py:116
  127.5 4.4 %collective-permute-done.18 = bf16[2,2,2,64,1024]{4,3,0,1,2:T(8,128)(2,1)} collective-permute-done((bf16[2,2,2,64,1024]{4,3,0,1,2:T(8,128)(2,1)}, bf16[2,2,2,64,1024]{4,3,0,1,2:T(8,128)(2,1)}, u32[]{:S(2)}, u32[]{:S(2)}) %collective-permute-start.18) | collective-permute-done | bytes 1048608 | tf_op jit(solution)/shard_map/ppermute | solution.py:116
  137.5 2.1 %collective-permute-done.14 = bf16[2,2,64,1024]{3,2,0,1:T(8,128)(2,1)S(1)} collective-permute-done((bf16[2,2,64,1024]{3,2,0,1:T(8,128)(2,1)S(1)}, bf16[2,2,64,1024]{3,2,0,1:T(8,128)(2,1)S(1)}, u32[]{:S(2)}, u32[]{:S(2)}) %collective-permute-start.14) | collective-permute-done | bytes 524320 | tf_op jit(solution)/shard_map/ppermute | solution.py:116
  141.3 4.4 %collective-permute-done.19 = bf16[2,2,64,1024]{3,2,0,1:T(8,128)(2,1)S(1)} collective-permute-done((bf16[2,2,64,1024]{3,2,0,1:T(8,128)(2,1)S(1)}, bf16[2,2,64,1024]{3,2,0,1:T(8,128)(2,1)S(1)}, u32[]{:S(2)}, u32[]{:S(2)}) %collective-permute-start.19) | collective-permute-done | bytes 524320 | tf_op jit(solution)/shard_map/ppermute | solution.py:116
  147.9 7.7 %collective-permute-done.20 = bf16[2,64,1024]{2,1,0:T(8,128)(2,1)S(1)} collective-permute-done((bf16[2,64,1024]{2,1,0:T(8,128)(2,1)S(1)}, bf16[2,64,1024]{2,1,0:T(8,128)(2,1)S(1)}, u32[]{:S(2)}, u32[]{:S(2)}) %collective-permute-start.20) | collective-permute-done | bytes 262176 | tf_op jit(solution)/shard_map/ppermute | solution.py:116
  156.0 7.2 %collective-permute-done.21 = bf16[64,1024]{1,0:T(8,128)(2,1)S(1)} collective-permute-done((bf16[64,1024]{1,0:T(8,128)(2,1)S(1)}, bf16[64,1024]{1,0:T(8,128)(2,1)S(1)}, u32[]{:S(2)}, u32[]{:S(2)}) %collective-permute-start.21) | collective-permute-done | bytes 131104 | tf_op jit(solution)/shard_map/ppermute | solution.py:116
  165.9 3.8 %collective-permute-done.22 = bf16[64,2048]{1,0:T(8,128)(2,1)S(1)} collective-permute-done((bf16[64,2048]{1,0:T(8,128)(2,1)S(1)}, bf16[64,2048]{1,0:T(8,128)(2,1)S(1)}, u32[]{:S(2)}, u32[]{:S(2)}) %collective-permute-start.22) | collective-permute-done | bytes 262176 | tf_op jit(solution)/shard_map/ppermute | solution.py:116
  169.8 2.5 %collective-permute-start.23 = (bf16[128,2048]{1,0:T(8,128)(2,1)S(1)}, bf16[128,2048]{1,0:T(8,128)(2,1)S(1)}, u32[]{:S(2)}, u32[]{:S(2)}) collective-permute-start(bf16[128,2048]{1,0:T(8,128)(2,1)S(1)} %maximum_select_fusion), channel_id=1, source_target_pairs={{0,8},{8,0},{16,24},{24,16},{1,9},{9,1},{17,25},{25,17},{2,10},{10... | collective-permute-start | bytes 1572872 | tf_op jit(solution)/shard_map/ppermute | solution.py:116
  172.2 2.3 %fusion.4 = bf16[1,512,1024]{2,1,0:T(8,128)(2,1)} fusion(f32[512,1024]{1,0:T(8,128)S(1)} %fusion.36, f32[512,1024]{1,0:T(8,128)S(1)} %fusion.8, bf16[512,1024]{1,0:T(8,128)(2,1)S(1)} %copy-done.22, bf16[1024,1024]{1,0:T(8,128)(2,1)S(1)} %copy-done.26), kind=kOutput, calls=%fused_computation.16 | convolution fusion | flops 1075314688 | bytes 8388608 | tf_op jit(solution)/shard_map/dot_general | solution.py:240
  (173 shorter events, 50.3 us)
Async XLA Ops:
  9.9 13.6 %collective-permute-start = (bf16[2,128,512]{2,1,0:T(8,128)(2,1)S(1)}, bf16[2,128,512]{2,1,0:T(8,128)(2,1)}, u32[]{:S(2)}, u32[]{:S(2)}) collective-permute-start(bf16[2,128,512]{2,1,0:T(8,128)(2,1)S(1)} %pad_maximum_fusion.10), channel_id=1, source_target_pairs={{0,1},{1,0},{2,3},{3,2},{4,5},{5,4},{6,7},{7,6},{8,9},{9,8},{10,11... | collective-permute-start | bytes 786440 | tf_op jit(solution)/shard_map/ppermute | solution.py:16
  12.0 12.4 %collective-permute-start.1 = (bf16[2,128,512]{2,1,0:T(8,128)(2,1)S(1)}, bf16[2,128,512]{2,1,0:T(8,128)(2,1)}, u32[]{:S(2)}, u32[]{:S(2)}) collective-permute-start(bf16[2,128,512]{2,1,0:T(8,128)(2,1)S(1)} %pad_maximum_fusion.11), channel_id=1, source_target_pairs={{0,2},{1,3},{2,0},{3,1},{4,6},{5,7},{6,4},{7,5},{8,10},{9,11},{10,... | collective-permute-start | bytes 786440 | tf_op jit(solution)/shard_map/ppermute | solution.py:16
  13.4 11.0 %collective-permute-start.2 = (bf16[2,128,512]{2,1,0:T(8,128)(2,1)S(1)}, bf16[2,128,512]{2,1,0:T(8,128)(2,1)}, u32[]{:S(2)}, u32[]{:S(2)}) collective-permute-start(bf16[2,128,512]{2,1,0:T(8,128)(2,1)S(1)} %pad_maximum_fusion.12), channel_id=1, source_target_pairs={{0,4},{1,5},{2,6},{3,7},{4,0},{5,1},{6,2},{7,3},{8,12},{9,13},{10,... | collective-permute-start | bytes 786440 | tf_op jit(solution)/shard_map/ppermute | solution.py:16
  24.6 25.2 %collective-permute-start.5 = (bf16[2,128,512]{2,1,0:T(8,128)(2,1)S(1)}, bf16[2,128,512]{2,1,0:T(8,128)(2,1)S(1)}, u32[]{:S(2)}, u32[]{:S(2)}) collective-permute-start(bf16[2,128,512]{2,1,0:T(8,128)(2,1)S(1)} %pad_maximum_fusion.15), channel_id=1, source_target_pairs={{0,4},{1,5},{2,6},{3,7},{4,0},{5,1},{6,2},{7,3},{8,12},{9,13},{10,... | collective-permute-start | bytes 786440 | tf_op jit(solution)/shard_map/ppermute | solution.py:16
  27.1 23.7 %collective-permute-start.4 = (bf16[2,128,512]{2,1,0:T(8,128)(2,1)S(1)}, bf16[2,128,512]{2,1,0:T(8,128)(2,1)S(1)}, u32[]{:S(2)}, u32[]{:S(2)}) collective-permute-start(bf16[2,128,512]{2,1,0:T(8,128)(2,1)S(1)} %pad_maximum_fusion.14), channel_id=1, source_target_pairs={{0,2},{1,3},{2,0},{3,1},{4,6},{5,7},{6,4},{7,5},{8,10},{9,11},{10,... | collective-permute-start | bytes 786440 | tf_op jit(solution)/shard_map/ppermute | solution.py:16
  27.4 23.4 %collective-permute-start.3 = (bf16[2,128,512]{2,1,0:T(8,128)(2,1)S(1)}, bf16[2,128,512]{2,1,0:T(8,128)(2,1)}, u32[]{:S(2)}, u32[]{:S(2)}) collective-permute-start(bf16[2,128,512]{2,1,0:T(8,128)(2,1)S(1)} %pad_maximum_fusion.13), channel_id=1, source_target_pairs={{0,1},{1,0},{2,3},{3,2},{4,5},{5,4},{6,7},{7,6},{8,9},{9,8},{10,11... | collective-permute-start | bytes 786440 | tf_op jit(solution)/shard_map/ppermute | solution.py:16
  45.4 24.9 %collective-permute-start.6 = (bf16[2,128,512]{2,1,0:T(8,128)(2,1)}, bf16[2,128,512]{2,1,0:T(8,128)(2,1)S(1)}, u32[]{:S(2)}, u32[]{:S(2)}) collective-permute-start(bf16[2,128,512]{2,1,0:T(8,128)(2,1)} %get-tuple-element.40), channel_id=1, source_target_pairs={{0,1},{1,0},{2,3},{3,2},{4,5},{5,4},{6,7},{7,6},{8,9},{9,8},{10,11... | collective-permute-start | bytes 786440 | tf_op jit(solution)/shard_map/ppermute | solution.py:16
  46.6 24.0 %collective-permute-start.7 = (bf16[2,128,512]{2,1,0:T(8,128)(2,1)}, bf16[2,128,512]{2,1,0:T(8,128)(2,1)S(1)}, u32[]{:S(2)}, u32[]{:S(2)}) collective-permute-start(bf16[2,128,512]{2,1,0:T(8,128)(2,1)} %get-tuple-element.39), channel_id=1, source_target_pairs={{0,2},{1,3},{2,0},{3,1},{4,6},{5,7},{6,4},{7,5},{8,10},{9,11},{10,... | collective-permute-start | bytes 786440 | tf_op jit(solution)/shard_map/ppermute | solution.py:16
  49.8 22.1 %collective-permute-start.8 = (bf16[2,128,512]{2,1,0:T(8,128)(2,1)}, bf16[2,128,512]{2,1,0:T(8,128)(2,1)S(1)}, u32[]{:S(2)}, u32[]{:S(2)}) collective-permute-start(bf16[2,128,512]{2,1,0:T(8,128)(2,1)} %get-tuple-element.38), channel_id=1, source_target_pairs={{0,4},{1,5},{2,6},{3,7},{4,0},{5,1},{6,2},{7,3},{8,12},{9,13},{10,... | collective-permute-start | bytes 786440 | tf_op jit(solution)/shard_map/ppermute | solution.py:16
  68.5 5.3 %collective-permute-start.9 = (bf16[2,128,512]{2,1,0:T(8,128)(2,1)S(1)}, bf16[2,128,512]{2,1,0:T(8,128)(2,1)S(1)}, u32[]{:S(2)}, u32[]{:S(2)}) collective-permute-start(bf16[2,128,512]{2,1,0:T(8,128)(2,1)S(1)} %get-tuple-element.43), channel_id=1, source_target_pairs={{0,1},{1,0},{2,3},{3,2},{4,5},{5,4},{6,7},{7,6},{8,9},{9,8},{10,11... | collective-permute-start | bytes 786440 | tf_op jit(solution)/shard_map/ppermute | solution.py:16
  68.8 6.8 %collective-permute-start.10 = (bf16[2,128,512]{2,1,0:T(8,128)(2,1)S(1)}, bf16[2,128,512]{2,1,0:T(8,128)(2,1)S(1)}, u32[]{:S(2)}, u32[]{:S(2)}) collective-permute-start(bf16[2,128,512]{2,1,0:T(8,128)(2,1)S(1)} %get-tuple-element.42), channel_id=1, source_target_pairs={{0,2},{1,3},{2,0},{3,1},{4,6},{5,7},{6,4},{7,5},{8,10},{9,11},{10,... | collective-permute-start | bytes 786440 | tf_op jit(solution)/shard_map/ppermute | solution.py:16
  70.3 10.2 %collective-permute-start.11 = (bf16[2,128,512]{2,1,0:T(8,128)(2,1)S(1)}, bf16[2,128,512]{2,1,0:T(8,128)(2,1)S(1)}, u32[]{:S(2)}, u32[]{:S(2)}) collective-permute-start(bf16[2,128,512]{2,1,0:T(8,128)(2,1)S(1)} %get-tuple-element.41), channel_id=1, source_target_pairs={{0,4},{1,5},{2,6},{3,7},{4,0},{5,1},{6,2},{7,3},{8,12},{9,13},{10,... | collective-permute-start | bytes 786440 | tf_op jit(solution)/shard_map/ppermute | solution.py:16
  85.3 9.7 %collective-permute-start.12 = (bf16[1024,1024]{1,0:T(8,128)(2,1)}, bf16[1024,1024]{1,0:T(8,128)(2,1)}, u32[]{:S(2)}, u32[]{:S(2)}) collective-permute-start(bf16[1024,1024]{1,0:T(8,128)(2,1)} %convert_bitcast_fusion), channel_id=1, source_target_pairs={{0,8},{8,0},{16,24},{24,16},{1,9},{9,1},{17,25},{25,17},{2,10},{10... | collective-permute-start | bytes 6291464 | tf_op jit(solution)/shard_map/ppermute | solution.py:116
  93.4 8.8 %collective-permute-start.17 = (bf16[1024,1024]{1,0:T(8,128)(2,1)}, bf16[1024,1024]{1,0:T(8,128)(2,1)}, u32[]{:S(2)}, u32[]{:S(2)}) collective-permute-start(bf16[1024,1024]{1,0:T(8,128)(2,1)} %convolution_convert_fusion), channel_id=1, source_target_pairs={{0,8},{8,0},{16,24},{24,16},{1,9},{9,1},{17,25},{25,17},{2,10},{10... | collective-permute-start | bytes 6291464 | tf_op jit(solution)/shard_map/ppermute | solution.py:116
  101.0 24.7 %collective-permute-start.13 = (bf16[2,2,2,64,1024]{4,3,0,2,1:T(8,128)(2,1)}, bf16[2,2,2,64,1024]{4,3,0,2,1:T(8,128)(2,1)}, u32[]{:S(2)}, u32[]{:S(2)}) collective-permute-start(bf16[2,2,2,64,1024]{4,3,0,2,1:T(8,128)(2,1)} %bitcast.209), channel_id=1, source_target_pairs={{0,1},{1,0},{2,3},{3,2},{4,5},{5,4},{6,7},{7,6},{8,9},{9,8},{10,11... | collective-permute-start | bytes 3145736 | tf_op jit(solution)/shard_map/ppermute | solution.py:116
  107.5 24.4 %collective-permute-start.18 = (bf16[2,2,2,64,1024]{4,3,0,1,2:T(8,128)(2,1)}, bf16[2,2,2,64,1024]{4,3,0,1,2:T(8,128)(2,1)}, u32[]{:S(2)}, u32[]{:S(2)}) collective-permute-start(bf16[2,2,2,64,1024]{4,3,0,1,2:T(8,128)(2,1)} %bitcast.208), channel_id=1, source_target_pairs={{0,16},{8,24},{16,0},{24,8},{1,17},{9,25},{17,1},{25,9},{2,18},{10... | collective-permute-start | bytes 3145736 | tf_op jit(solution)/shard_map/ppermute | solution.py:116
  127.4 12.3 %collective-permute-start.14 = (bf16[2,2,64,1024]{3,2,0,1:T(8,128)(2,1)S(1)}, bf16[2,2,64,1024]{3,2,0,1:T(8,128)(2,1)S(1)}, u32[]{:S(2)}, u32[]{:S(2)}) collective-permute-start(bf16[2,2,64,1024]{3,2,0,1:T(8,128)(2,1)S(1)} %dynamic-slice_bitcast_fusion.1), channel_id=1, source_target_pairs={{0,2},{1,3},{2,0},{3,1},{4,6},{5,7},{6,4},{7,5},{8,10},{9,11},{10,... | collective-permute-start | bytes 1572872 | tf_op jit(solution)/shard_map/ppermute | solution.py:116
  133.7 12.0 %collective-permute-start.19 = (bf16[2,2,64,1024]{3,2,0,1:T(8,128)(2,1)S(1)}, bf16[2,2,64,1024]{3,2,0,1:T(8,128)(2,1)S(1)}, u32[]{:S(2)}, u32[]{:S(2)}) collective-permute-start(bf16[2,2,64,1024]{3,2,0,1:T(8,128)(2,1)S(1)} %dynamic-slice_bitcast_fusion), channel_id=1, source_target_pairs={{0,1},{1,0},{2,3},{3,2},{4,5},{5,4},{6,7},{7,6},{8,9},{9,8},{10,11... | collective-permute-start | bytes 1572872 | tf_op jit(solution)/shard_map/ppermute | solution.py:116
  139.9 6.1 %collective-permute-start.15 = (bf16[2,64,1024]{2,1,0:T(8,128)(2,1)S(1)}, bf16[2,64,1024]{2,1,0:T(8,128)(2,1)S(1)}, u32[]{:S(2)}, u32[]{:S(2)}) collective-permute-start(bf16[2,64,1024]{2,1,0:T(8,128)(2,1)S(1)} %dynamic-slice_bitcast_fusion.3), channel_id=1, source_target_pairs={{0,16},{8,24},{16,0},{24,8},{1,17},{9,25},{17,1},{25,9},{2,18},{10... | collective-permute-start | bytes 786440 | tf_op jit(solution)/shard_map/ppermute | solution.py:116
  145.9 9.6 %collective-permute-start.20 = (bf16[2,64,1024]{2,1,0:T(8,128)(2,1)S(1)}, bf16[2,64,1024]{2,1,0:T(8,128)(2,1)S(1)}, u32[]{:S(2)}, u32[]{:S(2)}) collective-permute-start(bf16[2,64,1024]{2,1,0:T(8,128)(2,1)S(1)} %dynamic-slice_bitcast_fusion.2), channel_id=1, source_target_pairs={{0,2},{1,3},{2,0},{3,1},{4,6},{5,7},{6,4},{7,5},{8,10},{9,11},{10,... | collective-permute-start | bytes 786440 | tf_op jit(solution)/shard_map/ppermute | solution.py:116
  146.1 9.9 %collective-permute-start.16 = (bf16[64,1024]{1,0:T(8,128)(2,1)S(1)}, bf16[64,1024]{1,0:T(8,128)(2,1)S(1)}, u32[]{:S(2)}, u32[]{:S(2)}) collective-permute-start(bf16[64,1024]{1,0:T(8,128)(2,1)S(1)} %dynamic-slice_bitcast_fusion.5), channel_id=1, source_target_pairs={{0,4},{1,5},{2,6},{3,7},{4,0},{5,1},{6,2},{7,3},{8,12},{9,13},{10,... | collective-permute-start | bytes 393224 | tf_op jit(solution)/shard_map/ppermute | solution.py:116
  155.7 7.5 %collective-permute-start.21 = (bf16[64,1024]{1,0:T(8,128)(2,1)S(1)}, bf16[64,1024]{1,0:T(8,128)(2,1)S(1)}, u32[]{:S(2)}, u32[]{:S(2)}) collective-permute-start(bf16[64,1024]{1,0:T(8,128)(2,1)S(1)} %dynamic-slice_bitcast_fusion.4), channel_id=1, source_target_pairs={{0,4},{1,5},{2,6},{3,7},{4,0},{5,1},{6,2},{7,3},{8,12},{9,13},{10,... | collective-permute-start | bytes 393224 | tf_op jit(solution)/shard_map/ppermute | solution.py:116
  163.3 6.4 %collective-permute-start.22 = (bf16[64,2048]{1,0:T(8,128)(2,1)S(1)}, bf16[64,2048]{1,0:T(8,128)(2,1)S(1)}, u32[]{:S(2)}, u32[]{:S(2)}) collective-permute-start(bf16[64,2048]{1,0:T(8,128)(2,1)S(1)} %pad_maximum_fusion.16), channel_id=1, source_target_pairs={{0,16},{8,24},{16,0},{24,8},{1,17},{9,25},{17,1},{25,9},{2,18},{10... | collective-permute-start | bytes 786440 | tf_op jit(solution)/shard_map/ppermute | solution.py:116
  169.8 4.7 %collective-permute-start.23 = (bf16[128,2048]{1,0:T(8,128)(2,1)S(1)}, bf16[128,2048]{1,0:T(8,128)(2,1)S(1)}, u32[]{:S(2)}, u32[]{:S(2)}) collective-permute-start(bf16[128,2048]{1,0:T(8,128)(2,1)S(1)} %maximum_select_fusion), channel_id=1, source_target_pairs={{0,8},{8,0},{16,24},{24,16},{1,9},{9,1},{17,25},{25,17},{2,10},{10... | collective-permute-start | bytes 1572872 | tf_op jit(solution)/shard_map/ppermute | solution.py:116
  (40 other events, 188.7 us)

commit v15 on v14

--- a/solution.py
+++ b/solution.py
@@ -205,7 +205,7 @@
     query = jnp.dot(rows, w_query, preferred_element_type=jnp.float32).astype(jnp.bfloat16)
     keys_local = jnp.dot(rows, w_key, preferred_element_type=jnp.float32).astype(jnp.bfloat16)
     values_local = jnp.dot(rows, w_value, preferred_element_type=jnp.float32).astype(jnp.bfloat16)
-    half = (width // LANES) // 2 * LANES
+    half = (width // LANES) * 3 // 8 * LANES
     spans = [(0, half), (half, width)]
     remotes = [swap_blocks(keys_local, values_local, offsets, levels, *spans[0])]
     later_keys, later_values, _ = lax.optimization_barrier((keys_local, values_local, remotes[0]))

time: 177 us -> 200 us (1.13)
  waiting for transfers between devices: 52.1 us -> 69.6 us
  other arithmetic: 7.25 us -> 15.9 us
  local copies, waits for them, and re-layouts: 17.4 us -> 14.4 us
    ppermute x12, waiting for transfers between devices: 9.13 us -> 24.8 us  [partner(): lax.ppermute(array, axis, [(i, i ^ 1 << apart) for i in range(lax.axis_si...]
    dynamic_update_slice x5 -> x6, other arithmetic: 0.78 us -> 6.19 us  [body(): lax.dynamic_update_slice_in_dim(dkey_sum, lax.dynamic_slice_in_dim(dkey_s...]
    ppermute x12, starting transfers between devices: 17.7 us -> 20.6 us  [exchange(): lax.ppermute(array, axis, [(i, i ^ mask) for i in range(lax.axis_size(axi...]
    ppermute x12, starting transfers between devices: 14.3 us -> 11.6 us  [partner(): lax.ppermute(array, axis, [(i, i ^ 1 << apart) for i in range(lax.axis_si...]
    unnamed x77, local copies, waits for them, and re-layouts: 7.5 us -> 5.29 us
  transfers between devices with their start and end apart: 24 -> 24, of which waited for: 11 -> 14; matrix products, arithmetic and copies ran while one was open for 23% -> 23% of each run, Pallas kernels for 18% -> 6%
where the time goes in v15:
time: 200 us
  waiting for transfers between devices  69.6 us (35%)
  matrix products  32.9 us (16%)
  starting transfers between devices  32.3 us (16%)
  Pallas kernels  31.4 us (16%)
  other arithmetic  15.9 us (8%)
  local copies, waits for them, and re-layouts  14.4 us (7%)
  between operations  3.32 us (2%)
    ppermute x12, waiting for transfers between devices, exchange(): lax.ppermute(array, axis, [(i, i ^ mask) for i in range(lax.axis_size(axi...  44.8 us
    pallas_call x2, Pallas kernels, attention(): pl.pallas_call(functools.partial(attention_kernel, head=head, scale=head...  31.4 us
    ppermute x12, waiting for transfers between devices, partner(): lax.ppermute(array, axis, [(i, i ^ 1 << apart) for i in range(lax.axis_si...  24.8 us
    ppermute x12, starting transfers between devices, exchange(): lax.ppermute(array, axis, [(i, i ^ mask) for i in range(lax.axis_size(axi...  20.6 us
    dot_general x4, matrix products, term(): jnp.dot(left.T, right[:, lo:hi], preferred_element_type=jnp.float32)  12.2 us
    ppermute x12, starting transfers between devices, partner(): lax.ppermute(array, axis, [(i, i ^ 1 << apart) for i in range(lax.axis_si...  11.6 us
    dynamic_update_slice x6, other arithmetic, body(): lax.dynamic_update_slice_in_dim(dkey_sum, lax.dynamic_slice_in_dim(dkey_s...  6.19 us
    unnamed x77, local copies, waits for them, and re-layouts  5.29 us
  transfers between devices with their start and end apart: 24, of which 14 were waited for; matrix products, arithmetic and copies ran while one was open for 23% of the time, Pallas kernels for 6%

profile of v15, /device:TPU:1, one launch (start us, length us, event | category | flops | bytes accessed | tf_op | source)
XLA Modules:
  0.0 199.8 jit_solution(13067088949885623969)
XLA Ops:
  4.0 3.3 %convolution_convert_fusion.4.k_ref = bf16[512,1024]{1,0:T(8,128)(2,1)S(1)} fusion(bf16[1024,1024]{1,0:T(8,128)(2,1)} %param.9, bf16[1,512,1024]{2,1,0:T(8,128)(2,1)} %param.7), kind=kOutput, calls=%fused_computation.13 | convolution fusion | flops 1074266112 | bytes 4194304 | tf_op jit(solution)/shard_map/dot_general | solution.py:206
  9.9 2.1 %collective-permute-start = (bf16[2,128,384]{2,1,0:T(8,128)(2,1)S(1)}, bf16[2,128,384]{2,1,0:T(8,128)(2,1)S(1)}, u32[]{:S(2)}, u32[]{:S(2)}) collective-permute-start(bf16[2,128,384]{2,1,0:T(8,128)(2,1)S(1)} %pad_maximum_fusion.14), channel_id=1, source_target_pairs={{0,1},{1,0},{2,3},{3,2},{4,5},{5,4},{6,7},{7,6},{8,9},{9,8},{10,11... | collective-permute-start | bytes 589832 | tf_op jit(solution)/shard_map/ppermute | solution.py:16
  13.4 2.4 %collective-permute-start.2 = (bf16[2,128,384]{2,1,0:T(8,128)(2,1)S(1)}, bf16[2,128,384]{2,1,0:T(8,128)(2,1)S(1)}, u32[]{:S(2)}, u32[]{:S(2)}) collective-permute-start(bf16[2,128,384]{2,1,0:T(8,128)(2,1)S(1)} %pad_maximum_fusion.16), channel_id=1, source_target_pairs={{0,4},{1,5},{2,6},{3,7},{4,0},{5,1},{6,2},{7,3},{8,12},{9,13},{10,... | collective-permute-start | bytes 589832 | tf_op jit(solution)/shard_map/ppermute | solution.py:16
  15.8 4.1 %convolution_convert_fusion.5.q_ref = bf16[512,1024]{1,0:T(8,128)(2,1)} fusion(bf16[1024,1024]{1,0:T(8,128)(2,1)} %param.8, bf16[1,512,1024]{2,1,0:T(8,128)(2,1)} %param.7), kind=kOutput, calls=%fused_computation.14 | convolution fusion | flops 1074266112 | bytes 4194304 | tf_op jit(solution)/shard_map/dot_general | solution.py:205
  19.9 3.7 %convolution_convert_fusion.2.do_ref = bf16[512,1024]{1,0:T(8,128)(2,1)} fusion(bf16[1024,1024]{1,0:T(8,128)(2,1)S(1)} %copy-done, bf16[1,512,1024]{2,1,0:T(8,128)(2,1)} %param.13), kind=kOutput, calls=%fused_computation.11 | convolution fusion | flops 1074266112 | bytes 4194304 | tf_op jit(solution)/shard_map/dot_general | solution.py:213
  24.8 12.3 %shard_map.118 = (bf16[512,384]{1,0:T(8,128)(2,1)}, bf16[512,384]{1,0:T(8,128)(2,1)}, f32[512,384]{1,0:T(8,128)}, f32[512,384]{1,0:T(8,128)}, bf16[3,2,128,384]{3,2,1,0:T(8,128)(2,1)}) custom-call(bf16[512,1024]{1,0:T(8,128)(2,1)} %convolution_convert_fusion.5.q_ref, bf16[512,1024]{1,0:T(8,128)(2,1)} %copy-done.5, bf16[512,1024]{1,0:T(8,128)(2,1)} %copy-done.7, ...), custom_call_target="tpu_custom_call" | custom-call | flops 4227858432 | bytes 4915200 | tf_op jit(solution)/shard_map/pallas_call | solution.py:94
  45.4 14.4 %collective-permute-done.7 = bf16[2,128,384]{2,1,0:T(8,128)(2,1)S(1)} collective-permute-done((bf16[2,128,384]{2,1,0:T(8,128)(2,1)S(1)}, bf16[2,128,384]{2,1,0:T(8,128)(2,1)S(1)}, u32[]{:S(2)}, u32[]{:S(2)}) %collective-permute-start.7) | collective-permute-done | bytes 196640 | tf_op jit(solution)/shard_map/ppermute | solution.py:16
  65.0 19.1 %shard_map.119 = (bf16[512,640]{1,0:T(8,128)(2,1)}, bf16[512,640]{1,0:T(8,128)(2,1)}, f32[512,640]{1,0:T(8,128)}, f32[512,640]{1,0:T(8,128)}, bf16[3,2,128,640]{3,2,1,0:T(8,128)(2,1)}) custom-call(bf16[512,1024]{1,0:T(8,128)(2,1)} %convolution_convert_fusion.5.q_ref, bf16[512,1024]{1,0:T(8,128)(2,1)} %copy-done.5, bf16[512,1024]{1,0:T(8,128)(2,1)} %copy-done.7, ...), custom_call_target="tpu_custom_call" | custom-call | flops 7046430720 | bytes 8192000 | tf_op jit(solution)/shard_map/pallas_call | solution.py:94
  91.5 5.9 %collective-permute-done.10 = bf16[2,128,640]{2,1,0:T(8,128)(2,1)S(1)} collective-permute-done((bf16[2,128,640]{2,1,0:T(8,128)(2,1)S(1)}, bf16[2,128,640]{2,1,0:T(8,128)(2,1)S(1)}, u32[]{:S(2)}, u32[]{:S(2)}) %collective-permute-start.10) | collective-permute-done | bytes 327712 | tf_op jit(solution)/shard_map/ppermute | solution.py:16
  100.1 2.6 %convolution_convert_fusion = bf16[1024,1024]{1,0:T(8,128)(2,1)} fusion(bf16[1,512,1024]{2,1,0:T(8,128)(2,1)S(1)} %copy-done.26, bf16[1,512,1024]{2,1,0:T(8,128)(2,1)S(1)} %copy-done.28, pred[]{:T(512)S(6)} %eq.17, bf16[1,512,640]{2,1,0:T(8,128)(2,1)S(1)} %convert_bitcast_fusion.2, bf16[1,512,384]{2,1,0:T(8,128)(2,1)S(1)} %convert_bitcast_fusion.1, ...), kind=kOutput, calls=%fused_computation.9 | convolution fusion | flops 1080033280 | bytes 6291457 | tf_op jit(solution)/shard_map/dot_general | solution.py:124
  102.7 9.2 %collective-permute-start.17 = (bf16[1024,1024]{1,0:T(8,128)(2,1)}, bf16[1024,1024]{1,0:T(8,128)(2,1)}, u32[]{:S(2)}, u32[]{:S(2)}) collective-permute-start(bf16[1024,1024]{1,0:T(8,128)(2,1)} %convolution_convert_fusion), channel_id=1, source_target_pairs={{0,8},{8,0},{16,24},{24,16},{1,9},{9,1},{17,25},{25,17},{2,10},{10... | collective-permute-start | bytes 6291464 | tf_op jit(solution)/shard_map/ppermute | solution.py:116
  113.5 2.7 %convert_bitcast_fusion = bf16[1024,1024]{1,0:T(8,128)(2,1)} fusion(bf16[1,512,1024]{2,1,0:T(8,128)(2,1)S(1)} %copy-done.28, bf16[512,1024]{1,0:T(8,128)(2,1)S(1)} %constant_dynamic-update-slice_fusion, pred[]{:T(512)S(6)} %eq.17, bf16[512,640]{1,0:T(8,128)(2,1)S(1)} %convert_element_type.207, bf16[512,384]{1,0:T(8,128)(2,1)S(1)} %convert_element_type.206), kind=kOutput, calls=%fused_computation.7 | convolution fusion | flops 1077411840 | bytes 5242881 | tf_op jit(solution)/shard_map/dot_general | solution.py:124
  116.4 3.9 %add_convert_fusion = bf16[1024,1024]{1,0:T(8,128)(2,1)S(1)} fusion(bf16[1024,1024]{1,0:T(8,128)(2,1)} %collective-permute-done.17, bf16[1,512,1024]{2,1,0:T(8,128)(2,1)} %param.13, bf16[1,512,1024]{2,1,0:T(8,128)(2,1)} %param.7, pred[]{:T(512)S(6)} %eq.17, bf16[1,512,640]{2,1,0:T(8,128)(2,1)} %copy-done.13, bf16[1,512,384]{2,1,0:T(8,128)(2,1)} %copy-done.18, ...), kind=kOutput, calls=%fused_computation.2 | convolution fusion | flops 1084227584 | bytes 8388609 | tf_op jit(solution)/shard_map/dot_general | solution.py:124
  123.8 2.9 %fusion = bf16[1024,1024]{1,0:T(8,128)(2,1)S(1)} fusion(bf16[1024,1024]{1,0:T(8,128)(2,1)} %collective-permute-done.12, bf16[1,512,1024]{2,1,0:T(8,128)(2,1)S(1)} %copy-done.29, bf16[512,1024]{1,0:T(8,128)(2,1)S(1)} %copy-done.20, pred[]{:T(512)S(6)} %eq.17, bf16[512,640]{1,0:T(8,128)(2,1)S(1)} %copy-done.11, bf16[512,384]{1,0:T(8,128)(2,1)S(1)} %copy-done.16), kind=kOutput, calls=%fused_computation.1 | convolution fusion | flops 1081606144 | bytes 7340033 | tf_op jit(solution)/shard_map/dot_general | solution.py:124
  131.1 3.5 %fusion.3 = bf16[1,512,1024]{2,1,0:T(8,128)(2,1)} fusion(bf16[1024,1024]{1,0:T(8,128)(2,1)S(1)} %copy-done, bf16[512,640]{1,0:T(8,128)(2,1)} %get-tuple-element.21, bf16[512,384]{1,0:T(8,128)(2,1)} %get-tuple-element.18), kind=kOutput, calls=%fused_computation.15 | convolution fusion | flops 1076363264 | bytes 4194304 | tf_op jit(solution)/shard_map/dot_general | solution.py:220
  134.6 12.6 %collective-permute-done.18 = bf16[2,2,2,64,1024]{4,3,0,1,2:T(8,128)(2,1)} collective-permute-done((bf16[2,2,2,64,1024]{4,3,0,1,2:T(8,128)(2,1)}, bf16[2,2,2,64,1024]{4,3,0,1,2:T(8,128)(2,1)}, u32[]{:S(2)}, u32[]{:S(2)}) %collective-permute-start.18) | collective-permute-done | bytes 1048608 | tf_op jit(solution)/shard_map/ppermute | solution.py:116
  149.9 3.4 %collective-permute-done.13 = bf16[2,2,2,64,1024]{4,3,0,2,1:T(8,128)(2,1)} collective-permute-done((bf16[2,2,2,64,1024]{4,3,0,2,1:T(8,128)(2,1)}, bf16[2,2,2,64,1024]{4,3,0,2,1:T(8,128)(2,1)}, u32[]{:S(2)}, u32[]{:S(2)}) %collective-permute-start.13) | collective-permute-done | bytes 1048608 | tf_op jit(solution)/shard_map/ppermute | solution.py:116
  156.9 7.5 %collective-permute-done.19 = bf16[2,2,64,1024]{3,2,0,1:T(8,128)(2,1)S(1)} collective-permute-done((bf16[2,2,64,1024]{3,2,0,1:T(8,128)(2,1)S(1)}, bf16[2,2,64,1024]{3,2,0,1:T(8,128)(2,1)S(1)}, u32[]{:S(2)}, u32[]{:S(2)}) %collective-permute-start.19) | collective-permute-done | bytes 524320 | tf_op jit(solution)/shard_map/ppermute | solution.py:116
  168.0 5.1 %collective-permute-done.20 = bf16[2,64,1024]{2,1,0:T(8,128)(2,1)S(1)} collective-permute-done((bf16[2,64,1024]{2,1,0:T(8,128)(2,1)S(1)}, bf16[2,64,1024]{2,1,0:T(8,128)(2,1)S(1)}, u32[]{:S(2)}, u32[]{:S(2)}) %collective-permute-start.20) | collective-permute-done | bytes 262176 | tf_op jit(solution)/shard_map/ppermute | solution.py:116
  175.8 8.4 %collective-permute-done.21 = bf16[64,1024]{1,0:T(8,128)(2,1)S(1)} collective-permute-done((bf16[64,1024]{1,0:T(8,128)(2,1)S(1)}, bf16[64,1024]{1,0:T(8,128)(2,1)S(1)}, u32[]{:S(2)}, u32[]{:S(2)}) %collective-permute-start.21) | collective-permute-done | bytes 131104 | tf_op jit(solution)/shard_map/ppermute | solution.py:116
  184.3 2.8 %collective-permute-done.16 = bf16[64,1024]{1,0:T(8,128)(2,1)S(1)} collective-permute-done((bf16[64,1024]{1,0:T(8,128)(2,1)S(1)}, bf16[64,1024]{1,0:T(8,128)(2,1)S(1)}, u32[]{:S(2)}, u32[]{:S(2)}) %collective-permute-start.16) | collective-permute-done | bytes 131104 | tf_op jit(solution)/shard_map/ppermute | solution.py:116
  189.7 3.8 %collective-permute-done.22 = bf16[64,2048]{1,0:T(8,128)(2,1)S(1)} collective-permute-done((bf16[64,2048]{1,0:T(8,128)(2,1)S(1)}, bf16[64,2048]{1,0:T(8,128)(2,1)S(1)}, u32[]{:S(2)}, u32[]{:S(2)}) %collective-permute-start.22) | collective-permute-done | bytes 262176 | tf_op jit(solution)/shard_map/ppermute | solution.py:116
  193.6 2.5 %collective-permute-start.23 = (bf16[128,2048]{1,0:T(8,128)(2,1)S(1)}, bf16[128,2048]{1,0:T(8,128)(2,1)S(1)}, u32[]{:S(2)}, u32[]{:S(2)}) collective-permute-start(bf16[128,2048]{1,0:T(8,128)(2,1)S(1)} %maximum_select_fusion), channel_id=1, source_target_pairs={{0,8},{8,0},{16,24},{24,16},{1,9},{9,1},{17,25},{25,17},{2,10},{10... | collective-permute-start | bytes 1572872 | tf_op jit(solution)/shard_map/ppermute | solution.py:116
  196.1 2.3 %fusion.4 = bf16[1,512,1024]{2,1,0:T(8,128)(2,1)} fusion(f32[512,1024]{1,0:T(8,128)S(1)} %fusion.48, f32[512,1024]{1,0:T(8,128)S(1)} %fusion.8, bf16[512,1024]{1,0:T(8,128)(2,1)S(1)} %copy-done.21, bf16[1024,1024]{1,0:T(8,128)(2,1)S(1)} %copy-done.25), kind=kOutput, calls=%fused_computation.16 | convolution fusion | flops 1075314688 | bytes 8388608 | tf_op jit(solution)/shard_map/dot_general | solution.py:240
  (171 shorter events, 55.8 us)
Async XLA Ops:
  9.9 13.7 %collective-permute-start = (bf16[2,128,384]{2,1,0:T(8,128)(2,1)S(1)}, bf16[2,128,384]{2,1,0:T(8,128)(2,1)S(1)}, u32[]{:S(2)}, u32[]{:S(2)}) collective-permute-start(bf16[2,128,384]{2,1,0:T(8,128)(2,1)S(1)} %pad_maximum_fusion.14), channel_id=1, source_target_pairs={{0,1},{1,0},{2,3},{3,2},{4,5},{5,4},{6,7},{7,6},{8,9},{9,8},{10,11... | collective-permute-start | bytes 589832 | tf_op jit(solution)/shard_map/ppermute | solution.py:16
  12.0 11.6 %collective-permute-start.1 = (bf16[2,128,384]{2,1,0:T(8,128)(2,1)S(1)}, bf16[2,128,384]{2,1,0:T(8,128)(2,1)S(1)}, u32[]{:S(2)}, u32[]{:S(2)}) collective-permute-start(bf16[2,128,384]{2,1,0:T(8,128)(2,1)S(1)} %pad_maximum_fusion.15), channel_id=1, source_target_pairs={{0,2},{1,3},{2,0},{3,1},{4,6},{5,7},{6,4},{7,5},{8,10},{9,11},{10,... | collective-permute-start | bytes 589832 | tf_op jit(solution)/shard_map/ppermute | solution.py:16
  13.4 10.2 %collective-permute-start.2 = (bf16[2,128,384]{2,1,0:T(8,128)(2,1)S(1)}, bf16[2,128,384]{2,1,0:T(8,128)(2,1)S(1)}, u32[]{:S(2)}, u32[]{:S(2)}) collective-permute-start(bf16[2,128,384]{2,1,0:T(8,128)(2,1)S(1)} %pad_maximum_fusion.16), channel_id=1, source_target_pairs={{0,4},{1,5},{2,6},{3,7},{4,0},{5,1},{6,2},{7,3},{8,12},{9,13},{10,... | collective-permute-start | bytes 589832 | tf_op jit(solution)/shard_map/ppermute | solution.py:16
  24.5 38.9 %collective-permute-start.3 = (bf16[2,128,640]{2,1,0:T(8,128)(2,1)S(1)}, bf16[2,128,640]{2,1,0:T(8,128)(2,1)S(1)}, u32[]{:S(2)}, u32[]{:S(2)}) collective-permute-start(bf16[2,128,640]{2,1,0:T(8,128)(2,1)S(1)} %pad_maximum_fusion.7), channel_id=1, source_target_pairs={{0,1},{1,0},{2,3},{3,2},{4,5},{5,4},{6,7},{7,6},{8,9},{9,8},{10,11... | collective-permute-start | bytes 983048 | tf_op jit(solution)/shard_map/ppermute | solution.py:16
  38.3 4.6 %collective-permute-start.6 = (bf16[2,128,384]{2,1,0:T(8,128)(2,1)S(1)}, bf16[2,128,384]{2,1,0:T(8,128)(2,1)S(1)}, u32[]{:S(2)}, u32[]{:S(2)}) collective-permute-start(bf16[2,128,384]{2,1,0:T(8,128)(2,1)S(1)} %get-tuple-element.55), channel_id=1, source_target_pairs={{0,1},{1,0},{2,3},{3,2},{4,5},{5,4},{6,7},{7,6},{8,9},{9,8},{10,11... | collective-permute-start | bytes 589832 | tf_op jit(solution)/shard_map/ppermute | solution.py:16
  39.5 23.9 %collective-permute-start.4 = (bf16[2,128,640]{2,1,0:T(8,128)(2,1)S(1)}, bf16[2,128,640]{2,1,0:T(8,128)(2,1)S(1)}, u32[]{:S(2)}, u32[]{:S(2)}) collective-permute-start(bf16[2,128,640]{2,1,0:T(8,128)(2,1)S(1)} %pad_maximum_fusion.8), channel_id=1, source_target_pairs={{0,2},{1,3},{2,0},{3,1},{4,6},{5,7},{6,4},{7,5},{8,10},{9,11},{10,... | collective-permute-start | bytes 983048 | tf_op jit(solution)/shard_map/ppermute | solution.py:16
  39.9 23.4 %collective-permute-start.5 = (bf16[2,128,640]{2,1,0:T(8,128)(2,1)S(1)}, bf16[2,128,640]{2,1,0:T(8,128)(2,1)S(1)}, u32[]{:S(2)}, u32[]{:S(2)}) collective-permute-start(bf16[2,128,640]{2,1,0:T(8,128)(2,1)S(1)} %pad_maximum_fusion.9), channel_id=1, source_target_pairs={{0,4},{1,5},{2,6},{3,7},{4,0},{5,1},{6,2},{7,3},{8,12},{9,13},{10,... | collective-permute-start | bytes 983048 | tf_op jit(solution)/shard_map/ppermute | solution.py:16
  40.1 19.6 %collective-permute-start.7 = (bf16[2,128,384]{2,1,0:T(8,128)(2,1)S(1)}, bf16[2,128,384]{2,1,0:T(8,128)(2,1)S(1)}, u32[]{:S(2)}, u32[]{:S(2)}) collective-permute-start(bf16[2,128,384]{2,1,0:T(8,128)(2,1)S(1)} %get-tuple-element.54), channel_id=1, source_target_pairs={{0,2},{1,3},{2,0},{3,1},{4,6},{5,7},{6,4},{7,5},{8,10},{9,11},{10,... | collective-permute-start | bytes 589832 | tf_op jit(solution)/shard_map/ppermute | solution.py:16
  42.9 18.6 %collective-permute-start.8 = (bf16[2,128,384]{2,1,0:T(8,128)(2,1)S(1)}, bf16[2,128,384]{2,1,0:T(8,128)(2,1)S(1)}, u32[]{:S(2)}, u32[]{:S(2)}) collective-permute-start(bf16[2,128,384]{2,1,0:T(8,128)(2,1)S(1)} %get-tuple-element.53), channel_id=1, source_target_pairs={{0,4},{1,5},{2,6},{3,7},{4,0},{5,1},{6,2},{7,3},{8,12},{9,13},{10,... | collective-permute-start | bytes 589832 | tf_op jit(solution)/shard_map/ppermute | solution.py:16
  85.3 6.0 %collective-permute-start.9 = (bf16[2,128,640]{2,1,0:T(8,128)(2,1)S(1)}, bf16[2,128,640]{2,1,0:T(8,128)(2,1)S(1)}, u32[]{:S(2)}, u32[]{:S(2)}) collective-permute-start(bf16[2,128,640]{2,1,0:T(8,128)(2,1)S(1)} %get-tuple-element.40), channel_id=1, source_target_pairs={{0,1},{1,0},{2,3},{3,2},{4,5},{5,4},{6,7},{7,6},{8,9},{9,8},{10,11... | collective-permute-start | bytes 983048 | tf_op jit(solution)/shard_map/ppermute | solution.py:16
  87.8 9.6 %collective-permute-start.10 = (bf16[2,128,640]{2,1,0:T(8,128)(2,1)S(1)}, bf16[2,128,640]{2,1,0:T(8,128)(2,1)S(1)}, u32[]{:S(2)}, u32[]{:S(2)}) collective-permute-start(bf16[2,128,640]{2,1,0:T(8,128)(2,1)S(1)} %get-tuple-element.39), channel_id=1, source_target_pairs={{0,2},{1,3},{2,0},{3,1},{4,6},{5,7},{6,4},{7,5},{8,10},{9,11},{10,... | collective-permute-start | bytes 983048 | tf_op jit(solution)/shard_map/ppermute | solution.py:16
  89.0 8.9 %collective-permute-start.11 = (bf16[2,128,640]{2,1,0:T(8,128)(2,1)S(1)}, bf16[2,128,640]{2,1,0:T(8,128)(2,1)S(1)}, u32[]{:S(2)}, u32[]{:S(2)}) collective-permute-start(bf16[2,128,640]{2,1,0:T(8,128)(2,1)S(1)} %get-tuple-element.38), channel_id=1, source_target_pairs={{0,4},{1,5},{2,6},{3,7},{4,0},{5,1},{6,2},{7,3},{8,12},{9,13},{10,... | collective-permute-start | bytes 983048 | tf_op jit(solution)/shard_map/ppermute | solution.py:16
  102.7 13.6 %collective-permute-start.17 = (bf16[1024,1024]{1,0:T(8,128)(2,1)}, bf16[1024,1024]{1,0:T(8,128)(2,1)}, u32[]{:S(2)}, u32[]{:S(2)}) collective-permute-start(bf16[1024,1024]{1,0:T(8,128)(2,1)} %convolution_convert_fusion), channel_id=1, source_target_pairs={{0,8},{8,0},{16,24},{24,16},{1,9},{9,1},{17,25},{25,17},{2,10},{10... | collective-permute-start | bytes 6291464 | tf_op jit(solution)/shard_map/ppermute | solution.py:116
  116.2 7.6 %collective-permute-start.12 = (bf16[1024,1024]{1,0:T(8,128)(2,1)}, bf16[1024,1024]{1,0:T(8,128)(2,1)}, u32[]{:S(2)}, u32[]{:S(2)}) collective-permute-start(bf16[1024,1024]{1,0:T(8,128)(2,1)} %convert_bitcast_fusion), channel_id=1, source_target_pairs={{0,8},{8,0},{16,24},{24,16},{1,9},{9,1},{17,25},{25,17},{2,10},{10... | collective-permute-start | bytes 6291464 | tf_op jit(solution)/shard_map/ppermute | solution.py:116
  122.6 24.6 %collective-permute-start.18 = (bf16[2,2,2,64,1024]{4,3,0,1,2:T(8,128)(2,1)}, bf16[2,2,2,64,1024]{4,3,0,1,2:T(8,128)(2,1)}, u32[]{:S(2)}, u32[]{:S(2)}) collective-permute-start(bf16[2,2,2,64,1024]{4,3,0,1,2:T(8,128)(2,1)} %bitcast.208), channel_id=1, source_target_pairs={{0,16},{8,24},{16,0},{24,8},{1,17},{9,25},{17,1},{25,9},{2,18},{10... | collective-permute-start | bytes 3145736 | tf_op jit(solution)/shard_map/ppermute | solution.py:116
  129.0 24.3 %collective-permute-start.13 = (bf16[2,2,2,64,1024]{4,3,0,2,1:T(8,128)(2,1)}, bf16[2,2,2,64,1024]{4,3,0,2,1:T(8,128)(2,1)}, u32[]{:S(2)}, u32[]{:S(2)}) collective-permute-start(bf16[2,2,2,64,1024]{4,3,0,2,1:T(8,128)(2,1)} %bitcast.209), channel_id=1, source_target_pairs={{0,1},{1,0},{2,3},{3,2},{4,5},{5,4},{6,7},{7,6},{8,9},{9,8},{10,11... | collective-permute-start | bytes 3145736 | tf_op jit(solution)/shard_map/ppermute | solution.py:116
  148.9 15.5 %collective-permute-start.19 = (bf16[2,2,64,1024]{3,2,0,1:T(8,128)(2,1)S(1)}, bf16[2,2,64,1024]{3,2,0,1:T(8,128)(2,1)S(1)}, u32[]{:S(2)}, u32[]{:S(2)}) collective-permute-start(bf16[2,2,64,1024]{3,2,0,1:T(8,128)(2,1)S(1)} %dynamic-slice_bitcast_fusion), channel_id=1, source_target_pairs={{0,1},{1,0},{2,3},{3,2},{4,5},{5,4},{6,7},{7,6},{8,9},{9,8},{10,11... | collective-permute-start | bytes 1572872 | tf_op jit(solution)/shard_map/ppermute | solution.py:116
  155.2 10.7 %collective-permute-start.14 = (bf16[2,2,64,1024]{3,2,0,1:T(8,128)(2,1)S(1)}, bf16[2,2,64,1024]{3,2,0,1:T(8,128)(2,1)S(1)}, u32[]{:S(2)}, u32[]{:S(2)}) collective-permute-start(bf16[2,2,64,1024]{3,2,0,1:T(8,128)(2,1)S(1)} %dynamic-slice_bitcast_fusion.1), channel_id=1, source_target_pairs={{0,2},{1,3},{2,0},{3,1},{4,6},{5,7},{6,4},{7,5},{8,10},{9,11},{10,... | collective-permute-start | bytes 1572872 | tf_op jit(solution)/shard_map/ppermute | solution.py:116
  164.7 8.5 %collective-permute-start.20 = (bf16[2,64,1024]{2,1,0:T(8,128)(2,1)S(1)}, bf16[2,64,1024]{2,1,0:T(8,128)(2,1)S(1)}, u32[]{:S(2)}, u32[]{:S(2)}) collective-permute-start(bf16[2,64,1024]{2,1,0:T(8,128)(2,1)S(1)} %dynamic-slice_bitcast_fusion.2), channel_id=1, source_target_pairs={{0,2},{1,3},{2,0},{3,1},{4,6},{5,7},{6,4},{7,5},{8,10},{9,11},{10,... | collective-permute-start | bytes 786440 | tf_op jit(solution)/shard_map/ppermute | solution.py:116
  166.1 8.5 %collective-permute-start.15 = (bf16[2,64,1024]{2,1,0:T(8,128)(2,1)S(1)}, bf16[2,64,1024]{2,1,0:T(8,128)(2,1)S(1)}, u32[]{:S(2)}, u32[]{:S(2)}) collective-permute-start(bf16[2,64,1024]{2,1,0:T(8,128)(2,1)S(1)} %dynamic-slice_bitcast_fusion.3), channel_id=1, source_target_pairs={{0,16},{8,24},{16,0},{24,8},{1,17},{9,25},{17,1},{25,9},{2,18},{10... | collective-permute-start | bytes 786440 | tf_op jit(solution)/shard_map/ppermute | solution.py:116
  173.2 11.0 %collective-permute-start.21 = (bf16[64,1024]{1,0:T(8,128)(2,1)S(1)}, bf16[64,1024]{1,0:T(8,128)(2,1)S(1)}, u32[]{:S(2)}, u32[]{:S(2)}) collective-permute-start(bf16[64,1024]{1,0:T(8,128)(2,1)S(1)} %dynamic-slice_bitcast_fusion.10), channel_id=1, source_target_pairs={{0,4},{1,5},{2,6},{3,7},{4,0},{5,1},{6,2},{7,3},{8,12},{9,13},{10,... | collective-permute-start | bytes 393224 | tf_op jit(solution)/shard_map/ppermute | solution.py:116
  174.7 12.4 %collective-permute-start.16 = (bf16[64,1024]{1,0:T(8,128)(2,1)S(1)}, bf16[64,1024]{1,0:T(8,128)(2,1)S(1)}, u32[]{:S(2)}, u32[]{:S(2)}) collective-permute-start(bf16[64,1024]{1,0:T(8,128)(2,1)S(1)} %dynamic-slice_bitcast_fusion.11), channel_id=1, source_target_pairs={{0,4},{1,5},{2,6},{3,7},{4,0},{5,1},{6,2},{7,3},{8,12},{9,13},{10,... | collective-permute-start | bytes 393224 | tf_op jit(solution)/shard_map/ppermute | solution.py:116
  187.1 6.4 %collective-permute-start.22 = (bf16[64,2048]{1,0:T(8,128)(2,1)S(1)}, bf16[64,2048]{1,0:T(8,128)(2,1)S(1)}, u32[]{:S(2)}, u32[]{:S(2)}) collective-permute-start(bf16[64,2048]{1,0:T(8,128)(2,1)S(1)} %pad_maximum_fusion.13), channel_id=1, source_target_pairs={{0,16},{8,24},{16,0},{24,8},{1,17},{9,25},{17,1},{25,9},{2,18},{10... | collective-permute-start | bytes 786440 | tf_op jit(solution)/shard_map/ppermute | solution.py:116
  193.6 4.8 %collective-permute-start.23 = (bf16[128,2048]{1,0:T(8,128)(2,1)S(1)}, bf16[128,2048]{1,0:T(8,128)(2,1)S(1)}, u32[]{:S(2)}, u32[]{:S(2)}) collective-permute-start(bf16[128,2048]{1,0:T(8,128)(2,1)S(1)} %maximum_select_fusion), channel_id=1, source_target_pairs={{0,8},{8,0},{16,24},{24,16},{1,9},{9,1},{17,25},{25,17},{2,10},{10... | collective-permute-start | bytes 1572872 | tf_op jit(solution)/shard_map/ppermute | solution.py:116
  (38 other events, 184.2 us)
